TPU v7x, 32 devices: a whole 2x2x4 slice. The times are simulated.
32 devices in a mesh: groups: 2 (over y), queue: 4 (over z), dp: 4 (over x, core).
Axes of the slice: x: 2, y: 2, z: 4, core: 2. Of those that a mesh axis runs over, the one named last changes fastest.
Arguments:
- query_inputs: bfloat16 [8192, 1024], P(('groups', 'queue', 'dp')), parts along dimension 0, may hold values from -30 to 30
- key_inputs: bfloat16 [512, 1024], P(('groups', 'queue', 'dp')), parts along dimension 0, may hold values from -6 to 6
- query_weight: bfloat16 [1024, 1024], replicated, may hold values from -4 to 4
- key_weight: bfloat16 [1024, 1024], replicated, may hold values from -0.1875 to 0.1875
- queue_keys: bfloat16 [2048, 1024], P(('groups', 'queue')), parts along dimension 0, may hold values from -2 to 2
- write_pointer: int32 [2], P('groups'), parts along dimension 0, may hold values from 0 to 255
- slot_owner: int32 [32], P('groups'), parts along dimension 0, may hold values from 0 to 15, each once
- positive_index: int32 [8192], P(('groups', 'queue', 'dp')), parts along dimension 0, may hold values from 0 to 1023
Outputs:
- loss: float32 [8192], P(('groups', 'queue', 'dp')), parts along dimension 0
- query_weight_grad: float32 [2048, 1024], P(('groups', 'queue', 'dp')), parts along dimension 0
- new_queue: bfloat16 [2048, 1024], P(('groups', 'queue')), parts along dimension 0
There are 2 independent parts, one for each index of `groups`. A program takes and returns all parts, laid end to end along the dimension named above; an argument that names none is the same for every part. Nothing has to cross between parts.
Inputs may be any that keep to these rules, and one draw needn't show every extreme that they name: slot_owner is a permutation of 0 to 15.
All inputs are finite; a program needn't handle non-finite values.
Results may differ from a plain program's by a relative error of at most 0.0075.
Values may be sent and summed in bfloat16 or wider, within the bound.
No kernel may reach another device: no remote copies, remote signals or barrier semaphores. Data moves between devices by JAX's collectives and lax.ppermute only.
A program may use at most 192 MiB of HBM per device.

v0:
```python
import jax
import jax.numpy as jnp
from jax import lax
from jax.sharding import PartitionSpec as P

temper = 0.05


def make_fold(units, mapped):

    def fold(carry, piece, start):
        top, total, mixture, chosen = carry
        scores = (
            lax.dot_general(
                units, piece, (((1,), (1,)), ((), ())), preferred_element_type=jnp.float32
            )
            / temper
        )
        new_top = jnp.maximum(top, jnp.max(scores, -1))
        expo = jnp.exp(scores - new_top[:, None])
        total = jnp.sum(expo, -1)
        mixture = jnp.dot(expo.astype(jnp.bfloat16), piece, preferred_element_type=jnp.float32)
        count = piece.shape[0]
        hit = (mapped >= 0) & (mapped < count)
        picked = jnp.take(piece, jnp.clip(mapped, 0, count - 1), axis=0).astype(jnp.float32)
        chosen = jnp.where(hit[:, None], picked, 0.0)
        return (new_top, total, mixture, chosen)

    return fold


def start_carry(count, width):
    return (
        jnp.full((count,), -1e30, jnp.float32),
        jnp.zeros((count,), jnp.float32),
        jnp.zeros((count, width), jnp.float32),
        jnp.zeros((count, width), jnp.float32),
    )


def body(
    query_inputs,
    key_inputs,
    query_weight,
    key_weight,
    queue_keys,
    write_pointer,
    slot_owner,
    positive_index,
):
    q_dev, width = query_inputs.shape
    k_dev = queue_keys.shape[0]
    new_dev = key_inputs.shape[0]
    n_dp = lax.axis_size("dp")
    query = jnp.dot(query_inputs, query_weight, preferred_element_type=jnp.float32)
    inv_len = lax.rsqrt(jnp.sum(query * query, -1, keepdims=True) + 1e-06)
    unit_f = query * inv_len
    unit = unit_f.astype(jnp.bfloat16)
    fold = make_fold(unit, positive_index)
    top, total, mixture, chosen = fold(
        start_carry(q_dev, width),
        lax.all_gather(queue_keys, "queue", axis=0, tiled=True),
        jnp.int32(0),
    )
    mixture = mixture / total[:, None]
    positive = jnp.sum(unit.astype(jnp.float32) * chosen, -1) / temper
    loss = top + jnp.log(total) - positive
    grad_unit = (mixture - chosen) / temper
    grad_query = (
        (grad_unit - unit_f * jnp.sum(unit_f * grad_unit, -1, keepdims=True)) * inv_len
    ).astype(jnp.bfloat16)
    n_all = lax.axis_size(("queue", "dp"))
    share = width // n_all
    term = lax.dot_general(
        query_inputs, grad_query, (((0,), (0,)), ((), ())), preferred_element_type=jnp.float32
    )
    summed = lax.psum(term, ("queue", "dp"))
    grad_rows = lax.dynamic_slice_in_dim(summed, lax.axis_index(("queue", "dp")) * share, share, 0)
    fresh = jnp.dot(key_inputs, key_weight, preferred_element_type=jnp.float32)
    fresh = (fresh * lax.rsqrt(jnp.sum(fresh * fresh, -1, keepdims=True) + 1e-06)).astype(
        jnp.bfloat16
    )
    arrived = lax.all_gather(fresh, ("queue", "dp"), axis=0, tiled=True)
    n_blocks = slot_owner.shape[0]
    slots_here = lax.axis_index("queue") * n_dp + jnp.arange(n_dp, dtype=jnp.int32)
    match = slot_owner[None, :] == slots_here[:, None]
    owner_block = jnp.sum(jnp.where(match, jnp.arange(n_blocks, dtype=jnp.int32)[None, :], 0), -1)
    offset = (jnp.arange(k_dev, dtype=jnp.int32) - write_pointer[0]) % k_dev
    live = offset < n_dp * new_dev
    sub_block = jnp.minimum(offset // new_dev, n_dp - 1)
    source = jnp.take(owner_block, sub_block) * new_dev + offset % new_dev
    new_queue = jnp.where(live[:, None], jnp.take(arrived, source, axis=0), queue_keys)
    return (loss, grad_rows, new_queue)


def solution(mesh):
    in_specs = (
        P(("groups", "queue", "dp"), None),
        P(("groups", "queue", "dp"), None),
        P(),
        P(),
        P(("groups", "queue"), None),
        P("groups"),
        P("groups"),
        P(("groups", "queue", "dp")),
    )
    out_specs = (
        P(("groups", "queue", "dp")),
        P(("groups", "queue", "dp"), None),
        P(("groups", "queue"), None),
    )
    return jax.shard_map(body, mesh=mesh, in_specs=in_specs, out_specs=out_specs, check_vma=False)
```

profile of v0, /device:TPU:0, one launch (start us, length us, event | category | flops | bytes accessed | tf_op | source)
XLA Modules:
  0.0 193.4 jit_solution(15796007540766359770)
XLA Ops:
  7.2 0.7 all-gather.2.cloned.1.call-update
  8.6 0.7 compare_select_fusion.9
  9.3 0.7 compare_and_fusion.1
  10.0 1.8 multiply_reduce_fusion.2
  11.9 46.1 %all-gather.2.cloned.1.call-done = bf16[1024,1024]{1,0:T(8,128)(2,1)} async-done(((bf16[256,1024]{1,0:T(8,128)(2,1)}), bf16[1024,1024]{1,0:T(8,128)(2,1)}) %all-gather.2.cloned.1.call-update) | async-done | bytes 2097168 | tf_op jit(solution)/shard_map/all_gather | solution.py:62
  58.0 2.4 %fusion.14 = (f32[256]{0:T(256)S(1)}, f32[256,1024]{1,0:T(8,128)S(1)}) fusion(bf16[1024,1024]{1,0:T(8,128)(2,1)} %all-gather.2.cloned.1.call-done, f32[256,1024]{1,0:T(8,128)S(1)} %get-tuple-element.23, f32[256]{0:T(256)S(1)} %add_rsqrt_fusion), kind=kOutput, calls=%fused_computation.68 | convolution fusion | flops 537919232 | bytes 4196352 | tf_op jit(solution)/shard_map/dot_general | solution.py:14
  60.4 1.0 copy-done.1
  61.4 0.3 fusion.3
  61.7 4.2 %gather_fusion = bf16[256,1024]{1,0:T(8,128)(2,1)} fusion(bf16[1024,1024]{1,0:T(8,128)(2,1)} %all-gather.2.cloned.1.call-done, s32[1024]{0:T(1024)S(1)} %pad_clamp_fusion.1), kind=kCustom, calls=%fused_computation | custom fusion | bytes 1049600 | tf_op jit(solution)/shard_map/jit(_take)/gather | solution.py:25
  65.9 3.1 %multiply_reduce_fusion = (f32[256]{0:T(256)S(1)}, f32[256]{0:T(256)S(1)}, f32[256,1024]{1,0:T(8,128)S(1)}) fusion(f32[256,1024]{1,0:T(8,128)S(1)} %get-tuple-element.23, f32[256]{0:T(256)S(1)} %add_rsqrt_fusion, bf16[256,1024]{1,0:T(8,128)(2,1)} %gather_fusion, pred[256]{0:T(512)(128)(4,1)S(1)} %get-tuple-element.16, ...), kind=kOutput, calls=%fused_computation.8 | convolution fusion | flops 540802560 | bytes 5772800 | tf_op jit(solution)/shard_map/dot_general | solution.py:22
  69.0 3.0 %convolution_bitcast_fusion = f32[1024,1024]{0,1:T(8,128)} fusion(bf16[256,1024]{1,0:T(8,128)(2,1)S(1)} %copy-done.2, f32[256,1024]{1,0:T(8,128)S(1)} %get-tuple-element.26, f32[256,1024]{1,0:T(8,128)S(1)} %get-tuple-element.23, f32[256]{0:T(256)S(1)} %get-tuple-element.12, f32[256]{0:T(256)S(1)} %add_rsqrt_fusion), kind=kOutput, calls=%fused_computation.2 | convolution fusion | flops 538181632 | bytes 6817792 | tf_op jit(solution)/shard_map/dot_general | solution.py:74
  72.0 0.6 copy-done.4
  72.6 0.2 select_reduce_fusion
  72.8 0.6 fusion.13
  73.4 2.5 %compare_select_fusion = (s32[256,1]{0,1:T(1,128)S(1)}, s32[256,1]{0,1:T(1,128)S(1)}) fusion(s32[]{:T(128)} %bitcast.16, s32[]{:T(128)} %bitcast.5, s32[]{:T(128)} %bitcast.4, s32[]{:T(128)} %bitcast.3, s32[]{:T(128)} %bitcast.2), kind=kLoop, calls=%fused_computation.23 | loop fusion | flops 12800 | bytes 2068 | tf_op jit(solution)/shard_map/jit(_take)/jit(_where)/select_n | solution.py:92
  76.0 2.2 %multiply_reduce_fusion.3 = (f32[16]{0:T(128)S(1)}, f32[16,1024]{1,0:T(8,128)S(1)}) fusion(bf16[16,1024]{1,0:T(8,128)(2,1)S(1)} %copy-done.3, bf16[1024,1024]{1,0:T(8,128)(2,1)} %param.11), kind=kOutput, calls=%fused_computation.22 | convolution fusion | flops 33587184 | bytes 2195520 | tf_op jit(solution)/shard_map/dot_general | solution.py:79
  78.2 0.1 multiply_convert_fusion.3
  78.3 23.5 %all_gather.7 = bf16[256,1024]{1,0:T(8,128)(2,1)S(1)} all-gather(bf16[16,1024]{1,0:T(8,128)(2,1)S(1)} %multiply_convert_fusion.3), channel_id=1, replica_groups=mesh['groups'=2,'queue'=4,'dp'=4] {'queue','dp'}, dimensions={0}, use_global_device_ids=true | all-gather | bytes 557056 | tf_op jit(solution)/shard_map/all_gather | solution.py:83
  101.8 1.2 gather_fusion.1
  103.0 2.0 %select_select_fusion = bf16[256,1024]{1,0:T(8,128)(2,1)} fusion(bf16[256,1024]{1,0:T(8,128)(2,1)} %param.12, bf16[256,1024]{1,0:T(8,128)(2,1)S(1)} %gather_fusion.1, pred[256]{0:T(512)(128)(4,1)S(1)} %get-tuple-element.29, pred[256]{0:T(512)(128)(4,1)S(1)} %get-tuple-element.30), kind=kLoop, calls=%fused_computation.16 | loop fusion | flops 524288 | bytes 1573376 | tf_op jit(solution)/shard_map/jit(_where)/select_n | solution.py:92
  105.0 0.6 multiply_subtract_fusion
  105.6 78.9 %all-reduce.2.cloned.1.call-done = f32[1024,1024]{0,1:T(8,128)} async-done(((f32[1024,1024]{0,1:T(8,128)}), f32[1024,1024]{0,1:T(8,128)}) %all-reduce.2.cloned.1.call-update) | async-done | bytes 4194320 | tf_op jit(solution)/shard_map/psum | solution.py:77
  184.5 1.2 constant_dynamic-slice_fusion
  185.7 0.9 copy.13
  (18 shorter events, 0.2 us)
Async XLA Ops:
  7.2 2.8 %copy-start = (bf16[1024,1024]{1,0:T(8,128)(2,1)S(1)}, bf16[1024,1024]{1,0:T(8,128)(2,1)}, u32[]{:S(2)}) copy-start(bf16[1024,1024]{1,0:T(8,128)(2,1)} %param.10) | copy-start | bytes 6291460
  7.2 50.8 %all-gather.2.cloned.1.call-start = ((), (), s32[]{:S(2)}) async-start(), calls=%async_computation | async-start | bytes 2621440 | tf_op jit(solution)/shard_map/all_gather | solution.py:62
  7.9 176.6 %all-reduce.2.cloned.1.call-start = ((), (), s32[]{:S(2)}) async-start(), calls=%async_computation.1 | async-start | bytes 8388608 | tf_op jit(solution)/shard_map/psum | solution.py:77
  60.4 1.0 copy-start.1
  65.9 3.1 %copy-start.2 = (bf16[256,1024]{1,0:T(8,128)(2,1)S(1)}, bf16[256,1024]{1,0:T(8,128)(2,1)}, u32[]{:S(2)}) copy-start(bf16[256,1024]{1,0:T(8,128)(2,1)} %param.8) | copy-start | bytes 1572868
  72.0 0.7 copy-start.4
  72.0 4.0 %copy-start.3 = (bf16[16,1024]{1,0:T(8,128)(2,1)S(1)}, bf16[16,1024]{1,0:T(8,128)(2,1)}, u32[]{:S(2)}) copy-start(bf16[16,1024]{1,0:T(8,128)(2,1)} %param.9) | copy-start | bytes 98308
Sparse Core Ops, SparseCore 0:
  9.6 48.3 all-gather.1
  72.1 112.3 all-reduce.1
where the time goes:
time: 194 us; the launch traced here: 193 us
  waiting for transfers between devices  126 us (65%)
  blocking collectives  23.5 us (12%)
  between operations  14.8 us (8%)
  matrix products  12.6 us (6%)
  local copies, waits for them, and re-layouts  9.73 us (5%)
  other arithmetic  7.09 us (4%)
    psum x1, waiting for transfers between devices, body(): summed = lax.psum(term, ('queue', 'dp'))  78.9 us
    all_gather x1, waiting for transfers between devices, body(): lax.all_gather(queue_keys, 'queue', axis=0, tiled=True)  46.1 us
    all_gather x1, blocking collectives, body(): arrived = lax.all_gather(fresh, ('queue', 'dp'), axis=0, tiled=True)  23.5 us
    gather x1, local copies, waits for them, and re-layouts, fold(): jnp.take(piece, jnp.clip(mapped, 0, count - 1), axis=0).astype(jnp.float32)  4.21 us
  transfers between devices with their start and end apart: 2, of which 2 were waited for; matrix products, arithmetic and copies ran while one was open for 7% of the time, Pallas kernels for 0%

commit v1 on v0

v1 whole, which is shorter than its diff:
```python
import jax
import jax.numpy as jnp
from jax import lax
from jax.sharding import PartitionSpec as P

temper = 0.05


def shift(x, axis, n, step):
    return lax.ppermute(x, axis, [(i, (i + step) % n) for i in range(n)])


def swap(x, axis, n, bit):
    return lax.ppermute(x, axis, [(i, i ^ bit) for i in range(n)])


def dp_bits(n_dp):
    bits = []
    b = n_dp // 2
    while b >= 1:
        bits.append(b)
        b //= 2
    return bits


def gather_queue(queue_keys, fresh, n_q, n_dp):
    q = lax.axis_index("queue")
    dp = lax.axis_index("dp")
    k_dev, width = queue_keys.shape
    piece_rows = k_dev // n_dp
    piece = lax.dynamic_slice_in_dim(queue_keys, dp * piece_rows, piece_rows, 0)
    got = [shift((piece, fresh), "queue", n_q, s) for s in range(1, n_q)]
    remote = jnp.stack([g[0] for g in got])
    blocks = jnp.stack([fresh] + [g[1] for g in got])
    for t, bit in enumerate(dp_bits(n_dp)):
        other_remote, other_blocks = swap((remote, blocks), "dp", n_dp, bit)
        remote = jnp.stack([remote, other_remote], axis=t)
        blocks = jnp.stack([blocks, other_blocks], axis=t)
    remote = remote.reshape(-1, width)
    blocks = blocks.reshape(n_dp * n_q, -1, width)
    return remote, blocks


def reduce_scatter_rows(term, n_q, n_dp):
    q = lax.axis_index("queue")
    dp = lax.axis_index("dp")
    rows, width = term.shape
    share = rows // (n_q * n_dp)
    bits = dp_bits(n_dp)
    t = term.reshape((n_q,) + (2,) * len(bits) + (share, width))
    for axis in reversed(range(len(bits))):
        bit = bits[axis]
        mine = (dp // bit) % 2
        keep = lax.dynamic_index_in_dim(t, mine, 1 + axis, keepdims=False)
        send = lax.dynamic_index_in_dim(t, 1 - mine, 1 + axis, keepdims=False)
        t = keep + swap(send, "dp", n_dp, bit)
    t = t.reshape(n_q, share, width)
    acc = lax.dynamic_index_in_dim(t, q, 0, keepdims=False)
    for s in range(1, n_q):
        part = lax.dynamic_index_in_dim(t, (q + s) % n_q, 0, keepdims=False)
        acc = acc + shift(part, "queue", n_q, s)
    return acc


def body(
    query_inputs,
    key_inputs,
    query_weight,
    key_weight,
    queue_keys,
    write_pointer,
    slot_owner,
    positive_index,
):
    q_dev, width = query_inputs.shape
    k_dev = queue_keys.shape[0]
    new_dev = key_inputs.shape[0]
    n_dp = lax.axis_size("dp")
    n_q = lax.axis_size("queue")
    q = lax.axis_index("queue")
    dp = lax.axis_index("dp")
    piece_rows = k_dev // n_dp

    fresh = jnp.dot(key_inputs, key_weight, preferred_element_type=jnp.float32)
    fresh = (fresh * lax.rsqrt(jnp.sum(fresh * fresh, -1, keepdims=True) + 1e-06)).astype(
        jnp.bfloat16
    )
    remote, blocks = gather_queue(queue_keys, fresh, n_q, n_dp)

    query = jnp.dot(query_inputs, query_weight, preferred_element_type=jnp.float32)
    inv_len = lax.rsqrt(jnp.sum(query * query, -1, keepdims=True) + 1e-06)
    unit_f = query * inv_len
    unit = unit_f.astype(jnp.bfloat16)

    keys = jnp.concatenate([queue_keys, remote], axis=0)
    scores = (
        lax.dot_general(unit, keys, (((1,), (1,)), ((), ())), preferred_element_type=jnp.float32)
        / temper
    )
    top = jnp.max(scores, -1)
    expo = jnp.exp(scores - top[:, None])
    total = jnp.sum(expo, -1)
    mixture = jnp.dot(expo.astype(jnp.bfloat16), keys, preferred_element_type=jnp.float32)

    j = positive_index
    q_src = j // k_dev
    within = j % k_dev
    e = dp ^ (within // piece_rows)
    s = (q - q_src) % n_q
    far = k_dev + (e * (n_q - 1) + (s - 1)) * piece_rows + within % piece_rows
    where_row = jnp.where(q_src == q, within, far)
    chosen = jnp.take(keys, where_row, axis=0).astype(jnp.float32)

    mixture = mixture / total[:, None]
    positive = jnp.sum(unit.astype(jnp.float32) * chosen, -1) / temper
    loss = top + jnp.log(total) - positive
    grad_unit = (mixture - chosen) / temper
    grad_query = (
        (grad_unit - unit_f * jnp.sum(unit_f * grad_unit, -1, keepdims=True)) * inv_len
    ).astype(jnp.bfloat16)
    term = lax.dot_general(
        query_inputs, grad_query, (((0,), (0,)), ((), ())), preferred_element_type=jnp.float32
    )
    grad_rows = reduce_scatter_rows(term, n_q, n_dp)

    n_blocks = slot_owner.shape[0]
    slots_here = q * n_dp + jnp.arange(n_dp, dtype=jnp.int32)
    match = slot_owner[None, :] == slots_here[:, None]
    owner_block = jnp.sum(jnp.where(match, jnp.arange(n_blocks, dtype=jnp.int32)[None, :], 0), -1)
    offset = (jnp.arange(k_dev, dtype=jnp.int32) - write_pointer[0]) % k_dev
    live = offset < n_dp * new_dev
    sub_block = jnp.minimum(offset // new_dev, n_dp - 1)
    b = jnp.take(owner_block, sub_block)
    b_e = dp ^ (b % n_dp)
    b_s = (q - b // n_dp) % n_q
    flat = blocks.reshape(-1, width)
    source = (b_e * n_q + b_s) * new_dev + offset % new_dev
    new_queue = jnp.where(live[:, None], jnp.take(flat, source, axis=0), queue_keys)
    return (loss, grad_rows, new_queue)


def solution(mesh):
    in_specs = (
        P(("groups", "queue", "dp"), None),
        P(("groups", "queue", "dp"), None),
        P(),
        P(),
        P(("groups", "queue"), None),
        P("groups"),
        P("groups"),
        P(("groups", "queue", "dp")),
    )
    out_specs = (
        P(("groups", "queue", "dp")),
        P(("groups", "queue", "dp"), None),
        P(("groups", "queue"), None),
    )
    return jax.shard_map(body, mesh=mesh, in_specs=in_specs, out_specs=out_specs, check_vma=False)
```

time: 194 us -> 116 us (0.60)
  waiting for transfers between devices: 126 us -> 63.1 us
  blocking collectives: 23.5 us -> 0 us
  starting transfers between devices: 0.08 us -> 18.9 us
  between operations: 14.8 us -> 1.63 us
  matrix products: 12.6 us -> 5.84 us
  other arithmetic: 7.09 us -> 11.9 us
  local copies, waits for them, and re-layouts: 9.73 us -> 13.9 us
    psum x1 -> x0, waiting for transfers between devices: 78.9 us -> none  [body(): summed = lax.psum(term, ('queue', 'dp'))]
    ppermute x0 -> x15, waiting for transfers between devices: none -> 63.1 us  [the longest x6 32.9 us: swap(): return lax.ppermute(x, axis, [(i, i ^ bit) for i in range(n)])]
    all_gather x1 -> x0, waiting for transfers between devices: 46.1 us -> none  [body(): lax.all_gather(queue_keys, 'queue', axis=0, tiled=True)]
    all_gather x1 -> x0, blocking collectives: 23.5 us -> none  [body(): arrived = lax.all_gather(fresh, ('queue', 'dp'), axis=0, tiled=True)]
    ppermute x0 -> x15, starting transfers between devices: none -> 18.9 us  [the longest x9 15 us: shift(): return lax.ppermute(x, axis, [(i, (i + step) % n) for i in range(n)])]
    add x1 -> x4, other arithmetic: 0.01 us -> 5.12 us  [the longest x2 4.36 us: reduce_scatter_rows(): t = keep + swap(send, 'dp', n_dp, bit)]
    squeeze x0 -> x3, local copies, waits for them, and re-layouts: none -> 2.61 us  [the longest x2 2.55 us: reduce_scatter_rows(): send = lax.dynamic_index_in_dim(t, 1 - mine, 1 + axis, keepdims=False)]
    dot_general x1, matrix products: 2.96 us -> 0.91 us  [body(): lax.dot_general(query_inputs, grad_query, (((0,), (0,)), ((), ())), prefe...]
  transfers between devices with their start and end apart: 2 -> 15, of which waited for: 2 -> 8; matrix products, arithmetic and copies ran while one was open for 7% -> 10% of each run, Pallas kernels for 0% -> 0%
where the time goes in v1:
time: 116 us; the launch traced here: 115 us
  waiting for transfers between devices  63.1 us (54%)
  starting transfers between devices  18.9 us (16%)
  local copies, waits for them, and re-layouts  13.9 us (12%)
  other arithmetic  11.9 us (10%)
  matrix products  5.84 us (5%)
  between operations  1.63 us (1%)
    ppermute x6, waiting for transfers between devices, swap(): return lax.ppermute(x, axis, [(i, i ^ bit) for i in range(n)])  32.9 us
    ppermute x9, waiting for transfers between devices, shift(): return lax.ppermute(x, axis, [(i, (i + step) % n) for i in range(n)])  30.1 us
    ppermute x9, starting transfers between devices, shift(): return lax.ppermute(x, axis, [(i, (i + step) % n) for i in range(n)])  15 us
    add x2, other arithmetic, reduce_scatter_rows(): t = keep + swap(send, 'dp', n_dp, bit)  4.36 us
    gather x1, local copies, waits for them, and re-layouts, body(): chosen = jnp.take(keys, where_row, axis=0).astype(jnp.float32)  4.21 us
    unnamed x30, local copies, waits for them, and re-layouts  3.99 us
    ppermute x6, starting transfers between devices, swap(): return lax.ppermute(x, axis, [(i, i ^ bit) for i in range(n)])  3.9 us
    select_n x1, other arithmetic, body(): jnp.take(flat, source, axis=0)  2.59 us
  transfers between devices with their start and end apart: 15, of which 8 were waited for; matrix products, arithmetic and copies ran while one was open for 10% of the time, Pallas kernels for 0%

profile of v1, /device:TPU:0, one launch (start us, length us, event | category | flops | bytes accessed | tf_op | source)
XLA Modules:
  0.0 115.2 jit_solution(2717036152615860206)
XLA Ops:
  1.7 5.1 %collective-permute-start.2 = (bf16[64,1024]{1,0:T(8,128)(2,1)S(1)}, bf16[64,1024]{1,0:T(8,128)(2,1)S(1)}, u32[]{:S(2)}, u32[]{:S(2)}) collective-permute-start(bf16[64,1024]{1,0:T(8,128)(2,1)S(1)} %constant_dynamic-slice_fusion), channel_id=1, source_target_pairs={{0,12},{4,0},{8,4},{12,8},{1,13},{5,1},{9,5},{13,9},{2,14},{6,2},{... | collective-permute-start | bytes 393224 | tf_op jit(solution)/shard_map/ppermute | solution.py:10
  7.9 2.9 %collective-permute-done.2 = bf16[64,1024]{1,0:T(8,128)(2,1)S(1)} collective-permute-done((bf16[64,1024]{1,0:T(8,128)(2,1)S(1)}, bf16[64,1024]{1,0:T(8,128)(2,1)S(1)}, u32[]{:S(2)}, u32[]{:S(2)}) %collective-permute-start.2) | collective-permute-done | bytes 131104 | tf_op jit(solution)/shard_map/ppermute | solution.py:10
  10.7 7.3 %collective-permute-done.1 = bf16[64,1024]{1,0:T(8,128)(2,1)S(1)} collective-permute-done((bf16[64,1024]{1,0:T(8,128)(2,1)S(1)}, bf16[64,1024]{1,0:T(8,128)(2,1)S(1)}, u32[]{:S(2)}, u32[]{:S(2)}) %collective-permute-start.1) | collective-permute-done | bytes 131104 | tf_op jit(solution)/shard_map/ppermute | solution.py:10
  18.1 1.6 %collective-permute-start.3 = (bf16[3,64,1024]{2,1,0:T(8,128)(2,1)S(1)}, bf16[3,64,1024]{2,1,0:T(8,128)(2,1)S(1)}, u32[]{:S(2)}, u32[]{:S(2)}) collective-permute-start(bf16[3,64,1024]{2,1,0:T(8,128)(2,1)S(1)} %get-tuple-element.15), channel_id=1, source_target_pairs={{0,2},{1,3},{2,0},{3,1},{4,6},{5,7},{6,4},{7,5},{8,10},{9,11},{10,... | collective-permute-start | bytes 1179656 | tf_op jit(solution)/shard_map/ppermute | solution.py:14
  19.7 8.9 %collective-permute-done.3 = bf16[3,64,1024]{2,1,0:T(8,128)(2,1)S(1)} collective-permute-done((bf16[3,64,1024]{2,1,0:T(8,128)(2,1)S(1)}, bf16[3,64,1024]{2,1,0:T(8,128)(2,1)S(1)}, u32[]{:S(2)}, u32[]{:S(2)}) %collective-permute-start.3) | collective-permute-done | bytes 393248 | tf_op jit(solution)/shard_map/ppermute | solution.py:14
  29.7 1.4 %collective-permute-done.4 = bf16[2,3,64,1024]{3,2,1,0:T(8,128)(2,1)S(1)} collective-permute-done((bf16[2,3,64,1024]{3,2,1,0:T(8,128)(2,1)S(1)}, bf16[2,3,64,1024]{3,2,1,0:T(8,128)(2,1)S(1)}, u32[]{:S(2)}, u32[]{:S(2)}) %collective-permute-start.4) | collective-permute-done | bytes 786464 | tf_op jit(solution)/shard_map/ppermute | solution.py:14
  32.5 1.5 %pad_maximum_fusion = bf16[1024,1024]{1,0:T(8,128)(2,1)} fusion(bf16[768,1024]{1,0:T(8,128)(2,1)S(1)} %bitcast.62, bf16[256,1024]{1,0:T(8,128)(2,1)S(1)} %copy-done.5), kind=kLoop, calls=%fused_computation.2 | loop fusion | flops 4194304 | bytes 4194304 | tf_op jit(solution)/shard_map/concatenate | solution.py:95
  34.0 4.2 %gather_fusion = bf16[256,1024]{1,0:T(8,128)(2,1)} fusion(bf16[1024,1024]{1,0:T(8,128)(2,1)} %pad_maximum_fusion, s32[1024]{0:T(1024)S(1)} %pad_clamp_fusion.1), kind=kCustom, calls=%fused_computation | custom fusion | bytes 1049600 | tf_op jit(solution)/shard_map/jit(_take)/gather | solution.py:112
  38.2 2.5 %fusion.32 = (f32[256]{0:T(256)S(1)}, f32[256,1024]{1,0:T(8,128)S(1)}) fusion(bf16[768,1024]{1,0:T(8,128)(2,1)} %bitcast.63, bf16[256,1024]{1,0:T(8,128)(2,1)} %param.12, f32[256,1024]{1,0:T(8,128)S(1)} %get-tuple-element.25, f32[256]{0:T(256)S(1)} %add_rsqrt_fusion), kind=kOutput, calls=%fused_computation.127 | convolution fusion | flops 542113536 | bytes 4196352 | tf_op jit(solution)/shard_map/dot_general | solution.py:97
  43.2 1.5 %dynamic-slice_bitcast_fusion = f32[4,2,64,1024]{3,2,1,0:T(8,128)} fusion(f32[4,2,2,64,1024]{4,3,2,1,0:T(8,128)S(1)} %bitcast.60, s32[]{:T(128)S(6)} %select_n.271), kind=kLoop, calls=%fused_computation.4 | loop fusion | bytes 4194308 | tf_op jit(solution)/shard_map/jit(dynamic_index_in_dim)/squeeze | solution.py:55
  44.7 1.3 %copy-done.1 = f32[1024,1024]{0,1:T(8,128)} copy-done((f32[1024,1024]{0,1:T(8,128)}, f32[1024,1024]{0,1:T(8,128)S(1)}, u32[]{:S(2)}) %copy-start.1) | copy-done | bytes 4194328
  47.5 2.0 %collective-permute-start.11 = (bf16[16,1024]{1,0:T(8,128)(2,1)S(1)}, bf16[16,1024]{1,0:T(8,128)(2,1)S(1)}, u32[]{:S(2)}, u32[]{:S(2)}) collective-permute-start(bf16[16,1024]{1,0:T(8,128)(2,1)S(1)} %multiply_convert_fusion.3), channel_id=1, source_target_pairs={{0,8},{4,12},{8,0},{12,4},{1,9},{5,13},{9,1},{13,5},{2,10},{6,14},... | collective-permute-start | bytes 98312 | tf_op jit(solution)/shard_map/ppermute | solution.py:10
  49.5 2.0 %collective-permute-start.10 = (bf16[16,1024]{1,0:T(8,128)(2,1)S(1)}, bf16[16,1024]{1,0:T(8,128)(2,1)S(1)}, u32[]{:S(2)}, u32[]{:S(2)}) collective-permute-start(bf16[16,1024]{1,0:T(8,128)(2,1)S(1)} %multiply_convert_fusion.3), channel_id=1, source_target_pairs={{0,4},{4,8},{8,12},{12,0},{1,5},{5,9},{9,13},{13,1},{2,6},{6,10},{... | collective-permute-start | bytes 98312 | tf_op jit(solution)/shard_map/ppermute | solution.py:10
  51.5 2.6 %bitcast_add_fusion = f32[4,2,64,1024]{3,2,1,0:T(8,128)S(1)} fusion(f32[4,2,64,1024]{3,2,1,0:T(8,128)} %collective-permute-done.5, f32[4,2,2,64,1024]{4,3,2,1,0:T(8,128)} %bitcast.61, s32[]{:T(128)S(6)} %select_n.270), kind=kLoop, calls=%fused_computation.3 | loop fusion | flops 524288 | bytes 6291460 | tf_op jit(solution)/shard_map/add | solution.py:56
  54.1 1.3 %copy-done.2 = f32[4,2,64,1024]{3,2,1,0:T(8,128)} copy-done((f32[4,2,64,1024]{3,2,1,0:T(8,128)}, f32[4,2,64,1024]{3,2,1,0:T(8,128)S(1)}, u32[]{:S(2)}) %copy-start.2) | copy-done | bytes 2097176
  56.5 1.5 %collective-permute-start.6 = (f32[4,64,1024]{2,1,0:T(8,128)}, f32[4,64,1024]{2,1,0:T(8,128)}, u32[]{:S(2)}, u32[]{:S(2)}) collective-permute-start(f32[4,64,1024]{2,1,0:T(8,128)} %dynamic-slice_bitcast_fusion.1), channel_id=1, source_target_pairs={{0,2},{1,3},{2,0},{3,1},{4,6},{5,7},{6,4},{7,5},{8,10},{9,11},{10,... | collective-permute-start | bytes 3145736 | tf_op jit(solution)/shard_map/ppermute | solution.py:14
  60.1 2.6 %compare_select_fusion = (s32[256,1]{0,1:T(1,128)S(1)}, s32[256,1]{0,1:T(1,128)S(1)}) fusion(s32[]{:T(128)S(6)} %axis_index.17, s32[]{:T(128)S(6)} %axis_index.14, s32[]{:T(128)} %bitcast.57, s32[]{:T(128)} %bitcast.23, s32[]{:T(128)} %bitcast.22, s32[]{:T(128)} %bitcast.21, s32[]{:T(128)} %bitcast.20), kind=kLoop, calls=%fused_computation.40 | loop fusion | flops 21504 | bytes 2076 | tf_op jit(solution)/shard_map/jit(_take)/jit(_where)/select_n | solution.py:138
  62.7 21.2 %collective-permute-done.13 = bf16[4,16,1024]{2,1,0:T(8,128)(2,1)S(1)} collective-permute-done((bf16[4,16,1024]{2,1,0:T(8,128)(2,1)S(1)}, bf16[4,16,1024]{2,1,0:T(8,128)(2,1)S(1)}, u32[]{:S(2)}, u32[]{:S(2)}) %collective-permute-start.13) | collective-permute-done | bytes 131104 | tf_op jit(solution)/shard_map/ppermute | solution.py:14
  84.2 1.4 %collective-permute-done.14 = bf16[2,4,16,1024]{3,2,1,0:T(8,128)(2,1)S(1)} collective-permute-done((bf16[2,4,16,1024]{3,2,1,0:T(8,128)(2,1)S(1)}, bf16[2,4,16,1024]{3,2,1,0:T(8,128)(2,1)S(1)}, u32[]{:S(2)}, u32[]{:S(2)}) %collective-permute-start.14) | collective-permute-done | bytes 262176 | tf_op jit(solution)/shard_map/ppermute | solution.py:14
  86.9 1.7 %bitcast_add_fusion.1 = f32[4,64,1024]{2,1,0:T(8,128)S(1)} fusion(f32[4,64,1024]{2,1,0:T(8,128)} %collective-permute-done.6, f32[4,2,64,1024]{3,2,1,0:T(8,128)} %copy-done.2, s32[]{:T(128)S(6)} %select_n.274), kind=kLoop, calls=%fused_computation.12 | loop fusion | flops 262144 | bytes 3145732 | tf_op jit(solution)/shard_map/add | solution.py:56
  88.7 2.2 %collective-permute-start.9 = (f32[64,1024]{1,0:T(8,128)S(1)}, f32[64,1024]{1,0:T(8,128)S(1)}, u32[]{:S(2)}, u32[]{:S(2)}) collective-permute-start(f32[64,1024]{1,0:T(8,128)S(1)} %get-tuple-element.10), channel_id=1, source_target_pairs={{0,12},{4,0},{8,4},{12,8},{1,13},{5,1},{9,5},{13,9},{2,14},{6,2},{... | collective-permute-start | bytes 786440 | tf_op jit(solution)/shard_map/ppermute | solution.py:10
  91.1 1.9 %collective-permute-start.7 = (f32[64,1024]{1,0:T(8,128)S(1)}, f32[64,1024]{1,0:T(8,128)S(1)}, u32[]{:S(2)}, u32[]{:S(2)}) collective-permute-start(f32[64,1024]{1,0:T(8,128)S(1)} %get-tuple-element.9), channel_id=1, source_target_pairs={{0,4},{4,8},{8,12},{12,0},{1,5},{5,9},{9,13},{13,1},{2,6},{6,10},{... | collective-permute-start | bytes 786440 | tf_op jit(solution)/shard_map/ppermute | solution.py:10
  94.5 3.1 %collective-permute-done.9 = f32[64,1024]{1,0:T(8,128)S(1)} collective-permute-done((f32[64,1024]{1,0:T(8,128)S(1)}, f32[64,1024]{1,0:T(8,128)S(1)}, u32[]{:S(2)}, u32[]{:S(2)}) %collective-permute-start.9) | collective-permute-done | bytes 262176 | tf_op jit(solution)/shard_map/ppermute | solution.py:10
  97.7 16.8 %collective-permute-done.8 = f32[64,1024]{1,0:T(8,128)S(1)} collective-permute-done((f32[64,1024]{1,0:T(8,128)S(1)}, f32[64,1024]{1,0:T(8,128)S(1)}, u32[]{:S(2)}, u32[]{:S(2)}) %collective-permute-start.8) | collective-permute-done | bytes 262176 | tf_op jit(solution)/shard_map/ppermute | solution.py:10
  (74 shorter events, 15.0 us)
Async XLA Ops:
  0.6 28.2 %copy-start = (bf16[1024,1024]{1,0:T(8,128)(2,1)S(1)}, bf16[1024,1024]{1,0:T(8,128)(2,1)}, u32[]{:S(2)}) copy-start(bf16[1024,1024]{1,0:T(8,128)(2,1)} %param.10) | copy-start | bytes 6291460
  0.6 28.2 %copy-start.13 = (s32[256]{0:T(256)S(1)}, s32[256]{0:T(256)}, u32[]{:S(2)}) copy-start(s32[256]{0:T(256)} %param.15) | copy-start | bytes 3076
  1.7 9.0 %collective-permute-start.2 = (bf16[64,1024]{1,0:T(8,128)(2,1)S(1)}, bf16[64,1024]{1,0:T(8,128)(2,1)S(1)}, u32[]{:S(2)}, u32[]{:S(2)}) collective-permute-start(bf16[64,1024]{1,0:T(8,128)(2,1)S(1)} %constant_dynamic-slice_fusion), channel_id=1, source_target_pairs={{0,12},{4,0},{8,4},{12,8},{1,13},{5,1},{9,5},{13,9},{2,14},{6,2},{... | collective-permute-start | bytes 393224 | tf_op jit(solution)/shard_map/ppermute | solution.py:10
  6.9 11.2 %collective-permute-start.1 = (bf16[64,1024]{1,0:T(8,128)(2,1)S(1)}, bf16[64,1024]{1,0:T(8,128)(2,1)S(1)}, u32[]{:S(2)}, u32[]{:S(2)}) collective-permute-start(bf16[64,1024]{1,0:T(8,128)(2,1)S(1)} %constant_dynamic-slice_fusion), channel_id=1, source_target_pairs={{0,8},{4,12},{8,0},{12,4},{1,9},{5,13},{9,1},{13,5},{2,10},{6,14},... | collective-permute-start | bytes 393224 | tf_op jit(solution)/shard_map/ppermute | solution.py:10
  6.9 11.2 %collective-permute-start = (bf16[64,1024]{1,0:T(8,128)(2,1)S(1)}, bf16[64,1024]{1,0:T(8,128)(2,1)S(1)}, u32[]{:S(2)}, u32[]{:S(2)}) collective-permute-start(bf16[64,1024]{1,0:T(8,128)(2,1)S(1)} %constant_dynamic-slice_fusion), channel_id=1, source_target_pairs={{0,4},{4,8},{8,12},{12,0},{1,5},{5,9},{9,13},{13,1},{2,6},{6,10},{... | collective-permute-start | bytes 393224 | tf_op jit(solution)/shard_map/ppermute | solution.py:10
  18.1 10.5 %collective-permute-start.3 = (bf16[3,64,1024]{2,1,0:T(8,128)(2,1)S(1)}, bf16[3,64,1024]{2,1,0:T(8,128)(2,1)S(1)}, u32[]{:S(2)}, u32[]{:S(2)}) collective-permute-start(bf16[3,64,1024]{2,1,0:T(8,128)(2,1)S(1)} %get-tuple-element.15), channel_id=1, source_target_pairs={{0,2},{1,3},{2,0},{3,1},{4,6},{5,7},{6,4},{7,5},{8,10},{9,11},{10,... | collective-permute-start | bytes 1179656 | tf_op jit(solution)/shard_map/ppermute | solution.py:14
  19.7 9.2 %copy-start.9 = (bf16[256,1024]{1,0:T(8,128)(2,1)S(1)}, bf16[256,1024]{1,0:T(8,128)(2,1)}, u32[]{:S(2)}) copy-start(bf16[256,1024]{1,0:T(8,128)(2,1)} %param.8) | copy-start | bytes 1572868
  28.7 2.4 %collective-permute-start.4 = (bf16[2,3,64,1024]{3,2,1,0:T(8,128)(2,1)S(1)}, bf16[2,3,64,1024]{3,2,1,0:T(8,128)(2,1)S(1)}, u32[]{:S(2)}, u32[]{:S(2)}) collective-permute-start(bf16[2,3,64,1024]{3,2,1,0:T(8,128)(2,1)S(1)} %get-tuple-element.13), channel_id=1, source_target_pairs={{0,1},{1,0},{2,3},{3,2},{4,5},{5,4},{6,7},{7,6},{8,9},{9,8},{10,11... | collective-permute-start | bytes 2359304 | tf_op jit(solution)/shard_map/ppermute | solution.py:14
  38.2 2.8 %copy-start.4 = (bf16[2,2,3,64,1024]{4,3,2,1,0:T(8,128)(2,1)S(1)}, bf16[2,2,3,64,1024]{4,3,2,1,0:T(8,128)(2,1)}, u32[]{:S(2)}) copy-start(bf16[2,2,3,64,1024]{4,3,2,1,0:T(8,128)(2,1)} %copy-done.3) | copy-start | bytes 4718596
  38.2 2.8 %copy-start.6 = (bf16[256,1024]{1,0:T(8,128)(2,1)S(1)}, bf16[256,1024]{1,0:T(8,128)(2,1)}, u32[]{:S(2)}) copy-start(bf16[256,1024]{1,0:T(8,128)(2,1)} %param.12) | copy-start | bytes 1572868
  38.2 2.8 %copy-start.11 = (bf16[256,1024]{1,0:T(8,128)(2,1)S(1)}, bf16[256,1024]{1,0:T(8,128)(2,1)}, u32[]{:S(2)}) copy-start(bf16[256,1024]{1,0:T(8,128)(2,1)} %gather_fusion) | copy-start | bytes 1572868
  43.2 3.1 %copy-start.8 = (bf16[1024,1024]{1,0:T(8,128)(2,1)S(1)}, bf16[1024,1024]{1,0:T(8,128)(2,1)}, u32[]{:S(2)}) copy-start(bf16[1024,1024]{1,0:T(8,128)(2,1)} %param.11) | copy-start | bytes 6291460
  43.2 3.1 %copy-start.12 = (bf16[16,1024]{1,0:T(8,128)(2,1)S(1)}, bf16[16,1024]{1,0:T(8,128)(2,1)}, u32[]{:S(2)}) copy-start(bf16[16,1024]{1,0:T(8,128)(2,1)} %param.9) | copy-start | bytes 98308
  46.0 5.5 %collective-permute-start.5 = (f32[4,2,64,1024]{3,2,1,0:T(8,128)}, f32[4,2,64,1024]{3,2,1,0:T(8,128)}, u32[]{:S(2)}, u32[]{:S(2)}) collective-permute-start(f32[4,2,64,1024]{3,2,1,0:T(8,128)} %dynamic-slice_bitcast_fusion), channel_id=1, source_target_pairs={{0,1},{1,0},{2,3},{3,2},{4,5},{5,4},{6,7},{7,6},{8,9},{9,8},{10,11... | collective-permute-start | bytes 6291464 | tf_op jit(solution)/shard_map/ppermute | solution.py:14
  46.9 11.3 %collective-permute-start.12 = (bf16[16,1024]{1,0:T(8,128)(2,1)S(1)}, bf16[16,1024]{1,0:T(8,128)(2,1)S(1)}, u32[]{:S(2)}, u32[]{:S(2)}) collective-permute-start(bf16[16,1024]{1,0:T(8,128)(2,1)S(1)} %multiply_convert_fusion.3), channel_id=1, source_target_pairs={{0,12},{4,0},{8,4},{12,8},{1,13},{5,1},{9,5},{13,9},{2,14},{6,2},{... | collective-permute-start | bytes 98312 | tf_op jit(solution)/shard_map/ppermute | solution.py:10
  47.5 10.7 %collective-permute-start.11 = (bf16[16,1024]{1,0:T(8,128)(2,1)S(1)}, bf16[16,1024]{1,0:T(8,128)(2,1)S(1)}, u32[]{:S(2)}, u32[]{:S(2)}) collective-permute-start(bf16[16,1024]{1,0:T(8,128)(2,1)S(1)} %multiply_convert_fusion.3), channel_id=1, source_target_pairs={{0,8},{4,12},{8,0},{12,4},{1,9},{5,13},{9,1},{13,5},{2,10},{6,14},... | collective-permute-start | bytes 98312 | tf_op jit(solution)/shard_map/ppermute | solution.py:10
  49.5 8.7 %collective-permute-start.10 = (bf16[16,1024]{1,0:T(8,128)(2,1)S(1)}, bf16[16,1024]{1,0:T(8,128)(2,1)S(1)}, u32[]{:S(2)}, u32[]{:S(2)}) collective-permute-start(bf16[16,1024]{1,0:T(8,128)(2,1)S(1)} %multiply_convert_fusion.3), channel_id=1, source_target_pairs={{0,4},{4,8},{8,12},{12,0},{1,5},{5,9},{9,13},{13,1},{2,6},{6,10},{... | collective-permute-start | bytes 98312 | tf_op jit(solution)/shard_map/ppermute | solution.py:10
  56.5 30.4 %collective-permute-start.6 = (f32[4,64,1024]{2,1,0:T(8,128)}, f32[4,64,1024]{2,1,0:T(8,128)}, u32[]{:S(2)}, u32[]{:S(2)}) collective-permute-start(f32[4,64,1024]{2,1,0:T(8,128)} %dynamic-slice_bitcast_fusion.1), channel_id=1, source_target_pairs={{0,2},{1,3},{2,0},{3,1},{4,6},{5,7},{6,4},{7,5},{8,10},{9,11},{10,... | collective-permute-start | bytes 3145736 | tf_op jit(solution)/shard_map/ppermute | solution.py:14
  58.2 25.7 %collective-permute-start.13 = (bf16[4,16,1024]{2,1,0:T(8,128)(2,1)S(1)}, bf16[4,16,1024]{2,1,0:T(8,128)(2,1)S(1)}, u32[]{:S(2)}, u32[]{:S(2)}) collective-permute-start(bf16[4,16,1024]{2,1,0:T(8,128)(2,1)S(1)} %get-tuple-element.19), channel_id=1, source_target_pairs={{0,2},{1,3},{2,0},{3,1},{4,6},{5,7},{6,4},{7,5},{8,10},{9,11},{10,... | collective-permute-start | bytes 393224 | tf_op jit(solution)/shard_map/ppermute | solution.py:14
  84.0 1.6 %collective-permute-start.14 = (bf16[2,4,16,1024]{3,2,1,0:T(8,128)(2,1)S(1)}, bf16[2,4,16,1024]{3,2,1,0:T(8,128)(2,1)S(1)}, u32[]{:S(2)}, u32[]{:S(2)}) collective-permute-start(bf16[2,4,16,1024]{3,2,1,0:T(8,128)(2,1)S(1)} %get-tuple-element.17), channel_id=1, source_target_pairs={{0,1},{1,0},{2,3},{3,2},{4,5},{5,4},{6,7},{7,6},{8,9},{9,8},{10,11... | collective-permute-start | bytes 786440 | tf_op jit(solution)/shard_map/ppermute | solution.py:14
  86.9 6.2 %copy-start.7 = (bf16[256,1024]{1,0:T(8,128)(2,1)S(1)}, bf16[256,1024]{1,0:T(8,128)(2,1)}, u32[]{:S(2)}) copy-start(bf16[256,1024]{1,0:T(8,128)(2,1)} %param.12) | copy-start | bytes 1572868
  88.7 9.0 %collective-permute-start.9 = (f32[64,1024]{1,0:T(8,128)S(1)}, f32[64,1024]{1,0:T(8,128)S(1)}, u32[]{:S(2)}, u32[]{:S(2)}) collective-permute-start(f32[64,1024]{1,0:T(8,128)S(1)} %get-tuple-element.10), channel_id=1, source_target_pairs={{0,12},{4,0},{8,4},{12,8},{1,13},{5,1},{9,5},{13,9},{2,14},{6,2},{... | collective-permute-start | bytes 786440 | tf_op jit(solution)/shard_map/ppermute | solution.py:10
  90.9 23.6 %collective-permute-start.8 = (f32[64,1024]{1,0:T(8,128)S(1)}, f32[64,1024]{1,0:T(8,128)S(1)}, u32[]{:S(2)}, u32[]{:S(2)}) collective-permute-start(f32[64,1024]{1,0:T(8,128)S(1)} %get-tuple-element.11), channel_id=1, source_target_pairs={{0,8},{4,12},{8,0},{12,4},{1,9},{5,13},{9,1},{13,5},{2,10},{6,14},... | collective-permute-start | bytes 786440 | tf_op jit(solution)/shard_map/ppermute | solution.py:10
  91.1 23.4 %collective-permute-start.7 = (f32[64,1024]{1,0:T(8,128)S(1)}, f32[64,1024]{1,0:T(8,128)S(1)}, u32[]{:S(2)}, u32[]{:S(2)}) collective-permute-start(f32[64,1024]{1,0:T(8,128)S(1)} %get-tuple-element.9), channel_id=1, source_target_pairs={{0,4},{4,8},{8,12},{12,0},{1,5},{5,9},{9,13},{13,1},{2,6},{6,10},{... | collective-permute-start | bytes 786440 | tf_op jit(solution)/shard_map/ppermute | solution.py:10
  (6 other events, 10.3 us)

commit v2 on v1

v2 whole, which is shorter than its diff:
```python
import jax
import jax.numpy as jnp
from jax import lax
from jax.sharding import PartitionSpec as P

temper = 0.05


def shift(x, axis, n, step):
    return lax.ppermute(x, axis, [(i, (i + step) % n) for i in range(n)])


def swap(x, axis, n, bit):
    return lax.ppermute(x, axis, [(i, i ^ bit) for i in range(n)])


def dp_bits(n_dp):
    bits = []
    b = n_dp // 2
    while b >= 1:
        bits.append(b)
        b //= 2
    return bits


def gather_queue(queue_keys, fresh, n_q, n_dp):
    dp = lax.axis_index("dp")
    k_dev, width = queue_keys.shape
    piece_rows = k_dev // n_dp
    piece = lax.dynamic_slice_in_dim(queue_keys, dp * piece_rows, piece_rows, 0)
    packed = jnp.concatenate([piece, fresh], axis=0)
    got = [shift(packed, "queue", n_q, s) for s in range(1, n_q)]
    payload = jnp.concatenate(
        [g[:piece_rows] for g in got] + [fresh] + [g[piece_rows:] for g in got], axis=0
    )
    for t, bit in enumerate(dp_bits(n_dp)):
        payload = jnp.stack([payload, swap(payload, "dp", n_dp, bit)], axis=t)
    return payload.reshape(n_dp, -1, width)


def reduce_scatter_grad(query_inputs, grad_query, n_q, n_dp):
    q = lax.axis_index("queue")
    dp = lax.axis_index("dp")
    q_dev, rows = query_inputs.shape
    width = grad_query.shape[1]
    share = rows // (n_q * n_dp)
    bits = dp_bits(n_dp)
    hb = bits[0]
    side = dp // hb
    x4 = query_inputs.reshape(q_dev, n_q, 2, hb * share)
    mine = lax.dynamic_index_in_dim(x4, side, 2, keepdims=False)
    other = lax.dynamic_index_in_dim(x4, 1 - side, 2, keepdims=False)
    got_x, got_g = swap((other, grad_query), "dp", n_dp, hb)
    xs = jnp.concatenate([mine, got_x], axis=0).reshape(2 * q_dev, n_q * hb * share)
    gs = jnp.concatenate([grad_query, got_g], axis=0)
    term = lax.dot_general(xs, gs, (((0,), (0,)), ((), ())), preferred_element_type=jnp.float32)
    rest = bits[1:]
    t = term.reshape((n_q,) + (2,) * len(rest) + (share, width))
    for axis in reversed(range(len(rest))):
        bit = rest[axis]
        me = (dp // bit) % 2
        keep = lax.dynamic_index_in_dim(t, me, 1 + axis, keepdims=False)
        send = lax.dynamic_index_in_dim(t, 1 - me, 1 + axis, keepdims=False)
        t = keep + swap(send, "dp", n_dp, bit)
    t = t.reshape(n_q, share, width)
    acc = lax.dynamic_index_in_dim(t, q, 0, keepdims=False)
    for s in range(1, n_q):
        part = lax.dynamic_index_in_dim(t, (q + s) % n_q, 0, keepdims=False)
        acc = acc + shift(part, "queue", n_q, s)
    return acc


def body(
    query_inputs,
    key_inputs,
    query_weight,
    key_weight,
    queue_keys,
    write_pointer,
    slot_owner,
    positive_index,
):
    q_dev, width = query_inputs.shape
    k_dev = queue_keys.shape[0]
    new_dev = key_inputs.shape[0]
    n_dp = lax.axis_size("dp")
    n_q = lax.axis_size("queue")
    q = lax.axis_index("queue")
    dp = lax.axis_index("dp")
    piece_rows = k_dev // n_dp
    far_rows = (n_q - 1) * piece_rows

    fresh = jnp.dot(key_inputs, key_weight, preferred_element_type=jnp.float32)
    fresh = (fresh * lax.rsqrt(jnp.sum(fresh * fresh, -1, keepdims=True) + 1e-06)).astype(
        jnp.bfloat16
    )
    gathered = gather_queue(queue_keys, fresh, n_q, n_dp)
    rows0 = gathered.shape[1]
    remote = gathered.reshape(-1, width)
    is_key = (jnp.arange(n_dp * rows0, dtype=jnp.int32) % rows0) < far_rows

    query = jnp.dot(query_inputs, query_weight, preferred_element_type=jnp.float32)
    inv_len = lax.rsqrt(jnp.sum(query * query, -1, keepdims=True) + 1e-06)
    unit_f = query * inv_len
    unit = unit_f.astype(jnp.bfloat16)

    dims = (((1,), (1,)), ((), ()))
    near = lax.dot_general(unit, queue_keys, dims, preferred_element_type=jnp.float32) / temper
    far = lax.dot_general(unit, remote, dims, preferred_element_type=jnp.float32) / temper
    far = jnp.where(is_key[None, :], far, -jnp.inf)
    top = jnp.maximum(jnp.max(near, -1), jnp.max(far, -1))
    e_near = jnp.exp(near - top[:, None])
    e_far = jnp.exp(far - top[:, None])
    total = jnp.sum(e_near, -1) + jnp.sum(e_far, -1)
    mixture = jnp.dot(
        e_near.astype(jnp.bfloat16), queue_keys, preferred_element_type=jnp.float32
    ) + jnp.dot(e_far.astype(jnp.bfloat16), remote, preferred_element_type=jnp.float32)

    j = positive_index
    q_src = j // k_dev
    within = j % k_dev
    local = q_src == q
    e = dp ^ (within // piece_rows)
    s = (q - q_src) % n_q
    far_at = e * rows0 + (s - 1) * piece_rows + within % piece_rows
    pick_near = (local[:, None] & (within[:, None] == jnp.arange(k_dev)[None, :])).astype(
        jnp.bfloat16
    )
    pick_far = (
        (~local)[:, None] & (far_at[:, None] == jnp.arange(n_dp * rows0)[None, :])
    ).astype(jnp.bfloat16)
    chosen = jnp.dot(pick_near, queue_keys, preferred_element_type=jnp.float32) + jnp.dot(
        pick_far, remote, preferred_element_type=jnp.float32
    )

    mixture = mixture / total[:, None]
    positive = jnp.sum(unit.astype(jnp.float32) * chosen, -1) / temper
    loss = top + jnp.log(total) - positive
    grad_unit = (mixture - chosen) / temper
    grad_query = (
        (grad_unit - unit_f * jnp.sum(unit_f * grad_unit, -1, keepdims=True)) * inv_len
    ).astype(jnp.bfloat16)
    grad_rows = reduce_scatter_grad(query_inputs, grad_query, n_q, n_dp)

    n_blocks = slot_owner.shape[0]
    slots_here = q * n_dp + jnp.arange(n_dp, dtype=jnp.int32)
    match = slot_owner[None, :] == slots_here[:, None]
    owner_block = jnp.sum(jnp.where(match, jnp.arange(n_blocks, dtype=jnp.int32)[None, :], 0), -1)
    offset = (jnp.arange(k_dev, dtype=jnp.int32) - write_pointer[0]) % k_dev
    live = offset < n_dp * new_dev
    sub_block = jnp.minimum(offset // new_dev, n_dp - 1)
    b = jnp.take(owner_block, sub_block)
    b_e = dp ^ (b % n_dp)
    b_s = (q - b // n_dp) % n_q
    source = b_e * rows0 + far_rows + b_s * new_dev + offset % new_dev
    new_queue = jnp.where(live[:, None], jnp.take(remote, source, axis=0), queue_keys)
    return (loss, grad_rows, new_queue)


def solution(mesh):
    in_specs = (
        P(("groups", "queue", "dp"), None),
        P(("groups", "queue", "dp"), None),
        P(),
        P(),
        P(("groups", "queue"), None),
        P("groups"),
        P("groups"),
        P(("groups", "queue", "dp")),
    )
    out_specs = (
        P(("groups", "queue", "dp")),
        P(("groups", "queue", "dp"), None),
        P(("groups", "queue"), None),
    )
    return jax.shard_map(body, mesh=mesh, in_specs=in_specs, out_specs=out_specs, check_vma=False)
```

time: 116 us -> 112 us (0.966)
  starting transfers between devices: 18.9 us -> 15.6 us
  matrix products: 5.84 us -> 8.89 us
  waiting for transfers between devices: 63.1 us -> 60.8 us
    ppermute x6 -> x5, waiting for transfers between devices: 32.9 us -> 29.5 us  [swap(): return lax.ppermute(x, axis, [(i, i ^ bit) for i in range(n)])]
    ppermute x9 -> x6, starting transfers between devices: 15 us -> 12 us  [shift(): return lax.ppermute(x, axis, [(i, (i + step) % n) for i in range(n)])]
    add x3, other arithmetic: 5.12 us -> 2.47 us  [the longest x1 1.69 us: reduce_scatter_grad(): t = keep + swap(send, 'dp', n_dp, bit)]
    gather x2 -> x1, local copies, waits for them, and re-layouts: 5.38 us -> 3.42 us  [body(): jnp.take(remote, source, axis=0)]
    unnamed x30 -> x20, local copies, waits for them, and re-layouts: 3.99 us -> 5.81 us
    dot_general x1, matrix products: 0.5 us -> 2.28 us  [body(): fresh = jnp.dot(key_inputs, key_weight, preferred_element_type=jnp.float32)]
    squeeze x3 -> x2, local copies, waits for them, and re-layouts: 2.61 us -> 1.13 us  [the longest x1 1.07 us: reduce_scatter_grad(): send = lax.dynamic_index_in_dim(t, 1 - me, 1 + axis, keepdims=False)]
    dot_general x3 -> x7, matrix products: 4.55 us -> 5.82 us  [the longest x1 1.91 us: reduce_scatter_grad(): lax.dot_general(xs, gs, (((0,), (0,)), ((), ())), preferred_element_type=...]
  transfers between devices with their start and end apart: 15 -> 11, of which waited for: 8 -> 8; matrix products, arithmetic and copies ran while one was open for 10% -> 12% of each run, Pallas kernels for 0% -> 0%
where the time goes in v2:
time: 112 us; the launch traced here: 111 us
  waiting for transfers between devices  60.8 us (54%)
  starting transfers between devices  15.6 us (14%)
  local copies, waits for them, and re-layouts  12.8 us (11%)
  other arithmetic  11.5 us (10%)
  matrix products  8.89 us (8%)
  between operations  1.57 us (1%)
    ppermute x6, waiting for transfers between devices, shift(): return lax.ppermute(x, axis, [(i, (i + step) % n) for i in range(n)])  31.3 us
    ppermute x5, waiting for transfers between devices, swap(): return lax.ppermute(x, axis, [(i, i ^ bit) for i in range(n)])  29.5 us
    ppermute x6, starting transfers between devices, shift(): return lax.ppermute(x, axis, [(i, (i + step) % n) for i in range(n)])  12 us
    unnamed x20, local copies, waits for them, and re-layouts  5.81 us
    ppermute x5, starting transfers between devices, swap(): return lax.ppermute(x, axis, [(i, i ^ bit) for i in range(n)])  3.66 us
    gather x1, local copies, waits for them, and re-layouts, body(): jnp.take(remote, source, axis=0)  3.42 us
    select_n x1, other arithmetic, body(): jnp.take(remote, source, axis=0)  2.49 us
    dot_general x1, matrix products, body(): fresh = jnp.dot(key_inputs, key_weight, preferred_element_type=jnp.float32)  2.28 us
  transfers between devices with their start and end apart: 11, of which 8 were waited for; matrix products, arithmetic and copies ran while one was open for 12% of the time, Pallas kernels for 0%

profile of v2, /device:TPU:0, one launch (start us, length us, event | category | flops | bytes accessed | tf_op | source)
XLA Modules:
  0.0 111.2 jit_solution(13003239598627305915)
XLA Ops:
  0.7 2.3 %multiply_reduce_fusion.3 = (f32[16]{0:T(128)S(1)}, f32[16,1024]{1,0:T(8,128)S(1)}) fusion(bf16[16,1024]{1,0:T(8,128)(2,1)} %param.9, bf16[1024,1024]{1,0:T(8,128)(2,1)} %param.11), kind=kOutput, calls=%fused_computation.53 | convolution fusion | flops 33587184 | bytes 2195520 | tf_op jit(solution)/shard_map/dot_general | solution.py:93
  3.1 3.1 %collective-permute-start = (bf16[80,1024]{1,0:T(8,128)(2,1)S(1)}, bf16[80,1024]{1,0:T(8,128)(2,1)S(1)}, u32[]{:S(2)}, u32[]{:S(2)}) collective-permute-start(bf16[80,1024]{1,0:T(8,128)(2,1)S(1)} %pad_maximum_fusion.3), channel_id=1, source_target_pairs={{0,4},{4,8},{8,12},{12,0},{1,5},{5,9},{9,13},{13,1},{2,6},{6,10},{... | collective-permute-start | bytes 491528 | tf_op jit(solution)/shard_map/ppermute | solution.py:10
  6.2 2.6 %collective-permute-start.1 = (bf16[80,1024]{1,0:T(8,128)(2,1)S(1)}, bf16[80,1024]{1,0:T(8,128)(2,1)S(1)}, u32[]{:S(2)}, u32[]{:S(2)}) collective-permute-start(bf16[80,1024]{1,0:T(8,128)(2,1)S(1)} %pad_maximum_fusion.3), channel_id=1, source_target_pairs={{0,8},{4,12},{8,0},{12,4},{1,9},{5,13},{9,1},{13,5},{2,10},{6,14},... | collective-permute-start | bytes 491528 | tf_op jit(solution)/shard_map/ppermute | solution.py:10
  8.8 1.3 %collective-permute-start.2 = (bf16[80,1024]{1,0:T(8,128)(2,1)S(1)}, bf16[80,1024]{1,0:T(8,128)(2,1)S(1)}, u32[]{:S(2)}, u32[]{:S(2)}) collective-permute-start(bf16[80,1024]{1,0:T(8,128)(2,1)S(1)} %pad_maximum_fusion.3), channel_id=1, source_target_pairs={{0,12},{4,0},{8,4},{12,8},{1,13},{5,1},{9,5},{13,9},{2,14},{6,2},{... | collective-permute-start | bytes 491528 | tf_op jit(solution)/shard_map/ppermute | solution.py:10
  10.1 3.2 %collective-permute-done = bf16[80,1024]{1,0:T(8,128)(2,1)S(1)} collective-permute-done((bf16[80,1024]{1,0:T(8,128)(2,1)S(1)}, bf16[80,1024]{1,0:T(8,128)(2,1)S(1)}, u32[]{:S(2)}, u32[]{:S(2)}) %collective-permute-start) | collective-permute-done | bytes 163872 | tf_op jit(solution)/shard_map/ppermute | solution.py:10
  14.0 5.5 %collective-permute-done.1 = bf16[80,1024]{1,0:T(8,128)(2,1)S(1)} collective-permute-done((bf16[80,1024]{1,0:T(8,128)(2,1)S(1)}, bf16[80,1024]{1,0:T(8,128)(2,1)S(1)}, u32[]{:S(2)}, u32[]{:S(2)}) %collective-permute-start.1) | collective-permute-done | bytes 163872 | tf_op jit(solution)/shard_map/ppermute | solution.py:10
  23.4 1.5 %collective-permute-start.3 = (bf16[256,1024]{1,0:T(8,128)(2,1)}, bf16[256,1024]{1,0:T(8,128)(2,1)}, u32[]{:S(2)}, u32[]{:S(2)}) collective-permute-start(bf16[256,1024]{1,0:T(8,128)(2,1)} %slice_dynamic-update-slice_fusion.3), channel_id=1, source_target_pairs={{0,2},{1,3},{2,0},{3,1},{4,6},{5,7},{6,4},{7,5},{8,10},{9,11},{10,... | collective-permute-start | bytes 1572872 | tf_op jit(solution)/shard_map/ppermute | solution.py:14
  25.7 11.8 %collective-permute-done.3 = bf16[256,1024]{1,0:T(8,128)(2,1)} collective-permute-done((bf16[256,1024]{1,0:T(8,128)(2,1)}, bf16[256,1024]{1,0:T(8,128)(2,1)}, u32[]{:S(2)}, u32[]{:S(2)}) %collective-permute-start.3) | collective-permute-done | bytes 524320 | tf_op jit(solution)/shard_map/ppermute | solution.py:14
  37.5 1.3 %fusion.51 = (bf16[2,1,256,1024]{3,2,0,1:T(8,128)(2,1)S(1)}, bf16[2,256,1024]{2,1,0:T(8,128)(2,1)S(1)}) fusion(bf16[1,256,1024]{2,1,0:T(8,128)(2,1)} %bitcast.1, bf16[1,256,1024]{2,1,0:T(8,128)(2,1)} %bitcast), kind=kLoop, calls=%fused_computation.152 | loop fusion | flops 524288 | bytes 3145728 | tf_op jit(solution)/shard_map/stack | solution.py:37
  39.3 2.2 %collective-permute-done.4 = bf16[2,256,1024]{2,1,0:T(8,128)(2,1)S(1)} collective-permute-done((bf16[2,256,1024]{2,1,0:T(8,128)(2,1)S(1)}, bf16[2,256,1024]{2,1,0:T(8,128)(2,1)S(1)}, u32[]{:S(2)}, u32[]{:S(2)}) %collective-permute-start.4) | collective-permute-done | bytes 1048608 | tf_op jit(solution)/shard_map/ppermute | solution.py:14
  45.4 1.0 multiply_reduce_fusion
  47.5 1.5 %collective-permute-start.6 = (bf16[256,1024]{1,0:T(8,128)(2,1)}, bf16[256,1024]{1,0:T(8,128)(2,1)}, u32[]{:S(2)}, u32[]{:S(2)}) collective-permute-start(bf16[256,1024]{1,0:T(8,128)(2,1)} %multiply_convert_fusion), channel_id=1, source_target_pairs={{0,2},{1,3},{2,0},{3,1},{4,6},{5,7},{6,4},{7,5},{8,10},{9,11},{10,... | collective-permute-start | bytes 1572872 | tf_op jit(solution)/shard_map/ppermute | solution.py:14
  49.0 1.2 %copy.19 = bf16[256,1024]{0,1:T(8,128)(2,1)S(1)} copy(bf16[256,1024]{1,0:T(8,128)(2,1)} %param.8) | data formatting | bytes 1048576 | tf_op args[0]
  51.8 15.5 %collective-permute-done.5 = bf16[256,4,128]{2,0,1:T(8,128)(2,1)S(1)} collective-permute-done((bf16[256,4,128]{2,0,1:T(8,128)(2,1)S(1)}, bf16[256,4,128]{2,0,1:T(8,128)(2,1)S(1)}, u32[]{:S(2)}, u32[]{:S(2)}) %collective-permute-start.5) | collective-permute-done | bytes 262176 | tf_op jit(solution)/shard_map/ppermute | solution.py:14
  68.5 1.9 %fusion.4 = f32[4,2,64,1024]{3,2,1,0:T(8,128)S(1)} fusion(bf16[4,2,64,512]{3,2,1,0:T(8,128)(2,1)S(1)} %bitcast.60, bf16[256,1024]{1,0:T(8,128)(2,1)} %collective-permute-done.6, bf16[256,1024]{1,0:T(8,128)(2,1)} %multiply_convert_fusion), kind=kOutput, calls=%fused_computation.12 | convolution fusion | flops 538968064 | bytes 3670016 | tf_op jit(solution)/shard_map/dot_general | solution.py:56
  70.4 1.3 %copy-done.3 = f32[4,2,64,1024]{3,2,1,0:T(8,128)} copy-done((f32[4,2,64,1024]{3,2,1,0:T(8,128)}, f32[4,2,64,1024]{3,2,1,0:T(8,128)S(1)}, u32[]{:S(2)}) %copy-start.3) | copy-done | bytes 2097176
  71.7 1.1 dynamic-slice_bitcast_fusion
  74.2 2.5 %compare_select_fusion = (s32[256,1]{0,1:T(1,128)S(1)}, s32[256,1]{0,1:T(1,128)S(1)}) fusion(s32[]{:T(128)S(6)} %axis_index.17, s32[]{:T(128)S(6)} %axis_index.14, s32[]{:T(128)} %bitcast.54, s32[]{:T(128)} %bitcast.23, s32[]{:T(128)} %bitcast.22, s32[]{:T(128)} %bitcast.21, s32[]{:T(128)} %bitcast.20), kind=kLoop, calls=%fused_computation.59 | loop fusion | flops 21760 | bytes 2076 | tf_op jit(solution)/shard_map/jit(_take)/jit(_where)/select_n | solution.py:156
  76.8 3.4 %gather_fusion = bf16[256,1024]{1,0:T(8,128)(2,1)S(1)} fusion(bf16[1024,1024]{1,0:T(8,128)(2,1)} %bitcast.59, s32[1024]{0:T(1024)S(1)} %pad_clamp_fusion), kind=kCustom, calls=%fused_computation | custom fusion | bytes 1049600 | tf_op jit(solution)/shard_map/jit(_take)/gather | solution.py:156
  80.2 1.7 %bitcast_add_fusion = f32[4,64,1024]{2,1,0:T(8,128)S(1)} fusion(f32[4,64,1024]{2,1,0:T(8,128)} %collective-permute-done.7, f32[4,2,64,1024]{3,2,1,0:T(8,128)} %copy-done.3, s32[]{:T(128)S(6)} %select_n.271), kind=kLoop, calls=%fused_computation.15 | loop fusion | flops 262144 | bytes 3145732 | tf_op jit(solution)/shard_map/add | solution.py:64
  82.0 4.2 %collective-permute-start.10 = (f32[64,1024]{1,0:T(8,128)S(1)}, f32[64,1024]{1,0:T(8,128)S(1)}, u32[]{:S(2)}, u32[]{:S(2)}) collective-permute-start(f32[64,1024]{1,0:T(8,128)S(1)} %get-tuple-element.15), channel_id=1, source_target_pairs={{0,12},{4,0},{8,4},{12,8},{1,13},{5,1},{9,5},{13,9},{2,14},{6,2},{... | collective-permute-start | bytes 786440 | tf_op jit(solution)/shard_map/ppermute | solution.py:10
  87.9 5.0 %collective-permute-done.10 = f32[64,1024]{1,0:T(8,128)S(1)} collective-permute-done((f32[64,1024]{1,0:T(8,128)S(1)}, f32[64,1024]{1,0:T(8,128)S(1)}, u32[]{:S(2)}, u32[]{:S(2)}) %collective-permute-start.10) | collective-permute-done | bytes 262176 | tf_op jit(solution)/shard_map/ppermute | solution.py:10
  92.9 6.1 %collective-permute-done.8 = f32[64,1024]{1,0:T(8,128)S(1)} collective-permute-done((f32[64,1024]{1,0:T(8,128)S(1)}, f32[64,1024]{1,0:T(8,128)S(1)}, u32[]{:S(2)}, u32[]{:S(2)}) %collective-permute-start.8) | collective-permute-done | bytes 262176 | tf_op jit(solution)/shard_map/ppermute | solution.py:10
  99.0 11.4 %collective-permute-done.9 = f32[64,1024]{1,0:T(8,128)S(1)} collective-permute-done((f32[64,1024]{1,0:T(8,128)S(1)}, f32[64,1024]{1,0:T(8,128)S(1)}, u32[]{:S(2)}, u32[]{:S(2)}) %collective-permute-start.9) | collective-permute-done | bytes 262176 | tf_op jit(solution)/shard_map/ppermute | solution.py:10
  (61 shorter events, 16.9 us)
Async XLA Ops:
  0.6 24.3 %copy-start = (bf16[1024,1024]{1,0:T(8,128)(2,1)S(1)}, bf16[1024,1024]{1,0:T(8,128)(2,1)}, u32[]{:S(2)}) copy-start(bf16[1024,1024]{1,0:T(8,128)(2,1)} %param.10) | copy-start | bytes 6291460
  0.6 2.3 %copy-start.2 = (bf16[256,1024]{1,0:T(8,128)(2,1)S(1)}, bf16[256,1024]{1,0:T(8,128)(2,1)}, u32[]{:S(2)}) copy-start(bf16[256,1024]{1,0:T(8,128)(2,1)} %param.12) | copy-start | bytes 1572868
  0.7 24.3 %copy-start.4 = (bf16[256,1024]{1,0:T(8,128)(2,1)S(1)}, bf16[256,1024]{1,0:T(8,128)(2,1)}, u32[]{:S(2)}) copy-start(bf16[256,1024]{1,0:T(8,128)(2,1)} %param.8) | copy-start | bytes 1572868
  3.1 10.3 %collective-permute-start = (bf16[80,1024]{1,0:T(8,128)(2,1)S(1)}, bf16[80,1024]{1,0:T(8,128)(2,1)S(1)}, u32[]{:S(2)}, u32[]{:S(2)}) collective-permute-start(bf16[80,1024]{1,0:T(8,128)(2,1)S(1)} %pad_maximum_fusion.3), channel_id=1, source_target_pairs={{0,4},{4,8},{8,12},{12,0},{1,5},{5,9},{9,13},{13,1},{2,6},{6,10},{... | collective-permute-start | bytes 491528 | tf_op jit(solution)/shard_map/ppermute | solution.py:10
  6.2 13.3 %collective-permute-start.1 = (bf16[80,1024]{1,0:T(8,128)(2,1)S(1)}, bf16[80,1024]{1,0:T(8,128)(2,1)S(1)}, u32[]{:S(2)}, u32[]{:S(2)}) collective-permute-start(bf16[80,1024]{1,0:T(8,128)(2,1)S(1)} %pad_maximum_fusion.3), channel_id=1, source_target_pairs={{0,8},{4,12},{8,0},{12,4},{1,9},{5,13},{9,1},{13,5},{2,10},{6,14},... | collective-permute-start | bytes 491528 | tf_op jit(solution)/shard_map/ppermute | solution.py:10
  8.8 11.4 %collective-permute-start.2 = (bf16[80,1024]{1,0:T(8,128)(2,1)S(1)}, bf16[80,1024]{1,0:T(8,128)(2,1)S(1)}, u32[]{:S(2)}, u32[]{:S(2)}) collective-permute-start(bf16[80,1024]{1,0:T(8,128)(2,1)S(1)} %pad_maximum_fusion.3), channel_id=1, source_target_pairs={{0,12},{4,0},{8,4},{12,8},{1,13},{5,1},{9,5},{13,9},{2,14},{6,2},{... | collective-permute-start | bytes 491528 | tf_op jit(solution)/shard_map/ppermute | solution.py:10
  23.4 14.1 %collective-permute-start.3 = (bf16[256,1024]{1,0:T(8,128)(2,1)}, bf16[256,1024]{1,0:T(8,128)(2,1)}, u32[]{:S(2)}, u32[]{:S(2)}) collective-permute-start(bf16[256,1024]{1,0:T(8,128)(2,1)} %slice_dynamic-update-slice_fusion.3), channel_id=1, source_target_pairs={{0,2},{1,3},{2,0},{3,1},{4,6},{5,7},{6,4},{7,5},{8,10},{9,11},{10,... | collective-permute-start | bytes 1572872 | tf_op jit(solution)/shard_map/ppermute | solution.py:14
  25.7 13.2 %copy-start.5 = (s32[256]{0:T(256)S(1)}, s32[256]{0:T(256)}, u32[]{:S(2)}) copy-start(s32[256]{0:T(256)} %param.15) | copy-start | bytes 3076
  38.8 2.7 %collective-permute-start.4 = (bf16[2,256,1024]{2,1,0:T(8,128)(2,1)S(1)}, bf16[2,256,1024]{2,1,0:T(8,128)(2,1)S(1)}, u32[]{:S(2)}, u32[]{:S(2)}) collective-permute-start(bf16[2,256,1024]{2,1,0:T(8,128)(2,1)S(1)} %get-tuple-element.18), channel_id=1, source_target_pairs={{0,1},{1,0},{2,3},{3,2},{4,5},{5,4},{6,7},{7,6},{8,9},{9,8},{10,11... | collective-permute-start | bytes 3145736 | tf_op jit(solution)/shard_map/ppermute | solution.py:14
  41.9 3.5 %copy-start.1 = (bf16[2,2,256,1024]{3,2,1,0:T(8,128)(2,1)}, bf16[2,2,256,1024]{3,2,1,0:T(8,128)(2,1)S(1)}, u32[]{:S(2)}) copy-start(bf16[2,2,256,1024]{3,2,1,0:T(8,128)(2,1)S(1)} %copy.18) | copy-start | bytes 6291460
  47.5 20.9 %collective-permute-start.6 = (bf16[256,1024]{1,0:T(8,128)(2,1)}, bf16[256,1024]{1,0:T(8,128)(2,1)}, u32[]{:S(2)}, u32[]{:S(2)}) collective-permute-start(bf16[256,1024]{1,0:T(8,128)(2,1)} %multiply_convert_fusion), channel_id=1, source_target_pairs={{0,2},{1,3},{2,0},{3,1},{4,6},{5,7},{6,4},{7,5},{8,10},{9,11},{10,... | collective-permute-start | bytes 1572872 | tf_op jit(solution)/shard_map/ppermute | solution.py:14
  51.2 16.1 %collective-permute-start.5 = (bf16[256,4,128]{2,0,1:T(8,128)(2,1)S(1)}, bf16[256,4,128]{2,0,1:T(8,128)(2,1)S(1)}, u32[]{:S(2)}, u32[]{:S(2)}) collective-permute-start(bf16[256,4,128]{2,0,1:T(8,128)(2,1)S(1)} %bitcast.65), channel_id=1, source_target_pairs={{0,2},{1,3},{2,0},{3,1},{4,6},{5,7},{6,4},{7,5},{8,10},{9,11},{10,... | collective-permute-start | bytes 786440 | tf_op jit(solution)/shard_map/ppermute | solution.py:14
  68.4 5.0 %copy-start.6 = (s32[16]{0:T(128)S(1)}, s32[16]{0:T(128)}, u32[]{:S(2)}) copy-start(s32[16]{0:T(128)} %param.14) | copy-start | bytes 196
  70.4 1.3 %copy-start.3 = (f32[4,2,64,1024]{3,2,1,0:T(8,128)}, f32[4,2,64,1024]{3,2,1,0:T(8,128)S(1)}, u32[]{:S(2)}) copy-start(f32[4,2,64,1024]{3,2,1,0:T(8,128)S(1)} %fusion.4) | copy-start | bytes 6291460
  72.8 7.5 %collective-permute-start.7 = (f32[4,64,1024]{2,1,0:T(8,128)}, f32[4,64,1024]{2,1,0:T(8,128)}, u32[]{:S(2)}, u32[]{:S(2)}) collective-permute-start(f32[4,64,1024]{2,1,0:T(8,128)} %dynamic-slice_bitcast_fusion), channel_id=1, source_target_pairs={{0,1},{1,0},{2,3},{3,2},{4,5},{5,4},{6,7},{7,6},{8,9},{9,8},{10,11... | collective-permute-start | bytes 3145736 | tf_op jit(solution)/shard_map/ppermute | solution.py:14
  82.0 10.9 %collective-permute-start.10 = (f32[64,1024]{1,0:T(8,128)S(1)}, f32[64,1024]{1,0:T(8,128)S(1)}, u32[]{:S(2)}, u32[]{:S(2)}) collective-permute-start(f32[64,1024]{1,0:T(8,128)S(1)} %get-tuple-element.15), channel_id=1, source_target_pairs={{0,12},{4,0},{8,4},{12,8},{1,13},{5,1},{9,5},{13,9},{2,14},{6,2},{... | collective-permute-start | bytes 786440 | tf_op jit(solution)/shard_map/ppermute | solution.py:10
  86.1 12.9 %collective-permute-start.8 = (f32[64,1024]{1,0:T(8,128)S(1)}, f32[64,1024]{1,0:T(8,128)S(1)}, u32[]{:S(2)}, u32[]{:S(2)}) collective-permute-start(f32[64,1024]{1,0:T(8,128)S(1)} %get-tuple-element.14), channel_id=1, source_target_pairs={{0,4},{4,8},{8,12},{12,0},{1,5},{5,9},{9,13},{13,1},{2,6},{6,10},{... | collective-permute-start | bytes 786440 | tf_op jit(solution)/shard_map/ppermute | solution.py:10
  86.1 24.3 %collective-permute-start.9 = (f32[64,1024]{1,0:T(8,128)S(1)}, f32[64,1024]{1,0:T(8,128)S(1)}, u32[]{:S(2)}, u32[]{:S(2)}) collective-permute-start(f32[64,1024]{1,0:T(8,128)S(1)} %get-tuple-element.16), channel_id=1, source_target_pairs={{0,8},{4,12},{8,0},{12,4},{1,9},{5,13},{9,1},{13,5},{2,10},{6,14},... | collective-permute-start | bytes 786440 | tf_op jit(solution)/shard_map/ppermute | solution.py:10

commit v3 on v2

--- a/solution.py
+++ b/solution.py
@@ -50,24 +50,30 @@
     x4 = query_inputs.reshape(q_dev, n_q, 2, hb * share)
     mine = lax.dynamic_index_in_dim(x4, side, 2, keepdims=False)
     other = lax.dynamic_index_in_dim(x4, 1 - side, 2, keepdims=False)
-    got_x, got_g = swap((other, grad_query), "dp", n_dp, hb)
+    got_x = swap(other, "dp", n_dp, hb)
     xs = jnp.concatenate([mine, got_x], axis=0).reshape(2 * q_dev, n_q * hb * share)
-    gs = jnp.concatenate([grad_query, got_g], axis=0)
-    term = lax.dot_general(xs, gs, (((0,), (0,)), ((), ())), preferred_element_type=jnp.float32)
     rest = bits[1:]
-    t = term.reshape((n_q,) + (2,) * len(rest) + (share, width))
-    for axis in reversed(range(len(rest))):
-        bit = rest[axis]
-        me = (dp // bit) % 2
-        keep = lax.dynamic_index_in_dim(t, me, 1 + axis, keepdims=False)
-        send = lax.dynamic_index_in_dim(t, 1 - me, 1 + axis, keepdims=False)
-        t = keep + swap(send, "dp", n_dp, bit)
-    t = t.reshape(n_q, share, width)
-    acc = lax.dynamic_index_in_dim(t, q, 0, keepdims=False)
-    for s in range(1, n_q):
-        part = lax.dynamic_index_in_dim(t, (q + s) % n_q, 0, keepdims=False)
-        acc = acc + shift(part, "queue", n_q, s)
-    return acc
+    halves = 2
+    cols = width // halves
+    out = []
+    for h in range(halves):
+        g_h = grad_query[:, h * cols:(h + 1) * cols]
+        gs = jnp.concatenate([g_h, swap(g_h, "dp", n_dp, hb)], axis=0)
+        term = lax.dot_general(xs, gs, (((0,), (0,)), ((), ())), preferred_element_type=jnp.float32)
+        t = term.reshape((n_q,) + (2,) * len(rest) + (share, cols))
+        for axis in reversed(range(len(rest))):
+            bit = rest[axis]
+            me = (dp // bit) % 2
+            keep = lax.dynamic_index_in_dim(t, me, 1 + axis, keepdims=False)
+            send = lax.dynamic_index_in_dim(t, 1 - me, 1 + axis, keepdims=False)
+            t = keep + swap(send, "dp", n_dp, bit)
+        t = t.reshape(n_q, share, cols)
+        acc = lax.dynamic_index_in_dim(t, q, 0, keepdims=False)
+        for s in range(1, n_q):
+            part = lax.dynamic_index_in_dim(t, (q + s) % n_q, 0, keepdims=False)
+            acc = acc + shift(part, "queue", n_q, s)
+        out.append(acc)
+    return jnp.concatenate(out, axis=1)
 
 
 def body(

time: 112 us -> 91.3 us (0.82)
  waiting for transfers between devices: 60.8 us -> 32.2 us
  starting transfers between devices: 15.6 us -> 24.6 us
  other arithmetic: 11.5 us -> 8.14 us
  local copies, waits for them, and re-layouts: 12.8 us -> 14.1 us
    ppermute x5 -> x7, waiting for transfers between devices: 29.5 us -> 13.7 us  [swap(): return lax.ppermute(x, axis, [(i, i ^ bit) for i in range(n)])]
    ppermute x6 -> x9, waiting for transfers between devices: 31.3 us -> 18.6 us  [shift(): return lax.ppermute(x, axis, [(i, (i + step) % n) for i in range(n)])]
    ppermute x6 -> x9, starting transfers between devices: 12 us -> 19.2 us  [shift(): return lax.ppermute(x, axis, [(i, (i + step) % n) for i in range(n)])]
    ppermute x5 -> x7, starting transfers between devices: 3.66 us -> 5.35 us  [swap(): return lax.ppermute(x, axis, [(i, i ^ bit) for i in range(n)])]
    add x1 -> x2, other arithmetic: 1.69 us -> 0.17 us  [reduce_scatter_grad(): t = keep + swap(send, 'dp', n_dp, bit)]
    another operation x2, other arithmetic: 1.53 us -> 0.33 us  [gather_queue(): payload = jnp.stack([payload, swap(payload, 'dp', n_dp, bit)], axis=t)]
    unnamed x20 -> x22, local copies, waits for them, and re-layouts: 5.81 us -> 5.55 us
  transfers between devices with their start and end apart: 11 -> 16, of which waited for: 8 -> 9; matrix products, arithmetic and copies ran while one was open for 12% -> 31% of each run, Pallas kernels for 0% -> 0%
where the time goes in v3:
time: 91.3 us; the launch traced here: 90.7 us
  waiting for transfers between devices  32.2 us (35%)
  starting transfers between devices  24.6 us (27%)
  local copies, waits for them, and re-layouts  14.1 us (15%)
  matrix products  9.92 us (11%)
  other arithmetic  8.14 us (9%)
  between operations  1.7 us (2%)
    ppermute x9, starting transfers between devices, shift(): return lax.ppermute(x, axis, [(i, (i + step) % n) for i in range(n)])  19.2 us
    ppermute x9, waiting for transfers between devices, shift(): return lax.ppermute(x, axis, [(i, (i + step) % n) for i in range(n)])  18.6 us
    ppermute x7, waiting for transfers between devices, swap(): return lax.ppermute(x, axis, [(i, i ^ bit) for i in range(n)])  13.7 us
    unnamed x22, local copies, waits for them, and re-layouts  5.55 us
    ppermute x7, starting transfers between devices, swap(): return lax.ppermute(x, axis, [(i, i ^ bit) for i in range(n)])  5.35 us
    gather x1, local copies, waits for them, and re-layouts, body(): jnp.take(remote, source, axis=0)  4.21 us
    select_n x1, other arithmetic, body(): jnp.take(remote, source, axis=0)  2.59 us
    dot_general x1, matrix products, body(): fresh = jnp.dot(key_inputs, key_weight, preferred_element_type=jnp.float32)  2.27 us
  transfers between devices with their start and end apart: 16, of which 9 were waited for; matrix products, arithmetic and copies ran while one was open for 31% of the time, Pallas kernels for 0%

profile of v3, /device:TPU:0, one launch (start us, length us, event | category | flops | bytes accessed | tf_op | source)
XLA Modules:
  0.0 90.7 jit_solution(16845381110310550203)
XLA Ops:
  0.7 2.3 %multiply_reduce_fusion.3 = (f32[16]{0:T(128)S(1)}, f32[16,1024]{1,0:T(8,128)S(1)}) fusion(bf16[16,1024]{1,0:T(8,128)(2,1)} %param.9, bf16[1024,1024]{1,0:T(8,128)(2,1)} %param.11), kind=kOutput, calls=%fused_computation.66 | convolution fusion | flops 33587184 | bytes 2195520 | tf_op jit(solution)/shard_map/dot_general | solution.py:99
  3.7 3.1 %collective-permute-start = (bf16[80,1024]{1,0:T(8,128)(2,1)}, bf16[80,1024]{1,0:T(8,128)(2,1)}, u32[]{:S(2)}, u32[]{:S(2)}) collective-permute-start(bf16[80,1024]{1,0:T(8,128)(2,1)} %pad_maximum_fusion.4), channel_id=1, source_target_pairs={{0,4},{4,8},{8,12},{12,0},{1,5},{5,9},{9,13},{13,1},{2,6},{6,10},{... | collective-permute-start | bytes 491528 | tf_op jit(solution)/shard_map/ppermute | solution.py:10
  6.8 2.6 %collective-permute-start.1 = (bf16[80,1024]{1,0:T(8,128)(2,1)}, bf16[80,1024]{1,0:T(8,128)(2,1)}, u32[]{:S(2)}, u32[]{:S(2)}) collective-permute-start(bf16[80,1024]{1,0:T(8,128)(2,1)} %pad_maximum_fusion.4), channel_id=1, source_target_pairs={{0,8},{4,12},{8,0},{12,4},{1,9},{5,13},{9,1},{13,5},{2,10},{6,14},... | collective-permute-start | bytes 491528 | tf_op jit(solution)/shard_map/ppermute | solution.py:10
  9.4 1.3 %collective-permute-start.2 = (bf16[80,1024]{1,0:T(8,128)(2,1)}, bf16[80,1024]{1,0:T(8,128)(2,1)}, u32[]{:S(2)}, u32[]{:S(2)}) collective-permute-start(bf16[80,1024]{1,0:T(8,128)(2,1)} %pad_maximum_fusion.4), channel_id=1, source_target_pairs={{0,12},{4,0},{8,4},{12,8},{1,13},{5,1},{9,5},{13,9},{2,14},{6,2},{... | collective-permute-start | bytes 491528 | tf_op jit(solution)/shard_map/ppermute | solution.py:10
  10.7 1.2 %copy.19 = bf16[256,1024]{0,1:T(8,128)(2,1)S(1)} copy(bf16[256,1024]{1,0:T(8,128)(2,1)} %param.8) | data formatting | bytes 1048576 | tf_op args[0]
  12.9 1.6 %collective-permute-start.5 = (bf16[256,4,128]{2,0,1:T(8,128)(2,1)S(1)}, bf16[256,4,128]{2,0,1:T(8,128)(2,1)S(1)}, u32[]{:S(2)}, u32[]{:S(2)}) collective-permute-start(bf16[256,4,128]{2,0,1:T(8,128)(2,1)S(1)} %bitcast.90), channel_id=1, source_target_pairs={{0,2},{1,3},{2,0},{3,1},{4,6},{5,7},{6,4},{7,5},{8,10},{9,11},{10,... | collective-permute-start | bytes 786440 | tf_op jit(solution)/shard_map/ppermute | solution.py:14
  16.2 4.2 %collective-permute-done.1 = bf16[80,1024]{1,0:T(8,128)(2,1)} collective-permute-done((bf16[80,1024]{1,0:T(8,128)(2,1)}, bf16[80,1024]{1,0:T(8,128)(2,1)}, u32[]{:S(2)}, u32[]{:S(2)}) %collective-permute-start.1) | collective-permute-done | bytes 163872 | tf_op jit(solution)/shard_map/ppermute | solution.py:10
  24.7 1.5 %collective-permute-start.3 = (bf16[256,1024]{1,0:T(8,128)(2,1)S(1)}, bf16[256,1024]{1,0:T(8,128)(2,1)S(1)}, u32[]{:S(2)}, u32[]{:S(2)}) collective-permute-start(bf16[256,1024]{1,0:T(8,128)(2,1)S(1)} %slice_dynamic-update-slice_fusion.3), channel_id=1, source_target_pairs={{0,2},{1,3},{2,0},{3,1},{4,6},{5,7},{6,4},{7,5},{8,10},{9,11},{10,... | collective-permute-start | bytes 1572872 | tf_op jit(solution)/shard_map/ppermute | solution.py:14
  26.8 2.6 %compare_select_fusion = (s32[256,1]{0,1:T(1,128)S(1)}, s32[256,1]{0,1:T(1,128)S(1)}) fusion(s32[]{:T(128)S(6)} %axis_index.17, s32[]{:T(128)S(6)} %axis_index.14, s32[]{:T(128)} %bitcast.76, s32[]{:T(128)} %bitcast.32, s32[]{:T(128)} %bitcast.31, s32[]{:T(128)} %bitcast.30, s32[]{:T(128)} %bitcast.29), kind=kLoop, calls=%fused_computation.72 | loop fusion | flops 21760 | bytes 2076 | tf_op jit(solution)/shard_map/jit(_take)/jit(_where)/select_n | solution.py:162
  29.4 1.8 %multiply_reduce_fusion.2 = (f32[256]{0:T(256)S(1)}, f32[256,1024]{1,0:T(8,128)S(1)}) fusion(bf16[256,1024]{1,0:T(8,128)(2,1)} %param.8, bf16[1024,1024]{1,0:T(8,128)(2,1)S(1)} %copy-done), kind=kOutput, calls=%fused_computation.16 | convolution fusion | flops 537394944 | bytes 3671040 | tf_op jit(solution)/shard_map/dot_general | solution.py:108
  31.2 7.2 %collective-permute-done.3 = bf16[256,1024]{1,0:T(8,128)(2,1)S(1)} collective-permute-done((bf16[256,1024]{1,0:T(8,128)(2,1)S(1)}, bf16[256,1024]{1,0:T(8,128)(2,1)S(1)}, u32[]{:S(2)}, u32[]{:S(2)}) %collective-permute-start.3) | collective-permute-done | bytes 524320 | tf_op jit(solution)/shard_map/ppermute | solution.py:14
  39.1 2.2 %collective-permute-done.4 = bf16[2,256,1024]{2,1,0:T(8,128)(2,1)S(1)} collective-permute-done((bf16[2,256,1024]{2,1,0:T(8,128)(2,1)S(1)}, bf16[2,256,1024]{2,1,0:T(8,128)(2,1)S(1)}, u32[]{:S(2)}, u32[]{:S(2)}) %collective-permute-start.4) | collective-permute-done | bytes 1048608 | tf_op jit(solution)/shard_map/ppermute | solution.py:14
  45.2 1.0 %multiply_reduce_fusion = (f32[256]{0:T(256)S(1)}, f32[256,1024]{1,0:T(8,128)S(1)}) fusion(f32[256,1024]{1,0:T(8,128)S(1)} %get-tuple-element.33, f32[256]{0:T(256)S(1)} %add_rsqrt_fusion, f32[256,1024]{1,0:T(8,128)S(1)} %get-tuple-element.34, f32[256]{0:T(256)S(1)} %get-tuple-element.6, f32[256,1024]{1,0:T(8,128)S(1)} %fusion.23, ...), kind=kOutput, calls=%fused_computation.12 | convolution fusion | flops 539229952 | bytes 7344128 | tf_op jit(solution)/shard_map/dot_general | solution.py:123
  47.3 1.5 %collective-permute-start.6 = (bf16[256,512]{1,0:T(8,128)(2,1)}, bf16[256,512]{1,0:T(8,128)(2,1)}, u32[]{:S(2)}, u32[]{:S(2)}) collective-permute-start(bf16[256,512]{1,0:T(8,128)(2,1)} %get-tuple-element.19), channel_id=1, source_target_pairs={{0,2},{1,3},{2,0},{3,1},{4,6},{5,7},{6,4},{7,5},{8,10},{9,11},{10,... | collective-permute-start | bytes 786440 | tf_op jit(solution)/shard_map/ppermute | solution.py:14
  49.8 1.0 %pad_maximum_fusion.2 = bf16[512,512]{0,1:T(8,128)(2,1)S(1)} fusion(bf16[256,512]{0,1:T(8,128)(2,1)} %bitcast.86, bf16[256,512]{0,1:T(8,128)(2,1)S(1)} %bitcast.85), kind=kLoop, calls=%fused_computation.21 | loop fusion | flops 1048576 | bytes 1048576 | tf_op jit(solution)/shard_map/concatenate | solution.py:54
  51.4 4.2 %gather_fusion = bf16[256,1024]{1,0:T(8,128)(2,1)} fusion(bf16[1024,1024]{1,0:T(8,128)(2,1)} %bitcast.81, s32[1024]{0:T(1024)S(1)} %pad_clamp_fusion), kind=kCustom, calls=%fused_computation | custom fusion | bytes 1049600 | tf_op jit(solution)/shard_map/jit(_take)/gather | solution.py:162
  55.6 1.2 %collective-permute-done.6 = bf16[256,512]{1,0:T(8,128)(2,1)} collective-permute-done((bf16[256,512]{1,0:T(8,128)(2,1)}, bf16[256,512]{1,0:T(8,128)(2,1)}, u32[]{:S(2)}, u32[]{:S(2)}) %collective-permute-start.6) | collective-permute-done | bytes 262176 | tf_op jit(solution)/shard_map/ppermute | solution.py:14
  56.8 1.5 %fusion.9 = f32[4,2,64,512]{3,2,1,0:T(8,128)S(1)} fusion(bf16[4,2,64,512]{3,2,1,0:T(8,128)(2,1)S(1)} %bitcast.82, bf16[256,512]{1,0:T(8,128)(2,1)} %collective-permute-done.6, bf16[256,512]{1,0:T(8,128)(2,1)} %get-tuple-element.19), kind=kOutput, calls=%fused_computation.23 | convolution fusion | flops 269484032 | bytes 2097152 | tf_op jit(solution)/shard_map/dot_general | solution.py:62
  58.4 3.1 %collective-permute-done.11 = bf16[256,512]{1,0:T(8,128)(2,1)S(1)} collective-permute-done((bf16[256,512]{1,0:T(8,128)(2,1)}, bf16[256,512]{1,0:T(8,128)(2,1)S(1)}, u32[]{:S(2)}, u32[]{:S(2)}) %collective-permute-start.11) | collective-permute-done | bytes 262176 | tf_op jit(solution)/shard_map/ppermute | solution.py:14
  63.1 4.2 %collective-permute-start.10 = (f32[64,512]{1,0:T(8,128)S(1)}, f32[64,512]{1,0:T(8,128)S(1)}, u32[]{:S(2)}, u32[]{:S(2)}) collective-permute-start(f32[64,512]{1,0:T(8,128)S(1)} %get-tuple-element.17), channel_id=1, source_target_pairs={{0,12},{4,0},{8,4},{12,8},{1,13},{5,1},{9,5},{13,9},{2,14},{6,2},{... | collective-permute-start | bytes 393224 | tf_op jit(solution)/shard_map/ppermute | solution.py:10
  68.1 3.8 %collective-permute-start.13 = (f32[64,512]{1,0:T(8,128)S(1)}, f32[64,512]{1,0:T(8,128)S(1)}, u32[]{:S(2)}, u32[]{:S(2)}) collective-permute-start(f32[64,512]{1,0:T(8,128)S(1)} %get-tuple-element.21), channel_id=1, source_target_pairs={{0,4},{4,8},{8,12},{12,0},{1,5},{5,9},{9,13},{13,1},{2,6},{6,10},{... | collective-permute-start | bytes 393224 | tf_op jit(solution)/shard_map/ppermute | solution.py:10
  71.9 3.6 %collective-permute-start.15 = (f32[64,512]{1,0:T(8,128)S(1)}, f32[64,512]{1,0:T(8,128)S(1)}, u32[]{:S(2)}, u32[]{:S(2)}) collective-permute-start(f32[64,512]{1,0:T(8,128)S(1)} %get-tuple-element.22), channel_id=1, source_target_pairs={{0,12},{4,0},{8,4},{12,8},{1,13},{5,1},{9,5},{13,9},{2,14},{6,2},{... | collective-permute-start | bytes 393224 | tf_op jit(solution)/shard_map/ppermute | solution.py:10
  75.6 10.7 %collective-permute-done.9 = f32[64,512]{1,0:T(8,128)S(1)} collective-permute-done((f32[64,512]{1,0:T(8,128)S(1)}, f32[64,512]{1,0:T(8,128)S(1)}, u32[]{:S(2)}, u32[]{:S(2)}) %collective-permute-start.9) | collective-permute-done | bytes 131104 | tf_op jit(solution)/shard_map/ppermute | solution.py:10
  86.4 2.7 %collective-permute-done.14 = f32[64,512]{1,0:T(8,128)S(1)} collective-permute-done((f32[64,512]{1,0:T(8,128)S(1)}, f32[64,512]{1,0:T(8,128)S(1)}, u32[]{:S(2)}, u32[]{:S(2)}) %collective-permute-start.14) | collective-permute-done | bytes 131104 | tf_op jit(solution)/shard_map/ppermute | solution.py:10
  (80 shorter events, 19.0 us)
Async XLA Ops:
  0.6 28.8 %copy-start = (bf16[1024,1024]{1,0:T(8,128)(2,1)S(1)}, bf16[1024,1024]{1,0:T(8,128)(2,1)}, u32[]{:S(2)}) copy-start(bf16[1024,1024]{1,0:T(8,128)(2,1)} %param.10) | copy-start | bytes 6291460
  0.6 2.3 %copy-start.2 = (bf16[256,1024]{1,0:T(8,128)(2,1)S(1)}, bf16[256,1024]{1,0:T(8,128)(2,1)}, u32[]{:S(2)}) copy-start(bf16[256,1024]{1,0:T(8,128)(2,1)} %param.12) | copy-start | bytes 1572868
  2.9 12.2 %copy-start.7 = (s32[16]{0:T(128)S(1)}, s32[16]{0:T(128)}, u32[]{:S(2)}) copy-start(s32[16]{0:T(128)} %param.14) | copy-start | bytes 196
  3.7 11.6 %collective-permute-start = (bf16[80,1024]{1,0:T(8,128)(2,1)}, bf16[80,1024]{1,0:T(8,128)(2,1)}, u32[]{:S(2)}, u32[]{:S(2)}) collective-permute-start(bf16[80,1024]{1,0:T(8,128)(2,1)} %pad_maximum_fusion.4), channel_id=1, source_target_pairs={{0,4},{4,8},{8,12},{12,0},{1,5},{5,9},{9,13},{13,1},{2,6},{6,10},{... | collective-permute-start | bytes 491528 | tf_op jit(solution)/shard_map/ppermute | solution.py:10
  6.8 13.7 %collective-permute-start.1 = (bf16[80,1024]{1,0:T(8,128)(2,1)}, bf16[80,1024]{1,0:T(8,128)(2,1)}, u32[]{:S(2)}, u32[]{:S(2)}) collective-permute-start(bf16[80,1024]{1,0:T(8,128)(2,1)} %pad_maximum_fusion.4), channel_id=1, source_target_pairs={{0,8},{4,12},{8,0},{12,4},{1,9},{5,13},{9,1},{13,5},{2,10},{6,14},... | collective-permute-start | bytes 491528 | tf_op jit(solution)/shard_map/ppermute | solution.py:10
  9.4 12.0 %collective-permute-start.2 = (bf16[80,1024]{1,0:T(8,128)(2,1)}, bf16[80,1024]{1,0:T(8,128)(2,1)}, u32[]{:S(2)}, u32[]{:S(2)}) collective-permute-start(bf16[80,1024]{1,0:T(8,128)(2,1)} %pad_maximum_fusion.4), channel_id=1, source_target_pairs={{0,12},{4,0},{8,4},{12,8},{1,13},{5,1},{9,5},{13,9},{2,14},{6,2},{... | collective-permute-start | bytes 491528 | tf_op jit(solution)/shard_map/ppermute | solution.py:10
  12.9 36.0 %collective-permute-start.5 = (bf16[256,4,128]{2,0,1:T(8,128)(2,1)S(1)}, bf16[256,4,128]{2,0,1:T(8,128)(2,1)S(1)}, u32[]{:S(2)}, u32[]{:S(2)}) collective-permute-start(bf16[256,4,128]{2,0,1:T(8,128)(2,1)S(1)} %bitcast.90), channel_id=1, source_target_pairs={{0,2},{1,3},{2,0},{3,1},{4,6},{5,7},{6,4},{7,5},{8,10},{9,11},{10,... | collective-permute-start | bytes 786440 | tf_op jit(solution)/shard_map/ppermute | solution.py:14
  24.7 13.8 %collective-permute-start.3 = (bf16[256,1024]{1,0:T(8,128)(2,1)S(1)}, bf16[256,1024]{1,0:T(8,128)(2,1)S(1)}, u32[]{:S(2)}, u32[]{:S(2)}) collective-permute-start(bf16[256,1024]{1,0:T(8,128)(2,1)S(1)} %slice_dynamic-update-slice_fusion.3), channel_id=1, source_target_pairs={{0,2},{1,3},{2,0},{3,1},{4,6},{5,7},{6,4},{7,5},{8,10},{9,11},{10,... | collective-permute-start | bytes 1572872 | tf_op jit(solution)/shard_map/ppermute | solution.py:14
  31.2 7.4 %copy-start.6 = (s32[256]{0:T(256)S(1)}, s32[256]{0:T(256)}, u32[]{:S(2)}) copy-start(s32[256]{0:T(256)} %param.15) | copy-start | bytes 3076
  38.5 2.7 %collective-permute-start.4 = (bf16[2,256,1024]{2,1,0:T(8,128)(2,1)S(1)}, bf16[2,256,1024]{2,1,0:T(8,128)(2,1)S(1)}, u32[]{:S(2)}, u32[]{:S(2)}) collective-permute-start(bf16[2,256,1024]{2,1,0:T(8,128)(2,1)S(1)} %get-tuple-element.15), channel_id=1, source_target_pairs={{0,1},{1,0},{2,3},{3,2},{4,5},{5,4},{6,7},{7,6},{8,9},{9,8},{10,11... | collective-permute-start | bytes 3145736 | tf_op jit(solution)/shard_map/ppermute | solution.py:14
  41.7 3.5 %copy-start.1 = (bf16[2,2,256,1024]{3,2,1,0:T(8,128)(2,1)}, bf16[2,2,256,1024]{3,2,1,0:T(8,128)(2,1)S(1)}, u32[]{:S(2)}) copy-start(bf16[2,2,256,1024]{3,2,1,0:T(8,128)(2,1)S(1)} %copy.18) | copy-start | bytes 6291460
  46.2 3.6 %copy-start.4 = (bf16[256,4,1,128]{0,3,2,1:T(8,128)(2,1)S(1)}, bf16[256,4,1,128]{0,3,2,1:T(8,128)(2,1)}, u32[]{:S(2)}) copy-start(bf16[256,4,1,128]{0,3,2,1:T(8,128)(2,1)} %get-tuple-element.24) | copy-start | bytes 786436
  47.3 9.5 %collective-permute-start.6 = (bf16[256,512]{1,0:T(8,128)(2,1)}, bf16[256,512]{1,0:T(8,128)(2,1)}, u32[]{:S(2)}, u32[]{:S(2)}) collective-permute-start(bf16[256,512]{1,0:T(8,128)(2,1)} %get-tuple-element.19), channel_id=1, source_target_pairs={{0,2},{1,3},{2,0},{3,1},{4,6},{5,7},{6,4},{7,5},{8,10},{9,11},{10,... | collective-permute-start | bytes 786440 | tf_op jit(solution)/shard_map/ppermute | solution.py:14
  50.8 10.7 %collective-permute-start.11 = (bf16[256,512]{1,0:T(8,128)(2,1)}, bf16[256,512]{1,0:T(8,128)(2,1)S(1)}, u32[]{:S(2)}, u32[]{:S(2)}) collective-permute-start(bf16[256,512]{1,0:T(8,128)(2,1)} %get-tuple-element.20), channel_id=1, source_target_pairs={{0,2},{1,3},{2,0},{3,1},{4,6},{5,7},{6,4},{7,5},{8,10},{9,11},{10,... | collective-permute-start | bytes 786440 | tf_op jit(solution)/shard_map/ppermute | solution.py:14
  55.6 5.9 %copy-start.5 = (bf16[256,512]{1,0:T(8,128)(2,1)S(1)}, bf16[256,512]{1,0:T(8,128)(2,1)}, u32[]{:S(2)}) copy-start(bf16[256,512]{1,0:T(8,128)(2,1)} %get-tuple-element.20) | copy-start | bytes 786436
  58.3 3.8 %copy-start.3 = (bf16[256,1024]{1,0:T(8,128)(2,1)S(1)}, bf16[256,1024]{1,0:T(8,128)(2,1)}, u32[]{:S(2)}) copy-start(bf16[256,1024]{1,0:T(8,128)(2,1)} %gather_fusion) | copy-start | bytes 1572868
  58.3 4.7 %collective-permute-start.7 = (f32[4,64,512]{2,1,0:T(8,128)S(1)}, f32[4,64,512]{2,1,0:T(8,128)S(1)}, u32[]{:S(2)}, u32[]{:S(2)}) collective-permute-start(f32[4,64,512]{2,1,0:T(8,128)S(1)} %dynamic-slice_bitcast_fusion.1), channel_id=1, source_target_pairs={{0,1},{1,0},{2,3},{3,2},{4,5},{5,4},{6,7},{7,6},{8,9},{9,8},{10,11... | collective-permute-start | bytes 1572872 | tf_op jit(solution)/shard_map/ppermute | solution.py:14
  62.0 6.0 %collective-permute-start.12 = (f32[4,64,512]{2,1,0:T(8,128)S(1)}, f32[4,64,512]{2,1,0:T(8,128)S(1)}, u32[]{:S(2)}, u32[]{:S(2)}) collective-permute-start(f32[4,64,512]{2,1,0:T(8,128)S(1)} %dynamic-slice_bitcast_fusion), channel_id=1, source_target_pairs={{0,1},{1,0},{2,3},{3,2},{4,5},{5,4},{6,7},{7,6},{8,9},{9,8},{10,11... | collective-permute-start | bytes 1572872 | tf_op jit(solution)/shard_map/ppermute | solution.py:14
  63.1 8.7 %collective-permute-start.10 = (f32[64,512]{1,0:T(8,128)S(1)}, f32[64,512]{1,0:T(8,128)S(1)}, u32[]{:S(2)}, u32[]{:S(2)}) collective-permute-start(f32[64,512]{1,0:T(8,128)S(1)} %get-tuple-element.17), channel_id=1, source_target_pairs={{0,12},{4,0},{8,4},{12,8},{1,13},{5,1},{9,5},{13,9},{2,14},{6,2},{... | collective-permute-start | bytes 393224 | tf_op jit(solution)/shard_map/ppermute | solution.py:10
  67.3 8.3 %collective-permute-start.8 = (f32[64,512]{1,0:T(8,128)S(1)}, f32[64,512]{1,0:T(8,128)S(1)}, u32[]{:S(2)}, u32[]{:S(2)}) collective-permute-start(f32[64,512]{1,0:T(8,128)S(1)} %get-tuple-element.16), channel_id=1, source_target_pairs={{0,4},{4,8},{8,12},{12,0},{1,5},{5,9},{9,13},{13,1},{2,6},{6,10},{... | collective-permute-start | bytes 393224 | tf_op jit(solution)/shard_map/ppermute | solution.py:10
  67.3 19.0 %collective-permute-start.9 = (f32[64,512]{1,0:T(8,128)S(1)}, f32[64,512]{1,0:T(8,128)S(1)}, u32[]{:S(2)}, u32[]{:S(2)}) collective-permute-start(f32[64,512]{1,0:T(8,128)S(1)} %get-tuple-element.18), channel_id=1, source_target_pairs={{0,8},{4,12},{8,0},{12,4},{1,9},{5,13},{9,1},{13,5},{2,10},{6,14},... | collective-permute-start | bytes 393224 | tf_op jit(solution)/shard_map/ppermute | solution.py:10
  68.1 18.3 %collective-permute-start.13 = (f32[64,512]{1,0:T(8,128)S(1)}, f32[64,512]{1,0:T(8,128)S(1)}, u32[]{:S(2)}, u32[]{:S(2)}) collective-permute-start(f32[64,512]{1,0:T(8,128)S(1)} %get-tuple-element.21), channel_id=1, source_target_pairs={{0,4},{4,8},{8,12},{12,0},{1,5},{5,9},{9,13},{13,1},{2,6},{6,10},{... | collective-permute-start | bytes 393224 | tf_op jit(solution)/shard_map/ppermute | solution.py:10
  71.9 17.2 %collective-permute-start.14 = (f32[64,512]{1,0:T(8,128)S(1)}, f32[64,512]{1,0:T(8,128)S(1)}, u32[]{:S(2)}, u32[]{:S(2)}) collective-permute-start(f32[64,512]{1,0:T(8,128)S(1)} %get-tuple-element.23), channel_id=1, source_target_pairs={{0,8},{4,12},{8,0},{12,4},{1,9},{5,13},{9,1},{13,5},{2,10},{6,14},... | collective-permute-start | bytes 393224 | tf_op jit(solution)/shard_map/ppermute | solution.py:10
  71.9 18.0 %collective-permute-start.15 = (f32[64,512]{1,0:T(8,128)S(1)}, f32[64,512]{1,0:T(8,128)S(1)}, u32[]{:S(2)}, u32[]{:S(2)}) collective-permute-start(f32[64,512]{1,0:T(8,128)S(1)} %get-tuple-element.22), channel_id=1, source_target_pairs={{0,12},{4,0},{8,4},{12,8},{1,13},{5,1},{9,5},{13,9},{2,14},{6,2},{... | collective-permute-start | bytes 393224 | tf_op jit(solution)/shard_map/ppermute | solution.py:10

commit v4 on v3

--- a/solution.py
+++ b/solution.py
@@ -23,19 +23,24 @@
     return bits
 
 
-def gather_queue(queue_keys, fresh, n_q, n_dp):
+def gather_queue(queue_keys, key_inputs, n_q, n_dp, halves):
     dp = lax.axis_index("dp")
     k_dev, width = queue_keys.shape
     piece_rows = k_dev // n_dp
+    cols = width // halves
     piece = lax.dynamic_slice_in_dim(queue_keys, dp * piece_rows, piece_rows, 0)
-    packed = jnp.concatenate([piece, fresh], axis=0)
-    got = [shift(packed, "queue", n_q, s) for s in range(1, n_q)]
-    payload = jnp.concatenate(
-        [g[:piece_rows] for g in got] + [fresh] + [g[piece_rows:] for g in got], axis=0
-    )
-    for t, bit in enumerate(dp_bits(n_dp)):
-        payload = jnp.stack([payload, swap(payload, "dp", n_dp, bit)], axis=t)
-    return payload.reshape(n_dp, -1, width)
+    out = []
+    for h in range(halves):
+        mine = key_inputs[:, h * cols:(h + 1) * cols]
+        packed = jnp.concatenate([piece[:, h * cols:(h + 1) * cols], mine], axis=0)
+        got = [shift(packed, "queue", n_q, s) for s in range(1, n_q)]
+        payload = jnp.concatenate(
+            [g[:piece_rows] for g in got] + [mine] + [g[piece_rows:] for g in got], axis=0
+        )
+        for t, bit in enumerate(dp_bits(n_dp)):
+            payload = jnp.stack([payload, swap(payload, "dp", n_dp, bit)], axis=t)
+        out.append(payload.reshape(n_dp, -1, cols))
+    return out
 
 
 def reduce_scatter_grad(query_inputs, grad_query, n_q, n_dp):
@@ -96,31 +101,39 @@
     piece_rows = k_dev // n_dp
     far_rows = (n_q - 1) * piece_rows
 
-    fresh = jnp.dot(key_inputs, key_weight, preferred_element_type=jnp.float32)
-    fresh = (fresh * lax.rsqrt(jnp.sum(fresh * fresh, -1, keepdims=True) + 1e-06)).astype(
-        jnp.bfloat16
-    )
-    gathered = gather_queue(queue_keys, fresh, n_q, n_dp)
-    rows0 = gathered.shape[1]
-    remote = gathered.reshape(-1, width)
-    is_key = (jnp.arange(n_dp * rows0, dtype=jnp.int32) % rows0) < far_rows
+    halves = 2
+    cols = width // halves
+    gathered = gather_queue(queue_keys, key_inputs, n_q, n_dp, halves)
+    rows0 = gathered[0].shape[1]
+    n_far = n_dp * rows0
+    remote = [g.reshape(n_far, cols) for g in gathered]
+    is_key = (jnp.arange(n_far, dtype=jnp.int32) % rows0) < far_rows
 
     query = jnp.dot(query_inputs, query_weight, preferred_element_type=jnp.float32)
     inv_len = lax.rsqrt(jnp.sum(query * query, -1, keepdims=True) + 1e-06)
     unit_f = query * inv_len
     unit = unit_f.astype(jnp.bfloat16)
 
+    def by_halves(lhs, parts):
+        return jnp.concatenate(
+            [jnp.dot(lhs, p, preferred_element_type=jnp.float32) for p in parts], axis=1
+        )
+
     dims = (((1,), (1,)), ((), ()))
     near = lax.dot_general(unit, queue_keys, dims, preferred_element_type=jnp.float32) / temper
-    far = lax.dot_general(unit, remote, dims, preferred_element_type=jnp.float32) / temper
-    far = jnp.where(is_key[None, :], far, -jnp.inf)
+    far = lax.dot_general(unit[:, :cols], remote[0], dims, preferred_element_type=jnp.float32)
+    for h in range(1, halves):
+        far = far + lax.dot_general(
+            unit[:, h * cols:(h + 1) * cols], remote[h], dims, preferred_element_type=jnp.float32
+        )
+    far = jnp.where(is_key[None, :], far / temper, -jnp.inf)
     top = jnp.maximum(jnp.max(near, -1), jnp.max(far, -1))
     e_near = jnp.exp(near - top[:, None])
     e_far = jnp.exp(far - top[:, None])
     total = jnp.sum(e_near, -1) + jnp.sum(e_far, -1)
     mixture = jnp.dot(
         e_near.astype(jnp.bfloat16), queue_keys, preferred_element_type=jnp.float32
-    ) + jnp.dot(e_far.astype(jnp.bfloat16), remote, preferred_element_type=jnp.float32)
+    ) + by_halves(e_far.astype(jnp.bfloat16), remote)
 
     j = positive_index
     q_src = j // k_dev
@@ -132,11 +145,11 @@
     pick_near = (local[:, None] & (within[:, None] == jnp.arange(k_dev)[None, :])).astype(
         jnp.bfloat16
     )
-    pick_far = (
-        (~local)[:, None] & (far_at[:, None] == jnp.arange(n_dp * rows0)[None, :])
-    ).astype(jnp.bfloat16)
-    chosen = jnp.dot(pick_near, queue_keys, preferred_element_type=jnp.float32) + jnp.dot(
-        pick_far, remote, preferred_element_type=jnp.float32
+    pick_far = ((~local)[:, None] & (far_at[:, None] == jnp.arange(n_far)[None, :])).astype(
+        jnp.bfloat16
+    )
+    chosen = jnp.dot(pick_near, queue_keys, preferred_element_type=jnp.float32) + by_halves(
+        pick_far, remote
     )
 
     mixture = mixture / total[:, None]
@@ -159,7 +172,13 @@
     b_e = dp ^ (b % n_dp)
     b_s = (q - b // n_dp) % n_q
     source = b_e * rows0 + far_rows + b_s * new_dev + offset % new_dev
-    new_queue = jnp.where(live[:, None], jnp.take(remote, source, axis=0), queue_keys)
+    pick_new = (source[:, None] == jnp.arange(n_far)[None, :]).astype(jnp.bfloat16)
+    key_rows = by_halves(pick_new, remote).astype(jnp.bfloat16)
+    fresh = jnp.dot(key_rows, key_weight, preferred_element_type=jnp.float32)
+    fresh = (fresh * lax.rsqrt(jnp.sum(fresh * fresh, -1, keepdims=True) + 1e-06)).astype(
+        jnp.bfloat16
+    )
+    new_queue = jnp.where(live[:, None], fresh, queue_keys)
     return (loss, grad_rows, new_queue)
 
 

time: 91.3 us -> 102 us (1.12)
  other arithmetic: 8.14 us -> 14.2 us
  waiting for transfers between devices: 32.2 us -> 38.1 us
  matrix products: 9.92 us -> 8.87 us
    ppermute x7 -> x9, waiting for transfers between devices: 13.7 us -> 20.1 us  [swap(): return lax.ppermute(x, axis, [(i, i ^ bit) for i in range(n)])]
    another operation x2 -> x4, other arithmetic: 0.33 us -> 4.61 us  [gather_queue(): payload = jnp.stack([payload, swap(payload, 'dp', n_dp, bit)], axis=t)]
    gather x1 -> x0, local copies, waits for them, and re-layouts: 4.21 us -> none  [body(): jnp.take(remote, source, axis=0)]
    select_n x2 -> x1, other arithmetic: 3.53 us -> 1.01 us  [body(): new_queue = jnp.where(live[:, None], fresh, queue_keys)]
    gather x1, other arithmetic: 0.01 us -> 2.46 us  [body(): b = jnp.take(owner_block, sub_block)]
    slice x0 -> x2, local copies, waits for them, and re-layouts: none -> 1.77 us  [the longest x1 0.89 us: gather_queue(): mine = key_inputs[:, h * cols:(h + 1) * cols]]
    ppermute x9 -> x12, starting transfers between devices: 19.2 us -> 17.6 us  [shift(): return lax.ppermute(x, axis, [(i, (i + step) % n) for i in range(n)])]
    unnamed x22 -> x25, local copies, waits for them, and re-layouts: 5.55 us -> 7.01 us
  transfers between devices with their start and end apart: 16 -> 21, of which waited for: 9 -> 7; matrix products, arithmetic and copies ran while one was open for 31% -> 26% of each run, Pallas kernels for 0% -> 0%
where the time goes in v4:
time: 102 us; the launch traced here: 101 us
  waiting for transfers between devices  38.1 us (37%)
  starting transfers between devices  23.9 us (23%)
  local copies, waits for them, and re-layouts  14.8 us (15%)
  other arithmetic  14.2 us (14%)
  matrix products  8.87 us (9%)
  between operations  1.74 us (2%)
    ppermute x9, waiting for transfers between devices, swap(): return lax.ppermute(x, axis, [(i, i ^ bit) for i in range(n)])  20.1 us
    ppermute x12, waiting for transfers between devices, shift(): return lax.ppermute(x, axis, [(i, (i + step) % n) for i in range(n)])  17.9 us
    ppermute x12, starting transfers between devices, shift(): return lax.ppermute(x, axis, [(i, (i + step) % n) for i in range(n)])  17.6 us
    unnamed x25, local copies, waits for them, and re-layouts  7.01 us
    ppermute x9, starting transfers between devices, swap(): return lax.ppermute(x, axis, [(i, i ^ bit) for i in range(n)])  6.32 us
    another operation x4, other arithmetic, gather_queue(): payload = jnp.stack([payload, swap(payload, 'dp', n_dp, bit)], axis=t)  4.61 us
    dot_general x6, matrix products, by_halves(): jnp.dot(lhs, p, preferred_element_type=jnp.float32)  2.94 us
    gather x1, other arithmetic, body(): b = jnp.take(owner_block, sub_block)  2.46 us
  transfers between devices with their start and end apart: 21, of which 7 were waited for; matrix products, arithmetic and copies ran while one was open for 26% of the time, Pallas kernels for 0%

profile of v4, /device:TPU:0, one launch (start us, length us, event | category | flops | bytes accessed | tf_op | source)
XLA Modules:
  0.0 101.5 jit_solution(8039354159803942195)
XLA Ops:
  3.1 3.1 %collective-permute-start.5 = (bf16[80,512]{1,0:T(8,128)(2,1)}, bf16[80,512]{1,0:T(8,128)(2,1)}, u32[]{:S(2)}, u32[]{:S(2)}) collective-permute-start(bf16[80,512]{1,0:T(8,128)(2,1)} %pad_maximum_fusion.7), channel_id=1, source_target_pairs={{0,4},{4,8},{8,12},{12,0},{1,5},{5,9},{9,13},{13,1},{2,6},{6,10},{... | collective-permute-start | bytes 245768 | tf_op jit(solution)/shard_map/ppermute | solution.py:10
  6.1 2.6 %collective-permute-start.6 = (bf16[80,512]{1,0:T(8,128)(2,1)}, bf16[80,512]{1,0:T(8,128)(2,1)S(1)}, u32[]{:S(2)}, u32[]{:S(2)}) collective-permute-start(bf16[80,512]{1,0:T(8,128)(2,1)} %pad_maximum_fusion.7), channel_id=1, source_target_pairs={{0,8},{4,12},{8,0},{12,4},{1,9},{5,13},{9,1},{13,5},{2,10},{6,14},... | collective-permute-start | bytes 245768 | tf_op jit(solution)/shard_map/ppermute | solution.py:10
  8.7 1.3 %collective-permute-start.7 = (bf16[80,512]{1,0:T(8,128)(2,1)}, bf16[80,512]{1,0:T(8,128)(2,1)}, u32[]{:S(2)}, u32[]{:S(2)}) collective-permute-start(bf16[80,512]{1,0:T(8,128)(2,1)} %pad_maximum_fusion.7), channel_id=1, source_target_pairs={{0,12},{4,0},{8,4},{12,8},{1,13},{5,1},{9,5},{13,9},{2,14},{6,2},{... | collective-permute-start | bytes 245768 | tf_op jit(solution)/shard_map/ppermute | solution.py:10
  14.5 2.0 %copy.21 = bf16[256,1024]{0,1:T(8,128)(2,1)} copy(bf16[256,1024]{1,0:T(8,128)(2,1)} %param.8) | data formatting | bytes 1048576 | tf_op args[0]
  16.5 1.8 %multiply_reduce_fusion.3 = (f32[256]{0:T(256)S(1)}, f32[256,1024]{1,0:T(8,128)S(1)}) fusion(bf16[256,1024]{1,0:T(8,128)(2,1)} %param.8, bf16[1024,1024]{1,0:T(8,128)(2,1)S(1)} %copy-done), kind=kOutput, calls=%fused_computation.21 | convolution fusion | flops 537394944 | bytes 3671040 | tf_op jit(solution)/shard_map/dot_general | solution.py:112
  18.4 1.8 %constant_dynamic-slice_fusion.2 = (bf16[256,4,1,128]{0,3,2,1:T(8,128)(2,1)}, bf16[256,4,1,128]{0,3,2,1:T(8,128)(2,1)S(1)}) fusion(bf16[256,4,2,128]{0,3,2,1:T(8,128)(2,1)} %bitcast.99, s32[]{:T(128)S(6)} %select_n.218, s32[]{:T(128)S(6)} %select_n.219), kind=kLoop, calls=%fused_computation.111 | loop fusion | bytes 1048584 | tf_op jit(solution)/shard_map/jit(dynamic_index_in_dim)/dynamic_slice | solution.py:56
  21.0 2.5 %compare_select_fusion.3 = s32[256,1]{0,1:T(1,128)S(1)} fusion(s32[]{:T(128)} %bitcast.35, s32[]{:T(128)} %bitcast.36, s32[]{:T(128)} %bitcast.38, s32[]{:T(128)} %bitcast.37, s32[]{:T(128)} %bitcast.87), kind=kLoop, calls=%fused_computation.103 | loop fusion | flops 9472 | bytes 1044 | tf_op jit(solution)/shard_map/jit(_take)/gather | solution.py:171
  23.5 2.9 %collective-permute-start.2 = (bf16[80,512]{1,0:T(8,128)(2,1)}, bf16[80,512]{1,0:T(8,128)(2,1)S(1)}, u32[]{:S(2)}, u32[]{:S(2)}) collective-permute-start(bf16[80,512]{1,0:T(8,128)(2,1)} %pad_maximum_fusion.6), channel_id=1, source_target_pairs={{0,12},{4,0},{8,4},{12,8},{1,13},{5,1},{9,5},{13,9},{2,14},{6,2},{... | collective-permute-start | bytes 245768 | tf_op jit(solution)/shard_map/ppermute | solution.py:10
  27.2 1.6 %collective-permute-start.10 = (bf16[256,4,128]{2,0,1:T(8,128)(2,1)}, bf16[256,4,128]{2,0,1:T(8,128)(2,1)}, u32[]{:S(2)}, u32[]{:S(2)}) collective-permute-start(bf16[256,4,128]{2,0,1:T(8,128)(2,1)} %bitcast.104), channel_id=1, source_target_pairs={{0,2},{1,3},{2,0},{3,1},{4,6},{5,7},{6,4},{7,5},{8,10},{9,11},{10,... | collective-permute-start | bytes 786440 | tf_op jit(solution)/shard_map/ppermute | solution.py:14
  34.1 1.5 %collective-permute-start.8 = (bf16[256,512]{1,0:T(8,128)(2,1)S(1)}, bf16[256,512]{1,0:T(8,128)(2,1)S(1)}, u32[]{:S(2)}, u32[]{:S(2)}) collective-permute-start(bf16[256,512]{1,0:T(8,128)(2,1)S(1)} %constant_dynamic-update-slice_fusion.4), channel_id=1, source_target_pairs={{0,2},{1,3},{2,0},{3,1},{4,6},{5,7},{6,4},{7,5},{8,10},{9,11},{10,... | collective-permute-start | bytes 786440 | tf_op jit(solution)/shard_map/ppermute | solution.py:14
  35.7 9.7 %collective-permute-done.8 = bf16[256,512]{1,0:T(8,128)(2,1)S(1)} collective-permute-done((bf16[256,512]{1,0:T(8,128)(2,1)S(1)}, bf16[256,512]{1,0:T(8,128)(2,1)S(1)}, u32[]{:S(2)}, u32[]{:S(2)}) %collective-permute-start.8) | collective-permute-done | bytes 262176 | tf_op jit(solution)/shard_map/ppermute | solution.py:14
  48.1 1.8 %copy.23 = bf16[256,4,128]{0,2,1:T(8,128)(2,1)} copy(bf16[256,4,128]{2,0,1:T(8,128)(2,1)} %collective-permute-done.10) | data formatting | bytes 524288 | tf_op jit(solution)/shard_map/ppermute | solution.py:14
  50.9 1.4 %pad_maximum_fusion.1 = bf16[2,2,256,512]{3,2,0,1:T(8,128)(2,1)S(1)} fusion(bf16[2,1,256,512]{3,2,0,1:T(8,128)(2,1)} %bitcast.9, bf16[2,1,256,512]{3,2,0,1:T(8,128)(2,1)} %get-tuple-element.26), kind=kLoop, calls=%fused_computation.12 | loop fusion | flops 524288 | bytes 2097152 | tf_op jit(solution)/shard_map/stack | solution.py:41
  52.4 1.1 %pad_maximum_fusion = bf16[2,2,256,512]{3,2,1,0:T(8,128)(2,1)S(1)} fusion(bf16[2,1,256,512]{3,2,1,0:T(8,128)(2,1)} %bitcast.4, bf16[2,1,256,512]{3,2,1,0:T(8,128)(2,1)S(1)} %copy-done.2), kind=kLoop, calls=%fused_computation.11 | loop fusion | flops 524288 | bytes 2097152 | tf_op jit(solution)/shard_map/stack | solution.py:41
  60.3 1.6 %collective-permute-start.11 = (bf16[256,512]{1,0:T(8,128)(2,1)S(1)}, bf16[256,512]{1,0:T(8,128)(2,1)S(1)}, u32[]{:S(2)}, u32[]{:S(2)}) collective-permute-start(bf16[256,512]{1,0:T(8,128)(2,1)S(1)} %get-tuple-element.15), channel_id=1, source_target_pairs={{0,2},{1,3},{2,0},{3,1},{4,6},{5,7},{6,4},{7,5},{8,10},{9,11},{10,... | collective-permute-start | bytes 786440 | tf_op jit(solution)/shard_map/ppermute | solution.py:14
  63.2 6.3 %collective-permute-done.11 = bf16[256,512]{1,0:T(8,128)(2,1)S(1)} collective-permute-done((bf16[256,512]{1,0:T(8,128)(2,1)S(1)}, bf16[256,512]{1,0:T(8,128)(2,1)S(1)}, u32[]{:S(2)}, u32[]{:S(2)}) %collective-permute-start.11) | collective-permute-done | bytes 262176 | tf_op jit(solution)/shard_map/ppermute | solution.py:14
  70.1 4.1 %collective-permute-done.16 = bf16[256,512]{1,0:T(8,128)(2,1)S(1)} collective-permute-done((bf16[256,512]{1,0:T(8,128)(2,1)S(1)}, bf16[256,512]{1,0:T(8,128)(2,1)S(1)}, u32[]{:S(2)}, u32[]{:S(2)}) %collective-permute-start.16) | collective-permute-done | bytes 262176 | tf_op jit(solution)/shard_map/ppermute | solution.py:14
  76.6 1.3 %collective-permute-start.14 = (f32[64,512]{1,0:T(8,128)S(1)}, f32[64,512]{1,0:T(8,128)S(1)}, u32[]{:S(2)}, u32[]{:S(2)}) collective-permute-start(f32[64,512]{1,0:T(8,128)S(1)} %get-tuple-element.14), channel_id=1, source_target_pairs={{0,8},{4,12},{8,0},{12,4},{1,9},{5,13},{9,1},{13,5},{2,10},{6,14},... | collective-permute-start | bytes 393224 | tf_op jit(solution)/shard_map/ppermute | solution.py:10
  77.8 2.8 %collective-permute-start.15 = (f32[64,512]{1,0:T(8,128)S(1)}, f32[64,512]{1,0:T(8,128)S(1)}, u32[]{:S(2)}, u32[]{:S(2)}) collective-permute-start(f32[64,512]{1,0:T(8,128)S(1)} %get-tuple-element.13), channel_id=1, source_target_pairs={{0,12},{4,0},{8,4},{12,8},{1,13},{5,1},{9,5},{13,9},{2,14},{6,2},{... | collective-permute-start | bytes 393224 | tf_op jit(solution)/shard_map/ppermute | solution.py:10
  80.9 1.2 %collective-permute-start.19 = (f32[64,512]{1,0:T(8,128)S(1)}, f32[64,512]{1,0:T(8,128)S(1)}, u32[]{:S(2)}, u32[]{:S(2)}) collective-permute-start(f32[64,512]{1,0:T(8,128)S(1)} %get-tuple-element.19), channel_id=1, source_target_pairs={{0,8},{4,12},{8,0},{12,4},{1,9},{5,13},{9,1},{13,5},{2,10},{6,14},... | collective-permute-start | bytes 393224 | tf_op jit(solution)/shard_map/ppermute | solution.py:10
  82.1 2.2 %collective-permute-done.13 = f32[64,512]{1,0:T(8,128)S(1)} collective-permute-done((f32[64,512]{1,0:T(8,128)S(1)}, f32[64,512]{1,0:T(8,128)S(1)}, u32[]{:S(2)}, u32[]{:S(2)}) %collective-permute-start.13) | collective-permute-done | bytes 131104 | tf_op jit(solution)/shard_map/ppermute | solution.py:10
  84.9 5.0 %collective-permute-done.14 = f32[64,512]{1,0:T(8,128)S(1)} collective-permute-done((f32[64,512]{1,0:T(8,128)S(1)}, f32[64,512]{1,0:T(8,128)S(1)}, u32[]{:S(2)}, u32[]{:S(2)}) %collective-permute-start.14) | collective-permute-done | bytes 131104 | tf_op jit(solution)/shard_map/ppermute | solution.py:10
  90.0 2.8 %collective-permute-done.18 = f32[64,512]{1,0:T(8,128)S(1)} collective-permute-done((f32[64,512]{1,0:T(8,128)S(1)}, f32[64,512]{1,0:T(8,128)S(1)}, u32[]{:S(2)}, u32[]{:S(2)}) %collective-permute-start.18) | collective-permute-done | bytes 131104 | tf_op jit(solution)/shard_map/ppermute | solution.py:10
  92.8 7.9 %collective-permute-done.19 = f32[64,512]{1,0:T(8,128)S(1)} collective-permute-done((f32[64,512]{1,0:T(8,128)S(1)}, f32[64,512]{1,0:T(8,128)S(1)}, u32[]{:S(2)}, u32[]{:S(2)}) %collective-permute-start.19) | collective-permute-done | bytes 131104 | tf_op jit(solution)/shard_map/ppermute | solution.py:10
  (100 shorter events, 29.5 us)
Async XLA Ops:
  0.6 15.9 %copy-start = (bf16[1024,1024]{1,0:T(8,128)(2,1)S(1)}, bf16[1024,1024]{1,0:T(8,128)(2,1)}, u32[]{:S(2)}) copy-start(bf16[1024,1024]{1,0:T(8,128)(2,1)} %param.10) | copy-start | bytes 6291460
  3.1 20.4 %collective-permute-start.5 = (bf16[80,512]{1,0:T(8,128)(2,1)}, bf16[80,512]{1,0:T(8,128)(2,1)}, u32[]{:S(2)}, u32[]{:S(2)}) collective-permute-start(bf16[80,512]{1,0:T(8,128)(2,1)} %pad_maximum_fusion.7), channel_id=1, source_target_pairs={{0,4},{4,8},{8,12},{12,0},{1,5},{5,9},{9,13},{13,1},{2,6},{6,10},{... | collective-permute-start | bytes 245768 | tf_op jit(solution)/shard_map/ppermute | solution.py:10
  6.1 23.5 %collective-permute-start.6 = (bf16[80,512]{1,0:T(8,128)(2,1)}, bf16[80,512]{1,0:T(8,128)(2,1)S(1)}, u32[]{:S(2)}, u32[]{:S(2)}) collective-permute-start(bf16[80,512]{1,0:T(8,128)(2,1)} %pad_maximum_fusion.7), channel_id=1, source_target_pairs={{0,8},{4,12},{8,0},{12,4},{1,9},{5,13},{9,1},{13,5},{2,10},{6,14},... | collective-permute-start | bytes 245768 | tf_op jit(solution)/shard_map/ppermute | solution.py:10
  8.7 20.9 %collective-permute-start.7 = (bf16[80,512]{1,0:T(8,128)(2,1)}, bf16[80,512]{1,0:T(8,128)(2,1)}, u32[]{:S(2)}, u32[]{:S(2)}) collective-permute-start(bf16[80,512]{1,0:T(8,128)(2,1)} %pad_maximum_fusion.7), channel_id=1, source_target_pairs={{0,12},{4,0},{8,4},{12,8},{1,13},{5,1},{9,5},{13,9},{2,14},{6,2},{... | collective-permute-start | bytes 245768 | tf_op jit(solution)/shard_map/ppermute | solution.py:10
  10.7 16.5 %collective-permute-start = (bf16[80,512]{1,0:T(8,128)(2,1)}, bf16[80,512]{1,0:T(8,128)(2,1)}, u32[]{:S(2)}, u32[]{:S(2)}) collective-permute-start(bf16[80,512]{1,0:T(8,128)(2,1)} %pad_maximum_fusion.6), channel_id=1, source_target_pairs={{0,4},{4,8},{8,12},{12,0},{1,5},{5,9},{9,13},{13,1},{2,6},{6,10},{... | collective-permute-start | bytes 245768 | tf_op jit(solution)/shard_map/ppermute | solution.py:10
  11.4 19.1 %collective-permute-start.1 = (bf16[80,512]{1,0:T(8,128)(2,1)}, bf16[80,512]{1,0:T(8,128)(2,1)}, u32[]{:S(2)}, u32[]{:S(2)}) collective-permute-start(bf16[80,512]{1,0:T(8,128)(2,1)} %pad_maximum_fusion.6), channel_id=1, source_target_pairs={{0,8},{4,12},{8,0},{12,4},{1,9},{5,13},{9,1},{13,5},{2,10},{6,14},... | collective-permute-start | bytes 245768 | tf_op jit(solution)/shard_map/ppermute | solution.py:10
  23.5 7.8 %collective-permute-start.2 = (bf16[80,512]{1,0:T(8,128)(2,1)}, bf16[80,512]{1,0:T(8,128)(2,1)S(1)}, u32[]{:S(2)}, u32[]{:S(2)}) collective-permute-start(bf16[80,512]{1,0:T(8,128)(2,1)} %pad_maximum_fusion.6), channel_id=1, source_target_pairs={{0,12},{4,0},{8,4},{12,8},{1,13},{5,1},{9,5},{13,9},{2,14},{6,2},{... | collective-permute-start | bytes 245768 | tf_op jit(solution)/shard_map/ppermute | solution.py:10
  27.2 20.9 %copy-start.5 = (s32[256]{0:T(256)S(1)}, s32[256]{0:T(256)}, u32[]{:S(2)}) copy-start(s32[256]{0:T(256)} %param.15) | copy-start | bytes 3076
  27.2 20.9 %collective-permute-start.10 = (bf16[256,4,128]{2,0,1:T(8,128)(2,1)}, bf16[256,4,128]{2,0,1:T(8,128)(2,1)}, u32[]{:S(2)}, u32[]{:S(2)}) collective-permute-start(bf16[256,4,128]{2,0,1:T(8,128)(2,1)} %bitcast.104), channel_id=1, source_target_pairs={{0,2},{1,3},{2,0},{3,1},{4,6},{5,7},{6,4},{7,5},{8,10},{9,11},{10,... | collective-permute-start | bytes 786440 | tf_op jit(solution)/shard_map/ppermute | solution.py:14
  31.3 18.6 %copy-start.3 = (bf16[256,4,1,128]{0,3,2,1:T(8,128)(2,1)S(1)}, bf16[256,4,1,128]{0,3,2,1:T(8,128)(2,1)}, u32[]{:S(2)}) copy-start(bf16[256,4,1,128]{0,3,2,1:T(8,128)(2,1)} %get-tuple-element.20) | copy-start | bytes 786436
  32.9 13.5 %collective-permute-start.3 = (bf16[256,512]{1,0:T(8,128)(2,1)S(1)}, bf16[256,512]{1,0:T(8,128)(2,1)S(1)}, u32[]{:S(2)}, u32[]{:S(2)}) collective-permute-start(bf16[256,512]{1,0:T(8,128)(2,1)S(1)} %constant_dynamic-update-slice_fusion), channel_id=1, source_target_pairs={{0,2},{1,3},{2,0},{3,1},{4,6},{5,7},{6,4},{7,5},{8,10},{9,11},{10,... | collective-permute-start | bytes 786440 | tf_op jit(solution)/shard_map/ppermute | solution.py:14
  34.1 11.2 %collective-permute-start.8 = (bf16[256,512]{1,0:T(8,128)(2,1)S(1)}, bf16[256,512]{1,0:T(8,128)(2,1)S(1)}, u32[]{:S(2)}, u32[]{:S(2)}) collective-permute-start(bf16[256,512]{1,0:T(8,128)(2,1)S(1)} %constant_dynamic-update-slice_fusion.4), channel_id=1, source_target_pairs={{0,2},{1,3},{2,0},{3,1},{4,6},{5,7},{6,4},{7,5},{8,10},{9,11},{10,... | collective-permute-start | bytes 786440 | tf_op jit(solution)/shard_map/ppermute | solution.py:14
  46.4 4.5 %collective-permute-start.9 = (bf16[2,256,512]{2,1,0:T(8,128)(2,1)}, bf16[2,256,512]{2,1,0:T(8,128)(2,1)}, u32[]{:S(2)}, u32[]{:S(2)}) collective-permute-start(bf16[2,256,512]{2,1,0:T(8,128)(2,1)} %get-tuple-element.27), channel_id=1, source_target_pairs={{0,1},{1,0},{2,3},{3,2},{4,5},{5,4},{6,7},{7,6},{8,9},{9,8},{10,11... | collective-permute-start | bytes 1572872 | tf_op jit(solution)/shard_map/ppermute | solution.py:14
  47.5 4.9 %collective-permute-start.4 = (bf16[2,256,512]{2,1,0:T(8,128)(2,1)}, bf16[2,256,512]{2,1,0:T(8,128)(2,1)}, u32[]{:S(2)}, u32[]{:S(2)}) collective-permute-start(bf16[2,256,512]{2,1,0:T(8,128)(2,1)} %get-tuple-element.23), channel_id=1, source_target_pairs={{0,1},{1,0},{2,3},{3,2},{4,5},{5,4},{6,7},{7,6},{8,9},{9,8},{10,11... | collective-permute-start | bytes 1572872 | tf_op jit(solution)/shard_map/ppermute | solution.py:14
  60.3 9.2 %collective-permute-start.11 = (bf16[256,512]{1,0:T(8,128)(2,1)S(1)}, bf16[256,512]{1,0:T(8,128)(2,1)S(1)}, u32[]{:S(2)}, u32[]{:S(2)}) collective-permute-start(bf16[256,512]{1,0:T(8,128)(2,1)S(1)} %get-tuple-element.15), channel_id=1, source_target_pairs={{0,2},{1,3},{2,0},{3,1},{4,6},{5,7},{6,4},{7,5},{8,10},{9,11},{10,... | collective-permute-start | bytes 786440 | tf_op jit(solution)/shard_map/ppermute | solution.py:14
  61.9 12.3 %collective-permute-start.16 = (bf16[256,512]{1,0:T(8,128)(2,1)S(1)}, bf16[256,512]{1,0:T(8,128)(2,1)S(1)}, u32[]{:S(2)}, u32[]{:S(2)}) collective-permute-start(bf16[256,512]{1,0:T(8,128)(2,1)S(1)} %get-tuple-element.16), channel_id=1, source_target_pairs={{0,2},{1,3},{2,0},{3,1},{4,6},{5,7},{6,4},{7,5},{8,10},{9,11},{10,... | collective-permute-start | bytes 786440 | tf_op jit(solution)/shard_map/ppermute | solution.py:14
  70.0 5.7 %collective-permute-start.12 = (f32[4,64,512]{2,1,0:T(8,128)S(1)}, f32[4,64,512]{2,1,0:T(8,128)S(1)}, u32[]{:S(2)}, u32[]{:S(2)}) collective-permute-start(f32[4,64,512]{2,1,0:T(8,128)S(1)} %dynamic-slice_bitcast_fusion.1), channel_id=1, source_target_pairs={{0,1},{1,0},{2,3},{3,2},{4,5},{5,4},{6,7},{7,6},{8,9},{9,8},{10,11... | collective-permute-start | bytes 1572872 | tf_op jit(solution)/shard_map/ppermute | solution.py:14
  74.7 6.0 %collective-permute-start.17 = (f32[4,64,512]{2,1,0:T(8,128)S(1)}, f32[4,64,512]{2,1,0:T(8,128)S(1)}, u32[]{:S(2)}, u32[]{:S(2)}) collective-permute-start(f32[4,64,512]{2,1,0:T(8,128)S(1)} %dynamic-slice_bitcast_fusion), channel_id=1, source_target_pairs={{0,1},{1,0},{2,3},{3,2},{4,5},{5,4},{6,7},{7,6},{8,9},{9,8},{10,11... | collective-permute-start | bytes 1572872 | tf_op jit(solution)/shard_map/ppermute | solution.py:14
  75.9 8.4 %collective-permute-start.13 = (f32[64,512]{1,0:T(8,128)S(1)}, f32[64,512]{1,0:T(8,128)S(1)}, u32[]{:S(2)}, u32[]{:S(2)}) collective-permute-start(f32[64,512]{1,0:T(8,128)S(1)} %get-tuple-element.12), channel_id=1, source_target_pairs={{0,4},{4,8},{8,12},{12,0},{1,5},{5,9},{9,13},{13,1},{2,6},{6,10},{... | collective-permute-start | bytes 393224 | tf_op jit(solution)/shard_map/ppermute | solution.py:10
  76.6 13.4 %collective-permute-start.14 = (f32[64,512]{1,0:T(8,128)S(1)}, f32[64,512]{1,0:T(8,128)S(1)}, u32[]{:S(2)}, u32[]{:S(2)}) collective-permute-start(f32[64,512]{1,0:T(8,128)S(1)} %get-tuple-element.14), channel_id=1, source_target_pairs={{0,8},{4,12},{8,0},{12,4},{1,9},{5,13},{9,1},{13,5},{2,10},{6,14},... | collective-permute-start | bytes 393224 | tf_op jit(solution)/shard_map/ppermute | solution.py:10
  77.8 12.2 %collective-permute-start.15 = (f32[64,512]{1,0:T(8,128)S(1)}, f32[64,512]{1,0:T(8,128)S(1)}, u32[]{:S(2)}, u32[]{:S(2)}) collective-permute-start(f32[64,512]{1,0:T(8,128)S(1)} %get-tuple-element.13), channel_id=1, source_target_pairs={{0,12},{4,0},{8,4},{12,8},{1,13},{5,1},{9,5},{13,9},{2,14},{6,2},{... | collective-permute-start | bytes 393224 | tf_op jit(solution)/shard_map/ppermute | solution.py:10
  80.8 12.0 %collective-permute-start.18 = (f32[64,512]{1,0:T(8,128)S(1)}, f32[64,512]{1,0:T(8,128)S(1)}, u32[]{:S(2)}, u32[]{:S(2)}) collective-permute-start(f32[64,512]{1,0:T(8,128)S(1)} %get-tuple-element.17), channel_id=1, source_target_pairs={{0,4},{4,8},{8,12},{12,0},{1,5},{5,9},{9,13},{13,1},{2,6},{6,10},{... | collective-permute-start | bytes 393224 | tf_op jit(solution)/shard_map/ppermute | solution.py:10
  80.9 19.8 %collective-permute-start.19 = (f32[64,512]{1,0:T(8,128)S(1)}, f32[64,512]{1,0:T(8,128)S(1)}, u32[]{:S(2)}, u32[]{:S(2)}) collective-permute-start(f32[64,512]{1,0:T(8,128)S(1)} %get-tuple-element.19), channel_id=1, source_target_pairs={{0,8},{4,12},{8,0},{12,4},{1,9},{5,13},{9,1},{13,5},{2,10},{6,14},... | collective-permute-start | bytes 393224 | tf_op jit(solution)/shard_map/ppermute | solution.py:10
  84.3 16.4 %collective-permute-start.20 = (f32[64,512]{1,0:T(8,128)S(1)}, f32[64,512]{1,0:T(8,128)S(1)}, u32[]{:S(2)}, u32[]{:S(2)}) collective-permute-start(f32[64,512]{1,0:T(8,128)S(1)} %get-tuple-element.18), channel_id=1, source_target_pairs={{0,12},{4,0},{8,4},{12,8},{1,13},{5,1},{9,5},{13,9},{2,14},{6,2},{... | collective-permute-start | bytes 393224 | tf_op jit(solution)/shard_map/ppermute | solution.py:10
  (4 other events, 17.9 us)

commit v5 on v3

--- a/solution.py
+++ b/solution.py
@@ -23,15 +23,15 @@
     return bits
 
 
-def gather_queue(queue_keys, fresh, n_q, n_dp):
+def gather_queue(queue_keys, extra, n_q, n_dp):
     dp = lax.axis_index("dp")
     k_dev, width = queue_keys.shape
     piece_rows = k_dev // n_dp
     piece = lax.dynamic_slice_in_dim(queue_keys, dp * piece_rows, piece_rows, 0)
-    packed = jnp.concatenate([piece, fresh], axis=0)
+    packed = jnp.concatenate([piece, extra], axis=0)
     got = [shift(packed, "queue", n_q, s) for s in range(1, n_q)]
     payload = jnp.concatenate(
-        [g[:piece_rows] for g in got] + [fresh] + [g[piece_rows:] for g in got], axis=0
+        [g[:piece_rows] for g in got] + [extra] + [g[piece_rows:] for g in got], axis=0
     )
     for t, bit in enumerate(dp_bits(n_dp)):
         payload = jnp.stack([payload, swap(payload, "dp", n_dp, bit)], axis=t)
@@ -68,11 +68,15 @@
             send = lax.dynamic_index_in_dim(t, 1 - me, 1 + axis, keepdims=False)
             t = keep + swap(send, "dp", n_dp, bit)
         t = t.reshape(n_q, share, cols)
-        acc = lax.dynamic_index_in_dim(t, q, 0, keepdims=False)
-        for s in range(1, n_q):
-            part = lax.dynamic_index_in_dim(t, (q + s) % n_q, 0, keepdims=False)
-            acc = acc + shift(part, "queue", n_q, s)
-        out.append(acc)
+        bit = 1
+        while bit < n_q:
+            me = (q // bit) % 2
+            v = t.reshape(t.shape[0] // 2, 2, share, cols)
+            keep = lax.dynamic_index_in_dim(v, me, 1, keepdims=False)
+            send = lax.dynamic_index_in_dim(v, 1 - me, 1, keepdims=False)
+            t = keep + swap(send, "queue", n_q, bit)
+            bit *= 2
+        out.append(t.reshape(share, cols))
     return jnp.concatenate(out, axis=1)
 
 
@@ -96,11 +100,7 @@
     piece_rows = k_dev // n_dp
     far_rows = (n_q - 1) * piece_rows
 
-    fresh = jnp.dot(key_inputs, key_weight, preferred_element_type=jnp.float32)
-    fresh = (fresh * lax.rsqrt(jnp.sum(fresh * fresh, -1, keepdims=True) + 1e-06)).astype(
-        jnp.bfloat16
-    )
-    gathered = gather_queue(queue_keys, fresh, n_q, n_dp)
+    gathered = gather_queue(queue_keys, key_inputs, n_q, n_dp)
     rows0 = gathered.shape[1]
     remote = gathered.reshape(-1, width)
     is_key = (jnp.arange(n_dp * rows0, dtype=jnp.int32) % rows0) < far_rows
@@ -159,7 +159,13 @@
     b_e = dp ^ (b % n_dp)
     b_s = (q - b // n_dp) % n_q
     source = b_e * rows0 + far_rows + b_s * new_dev + offset % new_dev
-    new_queue = jnp.where(live[:, None], jnp.take(remote, source, axis=0), queue_keys)
+    pick_new = (source[:, None] == jnp.arange(n_dp * rows0)[None, :]).astype(jnp.bfloat16)
+    key_rows = jnp.dot(pick_new, remote, preferred_element_type=jnp.float32).astype(jnp.bfloat16)
+    fresh = jnp.dot(key_rows, key_weight, preferred_element_type=jnp.float32)
+    fresh = (fresh * lax.rsqrt(jnp.sum(fresh * fresh, -1, keepdims=True) + 1e-06)).astype(
+        jnp.bfloat16
+    )
+    new_queue = jnp.where(live[:, None], fresh, queue_keys)
     return (loss, grad_rows, new_queue)
 
 

time: 91.3 us -> 96.4 us (1.056)
  waiting for transfers between devices: 32.2 us -> 38.9 us
  starting transfers between devices: 24.6 us -> 18.6 us
  matrix products: 9.92 us -> 13.9 us
  other arithmetic: 8.14 us -> 11.8 us
  local copies, waits for them, and re-layouts: 14.1 us -> 10.9 us
    ppermute x7 -> x11, waiting for transfers between devices: 13.7 us -> 37.9 us  [swap(): return lax.ppermute(x, axis, [(i, i ^ bit) for i in range(n)])]
    ppermute x9 -> x3, waiting for transfers between devices: 18.6 us -> 0.98 us  [shift(): return lax.ppermute(x, axis, [(i, (i + step) % n) for i in range(n)])]
    ppermute x9 -> x3, starting transfers between devices: 19.2 us -> 6.99 us  [shift(): return lax.ppermute(x, axis, [(i, (i + step) % n) for i in range(n)])]
    ppermute x7 -> x11, starting transfers between devices: 5.35 us -> 11.6 us  [swap(): return lax.ppermute(x, axis, [(i, i ^ bit) for i in range(n)])]
    gather x1 -> x0, local copies, waits for them, and re-layouts: 4.21 us -> none  [body(): jnp.take(remote, source, axis=0)]
    another operation x2, other arithmetic: 0.33 us -> 3.32 us  [gather_queue(): payload = jnp.stack([payload, swap(payload, 'dp', n_dp, bit)], axis=t)]
    select_n x2 -> x1, other arithmetic: 3.53 us -> 1.01 us  [body(): new_queue = jnp.where(live[:, None], fresh, queue_keys)]
    gather x1, other arithmetic: 0.01 us -> 2.51 us  [body(): b = jnp.take(owner_block, sub_block)]
  transfers between devices with their start and end apart: 16 -> 14, of which waited for: 9 -> 7; matrix products, arithmetic and copies ran while one was open for 31% -> 27% of each run, Pallas kernels for 0% -> 0%
where the time goes in v5:
time: 96.4 us; the launch traced here: 95.8 us
  waiting for transfers between devices  38.9 us (40%)
  starting transfers between devices  18.6 us (19%)
  matrix products  13.9 us (14%)
  other arithmetic  11.8 us (12%)
  local copies, waits for them, and re-layouts  10.9 us (11%)
  between operations  1.7 us (2%)
    ppermute x11, waiting for transfers between devices, swap(): return lax.ppermute(x, axis, [(i, i ^ bit) for i in range(n)])  37.9 us
    ppermute x11, starting transfers between devices, swap(): return lax.ppermute(x, axis, [(i, i ^ bit) for i in range(n)])  11.6 us
    ppermute x3, starting transfers between devices, shift(): return lax.ppermute(x, axis, [(i, (i + step) % n) for i in range(n)])  6.99 us
    unnamed x29, local copies, waits for them, and re-layouts  5.81 us
    dot_general x1, matrix products, body(): fresh = jnp.dot(key_rows, key_weight, preferred_element_type=jnp.float32)  4.51 us
    another operation x2, other arithmetic, gather_queue(): payload = jnp.stack([payload, swap(payload, 'dp', n_dp, bit)], axis=t)  3.32 us
    dot_general x2, matrix products, reduce_scatter_grad(): lax.dot_general(xs, gs, (((0,), (0,)), ((), ())), preferred_element_type=...  2.85 us
    gather x1, other arithmetic, body(): b = jnp.take(owner_block, sub_block)  2.51 us
  transfers between devices with their start and end apart: 14, of which 7 were waited for; matrix products, arithmetic and copies ran while one was open for 27% of the time, Pallas kernels for 0%

profile of v5, /device:TPU:0, one launch (start us, length us, event | category | flops | bytes accessed | tf_op | source)
XLA Modules:
  0.0 95.8 jit_solution(15243827773693062459)
XLA Ops:
  1.7 1.5 %pad_maximum_fusion.4 = bf16[80,1024]{1,0:T(8,128)(2,1)} fusion(bf16[16,1024]{1,0:T(8,128)(2,1)} %param.9, bf16[64,1024]{1,0:T(8,128)(2,1)S(1)} %constant_dynamic-slice_fusion.4), kind=kLoop, calls=%fused_computation.54 | loop fusion | flops 327680 | bytes 327680 | tf_op jit(solution)/shard_map/concatenate | solution.py:31
  3.2 3.1 %collective-permute-start = (bf16[80,1024]{1,0:T(8,128)(2,1)}, bf16[80,1024]{1,0:T(8,128)(2,1)}, u32[]{:S(2)}, u32[]{:S(2)}) collective-permute-start(bf16[80,1024]{1,0:T(8,128)(2,1)} %pad_maximum_fusion.4), channel_id=1, source_target_pairs={{0,4},{4,8},{8,12},{12,0},{1,5},{5,9},{9,13},{13,1},{2,6},{6,10},{... | collective-permute-start | bytes 491528 | tf_op jit(solution)/shard_map/ppermute | solution.py:10
  6.3 2.6 %collective-permute-start.1 = (bf16[80,1024]{1,0:T(8,128)(2,1)}, bf16[80,1024]{1,0:T(8,128)(2,1)}, u32[]{:S(2)}, u32[]{:S(2)}) collective-permute-start(bf16[80,1024]{1,0:T(8,128)(2,1)} %pad_maximum_fusion.4), channel_id=1, source_target_pairs={{0,8},{4,12},{8,0},{12,4},{1,9},{5,13},{9,1},{13,5},{2,10},{6,14},... | collective-permute-start | bytes 491528 | tf_op jit(solution)/shard_map/ppermute | solution.py:10
  8.9 1.3 %collective-permute-start.2 = (bf16[80,1024]{1,0:T(8,128)(2,1)}, bf16[80,1024]{1,0:T(8,128)(2,1)}, u32[]{:S(2)}, u32[]{:S(2)}) collective-permute-start(bf16[80,1024]{1,0:T(8,128)(2,1)} %pad_maximum_fusion.4), channel_id=1, source_target_pairs={{0,12},{4,0},{8,4},{12,8},{1,13},{5,1},{9,5},{13,9},{2,14},{6,2},{... | collective-permute-start | bytes 491528 | tf_op jit(solution)/shard_map/ppermute | solution.py:10
  10.2 1.2 %copy.18 = bf16[256,1024]{0,1:T(8,128)(2,1)S(1)} copy(bf16[256,1024]{1,0:T(8,128)(2,1)} %param.8) | data formatting | bytes 1048576 | tf_op args[0]
  12.4 1.6 %collective-permute-start.5 = (bf16[256,4,128]{2,0,1:T(8,128)(2,1)S(1)}, bf16[256,4,128]{2,0,1:T(8,128)(2,1)S(1)}, u32[]{:S(2)}, u32[]{:S(2)}) collective-permute-start(bf16[256,4,128]{2,0,1:T(8,128)(2,1)S(1)} %bitcast.85), channel_id=1, source_target_pairs={{0,2},{1,3},{2,0},{3,1},{4,6},{5,7},{6,4},{7,5},{8,10},{9,11},{10,... | collective-permute-start | bytes 786440 | tf_op jit(solution)/shard_map/ppermute | solution.py:14
  15.5 2.5 %compare_select_fusion.3 = s32[256,1]{0,1:T(1,128)S(1)} fusion(s32[]{:T(128)} %bitcast.30, s32[]{:T(128)} %bitcast.31, s32[]{:T(128)} %bitcast.33, s32[]{:T(128)} %bitcast.32, s32[]{:T(128)} %bitcast.68), kind=kLoop, calls=%fused_computation.77 | loop fusion | flops 9472 | bytes 1044 | tf_op jit(solution)/shard_map/jit(_take)/gather | solution.py:158
  24.1 1.5 %collective-permute-start.3 = (bf16[256,1024]{1,0:T(8,128)(2,1)S(1)}, bf16[256,1024]{1,0:T(8,128)(2,1)S(1)}, u32[]{:S(2)}, u32[]{:S(2)}) collective-permute-start(bf16[256,1024]{1,0:T(8,128)(2,1)S(1)} %slice_dynamic-update-slice_fusion.3), channel_id=1, source_target_pairs={{0,2},{1,3},{2,0},{3,1},{4,6},{5,7},{6,4},{7,5},{8,10},{9,11},{10,... | collective-permute-start | bytes 1572872 | tf_op jit(solution)/shard_map/ppermute | solution.py:14
  25.6 1.7 %multiply_reduce_fusion.3 = (f32[256]{0:T(256)S(1)}, f32[256,1024]{1,0:T(8,128)}) fusion(bf16[256,1024]{1,0:T(8,128)(2,1)S(1)} %copy-done.5, bf16[1024,1024]{1,0:T(8,128)(2,1)S(1)} %copy-done), kind=kOutput, calls=%fused_computation.20 | convolution fusion | flops 537394944 | bytes 3671040 | tf_op jit(solution)/shard_map/dot_general | solution.py:108
  27.3 10.5 %collective-permute-done.3 = bf16[256,1024]{1,0:T(8,128)(2,1)S(1)} collective-permute-done((bf16[256,1024]{1,0:T(8,128)(2,1)S(1)}, bf16[256,1024]{1,0:T(8,128)(2,1)S(1)}, u32[]{:S(2)}, u32[]{:S(2)}) %collective-permute-start.3) | collective-permute-done | bytes 524320 | tf_op jit(solution)/shard_map/ppermute | solution.py:14
  37.9 1.4 %fusion.50 = (bf16[2,1,256,1024]{3,2,1,0:T(8,128)(2,1)}, bf16[2,256,1024]{2,1,0:T(8,128)(2,1)}) fusion(bf16[1,256,1024]{2,1,0:T(8,128)(2,1)S(1)} %bitcast.84, bf16[1,256,1024]{2,1,0:T(8,128)(2,1)S(1)} %bitcast.83), kind=kLoop, calls=%fused_computation.144 | loop fusion | flops 524288 | bytes 3145728 | tf_op jit(solution)/shard_map/stack | solution.py:37
  39.4 1.4 %fusion.23 = f32[256,1024]{1,0:T(8,128)} fusion(bf16[256,1024]{1,0:T(8,128)(2,1)S(1)} %copy-done.1, s32[256]{0:T(256)S(1)} %get-tuple-element.11, pred[256]{0:T(512)(128)(4,1)S(1)} %get-tuple-element.8), kind=kOutput, calls=%fused_computation.51 | convolution fusion | flops 134348800 | bytes 1574144 | tf_op jit(solution)/shard_map/dot_general | solution.py:138
  42.6 1.9 %pad_maximum_fusion = bf16[2,2,256,1024]{3,2,1,0:T(8,128)(2,1)S(1)} fusion(bf16[2,1,256,1024]{3,2,1,0:T(8,128)(2,1)} %bitcast.4, bf16[2,1,256,1024]{3,2,1,0:T(8,128)(2,1)} %get-tuple-element.12), kind=kLoop, calls=%fused_computation | loop fusion | flops 1048576 | bytes 4194304 | tf_op jit(solution)/shard_map/stack | solution.py:37
  50.2 1.5 %collective-permute-start.6 = (bf16[256,512]{1,0:T(8,128)(2,1)}, bf16[256,512]{1,0:T(8,128)(2,1)}, u32[]{:S(2)}, u32[]{:S(2)}) collective-permute-start(bf16[256,512]{1,0:T(8,128)(2,1)} %get-tuple-element.14), channel_id=1, source_target_pairs={{0,2},{1,3},{2,0},{3,1},{4,6},{5,7},{6,4},{7,5},{8,10},{9,11},{10,... | collective-permute-start | bytes 786440 | tf_op jit(solution)/shard_map/ppermute | solution.py:14
  52.3 4.5 %multiply_reduce_fusion = (f32[256]{0:T(256)S(1)}, f32[256,1024]{1,0:T(8,128)}) fusion(bf16[1024,1024]{1,0:T(8,128)(2,1)} %param.11, bf16[1024,1024]{1,0:T(8,128)(2,1)} %bitcast.73, s32[256]{0:T(256)S(1)} %fusion.43), kind=kOutput, calls=%fused_computation.13 | convolution fusion | flops 1074790144 | bytes 5244928 | tf_op jit(solution)/shard_map/dot_general | solution.py:164
  56.8 2.9 %collective-permute-done.6 = bf16[256,512]{1,0:T(8,128)(2,1)} collective-permute-done((bf16[256,512]{1,0:T(8,128)(2,1)}, bf16[256,512]{1,0:T(8,128)(2,1)}, u32[]{:S(2)}, u32[]{:S(2)}) %collective-permute-start.6) | collective-permute-done | bytes 262176 | tf_op jit(solution)/shard_map/ppermute | solution.py:14
  59.7 1.5 %fusion.11 = f32[4,2,64,512]{3,2,1,0:T(8,128)S(1)} fusion(bf16[4,2,64,512]{3,2,1,0:T(8,128)(2,1)S(1)} %bitcast.74, bf16[256,512]{1,0:T(8,128)(2,1)} %collective-permute-done.6, bf16[256,512]{1,0:T(8,128)(2,1)} %get-tuple-element.14), kind=kOutput, calls=%fused_computation.28 | convolution fusion | flops 269484032 | bytes 2097152 | tf_op jit(solution)/shard_map/dot_general | solution.py:62
  61.3 3.5 %collective-permute-done.10 = bf16[256,512]{1,0:T(8,128)(2,1)} collective-permute-done((bf16[256,512]{1,0:T(8,128)(2,1)S(1)}, bf16[256,512]{1,0:T(8,128)(2,1)}, u32[]{:S(2)}, u32[]{:S(2)}) %collective-permute-start.10) | collective-permute-done | bytes 262176 | tf_op jit(solution)/shard_map/ppermute | solution.py:14
  64.9 1.4 %fusion.14 = f32[4,2,64,512]{3,2,1,0:T(8,128)S(1)} fusion(bf16[4,2,64,512]{3,2,1,0:T(8,128)(2,1)S(1)} %bitcast.75, bf16[256,512]{1,0:T(8,128)(2,1)} %collective-permute-done.10, bf16[256,512]{1,0:T(8,128)(2,1)S(1)} %get-tuple-element.15), kind=kOutput, calls=%fused_computation.32 | convolution fusion | flops 269484032 | bytes 2097152 | tf_op jit(solution)/shard_map/dot_general | solution.py:62
  67.5 3.2 %collective-permute-start.8 = (f32[2,64,512]{2,1,0:T(8,128)S(1)}, f32[2,64,512]{2,1,0:T(8,128)S(1)}, u32[]{:S(2)}, u32[]{:S(2)}) collective-permute-start(f32[2,64,512]{2,1,0:T(8,128)S(1)} %dynamic-slice_bitcast_fusion.3), channel_id=1, source_target_pairs={{0,4},{4,0},{8,12},{12,8},{1,5},{5,1},{9,13},{13,9},{2,6},{6,2},{1... | collective-permute-start | bytes 786440 | tf_op jit(solution)/shard_map/ppermute | solution.py:14
  71.6 6.3 %collective-permute-done.8 = f32[2,64,512]{2,1,0:T(8,128)S(1)} collective-permute-done((f32[2,64,512]{2,1,0:T(8,128)S(1)}, f32[2,64,512]{2,1,0:T(8,128)S(1)}, u32[]{:S(2)}, u32[]{:S(2)}) %collective-permute-start.8) | collective-permute-done | bytes 262176 | tf_op jit(solution)/shard_map/ppermute | solution.py:14
  78.0 1.6 %collective-permute-start.9 = (f32[1,64,512]{2,1,0:T(8,128)S(1)}, f32[1,64,512]{2,1,0:T(8,128)S(1)}, u32[]{:S(2)}, u32[]{:S(2)}) collective-permute-start(f32[1,64,512]{2,1,0:T(8,128)S(1)} %constant_dynamic-slice_fusion.1), channel_id=1, source_target_pairs={{0,8},{4,12},{8,0},{12,4},{1,9},{5,13},{9,1},{13,5},{2,10},{6,14},... | collective-permute-start | bytes 393224 | tf_op jit(solution)/shard_map/ppermute | solution.py:14
  79.6 6.6 %collective-permute-done.12 = f32[2,64,512]{2,1,0:T(8,128)S(1)} collective-permute-done((f32[2,64,512]{2,1,0:T(8,128)S(1)}, f32[2,64,512]{2,1,0:T(8,128)S(1)}, u32[]{:S(2)}, u32[]{:S(2)}) %collective-permute-start.12) | collective-permute-done | bytes 262176 | tf_op jit(solution)/shard_map/ppermute | solution.py:14
  87.1 8.0 %collective-permute-done.13 = f32[1,64,512]{2,1,0:T(8,128)S(1)} collective-permute-done((f32[1,64,512]{2,1,0:T(8,128)S(1)}, f32[1,64,512]{2,1,0:T(8,128)S(1)}, u32[]{:S(2)}, u32[]{:S(2)}) %collective-permute-start.13) | collective-permute-done | bytes 131104 | tf_op jit(solution)/shard_map/ppermute | solution.py:14
  (83 shorter events, 20.9 us)
Async XLA Ops:
  0.6 25.0 %copy-start = (bf16[1024,1024]{1,0:T(8,128)(2,1)S(1)}, bf16[1024,1024]{1,0:T(8,128)(2,1)}, u32[]{:S(2)}) copy-start(bf16[1024,1024]{1,0:T(8,128)(2,1)} %param.10) | copy-start | bytes 6291460
  0.6 13.3 %copy-start.10 = (s32[16]{0:T(128)S(1)}, s32[16]{0:T(128)}, u32[]{:S(2)}) copy-start(s32[16]{0:T(128)} %param.14) | copy-start | bytes 196
  0.7 21.1 %copy-start.8 = (bf16[16,1024]{1,0:T(8,128)(2,1)S(1)}, bf16[16,1024]{1,0:T(8,128)(2,1)}, u32[]{:S(2)}) copy-start(bf16[16,1024]{1,0:T(8,128)(2,1)} %param.9) | copy-start | bytes 98308
  1.7 23.9 %copy-start.5 = (bf16[256,1024]{1,0:T(8,128)(2,1)S(1)}, bf16[256,1024]{1,0:T(8,128)(2,1)}, u32[]{:S(2)}) copy-start(bf16[256,1024]{1,0:T(8,128)(2,1)} %param.8) | copy-start | bytes 1572868
  3.2 14.8 %collective-permute-start = (bf16[80,1024]{1,0:T(8,128)(2,1)}, bf16[80,1024]{1,0:T(8,128)(2,1)}, u32[]{:S(2)}, u32[]{:S(2)}) collective-permute-start(bf16[80,1024]{1,0:T(8,128)(2,1)} %pad_maximum_fusion.4), channel_id=1, source_target_pairs={{0,4},{4,8},{8,12},{12,0},{1,5},{5,9},{9,13},{13,1},{2,6},{6,10},{... | collective-permute-start | bytes 491528 | tf_op jit(solution)/shard_map/ppermute | solution.py:10
  6.3 13.7 %collective-permute-start.1 = (bf16[80,1024]{1,0:T(8,128)(2,1)}, bf16[80,1024]{1,0:T(8,128)(2,1)}, u32[]{:S(2)}, u32[]{:S(2)}) collective-permute-start(bf16[80,1024]{1,0:T(8,128)(2,1)} %pad_maximum_fusion.4), channel_id=1, source_target_pairs={{0,8},{4,12},{8,0},{12,4},{1,9},{5,13},{9,1},{13,5},{2,10},{6,14},... | collective-permute-start | bytes 491528 | tf_op jit(solution)/shard_map/ppermute | solution.py:10
  8.9 12.0 %collective-permute-start.2 = (bf16[80,1024]{1,0:T(8,128)(2,1)}, bf16[80,1024]{1,0:T(8,128)(2,1)}, u32[]{:S(2)}, u32[]{:S(2)}) collective-permute-start(bf16[80,1024]{1,0:T(8,128)(2,1)} %pad_maximum_fusion.4), channel_id=1, source_target_pairs={{0,12},{4,0},{8,4},{12,8},{1,13},{5,1},{9,5},{13,9},{2,14},{6,2},{... | collective-permute-start | bytes 491528 | tf_op jit(solution)/shard_map/ppermute | solution.py:10
  12.4 28.3 %collective-permute-start.5 = (bf16[256,4,128]{2,0,1:T(8,128)(2,1)S(1)}, bf16[256,4,128]{2,0,1:T(8,128)(2,1)S(1)}, u32[]{:S(2)}, u32[]{:S(2)}) collective-permute-start(bf16[256,4,128]{2,0,1:T(8,128)(2,1)S(1)} %bitcast.85), channel_id=1, source_target_pairs={{0,2},{1,3},{2,0},{3,1},{4,6},{5,7},{6,4},{7,5},{8,10},{9,11},{10,... | collective-permute-start | bytes 786440 | tf_op jit(solution)/shard_map/ppermute | solution.py:14
  24.1 13.8 %collective-permute-start.3 = (bf16[256,1024]{1,0:T(8,128)(2,1)S(1)}, bf16[256,1024]{1,0:T(8,128)(2,1)S(1)}, u32[]{:S(2)}, u32[]{:S(2)}) collective-permute-start(bf16[256,1024]{1,0:T(8,128)(2,1)S(1)} %slice_dynamic-update-slice_fusion.3), channel_id=1, source_target_pairs={{0,2},{1,3},{2,0},{3,1},{4,6},{5,7},{6,4},{7,5},{8,10},{9,11},{10,... | collective-permute-start | bytes 1572872 | tf_op jit(solution)/shard_map/ppermute | solution.py:14
  27.3 12.0 %copy-start.9 = (s32[256]{0:T(256)S(1)}, s32[256]{0:T(256)}, u32[]{:S(2)}) copy-start(s32[256]{0:T(256)} %param.15) | copy-start | bytes 3076
  27.3 12.1 %copy-start.1 = (bf16[256,1024]{1,0:T(8,128)(2,1)S(1)}, bf16[256,1024]{1,0:T(8,128)(2,1)}, u32[]{:S(2)}) copy-start(bf16[256,1024]{1,0:T(8,128)(2,1)} %param.12) | copy-start | bytes 1572868
  37.9 3.8 %copy-start.7 = (bf16[256,4,1,128]{0,3,2,1:T(8,128)(2,1)S(1)}, bf16[256,4,1,128]{0,3,2,1:T(8,128)(2,1)}, u32[]{:S(2)}) copy-start(bf16[256,4,1,128]{0,3,2,1:T(8,128)(2,1)} %get-tuple-element.16) | copy-start | bytes 786436
  39.3 3.3 %collective-permute-start.4 = (bf16[2,256,1024]{2,1,0:T(8,128)(2,1)}, bf16[2,256,1024]{2,1,0:T(8,128)(2,1)}, u32[]{:S(2)}, u32[]{:S(2)}) collective-permute-start(bf16[2,256,1024]{2,1,0:T(8,128)(2,1)} %get-tuple-element.13), channel_id=1, source_target_pairs={{0,1},{1,0},{2,3},{3,2},{4,5},{5,4},{6,7},{7,6},{8,9},{9,8},{10,11... | collective-permute-start | bytes 3145736 | tf_op jit(solution)/shard_map/ppermute | solution.py:14
  42.6 2.2 %copy-start.4 = (f32[256,1024]{1,0:T(8,128)S(1)}, f32[256,1024]{1,0:T(8,128)}, u32[]{:S(2)}) copy-start(f32[256,1024]{1,0:T(8,128)} %fusion.23) | copy-start | bytes 3145732
  44.5 3.7 %copy-start.3 = (bf16[2,2,256,1024]{3,2,1,0:T(8,128)(2,1)}, bf16[2,2,256,1024]{3,2,1,0:T(8,128)(2,1)S(1)}, u32[]{:S(2)}) copy-start(bf16[2,2,256,1024]{3,2,1,0:T(8,128)(2,1)S(1)} %pad_maximum_fusion) | copy-start | bytes 6291460
  50.2 9.5 %collective-permute-start.6 = (bf16[256,512]{1,0:T(8,128)(2,1)}, bf16[256,512]{1,0:T(8,128)(2,1)}, u32[]{:S(2)}, u32[]{:S(2)}) collective-permute-start(bf16[256,512]{1,0:T(8,128)(2,1)} %get-tuple-element.14), channel_id=1, source_target_pairs={{0,2},{1,3},{2,0},{3,1},{4,6},{5,7},{6,4},{7,5},{8,10},{9,11},{10,... | collective-permute-start | bytes 786440 | tf_op jit(solution)/shard_map/ppermute | solution.py:14
  51.7 13.2 %collective-permute-start.10 = (bf16[256,512]{1,0:T(8,128)(2,1)S(1)}, bf16[256,512]{1,0:T(8,128)(2,1)}, u32[]{:S(2)}, u32[]{:S(2)}) collective-permute-start(bf16[256,512]{1,0:T(8,128)(2,1)S(1)} %get-tuple-element.15), channel_id=1, source_target_pairs={{0,2},{1,3},{2,0},{3,1},{4,6},{5,7},{6,4},{7,5},{8,10},{9,11},{10,... | collective-permute-start | bytes 786440 | tf_op jit(solution)/shard_map/ppermute | solution.py:14
  61.2 5.2 %copy-start.6 = (f32[256,1024]{1,0:T(8,128)S(1)}, f32[256,1024]{1,0:T(8,128)}, u32[]{:S(2)}) copy-start(f32[256,1024]{1,0:T(8,128)} %get-tuple-element.32) | copy-start | bytes 3145732
  61.3 6.2 %collective-permute-start.7 = (f32[4,64,512]{2,1,0:T(8,128)S(1)}, f32[4,64,512]{2,1,0:T(8,128)S(1)}, u32[]{:S(2)}, u32[]{:S(2)}) collective-permute-start(f32[4,64,512]{2,1,0:T(8,128)S(1)} %dynamic-slice_bitcast_fusion.1), channel_id=1, source_target_pairs={{0,1},{1,0},{2,3},{3,2},{4,5},{5,4},{6,7},{7,6},{8,9},{9,8},{10,11... | collective-permute-start | bytes 1572872 | tf_op jit(solution)/shard_map/ppermute | solution.py:14
  66.3 4.4 %collective-permute-start.11 = (f32[4,64,512]{2,1,0:T(8,128)S(1)}, f32[4,64,512]{2,1,0:T(8,128)S(1)}, u32[]{:S(2)}, u32[]{:S(2)}) collective-permute-start(f32[4,64,512]{2,1,0:T(8,128)S(1)} %dynamic-slice_bitcast_fusion), channel_id=1, source_target_pairs={{0,1},{1,0},{2,3},{3,2},{4,5},{5,4},{6,7},{7,6},{8,9},{9,8},{10,11... | collective-permute-start | bytes 1572872 | tf_op jit(solution)/shard_map/ppermute | solution.py:14
  67.5 10.4 %collective-permute-start.8 = (f32[2,64,512]{2,1,0:T(8,128)S(1)}, f32[2,64,512]{2,1,0:T(8,128)S(1)}, u32[]{:S(2)}, u32[]{:S(2)}) collective-permute-start(f32[2,64,512]{2,1,0:T(8,128)S(1)} %dynamic-slice_bitcast_fusion.3), channel_id=1, source_target_pairs={{0,4},{4,0},{8,12},{12,8},{1,5},{5,1},{9,13},{13,9},{2,6},{6,2},{1... | collective-permute-start | bytes 786440 | tf_op jit(solution)/shard_map/ppermute | solution.py:14
  70.9 15.2 %collective-permute-start.12 = (f32[2,64,512]{2,1,0:T(8,128)S(1)}, f32[2,64,512]{2,1,0:T(8,128)S(1)}, u32[]{:S(2)}, u32[]{:S(2)}) collective-permute-start(f32[2,64,512]{2,1,0:T(8,128)S(1)} %dynamic-slice_bitcast_fusion.2), channel_id=1, source_target_pairs={{0,4},{4,0},{8,12},{12,8},{1,5},{5,1},{9,13},{13,9},{2,6},{6,2},{1... | collective-permute-start | bytes 786440 | tf_op jit(solution)/shard_map/ppermute | solution.py:14
  78.0 9.1 %collective-permute-start.9 = (f32[1,64,512]{2,1,0:T(8,128)S(1)}, f32[1,64,512]{2,1,0:T(8,128)S(1)}, u32[]{:S(2)}, u32[]{:S(2)}) collective-permute-start(f32[1,64,512]{2,1,0:T(8,128)S(1)} %constant_dynamic-slice_fusion.1), channel_id=1, source_target_pairs={{0,8},{4,12},{8,0},{12,4},{1,9},{5,13},{9,1},{13,5},{2,10},{6,14},... | collective-permute-start | bytes 393224 | tf_op jit(solution)/shard_map/ppermute | solution.py:14
  86.2 8.9 %collective-permute-start.13 = (f32[1,64,512]{2,1,0:T(8,128)S(1)}, f32[1,64,512]{2,1,0:T(8,128)S(1)}, u32[]{:S(2)}, u32[]{:S(2)}) collective-permute-start(f32[1,64,512]{2,1,0:T(8,128)S(1)} %constant_dynamic-slice_fusion), channel_id=1, source_target_pairs={{0,8},{4,12},{8,0},{12,4},{1,9},{5,13},{9,1},{13,5},{2,10},{6,14},... | collective-permute-start | bytes 393224 | tf_op jit(solution)/shard_map/ppermute | solution.py:14
  (1 other events, 1.9 us)

commit v6 on v3

--- a/solution.py
+++ b/solution.py
@@ -38,6 +38,23 @@
     return payload.reshape(n_dp, -1, width)
 
 
+def line_reduce(acc, q, n_q):
+    for t in range(1, n_q):
+        right = lax.dynamic_index_in_dim(acc, (q + n_q - t) % n_q, 0, keepdims=False)
+        left = lax.dynamic_index_in_dim(acc, (q + t) % n_q, 0, keepdims=False)
+        got_r = lax.ppermute(right, "queue", [(i, i + 1) for i in range(t)])
+        got_l = lax.ppermute(left, "queue", [(i, i - 1) for i in range(n_q - t, n_q)])
+        at_r = (q - 1 + n_q - t) % n_q
+        at_l = (q + 1 + t) % n_q
+        acc = lax.dynamic_update_index_in_dim(
+            acc, lax.dynamic_index_in_dim(acc, at_r, 0, keepdims=False) + got_r, at_r, 0
+        )
+        acc = lax.dynamic_update_index_in_dim(
+            acc, lax.dynamic_index_in_dim(acc, at_l, 0, keepdims=False) + got_l, at_l, 0
+        )
+    return lax.dynamic_index_in_dim(acc, q, 0, keepdims=False)
+
+
 def reduce_scatter_grad(query_inputs, grad_query, n_q, n_dp):
     q = lax.axis_index("queue")
     dp = lax.axis_index("dp")
@@ -67,12 +84,7 @@
             keep = lax.dynamic_index_in_dim(t, me, 1 + axis, keepdims=False)
             send = lax.dynamic_index_in_dim(t, 1 - me, 1 + axis, keepdims=False)
             t = keep + swap(send, "dp", n_dp, bit)
-        t = t.reshape(n_q, share, cols)
-        acc = lax.dynamic_index_in_dim(t, q, 0, keepdims=False)
-        for s in range(1, n_q):
-            part = lax.dynamic_index_in_dim(t, (q + s) % n_q, 0, keepdims=False)
-            acc = acc + shift(part, "queue", n_q, s)
-        out.append(acc)
+        out.append(line_reduce(t.reshape(n_q, share, cols), q, n_q))
     return jnp.concatenate(out, axis=1)
 
 
@@ -159,7 +171,9 @@
     b_e = dp ^ (b % n_dp)
     b_s = (q - b // n_dp) % n_q
     source = b_e * rows0 + far_rows + b_s * new_dev + offset % new_dev
-    new_queue = jnp.where(live[:, None], jnp.take(remote, source, axis=0), queue_keys)
+    pick_new = (source[:, None] == jnp.arange(n_dp * rows0)[None, :]).astype(jnp.bfloat16)
+    placed = jnp.dot(pick_new, remote, preferred_element_type=jnp.float32).astype(jnp.bfloat16)
+    new_queue = jnp.where(live[:, None], placed, queue_keys)
     return (loss, grad_rows, new_queue)
 
 

time: 91.3 us -> 109 us (1.19)
  starting transfers between devices: 24.6 us -> 43.5 us
  local copies, waits for them, and re-layouts: 14.1 us -> 10 us
  waiting for transfers between devices: 32.2 us -> 34.9 us
  other arithmetic: 8.14 us -> 6.41 us
  matrix products: 9.92 us -> 11.4 us
    ppermute x0 -> x12, starting transfers between devices: none -> 31.1 us  [the longest x6 25.9 us: line_reduce(): got_r = lax.ppermute(right, 'queue', [(i, i + 1) for i in range(t)])]
    ppermute x9 -> x3, waiting for transfers between devices: 18.6 us -> 4.21 us  [shift(): return lax.ppermute(x, axis, [(i, (i + step) % n) for i in range(n)])]
    ppermute x9 -> x3, starting transfers between devices: 19.2 us -> 6.99 us  [shift(): return lax.ppermute(x, axis, [(i, (i + step) % n) for i in range(n)])]
    ppermute x0 -> x12, waiting for transfers between devices: none -> 11.4 us  [the longest x6 6.17 us: line_reduce(): lax.ppermute(left, 'queue', [(i, i - 1) for i in range(n_q - t, n_q)])]
    ppermute x7, waiting for transfers between devices: 13.7 us -> 19.3 us  [swap(): return lax.ppermute(x, axis, [(i, i ^ bit) for i in range(n)])]
    gather x1 -> x0, local copies, waits for them, and re-layouts: 4.21 us -> none  [body(): jnp.take(remote, source, axis=0)]
    select_n x2 -> x0, other arithmetic: 3.53 us -> none  [the longest x1 2.59 us: body(): jnp.take(remote, source, axis=0)]
    gather x1, other arithmetic: 0.01 us -> 2.52 us  [body(): b = jnp.take(owner_block, sub_block)]
  transfers between devices with their start and end apart: 16 -> 22, of which waited for: 9 -> 10; matrix products, arithmetic and copies ran while one was open for 31% -> 22% of each run, Pallas kernels for 0% -> 0%
where the time goes in v6:
time: 109 us; the launch traced here: 108 us
  starting transfers between devices  43.5 us (40%)
  waiting for transfers between devices  34.9 us (32%)
  matrix products  11.4 us (10%)
  local copies, waits for them, and re-layouts  10 us (9%)
  other arithmetic  6.41 us (6%)
  between operations  2.01 us (2%)
    ppermute x6, starting transfers between devices, line_reduce(): got_r = lax.ppermute(right, 'queue', [(i, i + 1) for i in range(t)])  25.9 us
    ppermute x7, waiting for transfers between devices, swap(): return lax.ppermute(x, axis, [(i, i ^ bit) for i in range(n)])  19.3 us
    ppermute x3, starting transfers between devices, shift(): return lax.ppermute(x, axis, [(i, (i + step) % n) for i in range(n)])  6.99 us
    ppermute x6, waiting for transfers between devices, line_reduce(): lax.ppermute(left, 'queue', [(i, i - 1) for i in range(n_q - t, n_q)])  6.17 us
    unnamed x20, local copies, waits for them, and re-layouts  5.54 us
    ppermute x7, starting transfers between devices, swap(): return lax.ppermute(x, axis, [(i, i ^ bit) for i in range(n)])  5.35 us
    ppermute x6, starting transfers between devices, line_reduce(): lax.ppermute(left, 'queue', [(i, i - 1) for i in range(n_q - t, n_q)])  5.26 us
    ppermute x6, waiting for transfers between devices, line_reduce(): got_r = lax.ppermute(right, 'queue', [(i, i + 1) for i in range(t)])  5.19 us
  transfers between devices with their start and end apart: 22, of which 10 were waited for; matrix products, arithmetic and copies ran while one was open for 22% of the time, Pallas kernels for 0%

profile of v6, /device:TPU:0, one launch (start us, length us, event | category | flops | bytes accessed | tf_op | source)
XLA Modules:
  0.0 108.2 jit_solution(7451849602460631135)
XLA Ops:
  0.7 2.3 %multiply_reduce_fusion.3 = (f32[16]{0:T(128)S(1)}, f32[16,1024]{1,0:T(8,128)S(1)}) fusion(bf16[16,1024]{1,0:T(8,128)(2,1)} %param.9, bf16[1024,1024]{1,0:T(8,128)(2,1)} %param.11), kind=kOutput, calls=%fused_computation.92 | convolution fusion | flops 33587184 | bytes 2195520 | tf_op jit(solution)/shard_map/dot_general | solution.py:111
  3.7 3.1 %collective-permute-start = (bf16[80,1024]{1,0:T(8,128)(2,1)}, bf16[80,1024]{1,0:T(8,128)(2,1)}, u32[]{:S(2)}, u32[]{:S(2)}) collective-permute-start(bf16[80,1024]{1,0:T(8,128)(2,1)} %pad_maximum_fusion.4), channel_id=1, source_target_pairs={{0,4},{4,8},{8,12},{12,0},{1,5},{5,9},{9,13},{13,1},{2,6},{6,10},{... | collective-permute-start | bytes 491528 | tf_op jit(solution)/shard_map/ppermute | solution.py:10
  6.8 2.6 %collective-permute-start.1 = (bf16[80,1024]{1,0:T(8,128)(2,1)}, bf16[80,1024]{1,0:T(8,128)(2,1)}, u32[]{:S(2)}, u32[]{:S(2)}) collective-permute-start(bf16[80,1024]{1,0:T(8,128)(2,1)} %pad_maximum_fusion.4), channel_id=1, source_target_pairs={{0,8},{4,12},{8,0},{12,4},{1,9},{5,13},{9,1},{13,5},{2,10},{6,14},... | collective-permute-start | bytes 491528 | tf_op jit(solution)/shard_map/ppermute | solution.py:10
  9.4 1.3 %collective-permute-start.2 = (bf16[80,1024]{1,0:T(8,128)(2,1)}, bf16[80,1024]{1,0:T(8,128)(2,1)}, u32[]{:S(2)}, u32[]{:S(2)}) collective-permute-start(bf16[80,1024]{1,0:T(8,128)(2,1)} %pad_maximum_fusion.4), channel_id=1, source_target_pairs={{0,12},{4,0},{8,4},{12,8},{1,13},{5,1},{9,5},{13,9},{2,14},{6,2},{... | collective-permute-start | bytes 491528 | tf_op jit(solution)/shard_map/ppermute | solution.py:10
  12.9 1.6 %collective-permute-start.5 = (bf16[256,4,128]{2,0,1:T(8,128)(2,1)S(1)}, bf16[256,4,128]{2,0,1:T(8,128)(2,1)}, u32[]{:S(2)}, u32[]{:S(2)}) collective-permute-start(bf16[256,4,128]{2,0,1:T(8,128)(2,1)S(1)} %bitcast.165), channel_id=1, source_target_pairs={{0,2},{1,3},{2,0},{3,1},{4,6},{5,7},{6,4},{7,5},{8,10},{9,11},{10,... | collective-permute-start | bytes 786440 | tf_op jit(solution)/shard_map/ppermute | solution.py:14
  16.2 4.2 %collective-permute-done.1 = bf16[80,1024]{1,0:T(8,128)(2,1)} collective-permute-done((bf16[80,1024]{1,0:T(8,128)(2,1)}, bf16[80,1024]{1,0:T(8,128)(2,1)}, u32[]{:S(2)}, u32[]{:S(2)}) %collective-permute-start.1) | collective-permute-done | bytes 163872 | tf_op jit(solution)/shard_map/ppermute | solution.py:10
  24.7 1.5 %collective-permute-start.3 = (bf16[256,1024]{1,0:T(8,128)(2,1)S(1)}, bf16[256,1024]{1,0:T(8,128)(2,1)S(1)}, u32[]{:S(2)}, u32[]{:S(2)}) collective-permute-start(bf16[256,1024]{1,0:T(8,128)(2,1)S(1)} %slice_dynamic-update-slice_fusion.3), channel_id=1, source_target_pairs={{0,2},{1,3},{2,0},{3,1},{4,6},{5,7},{6,4},{7,5},{8,10},{9,11},{10,... | collective-permute-start | bytes 1572872 | tf_op jit(solution)/shard_map/ppermute | solution.py:14
  26.8 1.8 %multiply_reduce_fusion.2 = (f32[256]{0:T(256)S(1)}, f32[256,1024]{1,0:T(8,128)S(1)}) fusion(bf16[256,1024]{1,0:T(8,128)(2,1)} %param.8, bf16[1024,1024]{1,0:T(8,128)(2,1)S(1)} %copy-done), kind=kOutput, calls=%fused_computation.18 | convolution fusion | flops 537394944 | bytes 3671040 | tf_op jit(solution)/shard_map/dot_general | solution.py:120
  28.6 9.8 %collective-permute-done.3 = bf16[256,1024]{1,0:T(8,128)(2,1)S(1)} collective-permute-done((bf16[256,1024]{1,0:T(8,128)(2,1)S(1)}, bf16[256,1024]{1,0:T(8,128)(2,1)S(1)}, u32[]{:S(2)}, u32[]{:S(2)}) %collective-permute-start.3) | collective-permute-done | bytes 524320 | tf_op jit(solution)/shard_map/ppermute | solution.py:14
  38.6 2.5 %compare_select_fusion.3 = s32[256,1]{0,1:T(1,128)S(1)} fusion(s32[]{:T(128)} %bitcast.58, s32[]{:T(128)} %bitcast.59, s32[]{:T(128)} %bitcast.61, s32[]{:T(128)} %bitcast.60, s32[]{:T(128)} %bitcast.151), kind=kLoop, calls=%fused_computation.121 | loop fusion | flops 9472 | bytes 1044 | tf_op jit(solution)/shard_map/jit(_take)/gather | solution.py:170
  47.2 1.5 %collective-permute-start.14 = (bf16[256,512]{1,0:T(8,128)(2,1)}, bf16[256,512]{1,0:T(8,128)(2,1)}, u32[]{:S(2)}, u32[]{:S(2)}) collective-permute-start(bf16[256,512]{1,0:T(8,128)(2,1)} %get-tuple-element.25), channel_id=1, source_target_pairs={{0,2},{1,3},{2,0},{3,1},{4,6},{5,7},{6,4},{7,5},{8,10},{9,11},{10,... | collective-permute-start | bytes 786440 | tf_op jit(solution)/shard_map/ppermute | solution.py:14
  50.6 6.1 %collective-permute-done.14 = bf16[256,512]{1,0:T(8,128)(2,1)} collective-permute-done((bf16[256,512]{1,0:T(8,128)(2,1)}, bf16[256,512]{1,0:T(8,128)(2,1)}, u32[]{:S(2)}, u32[]{:S(2)}) %collective-permute-start.14) | collective-permute-done | bytes 262176 | tf_op jit(solution)/shard_map/ppermute | solution.py:14
  56.7 1.5 %fusion.13 = f32[4,2,64,512]{3,2,1,0:T(8,128)S(1)} fusion(bf16[4,2,64,512]{3,2,1,0:T(8,128)(2,1)S(1)} %bitcast.157, bf16[256,512]{1,0:T(8,128)(2,1)} %collective-permute-done.14, bf16[256,512]{1,0:T(8,128)(2,1)} %get-tuple-element.25), kind=kOutput, calls=%fused_computation.29 | convolution fusion | flops 269484032 | bytes 2097152 | tf_op jit(solution)/shard_map/dot_general | solution.py:79
  58.3 3.4 %collective-permute-done.6 = bf16[256,512]{1,0:T(8,128)(2,1)S(1)} collective-permute-done((bf16[256,512]{1,0:T(8,128)(2,1)S(1)}, bf16[256,512]{1,0:T(8,128)(2,1)S(1)}, u32[]{:S(2)}, u32[]{:S(2)}) %collective-permute-start.6) | collective-permute-done | bytes 262176 | tf_op jit(solution)/shard_map/ppermute | solution.py:14
  62.4 1.6 %fusion.4 = bf16[256,1024]{1,0:T(8,128)(2,1)} fusion(bf16[256,1024]{1,0:T(8,128)(2,1)S(1)} %copy-done.3, bf16[1024,1024]{1,0:T(8,128)(2,1)S(1)} %bitcast.156, s32[256]{0:T(256)S(1)} %fusion.41, pred[256]{0:T(512)(128)(4,1)S(1)} %broadcast_compare_fusion), kind=kOutput, calls=%fused_computation.9 | convolution fusion | flops 537657344 | bytes 3147008 | tf_op jit(solution)/shard_map/dot_general | solution.py:175
  64.0 5.0 %collective-permute-start.16 = (f32[64,512]{1,0:T(8,128)S(1)}, f32[64,512]{1,0:T(8,128)S(1)}, u32[]{:S(2)}, u32[]{:S(2)}) collective-permute-start(f32[64,512]{1,0:T(8,128)S(1)} %get-tuple-element.35), channel_id=1, source_target_pairs={{0,4},{1,5},{2,6},{3,7},{16,20},{17,21},{18,22},{19,23}} | collective-permute-start | bytes 393224 | tf_op jit(solution)/shard_map/ppermute | solution.py:45
  70.5 2.4 %collective-permute-done.16 = f32[64,512]{1,0:T(8,128)S(1)} collective-permute-done((f32[64,512]{1,0:T(8,128)S(1)}, f32[64,512]{1,0:T(8,128)S(1)}, u32[]{:S(2)}, u32[]{:S(2)}) %collective-permute-start.16) | collective-permute-done | bytes 131104 | tf_op jit(solution)/shard_map/ppermute | solution.py:45
  73.7 1.6 %collective-permute-done.8 = f32[64,512]{1,0:T(8,128)S(1)} collective-permute-done((f32[64,512]{1,0:T(8,128)S(1)}, f32[64,512]{1,0:T(8,128)S(1)}, u32[]{:S(2)}, u32[]{:S(2)}) %collective-permute-start.8) | collective-permute-done | bytes 131104 | tf_op jit(solution)/shard_map/ppermute | solution.py:45
  76.1 4.4 %collective-permute-start.18 = (f32[64,512]{1,0:T(8,128)S(1)}, f32[64,512]{1,0:T(8,128)S(1)}, u32[]{:S(2)}, u32[]{:S(2)}) collective-permute-start(f32[64,512]{1,0:T(8,128)S(1)} %get-tuple-element.31), channel_id=1, source_target_pairs={{0,4},{4,8},{1,5},{5,9},{2,6},{6,10},{3,7},{7,11},{16,20},{20,24},... | collective-permute-start | bytes 393224 | tf_op jit(solution)/shard_map/ppermute | solution.py:45
  80.6 1.9 %collective-permute-start.10 = (f32[64,512]{1,0:T(8,128)S(1)}, f32[64,512]{1,0:T(8,128)S(1)}, u32[]{:S(2)}, u32[]{:S(2)}) collective-permute-start(f32[64,512]{1,0:T(8,128)S(1)} %get-tuple-element.19), channel_id=1, source_target_pairs={{0,4},{4,8},{1,5},{5,9},{2,6},{6,10},{3,7},{7,11},{16,20},{20,24},... | collective-permute-start | bytes 393224 | tf_op jit(solution)/shard_map/ppermute | solution.py:45
  84.0 10.2 %collective-permute-start.20 = (f32[64,512]{1,0:T(8,128)S(1)}, f32[64,512]{1,0:T(8,128)S(1)}, u32[]{:S(2)}, u32[]{:S(2)}) collective-permute-start(f32[64,512]{1,0:T(8,128)S(1)} %get-tuple-element.29), channel_id=1, source_target_pairs={{0,4},{4,8},{8,12},{1,5},{5,9},{9,13},{2,6},{6,10},{10,14},{3,7},{... | collective-permute-start | bytes 393224 | tf_op jit(solution)/shard_map/ppermute | solution.py:45
  94.4 3.0 %collective-permute-start.12 = (f32[64,512]{1,0:T(8,128)S(1)}, f32[64,512]{1,0:T(8,128)S(1)}, u32[]{:S(2)}, u32[]{:S(2)}) collective-permute-start(f32[64,512]{1,0:T(8,128)S(1)} %get-tuple-element.17), channel_id=1, source_target_pairs={{0,4},{4,8},{8,12},{1,5},{5,9},{9,13},{2,6},{6,10},{10,14},{3,7},{... | collective-permute-start | bytes 393224 | tf_op jit(solution)/shard_map/ppermute | solution.py:45
  101.2 4.8 %collective-permute-done.21 = f32[64,512]{1,0:T(8,128)S(1)} collective-permute-done((f32[64,512]{1,0:T(8,128)S(1)}, f32[64,512]{1,0:T(8,128)S(1)}, u32[]{:S(2)}, u32[]{:S(2)}) %collective-permute-start.21) | collective-permute-done | bytes 131104 | tf_op jit(solution)/shard_map/ppermute | solution.py:46
  106.1 1.4 %collective-permute-done.13 = f32[64,512]{1,0:T(8,128)S(1)} collective-permute-done((f32[64,512]{1,0:T(8,128)S(1)}, f32[64,512]{1,0:T(8,128)S(1)}, u32[]{:S(2)}, u32[]{:S(2)}) %collective-permute-start.13) | collective-permute-done | bytes 131104 | tf_op jit(solution)/shard_map/ppermute | solution.py:46
  (109 shorter events, 26.8 us)
Async XLA Ops:
  0.6 26.1 %copy-start = (bf16[1024,1024]{1,0:T(8,128)(2,1)S(1)}, bf16[1024,1024]{1,0:T(8,128)(2,1)}, u32[]{:S(2)}) copy-start(bf16[1024,1024]{1,0:T(8,128)(2,1)} %param.10) | copy-start | bytes 6291460
  3.7 11.6 %collective-permute-start = (bf16[80,1024]{1,0:T(8,128)(2,1)}, bf16[80,1024]{1,0:T(8,128)(2,1)}, u32[]{:S(2)}, u32[]{:S(2)}) collective-permute-start(bf16[80,1024]{1,0:T(8,128)(2,1)} %pad_maximum_fusion.4), channel_id=1, source_target_pairs={{0,4},{4,8},{8,12},{12,0},{1,5},{5,9},{9,13},{13,1},{2,6},{6,10},{... | collective-permute-start | bytes 491528 | tf_op jit(solution)/shard_map/ppermute | solution.py:10
  6.8 13.7 %collective-permute-start.1 = (bf16[80,1024]{1,0:T(8,128)(2,1)}, bf16[80,1024]{1,0:T(8,128)(2,1)}, u32[]{:S(2)}, u32[]{:S(2)}) collective-permute-start(bf16[80,1024]{1,0:T(8,128)(2,1)} %pad_maximum_fusion.4), channel_id=1, source_target_pairs={{0,8},{4,12},{8,0},{12,4},{1,9},{5,13},{9,1},{13,5},{2,10},{6,14},... | collective-permute-start | bytes 491528 | tf_op jit(solution)/shard_map/ppermute | solution.py:10
  9.4 12.0 %collective-permute-start.2 = (bf16[80,1024]{1,0:T(8,128)(2,1)}, bf16[80,1024]{1,0:T(8,128)(2,1)}, u32[]{:S(2)}, u32[]{:S(2)}) collective-permute-start(bf16[80,1024]{1,0:T(8,128)(2,1)} %pad_maximum_fusion.4), channel_id=1, source_target_pairs={{0,12},{4,0},{8,4},{12,8},{1,13},{5,1},{9,5},{13,9},{2,14},{6,2},{... | collective-permute-start | bytes 491528 | tf_op jit(solution)/shard_map/ppermute | solution.py:10
  12.9 36.0 %collective-permute-start.5 = (bf16[256,4,128]{2,0,1:T(8,128)(2,1)S(1)}, bf16[256,4,128]{2,0,1:T(8,128)(2,1)}, u32[]{:S(2)}, u32[]{:S(2)}) collective-permute-start(bf16[256,4,128]{2,0,1:T(8,128)(2,1)S(1)} %bitcast.165), channel_id=1, source_target_pairs={{0,2},{1,3},{2,0},{3,1},{4,6},{5,7},{6,4},{7,5},{8,10},{9,11},{10,... | collective-permute-start | bytes 786440 | tf_op jit(solution)/shard_map/ppermute | solution.py:14
  24.7 13.8 %collective-permute-start.3 = (bf16[256,1024]{1,0:T(8,128)(2,1)S(1)}, bf16[256,1024]{1,0:T(8,128)(2,1)S(1)}, u32[]{:S(2)}, u32[]{:S(2)}) collective-permute-start(bf16[256,1024]{1,0:T(8,128)(2,1)S(1)} %slice_dynamic-update-slice_fusion.3), channel_id=1, source_target_pairs={{0,2},{1,3},{2,0},{3,1},{4,6},{5,7},{6,4},{7,5},{8,10},{9,11},{10,... | collective-permute-start | bytes 1572872 | tf_op jit(solution)/shard_map/ppermute | solution.py:14
  28.6 12.6 %copy-start.5 = (s32[256]{0:T(256)S(1)}, s32[256]{0:T(256)}, u32[]{:S(2)}) copy-start(s32[256]{0:T(256)} %param.15) | copy-start | bytes 3076
  38.5 3.0 %collective-permute-start.4 = (bf16[2,256,1024]{2,1,0:T(8,128)(2,1)S(1)}, bf16[2,256,1024]{2,1,0:T(8,128)(2,1)S(1)}, u32[]{:S(2)}, u32[]{:S(2)}) collective-permute-start(bf16[2,256,1024]{2,1,0:T(8,128)(2,1)S(1)} %get-tuple-element.13), channel_id=1, source_target_pairs={{0,1},{1,0},{2,3},{3,2},{4,5},{5,4},{6,7},{7,6},{8,9},{9,8},{10,11... | collective-permute-start | bytes 3145736 | tf_op jit(solution)/shard_map/ppermute | solution.py:14
  47.2 9.5 %collective-permute-start.14 = (bf16[256,512]{1,0:T(8,128)(2,1)}, bf16[256,512]{1,0:T(8,128)(2,1)}, u32[]{:S(2)}, u32[]{:S(2)}) collective-permute-start(bf16[256,512]{1,0:T(8,128)(2,1)} %get-tuple-element.25), channel_id=1, source_target_pairs={{0,2},{1,3},{2,0},{3,1},{4,6},{5,7},{6,4},{7,5},{8,10},{9,11},{10,... | collective-permute-start | bytes 786440 | tf_op jit(solution)/shard_map/ppermute | solution.py:14
  50.0 11.7 %collective-permute-start.6 = (bf16[256,512]{1,0:T(8,128)(2,1)S(1)}, bf16[256,512]{1,0:T(8,128)(2,1)S(1)}, u32[]{:S(2)}, u32[]{:S(2)}) collective-permute-start(bf16[256,512]{1,0:T(8,128)(2,1)S(1)} %get-tuple-element.24), channel_id=1, source_target_pairs={{0,2},{1,3},{2,0},{3,1},{4,6},{5,7},{6,4},{7,5},{8,10},{9,11},{10,... | collective-permute-start | bytes 786440 | tf_op jit(solution)/shard_map/ppermute | solution.py:14
  58.3 5.7 %collective-permute-start.15 = (f32[4,64,512]{2,1,0:T(8,128)S(1)}, f32[4,64,512]{2,1,0:T(8,128)S(1)}, u32[]{:S(2)}, u32[]{:S(2)}) collective-permute-start(f32[4,64,512]{2,1,0:T(8,128)S(1)} %dynamic-slice_bitcast_fusion), channel_id=1, source_target_pairs={{0,1},{1,0},{2,3},{3,2},{4,5},{5,4},{6,7},{7,6},{8,9},{9,8},{10,11... | collective-permute-start | bytes 1572872 | tf_op jit(solution)/shard_map/ppermute | solution.py:14
  62.3 6.8 %collective-permute-start.7 = (f32[4,64,512]{2,1,0:T(8,128)S(1)}, f32[4,64,512]{2,1,0:T(8,128)S(1)}, u32[]{:S(2)}, u32[]{:S(2)}) collective-permute-start(f32[4,64,512]{2,1,0:T(8,128)S(1)} %dynamic-slice_bitcast_fusion.1), channel_id=1, source_target_pairs={{0,1},{1,0},{2,3},{3,2},{4,5},{5,4},{6,7},{7,6},{8,9},{9,8},{10,11... | collective-permute-start | bytes 1572872 | tf_op jit(solution)/shard_map/ppermute | solution.py:14
  64.0 8.9 %collective-permute-start.16 = (f32[64,512]{1,0:T(8,128)S(1)}, f32[64,512]{1,0:T(8,128)S(1)}, u32[]{:S(2)}, u32[]{:S(2)}) collective-permute-start(f32[64,512]{1,0:T(8,128)S(1)} %get-tuple-element.35), channel_id=1, source_target_pairs={{0,4},{1,5},{2,6},{3,7},{16,20},{17,21},{18,22},{19,23}} | collective-permute-start | bytes 393224 | tf_op jit(solution)/shard_map/ppermute | solution.py:45
  69.2 6.1 %collective-permute-start.8 = (f32[64,512]{1,0:T(8,128)S(1)}, f32[64,512]{1,0:T(8,128)S(1)}, u32[]{:S(2)}, u32[]{:S(2)}) collective-permute-start(f32[64,512]{1,0:T(8,128)S(1)} %get-tuple-element.23), channel_id=1, source_target_pairs={{0,4},{1,5},{2,6},{3,7},{16,20},{17,21},{18,22},{19,23}} | collective-permute-start | bytes 393224 | tf_op jit(solution)/shard_map/ppermute | solution.py:45
  73.0 3.1 %collective-permute-start.17 = (f32[64,512]{1,0:T(8,128)S(1)}, f32[64,512]{1,0:T(8,128)S(1)}, u32[]{:S(2)}, u32[]{:S(2)}) collective-permute-start(f32[64,512]{1,0:T(8,128)S(1)} %get-tuple-element.32), channel_id=1, source_target_pairs={{12,8},{13,9},{14,10},{15,11},{28,24},{29,25},{30,26},{31,27}} | collective-permute-start | bytes 393224 | tf_op jit(solution)/shard_map/ppermute | solution.py:46
  75.4 5.2 %collective-permute-start.9 = (f32[64,512]{1,0:T(8,128)S(1)}, f32[64,512]{1,0:T(8,128)S(1)}, u32[]{:S(2)}, u32[]{:S(2)}) collective-permute-start(f32[64,512]{1,0:T(8,128)S(1)} %get-tuple-element.20), channel_id=1, source_target_pairs={{12,8},{13,9},{14,10},{15,11},{28,24},{29,25},{30,26},{31,27}} | collective-permute-start | bytes 393224 | tf_op jit(solution)/shard_map/ppermute | solution.py:46
  76.1 7.8 %collective-permute-start.18 = (f32[64,512]{1,0:T(8,128)S(1)}, f32[64,512]{1,0:T(8,128)S(1)}, u32[]{:S(2)}, u32[]{:S(2)}) collective-permute-start(f32[64,512]{1,0:T(8,128)S(1)} %get-tuple-element.31), channel_id=1, source_target_pairs={{0,4},{4,8},{1,5},{5,9},{2,6},{6,10},{3,7},{7,11},{16,20},{20,24},... | collective-permute-start | bytes 393224 | tf_op jit(solution)/shard_map/ppermute | solution.py:45
  80.6 13.7 %collective-permute-start.10 = (f32[64,512]{1,0:T(8,128)S(1)}, f32[64,512]{1,0:T(8,128)S(1)}, u32[]{:S(2)}, u32[]{:S(2)}) collective-permute-start(f32[64,512]{1,0:T(8,128)S(1)} %get-tuple-element.19), channel_id=1, source_target_pairs={{0,4},{4,8},{1,5},{5,9},{2,6},{6,10},{3,7},{7,11},{16,20},{20,24},... | collective-permute-start | bytes 393224 | tf_op jit(solution)/shard_map/ppermute | solution.py:45
  82.5 11.8 %collective-permute-start.11 = (f32[64,512]{1,0:T(8,128)S(1)}, f32[64,512]{1,0:T(8,128)S(1)}, u32[]{:S(2)}, u32[]{:S(2)}) collective-permute-start(f32[64,512]{1,0:T(8,128)S(1)} %get-tuple-element.19), channel_id=1, source_target_pairs={{8,4},{12,8},{9,5},{13,9},{10,6},{14,10},{11,7},{15,11},{24,20},{2... | collective-permute-start | bytes 393224 | tf_op jit(solution)/shard_map/ppermute | solution.py:46
  83.2 0.7 collective-permute-start.19
  84.0 13.8 %collective-permute-start.20 = (f32[64,512]{1,0:T(8,128)S(1)}, f32[64,512]{1,0:T(8,128)S(1)}, u32[]{:S(2)}, u32[]{:S(2)}) collective-permute-start(f32[64,512]{1,0:T(8,128)S(1)} %get-tuple-element.29), channel_id=1, source_target_pairs={{0,4},{4,8},{8,12},{1,5},{5,9},{9,13},{2,6},{6,10},{10,14},{3,7},{... | collective-permute-start | bytes 393224 | tf_op jit(solution)/shard_map/ppermute | solution.py:45
  94.4 5.5 %collective-permute-start.12 = (f32[64,512]{1,0:T(8,128)S(1)}, f32[64,512]{1,0:T(8,128)S(1)}, u32[]{:S(2)}, u32[]{:S(2)}) collective-permute-start(f32[64,512]{1,0:T(8,128)S(1)} %get-tuple-element.17), channel_id=1, source_target_pairs={{0,4},{4,8},{8,12},{1,5},{5,9},{9,13},{2,6},{6,10},{10,14},{3,7},{... | collective-permute-start | bytes 393224 | tf_op jit(solution)/shard_map/ppermute | solution.py:45
  97.8 8.2 %collective-permute-start.21 = (f32[64,512]{1,0:T(8,128)S(1)}, f32[64,512]{1,0:T(8,128)S(1)}, u32[]{:S(2)}, u32[]{:S(2)}) collective-permute-start(f32[64,512]{1,0:T(8,128)S(1)} %get-tuple-element.26), channel_id=1, source_target_pairs={{4,0},{8,4},{12,8},{5,1},{9,5},{13,9},{6,2},{10,6},{14,10},{7,3},{... | collective-permute-start | bytes 393224 | tf_op jit(solution)/shard_map/ppermute | solution.py:46
  99.9 7.5 %collective-permute-start.13 = (f32[64,512]{1,0:T(8,128)S(1)}, f32[64,512]{1,0:T(8,128)S(1)}, u32[]{:S(2)}, u32[]{:S(2)}) collective-permute-start(f32[64,512]{1,0:T(8,128)S(1)} %get-tuple-element.14), channel_id=1, source_target_pairs={{4,0},{8,4},{12,8},{5,1},{9,5},{13,9},{6,2},{10,6},{14,10},{7,3},{... | collective-permute-start | bytes 393224 | tf_op jit(solution)/shard_map/ppermute | solution.py:46
  (5 other events, 25.8 us)

commit v7 on v3

--- a/solution.py
+++ b/solution.py
@@ -23,19 +23,22 @@
     return bits
 
 
-def gather_queue(queue_keys, fresh, n_q, n_dp):
+def gather_queue(queue_keys, n_q, n_dp):
     dp = lax.axis_index("dp")
     k_dev, width = queue_keys.shape
     piece_rows = k_dev // n_dp
     piece = lax.dynamic_slice_in_dim(queue_keys, dp * piece_rows, piece_rows, 0)
-    packed = jnp.concatenate([piece, fresh], axis=0)
-    got = [shift(packed, "queue", n_q, s) for s in range(1, n_q)]
-    payload = jnp.concatenate(
-        [g[:piece_rows] for g in got] + [fresh] + [g[piece_rows:] for g in got], axis=0
-    )
+    payload = jnp.stack([shift(piece, "queue", n_q, s) for s in range(1, n_q)])
     for t, bit in enumerate(dp_bits(n_dp)):
         payload = jnp.stack([payload, swap(payload, "dp", n_dp, bit)], axis=t)
-    return payload.reshape(n_dp, -1, width)
+    return payload.reshape(-1, width)
+
+
+def gather_blocks(block, n_q, n_dp):
+    got = jnp.stack([block] + [shift(block, "queue", n_q, s) for s in range(1, n_q)])
+    for t, bit in enumerate(dp_bits(n_dp)):
+        got = jnp.stack([got, swap(got, "dp", n_dp, bit)], axis=t)
+    return got.reshape(n_dp * n_q * block.shape[0], block.shape[1])
 
 
 def reduce_scatter_grad(query_inputs, grad_query, n_q, n_dp):
@@ -100,10 +103,8 @@
     fresh = (fresh * lax.rsqrt(jnp.sum(fresh * fresh, -1, keepdims=True) + 1e-06)).astype(
         jnp.bfloat16
     )
-    gathered = gather_queue(queue_keys, fresh, n_q, n_dp)
-    rows0 = gathered.shape[1]
-    remote = gathered.reshape(-1, width)
-    is_key = (jnp.arange(n_dp * rows0, dtype=jnp.int32) % rows0) < far_rows
+    remote = gather_queue(queue_keys, n_q, n_dp)
+    rows0 = far_rows
 
     query = jnp.dot(query_inputs, query_weight, preferred_element_type=jnp.float32)
     inv_len = lax.rsqrt(jnp.sum(query * query, -1, keepdims=True) + 1e-06)
@@ -113,7 +114,6 @@
     dims = (((1,), (1,)), ((), ()))
     near = lax.dot_general(unit, queue_keys, dims, preferred_element_type=jnp.float32) / temper
     far = lax.dot_general(unit, remote, dims, preferred_element_type=jnp.float32) / temper
-    far = jnp.where(is_key[None, :], far, -jnp.inf)
     top = jnp.maximum(jnp.max(near, -1), jnp.max(far, -1))
     e_near = jnp.exp(near - top[:, None])
     e_far = jnp.exp(far - top[:, None])
@@ -146,7 +146,9 @@
     grad_query = (
         (grad_unit - unit_f * jnp.sum(unit_f * grad_unit, -1, keepdims=True)) * inv_len
     ).astype(jnp.bfloat16)
+    fresh, grad_query = lax.optimization_barrier((fresh, grad_query))
     grad_rows = reduce_scatter_grad(query_inputs, grad_query, n_q, n_dp)
+    blocks = gather_blocks(fresh, n_q, n_dp)
 
     n_blocks = slot_owner.shape[0]
     slots_here = q * n_dp + jnp.arange(n_dp, dtype=jnp.int32)
@@ -158,8 +160,10 @@
     b = jnp.take(owner_block, sub_block)
     b_e = dp ^ (b % n_dp)
     b_s = (q - b // n_dp) % n_q
-    source = b_e * rows0 + far_rows + b_s * new_dev + offset % new_dev
-    new_queue = jnp.where(live[:, None], jnp.take(remote, source, axis=0), queue_keys)
+    source = (b_e * n_q + b_s) * new_dev + offset % new_dev
+    pick_new = (source[:, None] == jnp.arange(blocks.shape[0])[None, :]).astype(jnp.bfloat16)
+    placed = jnp.dot(pick_new, blocks, preferred_element_type=jnp.float32).astype(jnp.bfloat16)
+    new_queue = jnp.where(live[:, None], placed, queue_keys)
     return (loss, grad_rows, new_queue)
 
 

time: 91.3 us -> 86.4 us (0.946)
  local copies, waits for them, and re-layouts: 14.1 us -> 8.28 us
  waiting for transfers between devices: 32.2 us -> 33.7 us
    gather x1 -> x0, local copies, waits for them, and re-layouts: 4.21 us -> none  [body(): jnp.take(remote, source, axis=0)]
    select_n x2 -> x0, other arithmetic: 3.53 us -> none  [the longest x1 2.59 us: body(): jnp.take(remote, source, axis=0)]
    unnamed x22 -> x17, local copies, waits for them, and re-layouts: 5.55 us -> 2.36 us
    gather x1, other arithmetic: 0.01 us -> 2.53 us  [body(): b = jnp.take(owner_block, sub_block)]
    ppermute x7 -> x9, waiting for transfers between devices: 13.7 us -> 16.2 us  [swap(): return lax.ppermute(x, axis, [(i, i ^ bit) for i in range(n)])]
    dynamic_slice x1, local copies, waits for them, and re-layouts: 0.02 us -> 1.72 us  [gather_queue(): piece = lax.dynamic_slice_in_dim(queue_keys, dp * piece_rows, piece_rows, 0)]
    another operation x0 -> x3, other arithmetic: none -> 1.67 us  [gather_blocks(): got = jnp.stack([got, swap(got, 'dp', n_dp, bit)], axis=t)]
    ppermute x9 -> x12, starting transfers between devices: 19.2 us -> 17.7 us  [shift(): return lax.ppermute(x, axis, [(i, (i + step) % n) for i in range(n)])]
  transfers between devices with their start and end apart: 16 -> 21, of which waited for: 9 -> 8; matrix products, arithmetic and copies ran while one was open for 31% -> 27% of each run, Pallas kernels for 0% -> 0%
where the time goes in v7:
time: 86.4 us; the launch traced here: 86.1 us
  waiting for transfers between devices  33.7 us (39%)
  starting transfers between devices  24.1 us (28%)
  matrix products  10.3 us (12%)
  local copies, waits for them, and re-layouts  8.28 us (10%)
  other arithmetic  8 us (9%)
  between operations  1.7 us (2%)
    ppermute x12, starting transfers between devices, shift(): return lax.ppermute(x, axis, [(i, (i + step) % n) for i in range(n)])  17.7 us
    ppermute x12, waiting for transfers between devices, shift(): return lax.ppermute(x, axis, [(i, (i + step) % n) for i in range(n)])  17.5 us
    ppermute x9, waiting for transfers between devices, swap(): return lax.ppermute(x, axis, [(i, i ^ bit) for i in range(n)])  16.2 us
    ppermute x9, starting transfers between devices, swap(): return lax.ppermute(x, axis, [(i, i ^ bit) for i in range(n)])  6.44 us
    gather x1, other arithmetic, body(): b = jnp.take(owner_block, sub_block)  2.53 us
    unnamed x17, local copies, waits for them, and re-layouts  2.36 us
    dot_general x1, matrix products, body(): fresh = jnp.dot(key_inputs, key_weight, preferred_element_type=jnp.float32)  2.09 us
    dot_general x2, matrix products, reduce_scatter_grad(): lax.dot_general(xs, gs, (((0,), (0,)), ((), ())), preferred_element_type=...  1.9 us
  transfers between devices with their start and end apart: 21, of which 8 were waited for; matrix products, arithmetic and copies ran while one was open for 27% of the time, Pallas kernels for 0%

profile of v7, /device:TPU:0, one launch (start us, length us, event | category | flops | bytes accessed | tf_op | source)
XLA Modules:
  0.0 86.1 jit_solution(15772355996876010328)
XLA Ops:
  0.7 1.7 %constant_dynamic-slice_fusion.2 = bf16[64,1024]{1,0:T(8,128)(2,1)} fusion(bf16[256,1024]{1,0:T(8,128)(2,1)} %param.12, s32[]{:T(128)S(6)} %select_n.195), kind=kLoop, calls=%fused_computation.79 | loop fusion | bytes 262148 | tf_op jit(solution)/shard_map/dynamic_slice | solution.py:30
  2.4 3.1 %collective-permute-start = (bf16[64,1024]{1,0:T(8,128)(2,1)}, bf16[64,1024]{1,0:T(8,128)(2,1)S(1)}, u32[]{:S(2)}, u32[]{:S(2)}) collective-permute-start(bf16[64,1024]{1,0:T(8,128)(2,1)} %constant_dynamic-slice_fusion.2), channel_id=1, source_target_pairs={{0,4},{4,8},{8,12},{12,0},{1,5},{5,9},{9,13},{13,1},{2,6},{6,10},{... | collective-permute-start | bytes 393224 | tf_op jit(solution)/shard_map/ppermute | solution.py:10
  5.4 2.6 %collective-permute-start.1 = (bf16[64,1024]{1,0:T(8,128)(2,1)}, bf16[64,1024]{1,0:T(8,128)(2,1)}, u32[]{:S(2)}, u32[]{:S(2)}) collective-permute-start(bf16[64,1024]{1,0:T(8,128)(2,1)} %constant_dynamic-slice_fusion.2), channel_id=1, source_target_pairs={{0,8},{4,12},{8,0},{12,4},{1,9},{5,13},{9,1},{13,5},{2,10},{6,14},... | collective-permute-start | bytes 393224 | tf_op jit(solution)/shard_map/ppermute | solution.py:10
  8.0 1.3 %collective-permute-start.2 = (bf16[64,1024]{1,0:T(8,128)(2,1)}, bf16[64,1024]{1,0:T(8,128)(2,1)}, u32[]{:S(2)}, u32[]{:S(2)}) collective-permute-start(bf16[64,1024]{1,0:T(8,128)(2,1)} %constant_dynamic-slice_fusion.2), channel_id=1, source_target_pairs={{0,12},{4,0},{8,4},{12,8},{1,13},{5,1},{9,5},{13,9},{2,14},{6,2},{... | collective-permute-start | bytes 393224 | tf_op jit(solution)/shard_map/ppermute | solution.py:10
  9.4 1.2 %copy.20 = bf16[256,1024]{0,1:T(8,128)(2,1)S(1)} copy(bf16[256,1024]{1,0:T(8,128)(2,1)} %param.8) | data formatting | bytes 1048576 | tf_op args[0]
  12.2 1.5 %collective-permute-start.5 = (bf16[256,4,128]{2,0,1:T(8,128)(2,1)}, bf16[256,4,128]{2,0,1:T(8,128)(2,1)}, u32[]{:S(2)}, u32[]{:S(2)}) collective-permute-start(bf16[256,4,128]{2,0,1:T(8,128)(2,1)} %bitcast.11), channel_id=1, source_target_pairs={{0,2},{1,3},{2,0},{3,1},{4,6},{5,7},{6,4},{7,5},{8,10},{9,11},{10,... | collective-permute-start | bytes 786440 | tf_op jit(solution)/shard_map/ppermute | solution.py:14
  13.7 1.7 %multiply_reduce_fusion.2 = (f32[256]{0:T(256)S(1)}, f32[256,1024]{1,0:T(8,128)}) fusion(bf16[256,1024]{1,0:T(8,128)(2,1)S(1)} %copy-done.3, bf16[1024,1024]{1,0:T(8,128)(2,1)S(1)} %copy-done), kind=kOutput, calls=%fused_computation.13 | convolution fusion | flops 537394944 | bytes 3671040 | tf_op jit(solution)/shard_map/dot_general | solution.py:109
  16.9 2.5 %compare_select_fusion.3 = s32[256,1]{0,1:T(1,128)S(1)} fusion(s32[]{:T(128)} %bitcast.33, s32[]{:T(128)} %bitcast.34, s32[]{:T(128)} %bitcast.36, s32[]{:T(128)} %bitcast.35, s32[]{:T(128)} %bitcast.94), kind=kLoop, calls=%fused_computation.71 | loop fusion | flops 9472 | bytes 1044 | tf_op jit(solution)/shard_map/jit(_take)/gather | solution.py:160
  21.2 2.1 %multiply_reduce_fusion.3 = (f32[16]{0:T(128)S(1)}, f32[16,1024]{1,0:T(8,128)S(1)}) fusion(bf16[16,1024]{1,0:T(8,128)(2,1)S(1)} %copy-done.5, bf16[1024,1024]{1,0:T(8,128)(2,1)} %param.11), kind=kOutput, calls=%fused_computation.67 | convolution fusion | flops 33587184 | bytes 2195520 | tf_op jit(solution)/shard_map/dot_general | solution.py:102
  23.3 7.0 %collective-permute-done.3 = bf16[3,64,1024]{2,1,0:T(8,128)(2,1)S(1)} collective-permute-done((bf16[3,64,1024]{2,1,0:T(8,128)(2,1)S(1)}, bf16[3,64,1024]{2,1,0:T(8,128)(2,1)S(1)}, u32[]{:S(2)}, u32[]{:S(2)}) %collective-permute-start.3) | collective-permute-done | bytes 393248 | tf_op jit(solution)/shard_map/ppermute | solution.py:14
  31.0 1.8 %collective-permute-done.4 = bf16[2,3,64,1024]{3,2,1,0:T(8,128)(2,1)S(1)} collective-permute-done((bf16[2,3,64,1024]{3,2,1,0:T(8,128)(2,1)S(1)}, bf16[2,3,64,1024]{3,2,1,0:T(8,128)(2,1)S(1)}, u32[]{:S(2)}, u32[]{:S(2)}) %collective-permute-start.4) | collective-permute-done | bytes 786464 | tf_op jit(solution)/shard_map/ppermute | solution.py:14
  38.3 2.1 %collective-permute-start.16 = (bf16[16,1024]{1,0:T(8,128)(2,1)S(1)}, bf16[16,1024]{1,0:T(8,128)(2,1)S(1)}, u32[]{:S(2)}, u32[]{:S(2)}) collective-permute-start(bf16[16,1024]{1,0:T(8,128)(2,1)S(1)} %multiply_convert_fusion.2), channel_id=1, source_target_pairs={{0,4},{4,8},{8,12},{12,0},{1,5},{5,9},{9,13},{13,1},{2,6},{6,10},{... | collective-permute-start | bytes 98312 | tf_op jit(solution)/shard_map/ppermute | solution.py:10
  41.0 1.8 %collective-permute-start.18 = (bf16[16,1024]{1,0:T(8,128)(2,1)S(1)}, bf16[16,1024]{1,0:T(8,128)(2,1)S(1)}, u32[]{:S(2)}, u32[]{:S(2)}) collective-permute-start(bf16[16,1024]{1,0:T(8,128)(2,1)S(1)} %multiply_convert_fusion.2), channel_id=1, source_target_pairs={{0,12},{4,0},{8,4},{12,8},{1,13},{5,1},{9,5},{13,9},{2,14},{6,2},{... | collective-permute-start | bytes 98312 | tf_op jit(solution)/shard_map/ppermute | solution.py:10
  43.6 1.5 %collective-permute-start.6 = (bf16[256,512]{1,0:T(8,128)(2,1)}, bf16[256,512]{1,0:T(8,128)(2,1)}, u32[]{:S(2)}, u32[]{:S(2)}) collective-permute-start(bf16[256,512]{1,0:T(8,128)(2,1)} %get-tuple-element.21), channel_id=1, source_target_pairs={{0,2},{1,3},{2,0},{3,1},{4,6},{5,7},{6,4},{7,5},{8,10},{9,11},{10,... | collective-permute-start | bytes 786440 | tf_op jit(solution)/shard_map/ppermute | solution.py:14
  46.2 1.2 %collective-permute-start.19 = (bf16[4,16,1024]{2,1,0:T(8,128)(2,1)}, bf16[4,16,1024]{2,1,0:T(8,128)(2,1)}, u32[]{:S(2)}, u32[]{:S(2)}) collective-permute-start(bf16[4,16,1024]{2,1,0:T(8,128)(2,1)} %get-tuple-element.33), channel_id=1, source_target_pairs={{0,2},{1,3},{2,0},{3,1},{4,6},{5,7},{6,4},{7,5},{8,10},{9,11},{10,... | collective-permute-start | bytes 393224 | tf_op jit(solution)/shard_map/ppermute | solution.py:14
  47.6 1.1 %copy.22 = bf16[256,4,128]{0,2,1:T(8,128)(2,1)S(1)} copy(bf16[256,4,128]{2,0,1:T(8,128)(2,1)} %collective-permute-done.5) | data formatting | bytes 524288 | tf_op jit(solution)/shard_map/ppermute | solution.py:14
  49.6 6.3 %collective-permute-done.19 = bf16[4,16,1024]{2,1,0:T(8,128)(2,1)} collective-permute-done((bf16[4,16,1024]{2,1,0:T(8,128)(2,1)}, bf16[4,16,1024]{2,1,0:T(8,128)(2,1)}, u32[]{:S(2)}, u32[]{:S(2)}) %collective-permute-start.19) | collective-permute-done | bytes 131104 | tf_op jit(solution)/shard_map/ppermute | solution.py:14
  56.9 1.5 %fusion.8 = f32[4,2,64,512]{3,2,1,0:T(8,128)S(1)} fusion(bf16[4,2,64,512]{3,2,1,0:T(8,128)(2,1)S(1)} %bitcast.99, bf16[256,512]{1,0:T(8,128)(2,1)} %collective-permute-done.6, bf16[256,512]{1,0:T(8,128)(2,1)} %get-tuple-element.21), kind=kOutput, calls=%fused_computation.23 | convolution fusion | flops 269484032 | bytes 2097152 | tf_op jit(solution)/shard_map/dot_general | solution.py:65
  60.7 1.1 %fusion.3 = bf16[256,1024]{1,0:T(8,128)(2,1)} fusion(bf16[256,1024]{1,0:T(8,128)(2,1)S(1)} %copy-done.1, bf16[256,1024]{1,0:T(8,128)(2,1)S(1)} %bitcast.101, pred[256]{0:T(512)(128)(4,1)S(1)} %broadcast_compare_fusion, s32[256]{0:T(256)S(1)} %fusion.39), kind=kOutput, calls=%fused_computation.8 | convolution fusion | flops 134807552 | bytes 1574144 | tf_op jit(solution)/shard_map/dot_general | solution.py:165
  62.0 1.7 %collective-permute-start.10 = (f32[64,512]{1,0:T(8,128)S(1)}, f32[64,512]{1,0:T(8,128)S(1)}, u32[]{:S(2)}, u32[]{:S(2)}) collective-permute-start(f32[64,512]{1,0:T(8,128)S(1)} %get-tuple-element.19), channel_id=1, source_target_pairs={{0,12},{4,0},{8,4},{12,8},{1,13},{5,1},{9,5},{13,9},{2,14},{6,2},{... | collective-permute-start | bytes 393224 | tf_op jit(solution)/shard_map/ppermute | solution.py:10
  65.3 3.0 %collective-permute-start.13 = (f32[64,512]{1,0:T(8,128)S(1)}, f32[64,512]{1,0:T(8,128)S(1)}, u32[]{:S(2)}, u32[]{:S(2)}) collective-permute-start(f32[64,512]{1,0:T(8,128)S(1)} %get-tuple-element.23), channel_id=1, source_target_pairs={{0,4},{4,8},{8,12},{12,0},{1,5},{5,9},{9,13},{13,1},{2,6},{6,10},{... | collective-permute-start | bytes 393224 | tf_op jit(solution)/shard_map/ppermute | solution.py:10
  68.3 3.8 %collective-permute-done.10 = f32[64,512]{1,0:T(8,128)S(1)} collective-permute-done((f32[64,512]{1,0:T(8,128)S(1)}, f32[64,512]{1,0:T(8,128)S(1)}, u32[]{:S(2)}, u32[]{:S(2)}) %collective-permute-start.10) | collective-permute-done | bytes 131104 | tf_op jit(solution)/shard_map/ppermute | solution.py:10
  72.0 10.4 %collective-permute-done.9 = f32[64,512]{1,0:T(8,128)S(1)} collective-permute-done((f32[64,512]{1,0:T(8,128)S(1)}, f32[64,512]{1,0:T(8,128)S(1)}, u32[]{:S(2)}, u32[]{:S(2)}) %collective-permute-start.9) | collective-permute-done | bytes 131104 | tf_op jit(solution)/shard_map/ppermute | solution.py:10
  82.5 2.8 %collective-permute-done.14 = f32[64,512]{1,0:T(8,128)S(1)} collective-permute-done((f32[64,512]{1,0:T(8,128)S(1)}, f32[64,512]{1,0:T(8,128)S(1)}, u32[]{:S(2)}, u32[]{:S(2)}) %collective-permute-start.14) | collective-permute-done | bytes 131104 | tf_op jit(solution)/shard_map/ppermute | solution.py:10
  (84 shorter events, 19.4 us)
Async XLA Ops:
  0.6 13.1 %copy-start = (bf16[1024,1024]{1,0:T(8,128)(2,1)S(1)}, bf16[1024,1024]{1,0:T(8,128)(2,1)}, u32[]{:S(2)}) copy-start(bf16[1024,1024]{1,0:T(8,128)(2,1)} %param.10) | copy-start | bytes 6291460
  0.6 13.1 %copy-start.3 = (bf16[256,1024]{1,0:T(8,128)(2,1)S(1)}, bf16[256,1024]{1,0:T(8,128)(2,1)}, u32[]{:S(2)}) copy-start(bf16[256,1024]{1,0:T(8,128)(2,1)} %param.8) | copy-start | bytes 1572868
  2.4 17.1 %collective-permute-start = (bf16[64,1024]{1,0:T(8,128)(2,1)}, bf16[64,1024]{1,0:T(8,128)(2,1)S(1)}, u32[]{:S(2)}, u32[]{:S(2)}) collective-permute-start(bf16[64,1024]{1,0:T(8,128)(2,1)} %constant_dynamic-slice_fusion.2), channel_id=1, source_target_pairs={{0,4},{4,8},{8,12},{12,0},{1,5},{5,9},{9,13},{13,1},{2,6},{6,10},{... | collective-permute-start | bytes 393224 | tf_op jit(solution)/shard_map/ppermute | solution.py:10
  5.4 14.0 %collective-permute-start.1 = (bf16[64,1024]{1,0:T(8,128)(2,1)}, bf16[64,1024]{1,0:T(8,128)(2,1)}, u32[]{:S(2)}, u32[]{:S(2)}) collective-permute-start(bf16[64,1024]{1,0:T(8,128)(2,1)} %constant_dynamic-slice_fusion.2), channel_id=1, source_target_pairs={{0,8},{4,12},{8,0},{12,4},{1,9},{5,13},{9,1},{13,5},{2,10},{6,14},... | collective-permute-start | bytes 393224 | tf_op jit(solution)/shard_map/ppermute | solution.py:10
  8.0 11.5 %collective-permute-start.2 = (bf16[64,1024]{1,0:T(8,128)(2,1)}, bf16[64,1024]{1,0:T(8,128)(2,1)}, u32[]{:S(2)}, u32[]{:S(2)}) collective-permute-start(bf16[64,1024]{1,0:T(8,128)(2,1)} %constant_dynamic-slice_fusion.2), channel_id=1, source_target_pairs={{0,12},{4,0},{8,4},{12,8},{1,13},{5,1},{9,5},{13,9},{2,14},{6,2},{... | collective-permute-start | bytes 393224 | tf_op jit(solution)/shard_map/ppermute | solution.py:10
  12.2 35.3 %collective-permute-start.5 = (bf16[256,4,128]{2,0,1:T(8,128)(2,1)}, bf16[256,4,128]{2,0,1:T(8,128)(2,1)}, u32[]{:S(2)}, u32[]{:S(2)}) collective-permute-start(bf16[256,4,128]{2,0,1:T(8,128)(2,1)} %bitcast.11), channel_id=1, source_target_pairs={{0,2},{1,3},{2,0},{3,1},{4,6},{5,7},{6,4},{7,5},{8,10},{9,11},{10,... | collective-permute-start | bytes 786440 | tf_op jit(solution)/shard_map/ppermute | solution.py:14
  20.5 9.8 %collective-permute-start.3 = (bf16[3,64,1024]{2,1,0:T(8,128)(2,1)S(1)}, bf16[3,64,1024]{2,1,0:T(8,128)(2,1)S(1)}, u32[]{:S(2)}, u32[]{:S(2)}) collective-permute-start(bf16[3,64,1024]{2,1,0:T(8,128)(2,1)S(1)} %get-tuple-element.29), channel_id=1, source_target_pairs={{0,2},{1,3},{2,0},{3,1},{4,6},{5,7},{6,4},{7,5},{8,10},{9,11},{10,... | collective-permute-start | bytes 1179656 | tf_op jit(solution)/shard_map/ppermute | solution.py:14
  30.4 2.4 %collective-permute-start.4 = (bf16[2,3,64,1024]{3,2,1,0:T(8,128)(2,1)S(1)}, bf16[2,3,64,1024]{3,2,1,0:T(8,128)(2,1)S(1)}, u32[]{:S(2)}, u32[]{:S(2)}) collective-permute-start(bf16[2,3,64,1024]{3,2,1,0:T(8,128)(2,1)S(1)} %get-tuple-element.17), channel_id=1, source_target_pairs={{0,1},{1,0},{2,3},{3,2},{4,5},{5,4},{6,7},{7,6},{8,9},{9,8},{10,11... | collective-permute-start | bytes 2359304 | tf_op jit(solution)/shard_map/ppermute | solution.py:14
  38.3 10.4 %copy-start.4 = (bf16[256,4,1,128]{0,3,2,1:T(8,128)(2,1)S(1)}, bf16[256,4,1,128]{0,3,2,1:T(8,128)(2,1)}, u32[]{:S(2)}) copy-start(bf16[256,4,1,128]{0,3,2,1:T(8,128)(2,1)} %get-tuple-element.26) | copy-start | bytes 786436
  38.3 6.8 %collective-permute-start.16 = (bf16[16,1024]{1,0:T(8,128)(2,1)S(1)}, bf16[16,1024]{1,0:T(8,128)(2,1)S(1)}, u32[]{:S(2)}, u32[]{:S(2)}) collective-permute-start(bf16[16,1024]{1,0:T(8,128)(2,1)S(1)} %multiply_convert_fusion.2), channel_id=1, source_target_pairs={{0,4},{4,8},{8,12},{12,0},{1,5},{5,9},{9,13},{13,1},{2,6},{6,10},{... | collective-permute-start | bytes 98312 | tf_op jit(solution)/shard_map/ppermute | solution.py:10
  40.4 5.2 %collective-permute-start.17 = (bf16[16,1024]{1,0:T(8,128)(2,1)S(1)}, bf16[16,1024]{1,0:T(8,128)(2,1)S(1)}, u32[]{:S(2)}, u32[]{:S(2)}) collective-permute-start(bf16[16,1024]{1,0:T(8,128)(2,1)S(1)} %multiply_convert_fusion.2), channel_id=1, source_target_pairs={{0,8},{4,12},{8,0},{12,4},{1,9},{5,13},{9,1},{13,5},{2,10},{6,14},... | collective-permute-start | bytes 98312 | tf_op jit(solution)/shard_map/ppermute | solution.py:10
  41.0 4.6 %collective-permute-start.18 = (bf16[16,1024]{1,0:T(8,128)(2,1)S(1)}, bf16[16,1024]{1,0:T(8,128)(2,1)S(1)}, u32[]{:S(2)}, u32[]{:S(2)}) collective-permute-start(bf16[16,1024]{1,0:T(8,128)(2,1)S(1)} %multiply_convert_fusion.2), channel_id=1, source_target_pairs={{0,12},{4,0},{8,4},{12,8},{1,13},{5,1},{9,5},{13,9},{2,14},{6,2},{... | collective-permute-start | bytes 98312 | tf_op jit(solution)/shard_map/ppermute | solution.py:10
  43.6 13.3 %collective-permute-start.6 = (bf16[256,512]{1,0:T(8,128)(2,1)}, bf16[256,512]{1,0:T(8,128)(2,1)}, u32[]{:S(2)}, u32[]{:S(2)}) collective-permute-start(bf16[256,512]{1,0:T(8,128)(2,1)} %get-tuple-element.21), channel_id=1, source_target_pairs={{0,2},{1,3},{2,0},{3,1},{4,6},{5,7},{6,4},{7,5},{8,10},{9,11},{10,... | collective-permute-start | bytes 786440 | tf_op jit(solution)/shard_map/ppermute | solution.py:14
  46.2 9.6 %collective-permute-start.19 = (bf16[4,16,1024]{2,1,0:T(8,128)(2,1)}, bf16[4,16,1024]{2,1,0:T(8,128)(2,1)}, u32[]{:S(2)}, u32[]{:S(2)}) collective-permute-start(bf16[4,16,1024]{2,1,0:T(8,128)(2,1)} %get-tuple-element.33), channel_id=1, source_target_pairs={{0,2},{1,3},{2,0},{3,1},{4,6},{5,7},{6,4},{7,5},{8,10},{9,11},{10,... | collective-permute-start | bytes 393224 | tf_op jit(solution)/shard_map/ppermute | solution.py:14
  48.7 11.3 %collective-permute-start.11 = (bf16[256,512]{1,0:T(8,128)(2,1)S(1)}, bf16[256,512]{1,0:T(8,128)(2,1)S(1)}, u32[]{:S(2)}, u32[]{:S(2)}) collective-permute-start(bf16[256,512]{1,0:T(8,128)(2,1)S(1)} %get-tuple-element.22), channel_id=1, source_target_pairs={{0,2},{1,3},{2,0},{3,1},{4,6},{5,7},{6,4},{7,5},{8,10},{9,11},{10,... | collective-permute-start | bytes 786440 | tf_op jit(solution)/shard_map/ppermute | solution.py:14
  56.8 3.8 %collective-permute-start.20 = (bf16[2,4,16,1024]{3,2,1,0:T(8,128)(2,1)S(1)}, bf16[2,4,16,1024]{3,2,1,0:T(8,128)(2,1)S(1)}, u32[]{:S(2)}, u32[]{:S(2)}) collective-permute-start(bf16[2,4,16,1024]{3,2,1,0:T(8,128)(2,1)S(1)} %get-tuple-element.31), channel_id=1, source_target_pairs={{0,1},{1,0},{2,3},{3,2},{4,5},{5,4},{6,7},{7,6},{8,9},{9,8},{10,11... | collective-permute-start | bytes 786440 | tf_op jit(solution)/shard_map/ppermute | solution.py:14
  58.4 3.4 %collective-permute-start.7 = (f32[4,64,512]{2,1,0:T(8,128)S(1)}, f32[4,64,512]{2,1,0:T(8,128)S(1)}, u32[]{:S(2)}, u32[]{:S(2)}) collective-permute-start(f32[4,64,512]{2,1,0:T(8,128)S(1)} %dynamic-slice_bitcast_fusion.1), channel_id=1, source_target_pairs={{0,1},{1,0},{2,3},{3,2},{4,5},{5,4},{6,7},{7,6},{8,9},{9,8},{10,11... | collective-permute-start | bytes 1572872 | tf_op jit(solution)/shard_map/ppermute | solution.py:14
  60.5 4.6 %collective-permute-start.12 = (f32[4,64,512]{2,1,0:T(8,128)S(1)}, f32[4,64,512]{2,1,0:T(8,128)S(1)}, u32[]{:S(2)}, u32[]{:S(2)}) collective-permute-start(f32[4,64,512]{2,1,0:T(8,128)S(1)} %dynamic-slice_bitcast_fusion), channel_id=1, source_target_pairs={{0,1},{1,0},{2,3},{3,2},{4,5},{5,4},{6,7},{7,6},{8,9},{9,8},{10,11... | collective-permute-start | bytes 1572872 | tf_op jit(solution)/shard_map/ppermute | solution.py:14
  62.0 10.1 %collective-permute-start.10 = (f32[64,512]{1,0:T(8,128)S(1)}, f32[64,512]{1,0:T(8,128)S(1)}, u32[]{:S(2)}, u32[]{:S(2)}) collective-permute-start(f32[64,512]{1,0:T(8,128)S(1)} %get-tuple-element.19), channel_id=1, source_target_pairs={{0,12},{4,0},{8,4},{12,8},{1,13},{5,1},{9,5},{13,9},{2,14},{6,2},{... | collective-permute-start | bytes 393224 | tf_op jit(solution)/shard_map/ppermute | solution.py:10
  63.7 8.4 %collective-permute-start.8 = (f32[64,512]{1,0:T(8,128)S(1)}, f32[64,512]{1,0:T(8,128)S(1)}, u32[]{:S(2)}, u32[]{:S(2)}) collective-permute-start(f32[64,512]{1,0:T(8,128)S(1)} %get-tuple-element.18), channel_id=1, source_target_pairs={{0,4},{4,8},{8,12},{12,0},{1,5},{5,9},{9,13},{13,1},{2,6},{6,10},{... | collective-permute-start | bytes 393224 | tf_op jit(solution)/shard_map/ppermute | solution.py:10
  64.0 18.4 %collective-permute-start.9 = (f32[64,512]{1,0:T(8,128)S(1)}, f32[64,512]{1,0:T(8,128)S(1)}, u32[]{:S(2)}, u32[]{:S(2)}) collective-permute-start(f32[64,512]{1,0:T(8,128)S(1)} %get-tuple-element.20), channel_id=1, source_target_pairs={{0,8},{4,12},{8,0},{12,4},{1,9},{5,13},{9,1},{13,5},{2,10},{6,14},... | collective-permute-start | bytes 393224 | tf_op jit(solution)/shard_map/ppermute | solution.py:10
  65.3 17.3 %collective-permute-start.13 = (f32[64,512]{1,0:T(8,128)S(1)}, f32[64,512]{1,0:T(8,128)S(1)}, u32[]{:S(2)}, u32[]{:S(2)}) collective-permute-start(f32[64,512]{1,0:T(8,128)S(1)} %get-tuple-element.23), channel_id=1, source_target_pairs={{0,4},{4,8},{8,12},{12,0},{1,5},{5,9},{9,13},{13,1},{2,6},{6,10},{... | collective-permute-start | bytes 393224 | tf_op jit(solution)/shard_map/ppermute | solution.py:10
  68.3 17.0 %collective-permute-start.14 = (f32[64,512]{1,0:T(8,128)S(1)}, f32[64,512]{1,0:T(8,128)S(1)}, u32[]{:S(2)}, u32[]{:S(2)}) collective-permute-start(f32[64,512]{1,0:T(8,128)S(1)} %get-tuple-element.25), channel_id=1, source_target_pairs={{0,8},{4,12},{8,0},{12,4},{1,9},{5,13},{9,1},{13,5},{2,10},{6,14},... | collective-permute-start | bytes 393224 | tf_op jit(solution)/shard_map/ppermute | solution.py:10
  72.0 13.2 %collective-permute-start.15 = (f32[64,512]{1,0:T(8,128)S(1)}, f32[64,512]{1,0:T(8,128)S(1)}, u32[]{:S(2)}, u32[]{:S(2)}) collective-permute-start(f32[64,512]{1,0:T(8,128)S(1)} %get-tuple-element.24), channel_id=1, source_target_pairs={{0,12},{4,0},{8,4},{12,8},{1,13},{5,1},{9,5},{13,9},{2,14},{6,2},{... | collective-permute-start | bytes 393224 | tf_op jit(solution)/shard_map/ppermute | solution.py:10
  (5 other events, 19.5 us)

commit v8 on v7

--- a/solution.py
+++ b/solution.py
@@ -41,7 +41,7 @@
     return got.reshape(n_dp * n_q * block.shape[0], block.shape[1])
 
 
-def reduce_scatter_grad(query_inputs, grad_query, n_q, n_dp):
+def reduce_scatter_grad(query_inputs, grad_query, n_q, n_dp, held):
     q = lax.axis_index("queue")
     dp = lax.axis_index("dp")
     q_dev, rows = query_inputs.shape
@@ -71,12 +71,14 @@
             send = lax.dynamic_index_in_dim(t, 1 - me, 1 + axis, keepdims=False)
             t = keep + swap(send, "dp", n_dp, bit)
         t = t.reshape(n_q, share, cols)
+        if h == halves - 1:
+            held, t = lax.optimization_barrier((held, t))
         acc = lax.dynamic_index_in_dim(t, q, 0, keepdims=False)
         for s in range(1, n_q):
             part = lax.dynamic_index_in_dim(t, (q + s) % n_q, 0, keepdims=False)
             acc = acc + shift(part, "queue", n_q, s)
         out.append(acc)
-    return jnp.concatenate(out, axis=1)
+    return jnp.concatenate(out, axis=1), held
 
 
 def body(
@@ -146,8 +148,7 @@
     grad_query = (
         (grad_unit - unit_f * jnp.sum(unit_f * grad_unit, -1, keepdims=True)) * inv_len
     ).astype(jnp.bfloat16)
-    fresh, grad_query = lax.optimization_barrier((fresh, grad_query))
-    grad_rows = reduce_scatter_grad(query_inputs, grad_query, n_q, n_dp)
+    grad_rows, fresh = reduce_scatter_grad(query_inputs, grad_query, n_q, n_dp, fresh)
     blocks = gather_blocks(fresh, n_q, n_dp)
 
     n_blocks = slot_owner.shape[0]

time: 86.4 us -> 88.9 us (1.029)
  waiting for transfers between devices: 33.7 us -> 29 us
  starting transfers between devices: 24.1 us -> 27.5 us
  local copies, waits for them, and re-layouts: 8.28 us -> 10.2 us
  other arithmetic: 8 us -> 9.86 us
    ppermute x12, waiting for transfers between devices: 17.5 us -> 11.2 us  [shift(): return lax.ppermute(x, axis, [(i, (i + step) % n) for i in range(n)])]
    ppermute x12, starting transfers between devices: 17.7 us -> 21.7 us  [shift(): return lax.ppermute(x, axis, [(i, (i + step) % n) for i in range(n)])]
    another operation x3, other arithmetic: 1.28 us -> 3.47 us  [gather_queue(): payload = jnp.stack([payload, swap(payload, 'dp', n_dp, bit)], axis=t)]
    ppermute x9, waiting for transfers between devices: 16.2 us -> 17.9 us  [swap(): return lax.ppermute(x, axis, [(i, i ^ bit) for i in range(n)])]
    squeeze x2, local copies, waits for them, and re-layouts: 0.09 us -> 1.7 us  [reduce_scatter_grad(): send = lax.dynamic_index_in_dim(t, 1 - me, 1 + axis, keepdims=False)]
    another operation x3, other arithmetic: 1.67 us -> 0.11 us  [gather_blocks(): got = jnp.stack([got, swap(got, 'dp', n_dp, bit)], axis=t)]
    add x2, other arithmetic: 0.17 us -> 1.45 us  [reduce_scatter_grad(): t = keep + swap(send, 'dp', n_dp, bit)]
    unnamed x17 -> x23, local copies, waits for them, and re-layouts: 2.36 us -> 2.63 us
  transfers between devices with their start and end apart: 21 -> 21, of which waited for: 8 -> 7; matrix products, arithmetic and copies ran while one was open for 27% -> 29% of each run, Pallas kernels for 0% -> 0%
where the time goes in v8:
time: 88.9 us; the launch traced here: 88.5 us
  waiting for transfers between devices  29 us (33%)
  starting transfers between devices  27.5 us (31%)
  matrix products  10.3 us (12%)
  local copies, waits for them, and re-layouts  10.2 us (11%)
  other arithmetic  9.86 us (11%)
  between operations  1.67 us (2%)
    ppermute x12, starting transfers between devices, shift(): return lax.ppermute(x, axis, [(i, (i + step) % n) for i in range(n)])  21.7 us
    ppermute x9, waiting for transfers between devices, swap(): return lax.ppermute(x, axis, [(i, i ^ bit) for i in range(n)])  17.9 us
    ppermute x12, waiting for transfers between devices, shift(): return lax.ppermute(x, axis, [(i, (i + step) % n) for i in range(n)])  11.2 us
    ppermute x9, starting transfers between devices, swap(): return lax.ppermute(x, axis, [(i, i ^ bit) for i in range(n)])  5.81 us
    another operation x3, other arithmetic, gather_queue(): payload = jnp.stack([payload, swap(payload, 'dp', n_dp, bit)], axis=t)  3.47 us
    unnamed x23, local copies, waits for them, and re-layouts  2.63 us
    gather x1, other arithmetic, body(): b = jnp.take(owner_block, sub_block)  2.49 us
    dot_general x1, matrix products, body(): fresh = jnp.dot(key_inputs, key_weight, preferred_element_type=jnp.float32)  2.09 us
  transfers between devices with their start and end apart: 21, of which 7 were waited for; matrix products, arithmetic and copies ran while one was open for 29% of the time, Pallas kernels for 0%

profile of v8, /device:TPU:0, one launch (start us, length us, event | category | flops | bytes accessed | tf_op | source)
XLA Modules:
  0.0 88.5 jit_solution(10951209976416041712)
XLA Ops:
  0.7 1.7 %constant_dynamic-slice_fusion.2 = bf16[64,1024]{1,0:T(8,128)(2,1)} fusion(bf16[256,1024]{1,0:T(8,128)(2,1)} %param.12, s32[]{:T(128)S(6)} %select_n.195), kind=kLoop, calls=%fused_computation.79 | loop fusion | bytes 262148 | tf_op jit(solution)/shard_map/dynamic_slice | solution.py:30
  2.4 3.1 %collective-permute-start = (bf16[64,1024]{1,0:T(8,128)(2,1)}, bf16[64,1024]{1,0:T(8,128)(2,1)S(1)}, u32[]{:S(2)}, u32[]{:S(2)}) collective-permute-start(bf16[64,1024]{1,0:T(8,128)(2,1)} %constant_dynamic-slice_fusion.2), channel_id=1, source_target_pairs={{0,4},{4,8},{8,12},{12,0},{1,5},{5,9},{9,13},{13,1},{2,6},{6,10},{... | collective-permute-start | bytes 393224 | tf_op jit(solution)/shard_map/ppermute | solution.py:10
  5.4 2.6 %collective-permute-start.1 = (bf16[64,1024]{1,0:T(8,128)(2,1)}, bf16[64,1024]{1,0:T(8,128)(2,1)}, u32[]{:S(2)}, u32[]{:S(2)}) collective-permute-start(bf16[64,1024]{1,0:T(8,128)(2,1)} %constant_dynamic-slice_fusion.2), channel_id=1, source_target_pairs={{0,8},{4,12},{8,0},{12,4},{1,9},{5,13},{9,1},{13,5},{2,10},{6,14},... | collective-permute-start | bytes 393224 | tf_op jit(solution)/shard_map/ppermute | solution.py:10
  8.0 1.3 %collective-permute-start.2 = (bf16[64,1024]{1,0:T(8,128)(2,1)}, bf16[64,1024]{1,0:T(8,128)(2,1)}, u32[]{:S(2)}, u32[]{:S(2)}) collective-permute-start(bf16[64,1024]{1,0:T(8,128)(2,1)} %constant_dynamic-slice_fusion.2), channel_id=1, source_target_pairs={{0,12},{4,0},{8,4},{12,8},{1,13},{5,1},{9,5},{13,9},{2,14},{6,2},{... | collective-permute-start | bytes 393224 | tf_op jit(solution)/shard_map/ppermute | solution.py:10
  12.2 1.5 %collective-permute-start.5 = (bf16[256,4,128]{2,0,1:T(8,128)(2,1)}, bf16[256,4,128]{2,0,1:T(8,128)(2,1)}, u32[]{:S(2)}, u32[]{:S(2)}) collective-permute-start(bf16[256,4,128]{2,0,1:T(8,128)(2,1)} %bitcast.11), channel_id=1, source_target_pairs={{0,2},{1,3},{2,0},{3,1},{4,6},{5,7},{6,4},{7,5},{8,10},{9,11},{10,... | collective-permute-start | bytes 786440 | tf_op jit(solution)/shard_map/ppermute | solution.py:14
  13.7 1.7 %multiply_reduce_fusion.2 = (f32[256]{0:T(256)S(1)}, f32[256,1024]{1,0:T(8,128)}) fusion(bf16[256,1024]{1,0:T(8,128)(2,1)S(1)} %copy-done.6, bf16[1024,1024]{1,0:T(8,128)(2,1)S(1)} %copy-done), kind=kOutput, calls=%fused_computation.13 | convolution fusion | flops 537394944 | bytes 3671040 | tf_op jit(solution)/shard_map/dot_general | solution.py:111
  16.9 2.5 %compare_select_fusion.3 = s32[256,1]{0,1:T(1,128)S(1)} fusion(s32[]{:T(128)} %bitcast.33, s32[]{:T(128)} %bitcast.34, s32[]{:T(128)} %bitcast.36, s32[]{:T(128)} %bitcast.35, s32[]{:T(128)} %bitcast.94), kind=kLoop, calls=%fused_computation.71 | loop fusion | flops 9472 | bytes 1044 | tf_op jit(solution)/shard_map/jit(_take)/gather | solution.py:161
  21.2 9.2 %collective-permute-done.3 = bf16[3,64,1024]{2,1,0:T(8,128)(2,1)S(1)} collective-permute-done((bf16[3,64,1024]{2,1,0:T(8,128)(2,1)S(1)}, bf16[3,64,1024]{2,1,0:T(8,128)(2,1)S(1)}, u32[]{:S(2)}, u32[]{:S(2)}) %collective-permute-start.3) | collective-permute-done | bytes 393248 | tf_op jit(solution)/shard_map/ppermute | solution.py:14
  31.8 2.1 %multiply_reduce_fusion.3 = (f32[16]{0:T(128)S(1)}, f32[16,1024]{1,0:T(8,128)S(1)}) fusion(bf16[16,1024]{1,0:T(8,128)(2,1)S(1)} %copy-done.8, bf16[1024,1024]{1,0:T(8,128)(2,1)} %param.11), kind=kOutput, calls=%fused_computation.67 | convolution fusion | flops 33587184 | bytes 2195520 | tf_op jit(solution)/shard_map/dot_general | solution.py:104
  34.0 1.4 %pad_maximum_fusion = bf16[2,2,3,64,1024]{4,3,2,1,0:T(8,128)(2,1)S(1)} fusion(bf16[2,1,3,64,1024]{4,3,2,1,0:T(8,128)(2,1)} %bitcast.7, bf16[2,1,3,64,1024]{4,3,2,1,0:T(8,128)(2,1)S(1)} %get-tuple-element.16), kind=kLoop, calls=%fused_computation | loop fusion | flops 786432 | bytes 3145728 | tf_op jit(solution)/shard_map/stack | solution.py:33
  42.1 1.6 %collective-permute-start.6 = (bf16[256,512]{1,0:T(8,128)(2,1)S(1)}, bf16[256,512]{1,0:T(8,128)(2,1)S(1)}, u32[]{:S(2)}, u32[]{:S(2)}) collective-permute-start(bf16[256,512]{1,0:T(8,128)(2,1)S(1)} %get-tuple-element.21), channel_id=1, source_target_pairs={{0,2},{1,3},{2,0},{3,1},{4,6},{5,7},{6,4},{7,5},{8,10},{9,11},{10,... | collective-permute-start | bytes 786440 | tf_op jit(solution)/shard_map/ppermute | solution.py:14
  43.7 6.2 %collective-permute-done.11 = bf16[256,512]{1,0:T(8,128)(2,1)} collective-permute-done((bf16[256,512]{1,0:T(8,128)(2,1)}, bf16[256,512]{1,0:T(8,128)(2,1)}, u32[]{:S(2)}, u32[]{:S(2)}) %collective-permute-start.11) | collective-permute-done | bytes 262176 | tf_op jit(solution)/shard_map/ppermute | solution.py:14
  49.9 1.5 %fusion.11 = f32[4,2,64,512]{3,2,1,0:T(8,128)S(1)} fusion(bf16[4,2,64,512]{3,2,1,0:T(8,128)(2,1)S(1)} %bitcast.99, bf16[256,512]{1,0:T(8,128)(2,1)} %collective-permute-done.11, bf16[256,512]{1,0:T(8,128)(2,1)} %get-tuple-element.22), kind=kOutput, calls=%fused_computation.27 | convolution fusion | flops 269484032 | bytes 2097152 | tf_op jit(solution)/shard_map/dot_general | solution.py:65
  52.6 2.4 %collective-permute-done.6 = bf16[256,512]{1,0:T(8,128)(2,1)S(1)} collective-permute-done((bf16[256,512]{1,0:T(8,128)(2,1)S(1)}, bf16[256,512]{1,0:T(8,128)(2,1)S(1)}, u32[]{:S(2)}, u32[]{:S(2)}) %collective-permute-start.6) | collective-permute-done | bytes 262176 | tf_op jit(solution)/shard_map/ppermute | solution.py:14
  57.3 1.4 %bitcast_add_fusion = f32[4,64,512]{2,1,0:T(8,128)S(1)} fusion(f32[4,64,512]{2,1,0:T(8,128)} %collective-permute-done.12, f32[4,2,64,512]{3,2,1,0:T(8,128)} %copy-done.5, s32[]{:T(128)S(6)} %select_n.205), kind=kLoop, calls=%fused_computation.31 | loop fusion | flops 131072 | bytes 1572868 | tf_op jit(solution)/shard_map/add | solution.py:72
  58.7 2.2 %collective-permute-start.16 = (bf16[16,1024]{1,0:T(8,128)(2,1)S(1)}, bf16[16,1024]{1,0:T(8,128)(2,1)S(1)}, u32[]{:S(2)}, u32[]{:S(2)}) collective-permute-start(bf16[16,1024]{1,0:T(8,128)(2,1)S(1)} %multiply_convert_fusion.2), channel_id=1, source_target_pairs={{0,4},{4,8},{8,12},{12,0},{1,5},{5,9},{9,13},{13,1},{2,6},{6,10},{... | collective-permute-start | bytes 98312 | tf_op jit(solution)/shard_map/ppermute | solution.py:10
  61.4 1.9 %collective-permute-start.18 = (bf16[16,1024]{1,0:T(8,128)(2,1)S(1)}, bf16[16,1024]{1,0:T(8,128)(2,1)S(1)}, u32[]{:S(2)}, u32[]{:S(2)}) collective-permute-start(bf16[16,1024]{1,0:T(8,128)(2,1)S(1)} %multiply_convert_fusion.2), channel_id=1, source_target_pairs={{0,12},{4,0},{8,4},{12,8},{1,13},{5,1},{9,5},{13,9},{2,14},{6,2},{... | collective-permute-start | bytes 98312 | tf_op jit(solution)/shard_map/ppermute | solution.py:10
  63.5 2.0 %collective-permute-start.10 = (f32[64,512]{1,0:T(8,128)S(1)}, f32[64,512]{1,0:T(8,128)S(1)}, u32[]{:S(2)}, u32[]{:S(2)}) collective-permute-start(f32[64,512]{1,0:T(8,128)S(1)} %get-tuple-element.19), channel_id=1, source_target_pairs={{0,12},{4,0},{8,4},{12,8},{1,13},{5,1},{9,5},{13,9},{2,14},{6,2},{... | collective-permute-start | bytes 393224 | tf_op jit(solution)/shard_map/ppermute | solution.py:10
  65.5 1.3 %collective-permute-start.9 = (f32[64,512]{1,0:T(8,128)S(1)}, f32[64,512]{1,0:T(8,128)S(1)}, u32[]{:S(2)}, u32[]{:S(2)}) collective-permute-start(f32[64,512]{1,0:T(8,128)S(1)} %get-tuple-element.20), channel_id=1, source_target_pairs={{0,8},{4,12},{8,0},{12,4},{1,9},{5,13},{9,1},{13,5},{2,10},{6,14},... | collective-permute-start | bytes 393224 | tf_op jit(solution)/shard_map/ppermute | solution.py:10
  66.9 3.1 %collective-permute-start.13 = (f32[64,512]{1,0:T(8,128)S(1)}, f32[64,512]{1,0:T(8,128)S(1)}, u32[]{:S(2)}, u32[]{:S(2)}) collective-permute-start(f32[64,512]{1,0:T(8,128)S(1)} %get-tuple-element.23), channel_id=1, source_target_pairs={{0,4},{4,8},{8,12},{12,0},{1,5},{5,9},{9,13},{13,1},{2,6},{6,10},{... | collective-permute-start | bytes 393224 | tf_op jit(solution)/shard_map/ppermute | solution.py:10
  70.0 3.6 %collective-permute-start.15 = (f32[64,512]{1,0:T(8,128)S(1)}, f32[64,512]{1,0:T(8,128)S(1)}, u32[]{:S(2)}, u32[]{:S(2)}) collective-permute-start(f32[64,512]{1,0:T(8,128)S(1)} %get-tuple-element.24), channel_id=1, source_target_pairs={{0,12},{4,0},{8,4},{12,8},{1,13},{5,1},{9,5},{13,9},{2,14},{6,2},{... | collective-permute-start | bytes 393224 | tf_op jit(solution)/shard_map/ppermute | solution.py:10
  73.7 1.5 %collective-permute-start.19 = (bf16[4,16,1024]{2,1,0:T(8,128)(2,1)S(1)}, bf16[4,16,1024]{2,1,0:T(8,128)(2,1)S(1)}, u32[]{:S(2)}, u32[]{:S(2)}) collective-permute-start(bf16[4,16,1024]{2,1,0:T(8,128)(2,1)S(1)} %get-tuple-element.33), channel_id=1, source_target_pairs={{0,2},{1,3},{2,0},{3,1},{4,6},{5,7},{6,4},{7,5},{8,10},{9,11},{10,... | collective-permute-start | bytes 393224 | tf_op jit(solution)/shard_map/ppermute | solution.py:14
  75.3 8.4 %collective-permute-done.9 = f32[64,512]{1,0:T(8,128)S(1)} collective-permute-done((f32[64,512]{1,0:T(8,128)S(1)}, f32[64,512]{1,0:T(8,128)S(1)}, u32[]{:S(2)}, u32[]{:S(2)}) %collective-permute-start.9) | collective-permute-done | bytes 131104 | tf_op jit(solution)/shard_map/ppermute | solution.py:10
  83.9 2.6 %collective-permute-done.14 = f32[64,512]{1,0:T(8,128)S(1)} collective-permute-done((f32[64,512]{1,0:T(8,128)S(1)}, f32[64,512]{1,0:T(8,128)S(1)}, u32[]{:S(2)}, u32[]{:S(2)}) %collective-permute-start.14) | collective-permute-done | bytes 131104 | tf_op jit(solution)/shard_map/ppermute | solution.py:10
  (90 shorter events, 20.2 us)
Async XLA Ops:
  0.6 13.1 %copy-start = (bf16[1024,1024]{1,0:T(8,128)(2,1)S(1)}, bf16[1024,1024]{1,0:T(8,128)(2,1)}, u32[]{:S(2)}) copy-start(bf16[1024,1024]{1,0:T(8,128)(2,1)} %param.10) | copy-start | bytes 6291460
  0.6 13.1 %copy-start.6 = (bf16[256,1024]{1,0:T(8,128)(2,1)S(1)}, bf16[256,1024]{1,0:T(8,128)(2,1)}, u32[]{:S(2)}) copy-start(bf16[256,1024]{1,0:T(8,128)(2,1)} %param.8) | copy-start | bytes 1572868
  2.4 17.0 %collective-permute-start = (bf16[64,1024]{1,0:T(8,128)(2,1)}, bf16[64,1024]{1,0:T(8,128)(2,1)S(1)}, u32[]{:S(2)}, u32[]{:S(2)}) collective-permute-start(bf16[64,1024]{1,0:T(8,128)(2,1)} %constant_dynamic-slice_fusion.2), channel_id=1, source_target_pairs={{0,4},{4,8},{8,12},{12,0},{1,5},{5,9},{9,13},{13,1},{2,6},{6,10},{... | collective-permute-start | bytes 393224 | tf_op jit(solution)/shard_map/ppermute | solution.py:10
  5.4 14.0 %collective-permute-start.1 = (bf16[64,1024]{1,0:T(8,128)(2,1)}, bf16[64,1024]{1,0:T(8,128)(2,1)}, u32[]{:S(2)}, u32[]{:S(2)}) collective-permute-start(bf16[64,1024]{1,0:T(8,128)(2,1)} %constant_dynamic-slice_fusion.2), channel_id=1, source_target_pairs={{0,8},{4,12},{8,0},{12,4},{1,9},{5,13},{9,1},{13,5},{2,10},{6,14},... | collective-permute-start | bytes 393224 | tf_op jit(solution)/shard_map/ppermute | solution.py:10
  8.0 11.4 %collective-permute-start.2 = (bf16[64,1024]{1,0:T(8,128)(2,1)}, bf16[64,1024]{1,0:T(8,128)(2,1)}, u32[]{:S(2)}, u32[]{:S(2)}) collective-permute-start(bf16[64,1024]{1,0:T(8,128)(2,1)} %constant_dynamic-slice_fusion.2), channel_id=1, source_target_pairs={{0,12},{4,0},{8,4},{12,8},{1,13},{5,1},{9,5},{13,9},{2,14},{6,2},{... | collective-permute-start | bytes 393224 | tf_op jit(solution)/shard_map/ppermute | solution.py:10
  12.2 28.8 %collective-permute-start.5 = (bf16[256,4,128]{2,0,1:T(8,128)(2,1)}, bf16[256,4,128]{2,0,1:T(8,128)(2,1)}, u32[]{:S(2)}, u32[]{:S(2)}) collective-permute-start(bf16[256,4,128]{2,0,1:T(8,128)(2,1)} %bitcast.11), channel_id=1, source_target_pairs={{0,2},{1,3},{2,0},{3,1},{4,6},{5,7},{6,4},{7,5},{8,10},{9,11},{10,... | collective-permute-start | bytes 786440 | tf_op jit(solution)/shard_map/ppermute | solution.py:14
  19.4 12.0 %copy-start.1 = (bf16[256,1024]{1,0:T(8,128)(2,1)S(1)}, bf16[256,1024]{1,0:T(8,128)(2,1)}, u32[]{:S(2)}) copy-start(bf16[256,1024]{1,0:T(8,128)(2,1)} %param.12) | copy-start | bytes 1572868
  20.5 9.8 %collective-permute-start.3 = (bf16[3,64,1024]{2,1,0:T(8,128)(2,1)S(1)}, bf16[3,64,1024]{2,1,0:T(8,128)(2,1)S(1)}, u32[]{:S(2)}, u32[]{:S(2)}) collective-permute-start(bf16[3,64,1024]{2,1,0:T(8,128)(2,1)S(1)} %get-tuple-element.29), channel_id=1, source_target_pairs={{0,2},{1,3},{2,0},{3,1},{4,6},{5,7},{6,4},{7,5},{8,10},{9,11},{10,... | collective-permute-start | bytes 1179656 | tf_op jit(solution)/shard_map/ppermute | solution.py:14
  31.4 2.6 %collective-permute-start.4 = (bf16[2,3,64,1024]{3,2,1,0:T(8,128)(2,1)}, bf16[2,3,64,1024]{3,2,1,0:T(8,128)(2,1)}, u32[]{:S(2)}, u32[]{:S(2)}) collective-permute-start(bf16[2,3,64,1024]{3,2,1,0:T(8,128)(2,1)} %get-tuple-element.17), channel_id=1, source_target_pairs={{0,1},{1,0},{2,3},{3,2},{4,5},{5,4},{6,7},{7,6},{8,9},{9,8},{10,11... | collective-permute-start | bytes 2359304 | tf_op jit(solution)/shard_map/ppermute | solution.py:14
  40.4 9.5 %collective-permute-start.11 = (bf16[256,512]{1,0:T(8,128)(2,1)}, bf16[256,512]{1,0:T(8,128)(2,1)}, u32[]{:S(2)}, u32[]{:S(2)}) collective-permute-start(bf16[256,512]{1,0:T(8,128)(2,1)} %get-tuple-element.22), channel_id=1, source_target_pairs={{0,2},{1,3},{2,0},{3,1},{4,6},{5,7},{6,4},{7,5},{8,10},{9,11},{10,... | collective-permute-start | bytes 786440 | tf_op jit(solution)/shard_map/ppermute | solution.py:14
  42.1 12.8 %collective-permute-start.6 = (bf16[256,512]{1,0:T(8,128)(2,1)S(1)}, bf16[256,512]{1,0:T(8,128)(2,1)S(1)}, u32[]{:S(2)}, u32[]{:S(2)}) collective-permute-start(bf16[256,512]{1,0:T(8,128)(2,1)S(1)} %get-tuple-element.21), channel_id=1, source_target_pairs={{0,2},{1,3},{2,0},{3,1},{4,6},{5,7},{6,4},{7,5},{8,10},{9,11},{10,... | collective-permute-start | bytes 786440 | tf_op jit(solution)/shard_map/ppermute | solution.py:14
  52.3 5.0 %collective-permute-start.12 = (f32[4,64,512]{2,1,0:T(8,128)}, f32[4,64,512]{2,1,0:T(8,128)}, u32[]{:S(2)}, u32[]{:S(2)}) collective-permute-start(f32[4,64,512]{2,1,0:T(8,128)} %dynamic-slice_bitcast_fusion), channel_id=1, source_target_pairs={{0,1},{1,0},{2,3},{3,2},{4,5},{5,4},{6,7},{7,6},{8,9},{9,8},{10,11... | collective-permute-start | bytes 1572872 | tf_op jit(solution)/shard_map/ppermute | solution.py:14
  57.2 6.1 %collective-permute-start.7 = (f32[4,64,512]{2,1,0:T(8,128)}, f32[4,64,512]{2,1,0:T(8,128)S(1)}, u32[]{:S(2)}, u32[]{:S(2)}) collective-permute-start(f32[4,64,512]{2,1,0:T(8,128)} %dynamic-slice_bitcast_fusion.1), channel_id=1, source_target_pairs={{0,1},{1,0},{2,3},{3,2},{4,5},{5,4},{6,7},{7,6},{8,9},{9,8},{10,11... | collective-permute-start | bytes 1572872 | tf_op jit(solution)/shard_map/ppermute | solution.py:14
  58.7 6.8 %collective-permute-start.16 = (bf16[16,1024]{1,0:T(8,128)(2,1)S(1)}, bf16[16,1024]{1,0:T(8,128)(2,1)S(1)}, u32[]{:S(2)}, u32[]{:S(2)}) collective-permute-start(bf16[16,1024]{1,0:T(8,128)(2,1)S(1)} %multiply_convert_fusion.2), channel_id=1, source_target_pairs={{0,4},{4,8},{8,12},{12,0},{1,5},{5,9},{9,13},{13,1},{2,6},{6,10},{... | collective-permute-start | bytes 98312 | tf_op jit(solution)/shard_map/ppermute | solution.py:10
  60.9 6.0 %collective-permute-start.17 = (bf16[16,1024]{1,0:T(8,128)(2,1)S(1)}, bf16[16,1024]{1,0:T(8,128)(2,1)S(1)}, u32[]{:S(2)}, u32[]{:S(2)}) collective-permute-start(bf16[16,1024]{1,0:T(8,128)(2,1)S(1)} %multiply_convert_fusion.2), channel_id=1, source_target_pairs={{0,8},{4,12},{8,0},{12,4},{1,9},{5,13},{9,1},{13,5},{2,10},{6,14},... | collective-permute-start | bytes 98312 | tf_op jit(solution)/shard_map/ppermute | solution.py:10
  61.4 8.5 %collective-permute-start.18 = (bf16[16,1024]{1,0:T(8,128)(2,1)S(1)}, bf16[16,1024]{1,0:T(8,128)(2,1)S(1)}, u32[]{:S(2)}, u32[]{:S(2)}) collective-permute-start(bf16[16,1024]{1,0:T(8,128)(2,1)S(1)} %multiply_convert_fusion.2), channel_id=1, source_target_pairs={{0,12},{4,0},{8,4},{12,8},{1,13},{5,1},{9,5},{13,9},{2,14},{6,2},{... | collective-permute-start | bytes 98312 | tf_op jit(solution)/shard_map/ppermute | solution.py:10
  63.5 6.5 %collective-permute-start.10 = (f32[64,512]{1,0:T(8,128)S(1)}, f32[64,512]{1,0:T(8,128)S(1)}, u32[]{:S(2)}, u32[]{:S(2)}) collective-permute-start(f32[64,512]{1,0:T(8,128)S(1)} %get-tuple-element.19), channel_id=1, source_target_pairs={{0,12},{4,0},{8,4},{12,8},{1,13},{5,1},{9,5},{13,9},{2,14},{6,2},{... | collective-permute-start | bytes 393224 | tf_op jit(solution)/shard_map/ppermute | solution.py:10
  65.5 8.3 %collective-permute-start.8 = (f32[64,512]{1,0:T(8,128)S(1)}, f32[64,512]{1,0:T(8,128)S(1)}, u32[]{:S(2)}, u32[]{:S(2)}) collective-permute-start(f32[64,512]{1,0:T(8,128)S(1)} %get-tuple-element.18), channel_id=1, source_target_pairs={{0,4},{4,8},{8,12},{12,0},{1,5},{5,9},{9,13},{13,1},{2,6},{6,10},{... | collective-permute-start | bytes 393224 | tf_op jit(solution)/shard_map/ppermute | solution.py:10
  65.5 18.2 %collective-permute-start.9 = (f32[64,512]{1,0:T(8,128)S(1)}, f32[64,512]{1,0:T(8,128)S(1)}, u32[]{:S(2)}, u32[]{:S(2)}) collective-permute-start(f32[64,512]{1,0:T(8,128)S(1)} %get-tuple-element.20), channel_id=1, source_target_pairs={{0,8},{4,12},{8,0},{12,4},{1,9},{5,13},{9,1},{13,5},{2,10},{6,14},... | collective-permute-start | bytes 393224 | tf_op jit(solution)/shard_map/ppermute | solution.py:10
  66.9 17.0 %collective-permute-start.13 = (f32[64,512]{1,0:T(8,128)S(1)}, f32[64,512]{1,0:T(8,128)S(1)}, u32[]{:S(2)}, u32[]{:S(2)}) collective-permute-start(f32[64,512]{1,0:T(8,128)S(1)} %get-tuple-element.23), channel_id=1, source_target_pairs={{0,4},{4,8},{8,12},{12,0},{1,5},{5,9},{9,13},{13,1},{2,6},{6,10},{... | collective-permute-start | bytes 393224 | tf_op jit(solution)/shard_map/ppermute | solution.py:10
  69.9 16.6 %collective-permute-start.14 = (f32[64,512]{1,0:T(8,128)S(1)}, f32[64,512]{1,0:T(8,128)S(1)}, u32[]{:S(2)}, u32[]{:S(2)}) collective-permute-start(f32[64,512]{1,0:T(8,128)S(1)} %get-tuple-element.25), channel_id=1, source_target_pairs={{0,8},{4,12},{8,0},{12,4},{1,9},{5,13},{9,1},{13,5},{2,10},{6,14},... | collective-permute-start | bytes 393224 | tf_op jit(solution)/shard_map/ppermute | solution.py:10
  70.0 16.5 %collective-permute-start.15 = (f32[64,512]{1,0:T(8,128)S(1)}, f32[64,512]{1,0:T(8,128)S(1)}, u32[]{:S(2)}, u32[]{:S(2)}) collective-permute-start(f32[64,512]{1,0:T(8,128)S(1)} %get-tuple-element.24), channel_id=1, source_target_pairs={{0,12},{4,0},{8,4},{12,8},{1,13},{5,1},{9,5},{13,9},{2,14},{6,2},{... | collective-permute-start | bytes 393224 | tf_op jit(solution)/shard_map/ppermute | solution.py:10
  73.7 10.0 %collective-permute-start.19 = (bf16[4,16,1024]{2,1,0:T(8,128)(2,1)S(1)}, bf16[4,16,1024]{2,1,0:T(8,128)(2,1)S(1)}, u32[]{:S(2)}, u32[]{:S(2)}) collective-permute-start(bf16[4,16,1024]{2,1,0:T(8,128)(2,1)S(1)} %get-tuple-element.33), channel_id=1, source_target_pairs={{0,2},{1,3},{2,0},{3,1},{4,6},{5,7},{6,4},{7,5},{8,10},{9,11},{10,... | collective-permute-start | bytes 393224 | tf_op jit(solution)/shard_map/ppermute | solution.py:14
  83.8 3.5 %collective-permute-start.20 = (bf16[2,4,16,1024]{3,2,1,0:T(8,128)(2,1)S(1)}, bf16[2,4,16,1024]{3,2,1,0:T(8,128)(2,1)S(1)}, u32[]{:S(2)}, u32[]{:S(2)}) collective-permute-start(bf16[2,4,16,1024]{3,2,1,0:T(8,128)(2,1)S(1)} %get-tuple-element.31), channel_id=1, source_target_pairs={{0,1},{1,0},{2,3},{3,2},{4,5},{5,4},{6,7},{7,6},{8,9},{9,8},{10,11... | collective-permute-start | bytes 786440 | tf_op jit(solution)/shard_map/ppermute | solution.py:14
  (8 other events, 22.9 us)

commit v9 on v7

--- a/solution.py
+++ b/solution.py
@@ -59,9 +59,13 @@
     halves = 2
     cols = width // halves
     out = []
+    got = None
     for h in range(halves):
         g_h = grad_query[:, h * cols:(h + 1) * cols]
-        gs = jnp.concatenate([g_h, swap(g_h, "dp", n_dp, hb)], axis=0)
+        if got is not None:
+            g_h, got = lax.optimization_barrier((g_h, got))
+        got = swap(g_h, "dp", n_dp, hb)
+        gs = jnp.concatenate([g_h, got], axis=0)
         term = lax.dot_general(xs, gs, (((0,), (0,)), ((), ())), preferred_element_type=jnp.float32)
         t = term.reshape((n_q,) + (2,) * len(rest) + (share, cols))
         for axis in reversed(range(len(rest))):

time: 86.4 us -> 90.5 us (1.047)
  waiting for transfers between devices: 33.7 us -> 37.4 us
    ppermute x9, waiting for transfers between devices: 16.2 us -> 20 us  [swap(): return lax.ppermute(x, axis, [(i, i ^ bit) for i in range(n)])]
  transfers between devices with their start and end apart: 21 -> 21, of which waited for: 8 -> 8; matrix products, arithmetic and copies ran while one was open for 27% -> 25% of each run, Pallas kernels for 0% -> 0%
where the time goes in v9:
time: 90.5 us; the launch traced here: 90.2 us
  waiting for transfers between devices  37.4 us (41%)
  starting transfers between devices  24.5 us (27%)
  matrix products  10.3 us (11%)
  local copies, waits for them, and re-layouts  8.28 us (9%)
  other arithmetic  8 us (9%)
  between operations  1.69 us (2%)
    ppermute x9, waiting for transfers between devices, swap(): return lax.ppermute(x, axis, [(i, i ^ bit) for i in range(n)])  20 us
    ppermute x12, starting transfers between devices, shift(): return lax.ppermute(x, axis, [(i, (i + step) % n) for i in range(n)])  17.7 us
    ppermute x12, waiting for transfers between devices, shift(): return lax.ppermute(x, axis, [(i, (i + step) % n) for i in range(n)])  17.5 us
    ppermute x9, starting transfers between devices, swap(): return lax.ppermute(x, axis, [(i, i ^ bit) for i in range(n)])  6.79 us
    gather x1, other arithmetic, body(): b = jnp.take(owner_block, sub_block)  2.53 us
    unnamed x17, local copies, waits for them, and re-layouts  2.36 us
    dot_general x1, matrix products, body(): fresh = jnp.dot(key_inputs, key_weight, preferred_element_type=jnp.float32)  2.09 us
    dot_general x2, matrix products, reduce_scatter_grad(): lax.dot_general(xs, gs, (((0,), (0,)), ((), ())), preferred_element_type=...  1.89 us
  transfers between devices with their start and end apart: 21, of which 8 were waited for; matrix products, arithmetic and copies ran while one was open for 25% of the time, Pallas kernels for 0%

profile of v9, /device:TPU:0, one launch (start us, length us, event | category | flops | bytes accessed | tf_op | source)
XLA Modules:
  0.0 90.2 jit_solution(3734021276004631200)
XLA Ops:
  0.7 1.7 %constant_dynamic-slice_fusion.2 = bf16[64,1024]{1,0:T(8,128)(2,1)} fusion(bf16[256,1024]{1,0:T(8,128)(2,1)} %param.12, s32[]{:T(128)S(6)} %select_n.195), kind=kLoop, calls=%fused_computation.79 | loop fusion | bytes 262148 | tf_op jit(solution)/shard_map/dynamic_slice | solution.py:30
  2.4 3.1 %collective-permute-start = (bf16[64,1024]{1,0:T(8,128)(2,1)}, bf16[64,1024]{1,0:T(8,128)(2,1)S(1)}, u32[]{:S(2)}, u32[]{:S(2)}) collective-permute-start(bf16[64,1024]{1,0:T(8,128)(2,1)} %constant_dynamic-slice_fusion.2), channel_id=1, source_target_pairs={{0,4},{4,8},{8,12},{12,0},{1,5},{5,9},{9,13},{13,1},{2,6},{6,10},{... | collective-permute-start | bytes 393224 | tf_op jit(solution)/shard_map/ppermute | solution.py:10
  5.4 2.6 %collective-permute-start.1 = (bf16[64,1024]{1,0:T(8,128)(2,1)}, bf16[64,1024]{1,0:T(8,128)(2,1)}, u32[]{:S(2)}, u32[]{:S(2)}) collective-permute-start(bf16[64,1024]{1,0:T(8,128)(2,1)} %constant_dynamic-slice_fusion.2), channel_id=1, source_target_pairs={{0,8},{4,12},{8,0},{12,4},{1,9},{5,13},{9,1},{13,5},{2,10},{6,14},... | collective-permute-start | bytes 393224 | tf_op jit(solution)/shard_map/ppermute | solution.py:10
  8.0 1.3 %collective-permute-start.2 = (bf16[64,1024]{1,0:T(8,128)(2,1)}, bf16[64,1024]{1,0:T(8,128)(2,1)}, u32[]{:S(2)}, u32[]{:S(2)}) collective-permute-start(bf16[64,1024]{1,0:T(8,128)(2,1)} %constant_dynamic-slice_fusion.2), channel_id=1, source_target_pairs={{0,12},{4,0},{8,4},{12,8},{1,13},{5,1},{9,5},{13,9},{2,14},{6,2},{... | collective-permute-start | bytes 393224 | tf_op jit(solution)/shard_map/ppermute | solution.py:10
  9.4 1.2 %copy.20 = bf16[256,1024]{0,1:T(8,128)(2,1)S(1)} copy(bf16[256,1024]{1,0:T(8,128)(2,1)} %param.8) | data formatting | bytes 1048576 | tf_op args[0]
  12.2 1.5 %collective-permute-start.5 = (bf16[256,4,128]{2,0,1:T(8,128)(2,1)}, bf16[256,4,128]{2,0,1:T(8,128)(2,1)}, u32[]{:S(2)}, u32[]{:S(2)}) collective-permute-start(bf16[256,4,128]{2,0,1:T(8,128)(2,1)} %bitcast.11), channel_id=1, source_target_pairs={{0,2},{1,3},{2,0},{3,1},{4,6},{5,7},{6,4},{7,5},{8,10},{9,11},{10,... | collective-permute-start | bytes 786440 | tf_op jit(solution)/shard_map/ppermute | solution.py:14
  13.7 1.7 %multiply_reduce_fusion.2 = (f32[256]{0:T(256)S(1)}, f32[256,1024]{1,0:T(8,128)}) fusion(bf16[256,1024]{1,0:T(8,128)(2,1)S(1)} %copy-done.3, bf16[1024,1024]{1,0:T(8,128)(2,1)S(1)} %copy-done), kind=kOutput, calls=%fused_computation.13 | convolution fusion | flops 537394944 | bytes 3671040 | tf_op jit(solution)/shard_map/dot_general | solution.py:113
  16.9 2.5 %compare_select_fusion.3 = s32[256,1]{0,1:T(1,128)S(1)} fusion(s32[]{:T(128)} %bitcast.33, s32[]{:T(128)} %bitcast.34, s32[]{:T(128)} %bitcast.36, s32[]{:T(128)} %bitcast.35, s32[]{:T(128)} %bitcast.94), kind=kLoop, calls=%fused_computation.71 | loop fusion | flops 9472 | bytes 1044 | tf_op jit(solution)/shard_map/jit(_take)/gather | solution.py:164
  21.2 2.1 %multiply_reduce_fusion.3 = (f32[16]{0:T(128)S(1)}, f32[16,1024]{1,0:T(8,128)S(1)}) fusion(bf16[16,1024]{1,0:T(8,128)(2,1)S(1)} %copy-done.5, bf16[1024,1024]{1,0:T(8,128)(2,1)} %param.11), kind=kOutput, calls=%fused_computation.67 | convolution fusion | flops 33587184 | bytes 2195520 | tf_op jit(solution)/shard_map/dot_general | solution.py:106
  23.3 7.0 %collective-permute-done.3 = bf16[3,64,1024]{2,1,0:T(8,128)(2,1)S(1)} collective-permute-done((bf16[3,64,1024]{2,1,0:T(8,128)(2,1)S(1)}, bf16[3,64,1024]{2,1,0:T(8,128)(2,1)S(1)}, u32[]{:S(2)}, u32[]{:S(2)}) %collective-permute-start.3) | collective-permute-done | bytes 393248 | tf_op jit(solution)/shard_map/ppermute | solution.py:14
  31.0 1.8 %collective-permute-done.4 = bf16[2,3,64,1024]{3,2,1,0:T(8,128)(2,1)S(1)} collective-permute-done((bf16[2,3,64,1024]{3,2,1,0:T(8,128)(2,1)S(1)}, bf16[2,3,64,1024]{3,2,1,0:T(8,128)(2,1)S(1)}, u32[]{:S(2)}, u32[]{:S(2)}) %collective-permute-start.4) | collective-permute-done | bytes 786464 | tf_op jit(solution)/shard_map/ppermute | solution.py:14
  38.3 2.1 %collective-permute-start.16 = (bf16[16,1024]{1,0:T(8,128)(2,1)S(1)}, bf16[16,1024]{1,0:T(8,128)(2,1)S(1)}, u32[]{:S(2)}, u32[]{:S(2)}) collective-permute-start(bf16[16,1024]{1,0:T(8,128)(2,1)S(1)} %multiply_convert_fusion.2), channel_id=1, source_target_pairs={{0,4},{4,8},{8,12},{12,0},{1,5},{5,9},{9,13},{13,1},{2,6},{6,10},{... | collective-permute-start | bytes 98312 | tf_op jit(solution)/shard_map/ppermute | solution.py:10
  41.0 1.8 %collective-permute-start.18 = (bf16[16,1024]{1,0:T(8,128)(2,1)S(1)}, bf16[16,1024]{1,0:T(8,128)(2,1)S(1)}, u32[]{:S(2)}, u32[]{:S(2)}) collective-permute-start(bf16[16,1024]{1,0:T(8,128)(2,1)S(1)} %multiply_convert_fusion.2), channel_id=1, source_target_pairs={{0,12},{4,0},{8,4},{12,8},{1,13},{5,1},{9,5},{13,9},{2,14},{6,2},{... | collective-permute-start | bytes 98312 | tf_op jit(solution)/shard_map/ppermute | solution.py:10
  43.6 1.5 %collective-permute-start.6 = (bf16[256,512]{1,0:T(8,128)(2,1)}, bf16[256,512]{1,0:T(8,128)(2,1)}, u32[]{:S(2)}, u32[]{:S(2)}) collective-permute-start(bf16[256,512]{1,0:T(8,128)(2,1)} %get-tuple-element.26), channel_id=1, source_target_pairs={{0,2},{1,3},{2,0},{3,1},{4,6},{5,7},{6,4},{7,5},{8,10},{9,11},{10,... | collective-permute-start | bytes 786440 | tf_op jit(solution)/shard_map/ppermute | solution.py:14
  46.2 1.2 %collective-permute-start.19 = (bf16[4,16,1024]{2,1,0:T(8,128)(2,1)}, bf16[4,16,1024]{2,1,0:T(8,128)(2,1)}, u32[]{:S(2)}, u32[]{:S(2)}) collective-permute-start(bf16[4,16,1024]{2,1,0:T(8,128)(2,1)} %get-tuple-element.35), channel_id=1, source_target_pairs={{0,2},{1,3},{2,0},{3,1},{4,6},{5,7},{6,4},{7,5},{8,10},{9,11},{10,... | collective-permute-start | bytes 393224 | tf_op jit(solution)/shard_map/ppermute | solution.py:14
  48.7 5.8 %collective-permute-done.19 = bf16[4,16,1024]{2,1,0:T(8,128)(2,1)} collective-permute-done((bf16[4,16,1024]{2,1,0:T(8,128)(2,1)}, bf16[4,16,1024]{2,1,0:T(8,128)(2,1)}, u32[]{:S(2)}, u32[]{:S(2)}) %collective-permute-start.19) | collective-permute-done | bytes 131104 | tf_op jit(solution)/shard_map/ppermute | solution.py:14
  55.5 1.6 %collective-permute-start.11 = (bf16[256,512]{1,0:T(8,128)(2,1)S(1)}, bf16[256,512]{1,0:T(8,128)(2,1)S(1)}, u32[]{:S(2)}, u32[]{:S(2)}) collective-permute-start(bf16[256,512]{1,0:T(8,128)(2,1)S(1)} %get-tuple-element.7), channel_id=1, source_target_pairs={{0,2},{1,3},{2,0},{3,1},{4,6},{5,7},{6,4},{7,5},{8,10},{9,11},{10,... | collective-permute-start | bytes 786440 | tf_op jit(solution)/shard_map/ppermute | solution.py:14
  57.1 1.5 %fusion.8 = f32[4,2,64,512]{3,2,1,0:T(8,128)S(1)} fusion(bf16[4,2,64,512]{3,2,1,0:T(8,128)(2,1)S(1)} %bitcast.99, bf16[256,512]{1,0:T(8,128)(2,1)} %collective-permute-done.6, bf16[256,512]{1,0:T(8,128)(2,1)} %get-tuple-element.26), kind=kOutput, calls=%fused_computation.23 | convolution fusion | flops 269484032 | bytes 2097152 | tf_op jit(solution)/shard_map/dot_general | solution.py:69
  58.9 5.3 %collective-permute-done.11 = bf16[256,512]{1,0:T(8,128)(2,1)S(1)} collective-permute-done((bf16[256,512]{1,0:T(8,128)(2,1)S(1)}, bf16[256,512]{1,0:T(8,128)(2,1)S(1)}, u32[]{:S(2)}, u32[]{:S(2)}) %collective-permute-start.11) | collective-permute-done | bytes 262176 | tf_op jit(solution)/shard_map/ppermute | solution.py:14
  66.1 1.7 %collective-permute-start.10 = (f32[64,512]{1,0:T(8,128)S(1)}, f32[64,512]{1,0:T(8,128)S(1)}, u32[]{:S(2)}, u32[]{:S(2)}) collective-permute-start(f32[64,512]{1,0:T(8,128)S(1)} %get-tuple-element.21), channel_id=1, source_target_pairs={{0,12},{4,0},{8,4},{12,8},{1,13},{5,1},{9,5},{13,9},{2,14},{6,2},{... | collective-permute-start | bytes 393224 | tf_op jit(solution)/shard_map/ppermute | solution.py:10
  69.4 3.0 %collective-permute-start.13 = (f32[64,512]{1,0:T(8,128)S(1)}, f32[64,512]{1,0:T(8,128)S(1)}, u32[]{:S(2)}, u32[]{:S(2)}) collective-permute-start(f32[64,512]{1,0:T(8,128)S(1)} %get-tuple-element.23), channel_id=1, source_target_pairs={{0,4},{4,8},{8,12},{12,0},{1,5},{5,9},{9,13},{13,1},{2,6},{6,10},{... | collective-permute-start | bytes 393224 | tf_op jit(solution)/shard_map/ppermute | solution.py:10
  72.4 3.8 %collective-permute-done.10 = f32[64,512]{1,0:T(8,128)S(1)} collective-permute-done((f32[64,512]{1,0:T(8,128)S(1)}, f32[64,512]{1,0:T(8,128)S(1)}, u32[]{:S(2)}, u32[]{:S(2)}) %collective-permute-start.10) | collective-permute-done | bytes 131104 | tf_op jit(solution)/shard_map/ppermute | solution.py:10
  76.2 10.4 %collective-permute-done.9 = f32[64,512]{1,0:T(8,128)S(1)} collective-permute-done((f32[64,512]{1,0:T(8,128)S(1)}, f32[64,512]{1,0:T(8,128)S(1)}, u32[]{:S(2)}, u32[]{:S(2)}) %collective-permute-start.9) | collective-permute-done | bytes 131104 | tf_op jit(solution)/shard_map/ppermute | solution.py:10
  86.6 2.8 %collective-permute-done.14 = f32[64,512]{1,0:T(8,128)S(1)} collective-permute-done((f32[64,512]{1,0:T(8,128)S(1)}, f32[64,512]{1,0:T(8,128)S(1)}, u32[]{:S(2)}, u32[]{:S(2)}) %collective-permute-start.14) | collective-permute-done | bytes 131104 | tf_op jit(solution)/shard_map/ppermute | solution.py:10
  (84 shorter events, 19.4 us)
Async XLA Ops:
  0.6 13.1 %copy-start = (bf16[1024,1024]{1,0:T(8,128)(2,1)S(1)}, bf16[1024,1024]{1,0:T(8,128)(2,1)}, u32[]{:S(2)}) copy-start(bf16[1024,1024]{1,0:T(8,128)(2,1)} %param.10) | copy-start | bytes 6291460
  0.6 13.1 %copy-start.3 = (bf16[256,1024]{1,0:T(8,128)(2,1)S(1)}, bf16[256,1024]{1,0:T(8,128)(2,1)}, u32[]{:S(2)}) copy-start(bf16[256,1024]{1,0:T(8,128)(2,1)} %param.8) | copy-start | bytes 1572868
  2.4 17.1 %collective-permute-start = (bf16[64,1024]{1,0:T(8,128)(2,1)}, bf16[64,1024]{1,0:T(8,128)(2,1)S(1)}, u32[]{:S(2)}, u32[]{:S(2)}) collective-permute-start(bf16[64,1024]{1,0:T(8,128)(2,1)} %constant_dynamic-slice_fusion.2), channel_id=1, source_target_pairs={{0,4},{4,8},{8,12},{12,0},{1,5},{5,9},{9,13},{13,1},{2,6},{6,10},{... | collective-permute-start | bytes 393224 | tf_op jit(solution)/shard_map/ppermute | solution.py:10
  5.4 14.0 %collective-permute-start.1 = (bf16[64,1024]{1,0:T(8,128)(2,1)}, bf16[64,1024]{1,0:T(8,128)(2,1)}, u32[]{:S(2)}, u32[]{:S(2)}) collective-permute-start(bf16[64,1024]{1,0:T(8,128)(2,1)} %constant_dynamic-slice_fusion.2), channel_id=1, source_target_pairs={{0,8},{4,12},{8,0},{12,4},{1,9},{5,13},{9,1},{13,5},{2,10},{6,14},... | collective-permute-start | bytes 393224 | tf_op jit(solution)/shard_map/ppermute | solution.py:10
  8.0 11.5 %collective-permute-start.2 = (bf16[64,1024]{1,0:T(8,128)(2,1)}, bf16[64,1024]{1,0:T(8,128)(2,1)}, u32[]{:S(2)}, u32[]{:S(2)}) collective-permute-start(bf16[64,1024]{1,0:T(8,128)(2,1)} %constant_dynamic-slice_fusion.2), channel_id=1, source_target_pairs={{0,12},{4,0},{8,4},{12,8},{1,13},{5,1},{9,5},{13,9},{2,14},{6,2},{... | collective-permute-start | bytes 393224 | tf_op jit(solution)/shard_map/ppermute | solution.py:10
  12.2 35.3 %collective-permute-start.5 = (bf16[256,4,128]{2,0,1:T(8,128)(2,1)}, bf16[256,4,128]{2,0,1:T(8,128)(2,1)}, u32[]{:S(2)}, u32[]{:S(2)}) collective-permute-start(bf16[256,4,128]{2,0,1:T(8,128)(2,1)} %bitcast.11), channel_id=1, source_target_pairs={{0,2},{1,3},{2,0},{3,1},{4,6},{5,7},{6,4},{7,5},{8,10},{9,11},{10,... | collective-permute-start | bytes 786440 | tf_op jit(solution)/shard_map/ppermute | solution.py:14
  20.5 9.8 %collective-permute-start.3 = (bf16[3,64,1024]{2,1,0:T(8,128)(2,1)S(1)}, bf16[3,64,1024]{2,1,0:T(8,128)(2,1)S(1)}, u32[]{:S(2)}, u32[]{:S(2)}) collective-permute-start(bf16[3,64,1024]{2,1,0:T(8,128)(2,1)S(1)} %get-tuple-element.31), channel_id=1, source_target_pairs={{0,2},{1,3},{2,0},{3,1},{4,6},{5,7},{6,4},{7,5},{8,10},{9,11},{10,... | collective-permute-start | bytes 1179656 | tf_op jit(solution)/shard_map/ppermute | solution.py:14
  30.4 2.4 %collective-permute-start.4 = (bf16[2,3,64,1024]{3,2,1,0:T(8,128)(2,1)S(1)}, bf16[2,3,64,1024]{3,2,1,0:T(8,128)(2,1)S(1)}, u32[]{:S(2)}, u32[]{:S(2)}) collective-permute-start(bf16[2,3,64,1024]{3,2,1,0:T(8,128)(2,1)S(1)} %get-tuple-element.19), channel_id=1, source_target_pairs={{0,1},{1,0},{2,3},{3,2},{4,5},{5,4},{6,7},{7,6},{8,9},{9,8},{10,11... | collective-permute-start | bytes 2359304 | tf_op jit(solution)/shard_map/ppermute | solution.py:14
  38.3 10.4 %copy-start.4 = (bf16[256,4,1,128]{0,3,2,1:T(8,128)(2,1)S(1)}, bf16[256,4,1,128]{0,3,2,1:T(8,128)(2,1)}, u32[]{:S(2)}) copy-start(bf16[256,4,1,128]{0,3,2,1:T(8,128)(2,1)} %get-tuple-element.28) | copy-start | bytes 786436
  38.3 6.8 %collective-permute-start.16 = (bf16[16,1024]{1,0:T(8,128)(2,1)S(1)}, bf16[16,1024]{1,0:T(8,128)(2,1)S(1)}, u32[]{:S(2)}, u32[]{:S(2)}) collective-permute-start(bf16[16,1024]{1,0:T(8,128)(2,1)S(1)} %multiply_convert_fusion.2), channel_id=1, source_target_pairs={{0,4},{4,8},{8,12},{12,0},{1,5},{5,9},{9,13},{13,1},{2,6},{6,10},{... | collective-permute-start | bytes 98312 | tf_op jit(solution)/shard_map/ppermute | solution.py:10
  40.4 5.2 %collective-permute-start.17 = (bf16[16,1024]{1,0:T(8,128)(2,1)S(1)}, bf16[16,1024]{1,0:T(8,128)(2,1)S(1)}, u32[]{:S(2)}, u32[]{:S(2)}) collective-permute-start(bf16[16,1024]{1,0:T(8,128)(2,1)S(1)} %multiply_convert_fusion.2), channel_id=1, source_target_pairs={{0,8},{4,12},{8,0},{12,4},{1,9},{5,13},{9,1},{13,5},{2,10},{6,14},... | collective-permute-start | bytes 98312 | tf_op jit(solution)/shard_map/ppermute | solution.py:10
  41.0 4.6 %collective-permute-start.18 = (bf16[16,1024]{1,0:T(8,128)(2,1)S(1)}, bf16[16,1024]{1,0:T(8,128)(2,1)S(1)}, u32[]{:S(2)}, u32[]{:S(2)}) collective-permute-start(bf16[16,1024]{1,0:T(8,128)(2,1)S(1)} %multiply_convert_fusion.2), channel_id=1, source_target_pairs={{0,12},{4,0},{8,4},{12,8},{1,13},{5,1},{9,5},{13,9},{2,14},{6,2},{... | collective-permute-start | bytes 98312 | tf_op jit(solution)/shard_map/ppermute | solution.py:10
  43.6 11.9 %collective-permute-start.6 = (bf16[256,512]{1,0:T(8,128)(2,1)}, bf16[256,512]{1,0:T(8,128)(2,1)}, u32[]{:S(2)}, u32[]{:S(2)}) collective-permute-start(bf16[256,512]{1,0:T(8,128)(2,1)} %get-tuple-element.26), channel_id=1, source_target_pairs={{0,2},{1,3},{2,0},{3,1},{4,6},{5,7},{6,4},{7,5},{8,10},{9,11},{10,... | collective-permute-start | bytes 786440 | tf_op jit(solution)/shard_map/ppermute | solution.py:14
  46.2 8.2 %collective-permute-start.19 = (bf16[4,16,1024]{2,1,0:T(8,128)(2,1)}, bf16[4,16,1024]{2,1,0:T(8,128)(2,1)}, u32[]{:S(2)}, u32[]{:S(2)}) collective-permute-start(bf16[4,16,1024]{2,1,0:T(8,128)(2,1)} %get-tuple-element.35), channel_id=1, source_target_pairs={{0,2},{1,3},{2,0},{3,1},{4,6},{5,7},{6,4},{7,5},{8,10},{9,11},{10,... | collective-permute-start | bytes 393224 | tf_op jit(solution)/shard_map/ppermute | solution.py:14
  55.4 3.4 %collective-permute-start.20 = (bf16[2,4,16,1024]{3,2,1,0:T(8,128)(2,1)S(1)}, bf16[2,4,16,1024]{3,2,1,0:T(8,128)(2,1)S(1)}, u32[]{:S(2)}, u32[]{:S(2)}) collective-permute-start(bf16[2,4,16,1024]{3,2,1,0:T(8,128)(2,1)S(1)} %get-tuple-element.33), channel_id=1, source_target_pairs={{0,1},{1,0},{2,3},{3,2},{4,5},{5,4},{6,7},{7,6},{8,9},{9,8},{10,11... | collective-permute-start | bytes 786440 | tf_op jit(solution)/shard_map/ppermute | solution.py:14
  55.5 8.7 %collective-permute-start.11 = (bf16[256,512]{1,0:T(8,128)(2,1)S(1)}, bf16[256,512]{1,0:T(8,128)(2,1)S(1)}, u32[]{:S(2)}, u32[]{:S(2)}) collective-permute-start(bf16[256,512]{1,0:T(8,128)(2,1)S(1)} %get-tuple-element.7), channel_id=1, source_target_pairs={{0,2},{1,3},{2,0},{3,1},{4,6},{5,7},{6,4},{7,5},{8,10},{9,11},{10,... | collective-permute-start | bytes 786440 | tf_op jit(solution)/shard_map/ppermute | solution.py:14
  58.6 7.3 %collective-permute-start.7 = (f32[4,64,512]{2,1,0:T(8,128)S(1)}, f32[4,64,512]{2,1,0:T(8,128)S(1)}, u32[]{:S(2)}, u32[]{:S(2)}) collective-permute-start(f32[4,64,512]{2,1,0:T(8,128)S(1)} %dynamic-slice_bitcast_fusion.1), channel_id=1, source_target_pairs={{0,1},{1,0},{2,3},{3,2},{4,5},{5,4},{6,7},{7,6},{8,9},{9,8},{10,11... | collective-permute-start | bytes 1572872 | tf_op jit(solution)/shard_map/ppermute | solution.py:14
  64.7 4.5 %collective-permute-start.12 = (f32[4,64,512]{2,1,0:T(8,128)S(1)}, f32[4,64,512]{2,1,0:T(8,128)S(1)}, u32[]{:S(2)}, u32[]{:S(2)}) collective-permute-start(f32[4,64,512]{2,1,0:T(8,128)S(1)} %dynamic-slice_bitcast_fusion), channel_id=1, source_target_pairs={{0,1},{1,0},{2,3},{3,2},{4,5},{5,4},{6,7},{7,6},{8,9},{9,8},{10,11... | collective-permute-start | bytes 1572872 | tf_op jit(solution)/shard_map/ppermute | solution.py:14
  66.1 10.1 %collective-permute-start.10 = (f32[64,512]{1,0:T(8,128)S(1)}, f32[64,512]{1,0:T(8,128)S(1)}, u32[]{:S(2)}, u32[]{:S(2)}) collective-permute-start(f32[64,512]{1,0:T(8,128)S(1)} %get-tuple-element.21), channel_id=1, source_target_pairs={{0,12},{4,0},{8,4},{12,8},{1,13},{5,1},{9,5},{13,9},{2,14},{6,2},{... | collective-permute-start | bytes 393224 | tf_op jit(solution)/shard_map/ppermute | solution.py:10
  67.8 8.4 %collective-permute-start.8 = (f32[64,512]{1,0:T(8,128)S(1)}, f32[64,512]{1,0:T(8,128)S(1)}, u32[]{:S(2)}, u32[]{:S(2)}) collective-permute-start(f32[64,512]{1,0:T(8,128)S(1)} %get-tuple-element.20), channel_id=1, source_target_pairs={{0,4},{4,8},{8,12},{12,0},{1,5},{5,9},{9,13},{13,1},{2,6},{6,10},{... | collective-permute-start | bytes 393224 | tf_op jit(solution)/shard_map/ppermute | solution.py:10
  68.1 18.4 %collective-permute-start.9 = (f32[64,512]{1,0:T(8,128)S(1)}, f32[64,512]{1,0:T(8,128)S(1)}, u32[]{:S(2)}, u32[]{:S(2)}) collective-permute-start(f32[64,512]{1,0:T(8,128)S(1)} %get-tuple-element.22), channel_id=1, source_target_pairs={{0,8},{4,12},{8,0},{12,4},{1,9},{5,13},{9,1},{13,5},{2,10},{6,14},... | collective-permute-start | bytes 393224 | tf_op jit(solution)/shard_map/ppermute | solution.py:10
  69.4 17.3 %collective-permute-start.13 = (f32[64,512]{1,0:T(8,128)S(1)}, f32[64,512]{1,0:T(8,128)S(1)}, u32[]{:S(2)}, u32[]{:S(2)}) collective-permute-start(f32[64,512]{1,0:T(8,128)S(1)} %get-tuple-element.23), channel_id=1, source_target_pairs={{0,4},{4,8},{8,12},{12,0},{1,5},{5,9},{9,13},{13,1},{2,6},{6,10},{... | collective-permute-start | bytes 393224 | tf_op jit(solution)/shard_map/ppermute | solution.py:10
  72.4 17.0 %collective-permute-start.14 = (f32[64,512]{1,0:T(8,128)S(1)}, f32[64,512]{1,0:T(8,128)S(1)}, u32[]{:S(2)}, u32[]{:S(2)}) collective-permute-start(f32[64,512]{1,0:T(8,128)S(1)} %get-tuple-element.25), channel_id=1, source_target_pairs={{0,8},{4,12},{8,0},{12,4},{1,9},{5,13},{9,1},{13,5},{2,10},{6,14},... | collective-permute-start | bytes 393224 | tf_op jit(solution)/shard_map/ppermute | solution.py:10
  76.2 13.2 %collective-permute-start.15 = (f32[64,512]{1,0:T(8,128)S(1)}, f32[64,512]{1,0:T(8,128)S(1)}, u32[]{:S(2)}, u32[]{:S(2)}) collective-permute-start(f32[64,512]{1,0:T(8,128)S(1)} %get-tuple-element.24), channel_id=1, source_target_pairs={{0,12},{4,0},{8,4},{12,8},{1,13},{5,1},{9,5},{13,9},{2,14},{6,2},{... | collective-permute-start | bytes 393224 | tf_op jit(solution)/shard_map/ppermute | solution.py:10
  (5 other events, 19.5 us)

commit v10 on v7

--- a/solution.py
+++ b/solution.py
@@ -99,10 +99,7 @@
     piece_rows = k_dev // n_dp
     far_rows = (n_q - 1) * piece_rows
 
-    fresh = jnp.dot(key_inputs, key_weight, preferred_element_type=jnp.float32)
-    fresh = (fresh * lax.rsqrt(jnp.sum(fresh * fresh, -1, keepdims=True) + 1e-06)).astype(
-        jnp.bfloat16
-    )
+    blocks = gather_blocks(key_inputs, n_q, n_dp)
     remote = gather_queue(queue_keys, n_q, n_dp)
     rows0 = far_rows
 
@@ -146,9 +143,7 @@
     grad_query = (
         (grad_unit - unit_f * jnp.sum(unit_f * grad_unit, -1, keepdims=True)) * inv_len
     ).astype(jnp.bfloat16)
-    fresh, grad_query = lax.optimization_barrier((fresh, grad_query))
     grad_rows = reduce_scatter_grad(query_inputs, grad_query, n_q, n_dp)
-    blocks = gather_blocks(fresh, n_q, n_dp)
 
     n_blocks = slot_owner.shape[0]
     slots_here = q * n_dp + jnp.arange(n_dp, dtype=jnp.int32)
@@ -162,8 +157,12 @@
     b_s = (q - b // n_dp) % n_q
     source = (b_e * n_q + b_s) * new_dev + offset % new_dev
     pick_new = (source[:, None] == jnp.arange(blocks.shape[0])[None, :]).astype(jnp.bfloat16)
-    placed = jnp.dot(pick_new, blocks, preferred_element_type=jnp.float32).astype(jnp.bfloat16)
-    new_queue = jnp.where(live[:, None], placed, queue_keys)
+    key_rows = jnp.dot(pick_new, blocks, preferred_element_type=jnp.float32).astype(jnp.bfloat16)
+    fresh = jnp.dot(key_rows, key_weight, preferred_element_type=jnp.float32)
+    fresh = (fresh * lax.rsqrt(jnp.sum(fresh * fresh, -1, keepdims=True) + 1e-06)).astype(
+        jnp.bfloat16
+    )
+    new_queue = jnp.where(live[:, None], fresh, queue_keys)
     return (loss, grad_rows, new_queue)
 
 

time: 86.4 us -> 94.7 us (1.096)
  other arithmetic: 8 us -> 16.3 us
  waiting for transfers between devices: 33.7 us -> 30.9 us
  matrix products: 10.3 us -> 12.7 us
  starting transfers between devices: 24.1 us -> 25.8 us
  local copies, waits for them, and re-layouts: 8.28 us -> 6.85 us
    ppermute x12, waiting for transfers between devices: 17.5 us -> 14.6 us  [shift(): return lax.ppermute(x, axis, [(i, (i + step) % n) for i in range(n)])]
    another operation x3, other arithmetic: 1.28 us -> 3.92 us  [gather_queue(): payload = jnp.stack([payload, swap(payload, 'dp', n_dp, bit)], axis=t)]
    another operation x3, other arithmetic: 1.67 us -> 3.52 us  [gather_blocks(): got = jnp.stack([got, swap(got, 'dp', n_dp, bit)], axis=t)]
    ppermute x12, starting transfers between devices: 17.7 us -> 19.4 us  [shift(): return lax.ppermute(x, axis, [(i, (i + step) % n) for i in range(n)])]
    not x1, other arithmetic: 0.01 us -> 1.2 us  [body(): ~local]
    dot_general x1, matrix products: 1.71 us -> 2.74 us  [body(): jnp.dot(query_inputs, query_weight, preferred_element_type=jnp.float32)]
    select_n x0 -> x1, other arithmetic: none -> 1 us  [body(): new_queue = jnp.where(live[:, None], fresh, queue_keys)]
    dot_general x1, matrix products: 0.35 us -> 1.33 us  [body(): jnp.dot(pick_near, queue_keys, preferred_element_type=jnp.float32)]
  transfers between devices with their start and end apart: 21 -> 21, of which waited for: 8 -> 7; matrix products, arithmetic and copies ran while one was open for 27% -> 28% of each run, Pallas kernels for 0% -> 0%
where the time goes in v10:
time: 94.7 us; the launch traced here: 94.1 us
  waiting for transfers between devices  30.9 us (33%)
  starting transfers between devices  25.8 us (27%)
  other arithmetic  16.3 us (17%)
  matrix products  12.7 us (13%)
  local copies, waits for them, and re-layouts  6.85 us (7%)
  between operations  1.61 us (2%)
    ppermute x12, starting transfers between devices, shift(): return lax.ppermute(x, axis, [(i, (i + step) % n) for i in range(n)])  19.4 us
    ppermute x9, waiting for transfers between devices, swap(): return lax.ppermute(x, axis, [(i, i ^ bit) for i in range(n)])  16.2 us
    ppermute x12, waiting for transfers between devices, shift(): return lax.ppermute(x, axis, [(i, (i + step) % n) for i in range(n)])  14.6 us
    ppermute x9, starting transfers between devices, swap(): return lax.ppermute(x, axis, [(i, i ^ bit) for i in range(n)])  6.33 us
    another operation x3, other arithmetic, gather_queue(): payload = jnp.stack([payload, swap(payload, 'dp', n_dp, bit)], axis=t)  3.92 us
    dot_general x1, matrix products, body(): fresh = jnp.dot(key_rows, key_weight, preferred_element_type=jnp.float32)  3.65 us
    another operation x3, other arithmetic, gather_blocks(): got = jnp.stack([got, swap(got, 'dp', n_dp, bit)], axis=t)  3.52 us
    dot_general x1, matrix products, body(): jnp.dot(query_inputs, query_weight, preferred_element_type=jnp.float32)  2.74 us
  transfers between devices with their start and end apart: 21, of which 7 were waited for; matrix products, arithmetic and copies ran while one was open for 28% of the time, Pallas kernels for 0%

profile of v10, /device:TPU:0, one launch (start us, length us, event | category | flops | bytes accessed | tf_op | source)
XLA Modules:
  0.0 94.1 jit_solution(5556041368821778442)
XLA Ops:
  0.7 1.7 %constant_dynamic-slice_fusion.2 = bf16[64,1024]{1,0:T(8,128)(2,1)} fusion(bf16[256,1024]{1,0:T(8,128)(2,1)} %param.12, s32[]{:T(128)S(6)} %select_n.195), kind=kLoop, calls=%fused_computation.80 | loop fusion | bytes 262148 | tf_op jit(solution)/shard_map/dynamic_slice | solution.py:30
  2.4 3.1 %collective-permute-start = (bf16[64,1024]{1,0:T(8,128)(2,1)}, bf16[64,1024]{1,0:T(8,128)(2,1)S(1)}, u32[]{:S(2)}, u32[]{:S(2)}) collective-permute-start(bf16[64,1024]{1,0:T(8,128)(2,1)} %constant_dynamic-slice_fusion.2), channel_id=1, source_target_pairs={{0,4},{4,8},{8,12},{12,0},{1,5},{5,9},{9,13},{13,1},{2,6},{6,10},{... | collective-permute-start | bytes 393224 | tf_op jit(solution)/shard_map/ppermute | solution.py:10
  5.4 2.6 %collective-permute-start.1 = (bf16[64,1024]{1,0:T(8,128)(2,1)}, bf16[64,1024]{1,0:T(8,128)(2,1)}, u32[]{:S(2)}, u32[]{:S(2)}) collective-permute-start(bf16[64,1024]{1,0:T(8,128)(2,1)} %constant_dynamic-slice_fusion.2), channel_id=1, source_target_pairs={{0,8},{4,12},{8,0},{12,4},{1,9},{5,13},{9,1},{13,5},{2,10},{6,14},... | collective-permute-start | bytes 393224 | tf_op jit(solution)/shard_map/ppermute | solution.py:10
  8.0 1.3 %collective-permute-start.2 = (bf16[64,1024]{1,0:T(8,128)(2,1)}, bf16[64,1024]{1,0:T(8,128)(2,1)}, u32[]{:S(2)}, u32[]{:S(2)}) collective-permute-start(bf16[64,1024]{1,0:T(8,128)(2,1)} %constant_dynamic-slice_fusion.2), channel_id=1, source_target_pairs={{0,12},{4,0},{8,4},{12,8},{1,13},{5,1},{9,5},{13,9},{2,14},{6,2},{... | collective-permute-start | bytes 393224 | tf_op jit(solution)/shard_map/ppermute | solution.py:10
  13.5 2.7 %multiply_reduce_fusion.3 = (f32[256]{0:T(256)S(1)}, f32[256,1024]{1,0:T(8,128)}) fusion(bf16[256,1024]{1,0:T(8,128)(2,1)} %param.8, bf16[1024,1024]{1,0:T(8,128)(2,1)S(1)} %copy-done), kind=kOutput, calls=%fused_computation.15 | convolution fusion | flops 537394944 | bytes 3671040 | tf_op jit(solution)/shard_map/dot_general | solution.py:106
  17.4 1.3 %fusion.20 = f32[256,1024]{1,0:T(8,128)} fusion(bf16[256,1024]{1,0:T(8,128)(2,1)S(1)} %copy-done.1, s32[256]{0:T(256)S(1)} %get-tuple-element.11, pred[256]{0:T(512)(128)(4,1)S(1)} %get-tuple-element.8), kind=kOutput, calls=%fused_computation.48 | convolution fusion | flops 134348800 | bytes 1574144 | tf_op jit(solution)/shard_map/dot_general | solution.py:135
  18.8 2.9 %collective-permute-start.18 = (bf16[16,1024]{1,0:T(8,128)(2,1)S(1)}, bf16[16,1024]{1,0:T(8,128)(2,1)S(1)}, u32[]{:S(2)}, u32[]{:S(2)}) collective-permute-start(bf16[16,1024]{1,0:T(8,128)(2,1)S(1)} %copy-done.6), channel_id=1, source_target_pairs={{0,12},{4,0},{8,4},{12,8},{1,13},{5,1},{9,5},{13,9},{2,14},{6,2},{... | collective-permute-start | bytes 98312 | tf_op jit(solution)/shard_map/ppermute | solution.py:10
  21.6 1.5 %collective-permute-start.5 = (bf16[256,4,128]{2,0,1:T(8,128)(2,1)S(1)}, bf16[256,4,128]{2,0,1:T(8,128)(2,1)S(1)}, u32[]{:S(2)}, u32[]{:S(2)}) collective-permute-start(bf16[256,4,128]{2,0,1:T(8,128)(2,1)S(1)} %bitcast.107), channel_id=1, source_target_pairs={{0,2},{1,3},{2,0},{3,1},{4,6},{5,7},{6,4},{7,5},{8,10},{9,11},{10,... | collective-permute-start | bytes 786440 | tf_op jit(solution)/shard_map/ppermute | solution.py:14
  27.1 1.6 %collective-permute-start.19 = (bf16[4,16,1024]{2,1,0:T(8,128)(2,1)S(1)}, bf16[4,16,1024]{2,1,0:T(8,128)(2,1)S(1)}, u32[]{:S(2)}, u32[]{:S(2)}) collective-permute-start(bf16[4,16,1024]{2,1,0:T(8,128)(2,1)S(1)} %get-tuple-element.29), channel_id=1, source_target_pairs={{0,2},{1,3},{2,0},{3,1},{4,6},{5,7},{6,4},{7,5},{8,10},{9,11},{10,... | collective-permute-start | bytes 393224 | tf_op jit(solution)/shard_map/ppermute | solution.py:14
  28.6 9.5 %collective-permute-done.3 = bf16[3,64,1024]{2,1,0:T(8,128)(2,1)S(1)} collective-permute-done((bf16[3,64,1024]{2,1,0:T(8,128)(2,1)S(1)}, bf16[3,64,1024]{2,1,0:T(8,128)(2,1)S(1)}, u32[]{:S(2)}, u32[]{:S(2)}) %collective-permute-start.3) | collective-permute-done | bytes 393248 | tf_op jit(solution)/shard_map/ppermute | solution.py:14
  39.3 2.6 %compare_select_fusion.3 = s32[256,1]{0,1:T(1,128)S(1)} fusion(s32[]{:T(128)} %bitcast.33, s32[]{:T(128)} %bitcast.34, s32[]{:T(128)} %bitcast.36, s32[]{:T(128)} %bitcast.35, s32[]{:T(128)} %bitcast.95), kind=kLoop, calls=%fused_computation.72 | loop fusion | flops 9472 | bytes 1044 | tf_op jit(solution)/shard_map/jit(_take)/gather | solution.py:155
  45.3 1.9 %pad_maximum_fusion.3 = bf16[2,2,4,16,1024]{4,3,2,1,0:T(8,128)(2,1)} fusion(bf16[2,1,4,16,1024]{4,3,2,1,0:T(8,128)(2,1)} %bitcast.46, bf16[2,1,4,16,1024]{4,3,2,1,0:T(8,128)(2,1)} %get-tuple-element.26), kind=kLoop, calls=%fused_computation.33 | loop fusion | flops 262144 | bytes 1048576 | tf_op jit(solution)/shard_map/stack | solution.py:40
  47.2 1.7 %pad_maximum_fusion = bf16[2,2,3,64,1024]{4,3,2,1,0:T(8,128)(2,1)S(1)} fusion(bf16[2,1,3,64,1024]{4,3,2,1,0:T(8,128)(2,1)} %bitcast.7, bf16[2,1,3,64,1024]{4,3,2,1,0:T(8,128)(2,1)} %get-tuple-element.12), kind=kLoop, calls=%fused_computation | loop fusion | flops 786432 | bytes 3145728 | tf_op jit(solution)/shard_map/stack | solution.py:33
  54.2 1.5 %collective-permute-start.6 = (bf16[256,512]{1,0:T(8,128)(2,1)}, bf16[256,512]{1,0:T(8,128)(2,1)}, u32[]{:S(2)}, u32[]{:S(2)}) collective-permute-start(bf16[256,512]{1,0:T(8,128)(2,1)} %get-tuple-element.17), channel_id=1, source_target_pairs={{0,2},{1,3},{2,0},{3,1},{4,6},{5,7},{6,4},{7,5},{8,10},{9,11},{10,... | collective-permute-start | bytes 786440 | tf_op jit(solution)/shard_map/ppermute | solution.py:14
  55.7 3.6 %multiply_reduce_fusion = (f32[256]{0:T(256)S(1)}, f32[256,1024]{1,0:T(8,128)}) fusion(bf16[1024,1024]{1,0:T(8,128)(2,1)} %param.11, bf16[256,1024]{1,0:T(8,128)(2,1)} %bitcast.105, s32[256]{0:T(256)S(1)} %fusion.41), kind=kOutput, calls=%fused_computation.11 | convolution fusion | flops 671940352 | bytes 3672064 | tf_op jit(solution)/shard_map/dot_general | solution.py:161
  59.9 3.8 %collective-permute-done.6 = bf16[256,512]{1,0:T(8,128)(2,1)} collective-permute-done((bf16[256,512]{1,0:T(8,128)(2,1)}, bf16[256,512]{1,0:T(8,128)(2,1)}, u32[]{:S(2)}, u32[]{:S(2)}) %collective-permute-start.6) | collective-permute-done | bytes 262176 | tf_op jit(solution)/shard_map/ppermute | solution.py:14
  63.7 1.5 %fusion.9 = f32[4,2,64,512]{3,2,1,0:T(8,128)S(1)} fusion(bf16[4,2,64,512]{3,2,1,0:T(8,128)(2,1)S(1)} %bitcast.100, bf16[256,512]{1,0:T(8,128)(2,1)} %collective-permute-done.6, bf16[256,512]{1,0:T(8,128)(2,1)} %get-tuple-element.17), kind=kOutput, calls=%fused_computation.26 | convolution fusion | flops 269484032 | bytes 2097152 | tf_op jit(solution)/shard_map/dot_general | solution.py:65
  65.3 3.0 %collective-permute-done.11 = bf16[256,512]{1,0:T(8,128)(2,1)S(1)} collective-permute-done((bf16[256,512]{1,0:T(8,128)(2,1)S(1)}, bf16[256,512]{1,0:T(8,128)(2,1)S(1)}, u32[]{:S(2)}, u32[]{:S(2)}) %collective-permute-start.11) | collective-permute-done | bytes 262176 | tf_op jit(solution)/shard_map/ppermute | solution.py:14
  72.0 1.7 %collective-permute-start.9 = (f32[64,512]{1,0:T(8,128)S(1)}, f32[64,512]{1,0:T(8,128)S(1)}, u32[]{:S(2)}, u32[]{:S(2)}) collective-permute-start(f32[64,512]{1,0:T(8,128)S(1)} %get-tuple-element.16), channel_id=1, source_target_pairs={{0,8},{4,12},{8,0},{12,4},{1,9},{5,13},{9,1},{13,5},{2,10},{6,14},... | collective-permute-start | bytes 393224 | tf_op jit(solution)/shard_map/ppermute | solution.py:10
  73.9 1.6 %collective-permute-start.13 = (f32[64,512]{1,0:T(8,128)S(1)}, f32[64,512]{1,0:T(8,128)S(1)}, u32[]{:S(2)}, u32[]{:S(2)}) collective-permute-start(f32[64,512]{1,0:T(8,128)S(1)} %get-tuple-element.19), channel_id=1, source_target_pairs={{0,4},{4,8},{8,12},{12,0},{1,5},{5,9},{9,13},{13,1},{2,6},{6,10},{... | collective-permute-start | bytes 393224 | tf_op jit(solution)/shard_map/ppermute | solution.py:10
  76.3 2.9 %collective-permute-start.15 = (f32[64,512]{1,0:T(8,128)S(1)}, f32[64,512]{1,0:T(8,128)S(1)}, u32[]{:S(2)}, u32[]{:S(2)}) collective-permute-start(f32[64,512]{1,0:T(8,128)S(1)} %get-tuple-element.20), channel_id=1, source_target_pairs={{0,12},{4,0},{8,4},{12,8},{1,13},{5,1},{9,5},{13,9},{2,14},{6,2},{... | collective-permute-start | bytes 393224 | tf_op jit(solution)/shard_map/ppermute | solution.py:10
  79.2 1.3 %collective-permute-done.8 = f32[64,512]{1,0:T(8,128)S(1)} collective-permute-done((f32[64,512]{1,0:T(8,128)S(1)}, f32[64,512]{1,0:T(8,128)S(1)}, u32[]{:S(2)}, u32[]{:S(2)}) %collective-permute-start.8) | collective-permute-done | bytes 131104 | tf_op jit(solution)/shard_map/ppermute | solution.py:10
  80.5 10.1 %collective-permute-done.9 = f32[64,512]{1,0:T(8,128)S(1)} collective-permute-done((f32[64,512]{1,0:T(8,128)S(1)}, f32[64,512]{1,0:T(8,128)S(1)}, u32[]{:S(2)}, u32[]{:S(2)}) %collective-permute-start.9) | collective-permute-done | bytes 131104 | tf_op jit(solution)/shard_map/ppermute | solution.py:10
  90.6 2.8 %collective-permute-done.14 = f32[64,512]{1,0:T(8,128)S(1)} collective-permute-done((f32[64,512]{1,0:T(8,128)S(1)}, f32[64,512]{1,0:T(8,128)S(1)}, u32[]{:S(2)}, u32[]{:S(2)}) %collective-permute-start.14) | collective-permute-done | bytes 131104 | tf_op jit(solution)/shard_map/ppermute | solution.py:10
  (84 shorter events, 24.5 us)
Async XLA Ops:
  0.6 12.9 %copy-start = (bf16[1024,1024]{1,0:T(8,128)(2,1)S(1)}, bf16[1024,1024]{1,0:T(8,128)(2,1)}, u32[]{:S(2)}) copy-start(bf16[1024,1024]{1,0:T(8,128)(2,1)} %param.10) | copy-start | bytes 6291460
  2.4 16.4 %collective-permute-start = (bf16[64,1024]{1,0:T(8,128)(2,1)}, bf16[64,1024]{1,0:T(8,128)(2,1)S(1)}, u32[]{:S(2)}, u32[]{:S(2)}) collective-permute-start(bf16[64,1024]{1,0:T(8,128)(2,1)} %constant_dynamic-slice_fusion.2), channel_id=1, source_target_pairs={{0,4},{4,8},{8,12},{12,0},{1,5},{5,9},{9,13},{13,1},{2,6},{6,10},{... | collective-permute-start | bytes 393224 | tf_op jit(solution)/shard_map/ppermute | solution.py:10
  5.4 16.2 %collective-permute-start.1 = (bf16[64,1024]{1,0:T(8,128)(2,1)}, bf16[64,1024]{1,0:T(8,128)(2,1)}, u32[]{:S(2)}, u32[]{:S(2)}) collective-permute-start(bf16[64,1024]{1,0:T(8,128)(2,1)} %constant_dynamic-slice_fusion.2), channel_id=1, source_target_pairs={{0,8},{4,12},{8,0},{12,4},{1,9},{5,13},{9,1},{13,5},{2,10},{6,14},... | collective-permute-start | bytes 393224 | tf_op jit(solution)/shard_map/ppermute | solution.py:10
  8.0 15.1 %collective-permute-start.2 = (bf16[64,1024]{1,0:T(8,128)(2,1)}, bf16[64,1024]{1,0:T(8,128)(2,1)}, u32[]{:S(2)}, u32[]{:S(2)}) collective-permute-start(bf16[64,1024]{1,0:T(8,128)(2,1)} %constant_dynamic-slice_fusion.2), channel_id=1, source_target_pairs={{0,12},{4,0},{8,4},{12,8},{1,13},{5,1},{9,5},{13,9},{2,14},{6,2},{... | collective-permute-start | bytes 393224 | tf_op jit(solution)/shard_map/ppermute | solution.py:10
  9.4 16.9 %collective-permute-start.16 = (bf16[16,1024]{1,0:T(8,128)(2,1)}, bf16[16,1024]{1,0:T(8,128)(2,1)}, u32[]{:S(2)}, u32[]{:S(2)}) collective-permute-start(bf16[16,1024]{1,0:T(8,128)(2,1)} %param.9), channel_id=1, source_target_pairs={{0,4},{4,8},{8,12},{12,0},{1,5},{5,9},{9,13},{13,1},{2,6},{6,10},{... | collective-permute-start | bytes 98312 | tf_op jit(solution)/shard_map/ppermute | solution.py:10
  10.0 16.2 %collective-permute-start.17 = (bf16[16,1024]{1,0:T(8,128)(2,1)}, bf16[16,1024]{1,0:T(8,128)(2,1)}, u32[]{:S(2)}, u32[]{:S(2)}) collective-permute-start(bf16[16,1024]{1,0:T(8,128)(2,1)} %param.9), channel_id=1, source_target_pairs={{0,8},{4,12},{8,0},{12,4},{1,9},{5,13},{9,1},{13,5},{2,10},{6,14},... | collective-permute-start | bytes 98312 | tf_op jit(solution)/shard_map/ppermute | solution.py:10
  17.0 7.7 %copy-start.8 = (s32[16]{0:T(128)S(1)}, s32[16]{0:T(128)}, u32[]{:S(2)}) copy-start(s32[16]{0:T(128)} %param.14) | copy-start | bytes 196
  18.8 7.5 %collective-permute-start.18 = (bf16[16,1024]{1,0:T(8,128)(2,1)S(1)}, bf16[16,1024]{1,0:T(8,128)(2,1)S(1)}, u32[]{:S(2)}, u32[]{:S(2)}) collective-permute-start(bf16[16,1024]{1,0:T(8,128)(2,1)S(1)} %copy-done.6), channel_id=1, source_target_pairs={{0,12},{4,0},{8,4},{12,8},{1,13},{5,1},{9,5},{13,9},{2,14},{6,2},{... | collective-permute-start | bytes 98312 | tf_op jit(solution)/shard_map/ppermute | solution.py:10
  21.6 21.8 %collective-permute-start.5 = (bf16[256,4,128]{2,0,1:T(8,128)(2,1)S(1)}, bf16[256,4,128]{2,0,1:T(8,128)(2,1)S(1)}, u32[]{:S(2)}, u32[]{:S(2)}) collective-permute-start(bf16[256,4,128]{2,0,1:T(8,128)(2,1)S(1)} %bitcast.107), channel_id=1, source_target_pairs={{0,2},{1,3},{2,0},{3,1},{4,6},{5,7},{6,4},{7,5},{8,10},{9,11},{10,... | collective-permute-start | bytes 786440 | tf_op jit(solution)/shard_map/ppermute | solution.py:14
  24.1 14.0 %collective-permute-start.3 = (bf16[3,64,1024]{2,1,0:T(8,128)(2,1)S(1)}, bf16[3,64,1024]{2,1,0:T(8,128)(2,1)S(1)}, u32[]{:S(2)}, u32[]{:S(2)}) collective-permute-start(bf16[3,64,1024]{2,1,0:T(8,128)(2,1)S(1)} %get-tuple-element.25), channel_id=1, source_target_pairs={{0,2},{1,3},{2,0},{3,1},{4,6},{5,7},{6,4},{7,5},{8,10},{9,11},{10,... | collective-permute-start | bytes 1179656 | tf_op jit(solution)/shard_map/ppermute | solution.py:14
  27.1 14.9 %collective-permute-start.19 = (bf16[4,16,1024]{2,1,0:T(8,128)(2,1)S(1)}, bf16[4,16,1024]{2,1,0:T(8,128)(2,1)S(1)}, u32[]{:S(2)}, u32[]{:S(2)}) collective-permute-start(bf16[4,16,1024]{2,1,0:T(8,128)(2,1)S(1)} %get-tuple-element.29), channel_id=1, source_target_pairs={{0,2},{1,3},{2,0},{3,1},{4,6},{5,7},{6,4},{7,5},{8,10},{9,11},{10,... | collective-permute-start | bytes 393224 | tf_op jit(solution)/shard_map/ppermute | solution.py:14
  38.1 6.2 %copy-start.5 = (bf16[256,4,1,128]{0,3,2,1:T(8,128)(2,1)S(1)}, bf16[256,4,1,128]{0,3,2,1:T(8,128)(2,1)}, u32[]{:S(2)}) copy-start(bf16[256,4,1,128]{0,3,2,1:T(8,128)(2,1)} %get-tuple-element.22) | copy-start | bytes 786436
  39.3 7.8 %collective-permute-start.4 = (bf16[2,3,64,1024]{3,2,1,0:T(8,128)(2,1)}, bf16[2,3,64,1024]{3,2,1,0:T(8,128)(2,1)}, u32[]{:S(2)}, u32[]{:S(2)}) collective-permute-start(bf16[2,3,64,1024]{3,2,1,0:T(8,128)(2,1)} %get-tuple-element.13), channel_id=1, source_target_pairs={{0,1},{1,0},{2,3},{3,2},{4,5},{5,4},{6,7},{7,6},{8,9},{9,8},{10,11... | collective-permute-start | bytes 2359304 | tf_op jit(solution)/shard_map/ppermute | solution.py:14
  42.8 2.5 %collective-permute-start.20 = (bf16[2,4,16,1024]{3,2,1,0:T(8,128)(2,1)}, bf16[2,4,16,1024]{3,2,1,0:T(8,128)(2,1)}, u32[]{:S(2)}, u32[]{:S(2)}) collective-permute-start(bf16[2,4,16,1024]{3,2,1,0:T(8,128)(2,1)} %get-tuple-element.27), channel_id=1, source_target_pairs={{0,1},{1,0},{2,3},{3,2},{4,5},{5,4},{6,7},{7,6},{8,9},{9,8},{10,11... | collective-permute-start | bytes 786440 | tf_op jit(solution)/shard_map/ppermute | solution.py:14
  54.2 9.5 %collective-permute-start.6 = (bf16[256,512]{1,0:T(8,128)(2,1)}, bf16[256,512]{1,0:T(8,128)(2,1)}, u32[]{:S(2)}, u32[]{:S(2)}) collective-permute-start(bf16[256,512]{1,0:T(8,128)(2,1)} %get-tuple-element.17), channel_id=1, source_target_pairs={{0,2},{1,3},{2,0},{3,1},{4,6},{5,7},{6,4},{7,5},{8,10},{9,11},{10,... | collective-permute-start | bytes 786440 | tf_op jit(solution)/shard_map/ppermute | solution.py:14
  59.3 8.9 %collective-permute-start.11 = (bf16[256,512]{1,0:T(8,128)(2,1)S(1)}, bf16[256,512]{1,0:T(8,128)(2,1)S(1)}, u32[]{:S(2)}, u32[]{:S(2)}) collective-permute-start(bf16[256,512]{1,0:T(8,128)(2,1)S(1)} %get-tuple-element.18), channel_id=1, source_target_pairs={{0,2},{1,3},{2,0},{3,1},{4,6},{5,7},{6,4},{7,5},{8,10},{9,11},{10,... | collective-permute-start | bytes 786440 | tf_op jit(solution)/shard_map/ppermute | solution.py:14
  65.2 4.6 %collective-permute-start.7 = (f32[4,64,512]{2,1,0:T(8,128)S(1)}, f32[4,64,512]{2,1,0:T(8,128)S(1)}, u32[]{:S(2)}, u32[]{:S(2)}) collective-permute-start(f32[4,64,512]{2,1,0:T(8,128)S(1)} %dynamic-slice_bitcast_fusion.1), channel_id=1, source_target_pairs={{0,1},{1,0},{2,3},{3,2},{4,5},{5,4},{6,7},{7,6},{8,9},{9,8},{10,11... | collective-permute-start | bytes 1572872 | tf_op jit(solution)/shard_map/ppermute | solution.py:14
  68.7 5.1 %collective-permute-start.12 = (f32[4,64,512]{2,1,0:T(8,128)S(1)}, f32[4,64,512]{2,1,0:T(8,128)S(1)}, u32[]{:S(2)}, u32[]{:S(2)}) collective-permute-start(f32[4,64,512]{2,1,0:T(8,128)S(1)} %dynamic-slice_bitcast_fusion), channel_id=1, source_target_pairs={{0,1},{1,0},{2,3},{3,2},{4,5},{5,4},{6,7},{7,6},{8,9},{9,8},{10,11... | collective-permute-start | bytes 1572872 | tf_op jit(solution)/shard_map/ppermute | solution.py:14
  70.0 6.3 %collective-permute-start.10 = (f32[64,512]{1,0:T(8,128)S(1)}, f32[64,512]{1,0:T(8,128)S(1)}, u32[]{:S(2)}, u32[]{:S(2)}) collective-permute-start(f32[64,512]{1,0:T(8,128)S(1)} %get-tuple-element.15), channel_id=1, source_target_pairs={{0,12},{4,0},{8,4},{12,8},{1,13},{5,1},{9,5},{13,9},{2,14},{6,2},{... | collective-permute-start | bytes 393224 | tf_op jit(solution)/shard_map/ppermute | solution.py:10
  71.0 9.5 %collective-permute-start.8 = (f32[64,512]{1,0:T(8,128)S(1)}, f32[64,512]{1,0:T(8,128)S(1)}, u32[]{:S(2)}, u32[]{:S(2)}) collective-permute-start(f32[64,512]{1,0:T(8,128)S(1)} %get-tuple-element.14), channel_id=1, source_target_pairs={{0,4},{4,8},{8,12},{12,0},{1,5},{5,9},{9,13},{13,1},{2,6},{6,10},{... | collective-permute-start | bytes 393224 | tf_op jit(solution)/shard_map/ppermute | solution.py:10
  72.0 18.5 %collective-permute-start.9 = (f32[64,512]{1,0:T(8,128)S(1)}, f32[64,512]{1,0:T(8,128)S(1)}, u32[]{:S(2)}, u32[]{:S(2)}) collective-permute-start(f32[64,512]{1,0:T(8,128)S(1)} %get-tuple-element.16), channel_id=1, source_target_pairs={{0,8},{4,12},{8,0},{12,4},{1,9},{5,13},{9,1},{13,5},{2,10},{6,14},... | collective-permute-start | bytes 393224 | tf_op jit(solution)/shard_map/ppermute | solution.py:10
  73.9 16.7 %collective-permute-start.13 = (f32[64,512]{1,0:T(8,128)S(1)}, f32[64,512]{1,0:T(8,128)S(1)}, u32[]{:S(2)}, u32[]{:S(2)}) collective-permute-start(f32[64,512]{1,0:T(8,128)S(1)} %get-tuple-element.19), channel_id=1, source_target_pairs={{0,4},{4,8},{8,12},{12,0},{1,5},{5,9},{9,13},{13,1},{2,6},{6,10},{... | collective-permute-start | bytes 393224 | tf_op jit(solution)/shard_map/ppermute | solution.py:10
  75.5 17.8 %collective-permute-start.14 = (f32[64,512]{1,0:T(8,128)S(1)}, f32[64,512]{1,0:T(8,128)S(1)}, u32[]{:S(2)}, u32[]{:S(2)}) collective-permute-start(f32[64,512]{1,0:T(8,128)S(1)} %get-tuple-element.21), channel_id=1, source_target_pairs={{0,8},{4,12},{8,0},{12,4},{1,9},{5,13},{9,1},{13,5},{2,10},{6,14},... | collective-permute-start | bytes 393224 | tf_op jit(solution)/shard_map/ppermute | solution.py:10
  76.3 17.1 %collective-permute-start.15 = (f32[64,512]{1,0:T(8,128)S(1)}, f32[64,512]{1,0:T(8,128)S(1)}, u32[]{:S(2)}, u32[]{:S(2)}) collective-permute-start(f32[64,512]{1,0:T(8,128)S(1)} %get-tuple-element.20), channel_id=1, source_target_pairs={{0,12},{4,0},{8,4},{12,8},{1,13},{5,1},{9,5},{13,9},{2,14},{6,2},{... | collective-permute-start | bytes 393224 | tf_op jit(solution)/shard_map/ppermute | solution.py:10
  (6 other events, 12.2 us)

commit v11 on v7

--- a/solution.py
+++ b/solution.py
@@ -71,11 +71,7 @@
             send = lax.dynamic_index_in_dim(t, 1 - me, 1 + axis, keepdims=False)
             t = keep + swap(send, "dp", n_dp, bit)
         t = t.reshape(n_q, share, cols)
-        acc = lax.dynamic_index_in_dim(t, q, 0, keepdims=False)
-        for s in range(1, n_q):
-            part = lax.dynamic_index_in_dim(t, (q + s) % n_q, 0, keepdims=False)
-            acc = acc + shift(part, "queue", n_q, s)
-        out.append(acc)
+        out.append(jnp.sum(lax.all_to_all(t, "queue", 0, 0, tiled=False), 0))
     return jnp.concatenate(out, axis=1)
 
 

time: 86.4 us -> 104 us (1.20)
  waiting for transfers between devices: 33.7 us -> 39.4 us
  starting transfers between devices: 24.1 us -> 28.5 us
  other arithmetic: 8 us -> 12.3 us
  local copies, waits for them, and re-layouts: 8.28 us -> 11.7 us
    all_to_all x0 -> x2, waiting for transfers between devices: none -> 11.1 us  [reduce_scatter_grad(): out.append(jnp.sum(lax.all_to_all(t, 'queue', 0, 0, tiled=False), 0))]
    all_to_all x0 -> x2, starting transfers between devices: none -> 8.81 us  [reduce_scatter_grad(): out.append(jnp.sum(lax.all_to_all(t, 'queue', 0, 0, tiled=False), 0))]
    ppermute x12 -> x6, waiting for transfers between devices: 17.5 us -> 10.8 us  [shift(): return lax.ppermute(x, axis, [(i, (i + step) % n) for i in range(n)])]
    ppermute x12 -> x6, starting transfers between devices: 17.7 us -> 12.8 us  [shift(): return lax.ppermute(x, axis, [(i, (i + step) % n) for i in range(n)])]
    add x2, other arithmetic: 0.17 us -> 4.04 us  [reduce_scatter_grad(): t = keep + swap(send, 'dp', n_dp, bit)]
    squeeze x2, local copies, waits for them, and re-layouts: 0.09 us -> 2.72 us  [reduce_scatter_grad(): send = lax.dynamic_index_in_dim(t, 1 - me, 1 + axis, keepdims=False)]
    dot_general x2, matrix products: 1.9 us -> 3.86 us  [reduce_scatter_grad(): lax.dot_general(xs, gs, (((0,), (0,)), ((), ())), preferred_element_type=...]
    dot_general x1, matrix products: 2.09 us -> 0.5 us  [body(): fresh = jnp.dot(key_inputs, key_weight, preferred_element_type=jnp.float32)]
  transfers between devices with their start and end apart: 21 -> 17, of which waited for: 8 -> 9; matrix products, arithmetic and copies ran while one was open for 27% -> 28% of each run, Pallas kernels for 0% -> 0%
where the time goes in v11:
time: 104 us; the launch traced here: 103 us
  waiting for transfers between devices  39.4 us (38%)
  starting transfers between devices  28.5 us (27%)
  other arithmetic  12.3 us (12%)
  local copies, waits for them, and re-layouts  11.7 us (11%)
  matrix products  9.72 us (9%)
  between operations  1.56 us (2%)
    ppermute x9, waiting for transfers between devices, swap(): return lax.ppermute(x, axis, [(i, i ^ bit) for i in range(n)])  17.6 us
    ppermute x6, starting transfers between devices, shift(): return lax.ppermute(x, axis, [(i, (i + step) % n) for i in range(n)])  12.8 us
    all_to_all x2, waiting for transfers between devices, reduce_scatter_grad(): out.append(jnp.sum(lax.all_to_all(t, 'queue', 0, 0, tiled=False), 0))  11.1 us
    ppermute x6, waiting for transfers between devices, shift(): return lax.ppermute(x, axis, [(i, (i + step) % n) for i in range(n)])  10.8 us
    all_to_all x2, starting transfers between devices, reduce_scatter_grad(): out.append(jnp.sum(lax.all_to_all(t, 'queue', 0, 0, tiled=False), 0))  8.81 us
    ppermute x9, starting transfers between devices, swap(): return lax.ppermute(x, axis, [(i, i ^ bit) for i in range(n)])  6.84 us
    add x2, other arithmetic, reduce_scatter_grad(): t = keep + swap(send, 'dp', n_dp, bit)  4.04 us
    dot_general x2, matrix products, reduce_scatter_grad(): lax.dot_general(xs, gs, (((0,), (0,)), ((), ())), preferred_element_type=...  3.86 us
  transfers between devices with their start and end apart: 17, of which 9 were waited for; matrix products, arithmetic and copies ran while one was open for 28% of the time, Pallas kernels for 0%

profile of v11, /device:TPU:0, one launch (start us, length us, event | category | flops | bytes accessed | tf_op | source)
XLA Modules:
  0.0 103.2 jit_solution(8293304261968724511)
XLA Ops:
  0.7 1.7 %constant_dynamic-slice_fusion.2 = bf16[64,1024]{1,0:T(8,128)(2,1)} fusion(bf16[256,1024]{1,0:T(8,128)(2,1)} %param.12, s32[]{:T(128)S(6)} %select_n.160), kind=kLoop, calls=%fused_computation.89 | loop fusion | bytes 262148 | tf_op jit(solution)/shard_map/dynamic_slice | solution.py:30
  2.4 3.1 %collective-permute-start = (bf16[64,1024]{1,0:T(8,128)(2,1)}, bf16[64,1024]{1,0:T(8,128)(2,1)S(1)}, u32[]{:S(2)}, u32[]{:S(2)}) collective-permute-start(bf16[64,1024]{1,0:T(8,128)(2,1)} %constant_dynamic-slice_fusion.2), channel_id=1, source_target_pairs={{0,4},{4,8},{8,12},{12,0},{1,5},{5,9},{9,13},{13,1},{2,6},{6,10},{... | collective-permute-start | bytes 393224 | tf_op jit(solution)/shard_map/ppermute | solution.py:10
  5.4 2.6 %collective-permute-start.1 = (bf16[64,1024]{1,0:T(8,128)(2,1)}, bf16[64,1024]{1,0:T(8,128)(2,1)}, u32[]{:S(2)}, u32[]{:S(2)}) collective-permute-start(bf16[64,1024]{1,0:T(8,128)(2,1)} %constant_dynamic-slice_fusion.2), channel_id=1, source_target_pairs={{0,8},{4,12},{8,0},{12,4},{1,9},{5,13},{9,1},{13,5},{2,10},{6,14},... | collective-permute-start | bytes 393224 | tf_op jit(solution)/shard_map/ppermute | solution.py:10
  14.6 2.4 %collective-permute-done.1 = bf16[64,1024]{1,0:T(8,128)(2,1)} collective-permute-done((bf16[64,1024]{1,0:T(8,128)(2,1)}, bf16[64,1024]{1,0:T(8,128)(2,1)}, u32[]{:S(2)}, u32[]{:S(2)}) %collective-permute-start.1) | collective-permute-done | bytes 131104 | tf_op jit(solution)/shard_map/ppermute | solution.py:10
  18.0 1.6 %collective-permute-start.3 = (bf16[3,64,1024]{2,1,0:T(8,128)(2,1)S(1)}, bf16[3,64,1024]{2,1,0:T(8,128)(2,1)S(1)}, u32[]{:S(2)}, u32[]{:S(2)}) collective-permute-start(bf16[3,64,1024]{2,1,0:T(8,128)(2,1)S(1)} %get-tuple-element.23), channel_id=1, source_target_pairs={{0,2},{1,3},{2,0},{3,1},{4,6},{5,7},{6,4},{7,5},{8,10},{9,11},{10,... | collective-permute-start | bytes 1179656 | tf_op jit(solution)/shard_map/ppermute | solution.py:14
  20.1 8.9 %collective-permute-done.3 = bf16[3,64,1024]{2,1,0:T(8,128)(2,1)S(1)} collective-permute-done((bf16[3,64,1024]{2,1,0:T(8,128)(2,1)S(1)}, bf16[3,64,1024]{2,1,0:T(8,128)(2,1)S(1)}, u32[]{:S(2)}, u32[]{:S(2)}) %collective-permute-start.3) | collective-permute-done | bytes 393248 | tf_op jit(solution)/shard_map/ppermute | solution.py:14
  29.7 1.8 %collective-permute-done.4 = bf16[2,3,64,1024]{3,2,1,0:T(8,128)(2,1)S(1)} collective-permute-done((bf16[2,3,64,1024]{3,2,1,0:T(8,128)(2,1)S(1)}, bf16[2,3,64,1024]{3,2,1,0:T(8,128)(2,1)S(1)}, u32[]{:S(2)}, u32[]{:S(2)}) %collective-permute-start.4) | collective-permute-done | bytes 786464 | tf_op jit(solution)/shard_map/ppermute | solution.py:14
  36.7 1.5 %collective-permute-start.6 = (bf16[256,512]{1,0:T(8,128)(2,1)}, bf16[256,512]{1,0:T(8,128)(2,1)}, u32[]{:S(2)}, u32[]{:S(2)}) collective-permute-start(bf16[256,512]{1,0:T(8,128)(2,1)} %get-tuple-element.18), channel_id=1, source_target_pairs={{0,2},{1,3},{2,0},{3,1},{4,6},{5,7},{6,4},{7,5},{8,10},{9,11},{10,... | collective-permute-start | bytes 786440 | tf_op jit(solution)/shard_map/ppermute | solution.py:14
  38.2 1.8 %copy.22 = bf16[256,4,128]{0,2,1:T(8,128)(2,1)} copy(bf16[256,4,128]{2,0,1:T(8,128)(2,1)} %collective-permute-done.5) | data formatting | bytes 524288 | tf_op jit(solution)/shard_map/ppermute | solution.py:14
  41.6 4.6 %collective-permute-done.6 = bf16[256,512]{1,0:T(8,128)(2,1)} collective-permute-done((bf16[256,512]{1,0:T(8,128)(2,1)}, bf16[256,512]{1,0:T(8,128)(2,1)}, u32[]{:S(2)}, u32[]{:S(2)}) %collective-permute-start.6) | collective-permute-done | bytes 262176 | tf_op jit(solution)/shard_map/ppermute | solution.py:14
  46.2 1.5 %fusion.8 = f32[4,2,64,512]{3,2,1,0:T(8,128)S(1)} fusion(bf16[4,2,64,512]{3,2,1,0:T(8,128)(2,1)S(1)} %bitcast.75, bf16[256,512]{1,0:T(8,128)(2,1)} %collective-permute-done.6, bf16[256,512]{1,0:T(8,128)(2,1)} %get-tuple-element.18), kind=kOutput, calls=%fused_computation.23 | convolution fusion | flops 269484032 | bytes 2097152 | tf_op jit(solution)/shard_map/dot_general | solution.py:65
  51.0 2.4 %fusion.11 = f32[4,2,64,512]{3,2,1,0:T(8,128)} fusion(bf16[4,2,64,512]{3,2,1,0:T(8,128)(2,1)S(1)} %bitcast.76, bf16[256,512]{1,0:T(8,128)(2,1)} %collective-permute-done.8, bf16[256,512]{1,0:T(8,128)(2,1)S(1)} %copy-done.7), kind=kOutput, calls=%fused_computation.27 | convolution fusion | flops 269484032 | bytes 2097152 | tf_op jit(solution)/shard_map/dot_general | solution.py:65
  53.4 1.9 %dynamic-slice_bitcast_fusion = f32[4,64,512]{2,1,0:T(8,128)} fusion(f32[4,2,64,512]{3,2,1,0:T(8,128)} %fusion.11, s32[]{:T(128)S(6)} %select_n.171), kind=kLoop, calls=%fused_computation.33 | loop fusion | bytes 1048580 | tf_op jit(solution)/shard_map/jit(dynamic_index_in_dim)/squeeze | solution.py:71
  55.3 2.0 %bitcast_add_fusion.1 = f32[4,64,512]{2,1,0:T(8,128)} fusion(f32[4,64,512]{2,1,0:T(8,128)} %collective-permute-done.7, f32[4,2,64,512]{3,2,1,0:T(8,128)S(1)} %copy-done.3, s32[]{:T(128)S(6)} %select_n.170), kind=kLoop, calls=%fused_computation.32 | loop fusion | flops 131072 | bytes 1572868 | tf_op jit(solution)/shard_map/add | solution.py:72
  57.2 4.7 %all-to-all-start = ((f32[4,64,512]{2,1,0:T(8,128)}), f32[4,64,512]{2,1,0:T(8,128)S(1)}, u32[]{:S(2)}, u32[]{:S(2)}) async-start(f32[4,64,512]{2,1,0:T(8,128)} %bitcast_add_fusion.1), calls=%async_computation | async-start | bytes 1048576 | tf_op jit(solution)/shard_map/all_to_all | solution.py:74
  62.8 2.2 %collective-permute-start.10 = (bf16[16,1024]{1,0:T(8,128)(2,1)S(1)}, bf16[16,1024]{1,0:T(8,128)(2,1)S(1)}, u32[]{:S(2)}, u32[]{:S(2)}) collective-permute-start(bf16[16,1024]{1,0:T(8,128)(2,1)S(1)} %multiply_convert_fusion.2), channel_id=1, source_target_pairs={{0,4},{4,8},{8,12},{12,0},{1,5},{5,9},{9,13},{13,1},{2,6},{6,10},{... | collective-permute-start | bytes 98312 | tf_op jit(solution)/shard_map/ppermute | solution.py:10
  64.9 2.2 %collective-permute-start.11 = (bf16[16,1024]{1,0:T(8,128)(2,1)S(1)}, bf16[16,1024]{1,0:T(8,128)(2,1)S(1)}, u32[]{:S(2)}, u32[]{:S(2)}) collective-permute-start(bf16[16,1024]{1,0:T(8,128)(2,1)S(1)} %multiply_convert_fusion.2), channel_id=1, source_target_pairs={{0,8},{4,12},{8,0},{12,4},{1,9},{5,13},{9,1},{13,5},{2,10},{6,14},... | collective-permute-start | bytes 98312 | tf_op jit(solution)/shard_map/ppermute | solution.py:10
  68.6 2.5 %compare_select_fusion.3 = s32[256,1]{0,1:T(1,128)S(1)} fusion(s32[]{:T(128)} %bitcast.25, s32[]{:T(128)} %bitcast.26, s32[]{:T(128)} %bitcast.28, s32[]{:T(128)} %bitcast.27, s32[]{:T(128)} %bitcast.70), kind=kLoop, calls=%fused_computation.59 | loop fusion | flops 9472 | bytes 1044 | tf_op jit(solution)/shard_map/jit(_take)/gather | solution.py:156
  71.2 5.5 %collective-permute-done.10 = bf16[16,1024]{1,0:T(8,128)(2,1)S(1)} collective-permute-done((bf16[16,1024]{1,0:T(8,128)(2,1)S(1)}, bf16[16,1024]{1,0:T(8,128)(2,1)S(1)}, u32[]{:S(2)}, u32[]{:S(2)}) %collective-permute-start.10) | collective-permute-done | bytes 32800 | tf_op jit(solution)/shard_map/ppermute | solution.py:10
  76.6 2.9 %collective-permute-done.11 = bf16[16,1024]{1,0:T(8,128)(2,1)S(1)} collective-permute-done((bf16[16,1024]{1,0:T(8,128)(2,1)S(1)}, bf16[16,1024]{1,0:T(8,128)(2,1)S(1)}, u32[]{:S(2)}, u32[]{:S(2)}) %collective-permute-start.11) | collective-permute-done | bytes 32800 | tf_op jit(solution)/shard_map/ppermute | solution.py:10
  79.5 1.6 %collective-permute-start.13 = (bf16[4,16,1024]{2,1,0:T(8,128)(2,1)S(1)}, bf16[4,16,1024]{2,1,0:T(8,128)(2,1)S(1)}, u32[]{:S(2)}, u32[]{:S(2)}) collective-permute-start(bf16[4,16,1024]{2,1,0:T(8,128)(2,1)S(1)} %get-tuple-element.27), channel_id=1, source_target_pairs={{0,2},{1,3},{2,0},{3,1},{4,6},{5,7},{6,4},{7,5},{8,10},{9,11},{10,... | collective-permute-start | bytes 393224 | tf_op jit(solution)/shard_map/ppermute | solution.py:14
  81.1 2.1 %bitcast_add_fusion = f32[4,64,512]{2,1,0:T(8,128)} fusion(f32[4,64,512]{2,1,0:T(8,128)} %collective-permute-done.9, f32[4,2,64,512]{3,2,1,0:T(8,128)} %fusion.11, s32[]{:T(128)S(6)} %select_n.170), kind=kLoop, calls=%fused_computation.31 | loop fusion | flops 131072 | bytes 1572868 | tf_op jit(solution)/shard_map/add | solution.py:72
  83.2 4.1 %all-to-all-start.1 = ((f32[4,64,512]{2,1,0:T(8,128)}), f32[4,64,512]{2,1,0:T(8,128)}, u32[]{:S(2)}, u32[]{:S(2)}) async-start(f32[4,64,512]{2,1,0:T(8,128)} %bitcast_add_fusion), calls=%async_computation.1 | async-start | bytes 1048576 | tf_op jit(solution)/shard_map/all_to_all | solution.py:74
  90.3 11.1 %all-to-all-done.1 = f32[4,64,512]{2,1,0:T(8,128)} async-done(((f32[4,64,512]{2,1,0:T(8,128)}), f32[4,64,512]{2,1,0:T(8,128)}, u32[]{:S(2)}, u32[]{:S(2)}) %all-to-all-start.1) | async-done | bytes 524320 | tf_op jit(solution)/shard_map/all_to_all | solution.py:74
  (80 shorter events, 25.1 us)
Async XLA Ops:
  0.6 13.1 %copy-start = (bf16[1024,1024]{1,0:T(8,128)(2,1)S(1)}, bf16[1024,1024]{1,0:T(8,128)(2,1)}, u32[]{:S(2)}) copy-start(bf16[1024,1024]{1,0:T(8,128)(2,1)} %param.10) | copy-start | bytes 6291460
  0.6 13.1 %copy-start.5 = (bf16[256,1024]{1,0:T(8,128)(2,1)S(1)}, bf16[256,1024]{1,0:T(8,128)(2,1)}, u32[]{:S(2)}) copy-start(bf16[256,1024]{1,0:T(8,128)(2,1)} %param.8) | copy-start | bytes 1572868
  2.4 12.2 %collective-permute-start = (bf16[64,1024]{1,0:T(8,128)(2,1)}, bf16[64,1024]{1,0:T(8,128)(2,1)S(1)}, u32[]{:S(2)}, u32[]{:S(2)}) collective-permute-start(bf16[64,1024]{1,0:T(8,128)(2,1)} %constant_dynamic-slice_fusion.2), channel_id=1, source_target_pairs={{0,4},{4,8},{8,12},{12,0},{1,5},{5,9},{9,13},{13,1},{2,6},{6,10},{... | collective-permute-start | bytes 393224 | tf_op jit(solution)/shard_map/ppermute | solution.py:10
  5.4 11.5 %collective-permute-start.1 = (bf16[64,1024]{1,0:T(8,128)(2,1)}, bf16[64,1024]{1,0:T(8,128)(2,1)}, u32[]{:S(2)}, u32[]{:S(2)}) collective-permute-start(bf16[64,1024]{1,0:T(8,128)(2,1)} %constant_dynamic-slice_fusion.2), channel_id=1, source_target_pairs={{0,8},{4,12},{8,0},{12,4},{1,9},{5,13},{9,1},{13,5},{2,10},{6,14},... | collective-permute-start | bytes 393224 | tf_op jit(solution)/shard_map/ppermute | solution.py:10
  8.0 9.0 %collective-permute-start.2 = (bf16[64,1024]{1,0:T(8,128)(2,1)}, bf16[64,1024]{1,0:T(8,128)(2,1)}, u32[]{:S(2)}, u32[]{:S(2)}) collective-permute-start(bf16[64,1024]{1,0:T(8,128)(2,1)} %constant_dynamic-slice_fusion.2), channel_id=1, source_target_pairs={{0,12},{4,0},{8,4},{12,8},{1,13},{5,1},{9,5},{13,9},{2,14},{6,2},{... | collective-permute-start | bytes 393224 | tf_op jit(solution)/shard_map/ppermute | solution.py:10
  12.2 26.0 %collective-permute-start.5 = (bf16[256,4,128]{2,0,1:T(8,128)(2,1)}, bf16[256,4,128]{2,0,1:T(8,128)(2,1)}, u32[]{:S(2)}, u32[]{:S(2)}) collective-permute-start(bf16[256,4,128]{2,0,1:T(8,128)(2,1)} %bitcast.11), channel_id=1, source_target_pairs={{0,2},{1,3},{2,0},{3,1},{4,6},{5,7},{6,4},{7,5},{8,10},{9,11},{10,... | collective-permute-start | bytes 786440 | tf_op jit(solution)/shard_map/ppermute | solution.py:14
  13.7 5.9 %copy-start.4 = (bf16[1024,1024]{1,0:T(8,128)(2,1)S(1)}, bf16[1024,1024]{1,0:T(8,128)(2,1)}, u32[]{:S(2)}) copy-start(bf16[1024,1024]{1,0:T(8,128)(2,1)} %param.11) | copy-start | bytes 6291460
  13.7 5.9 %copy-start.8 = (bf16[16,1024]{1,0:T(8,128)(2,1)S(1)}, bf16[16,1024]{1,0:T(8,128)(2,1)}, u32[]{:S(2)}) copy-start(bf16[16,1024]{1,0:T(8,128)(2,1)} %param.9) | copy-start | bytes 98308
  18.0 11.0 %collective-permute-start.3 = (bf16[3,64,1024]{2,1,0:T(8,128)(2,1)S(1)}, bf16[3,64,1024]{2,1,0:T(8,128)(2,1)S(1)}, u32[]{:S(2)}, u32[]{:S(2)}) collective-permute-start(bf16[3,64,1024]{2,1,0:T(8,128)(2,1)S(1)} %get-tuple-element.23), channel_id=1, source_target_pairs={{0,2},{1,3},{2,0},{3,1},{4,6},{5,7},{6,4},{7,5},{8,10},{9,11},{10,... | collective-permute-start | bytes 1179656 | tf_op jit(solution)/shard_map/ppermute | solution.py:14
  20.1 9.2 %copy-start.1 = (bf16[256,1024]{1,0:T(8,128)(2,1)S(1)}, bf16[256,1024]{1,0:T(8,128)(2,1)}, u32[]{:S(2)}) copy-start(bf16[256,1024]{1,0:T(8,128)(2,1)} %param.12) | copy-start | bytes 1572868
  29.1 2.4 %collective-permute-start.4 = (bf16[2,3,64,1024]{3,2,1,0:T(8,128)(2,1)S(1)}, bf16[2,3,64,1024]{3,2,1,0:T(8,128)(2,1)S(1)}, u32[]{:S(2)}, u32[]{:S(2)}) collective-permute-start(bf16[2,3,64,1024]{3,2,1,0:T(8,128)(2,1)S(1)} %get-tuple-element.17), channel_id=1, source_target_pairs={{0,1},{1,0},{2,3},{3,2},{4,5},{5,4},{6,7},{7,6},{8,9},{9,8},{10,11... | collective-permute-start | bytes 2359304 | tf_op jit(solution)/shard_map/ppermute | solution.py:14
  36.7 9.5 %collective-permute-start.6 = (bf16[256,512]{1,0:T(8,128)(2,1)}, bf16[256,512]{1,0:T(8,128)(2,1)}, u32[]{:S(2)}, u32[]{:S(2)}) collective-permute-start(bf16[256,512]{1,0:T(8,128)(2,1)} %get-tuple-element.18), channel_id=1, source_target_pairs={{0,2},{1,3},{2,0},{3,1},{4,6},{5,7},{6,4},{7,5},{8,10},{9,11},{10,... | collective-permute-start | bytes 786440 | tf_op jit(solution)/shard_map/ppermute | solution.py:14
  41.0 10.0 %collective-permute-start.8 = (bf16[256,512]{1,0:T(8,128)(2,1)}, bf16[256,512]{1,0:T(8,128)(2,1)}, u32[]{:S(2)}, u32[]{:S(2)}) collective-permute-start(bf16[256,512]{1,0:T(8,128)(2,1)} %get-tuple-element.19), channel_id=1, source_target_pairs={{0,2},{1,3},{2,0},{3,1},{4,6},{5,7},{6,4},{7,5},{8,10},{9,11},{10,... | collective-permute-start | bytes 786440 | tf_op jit(solution)/shard_map/ppermute | solution.py:14
  49.6 5.7 %collective-permute-start.7 = (f32[4,64,512]{2,1,0:T(8,128)}, f32[4,64,512]{2,1,0:T(8,128)}, u32[]{:S(2)}, u32[]{:S(2)}) collective-permute-start(f32[4,64,512]{2,1,0:T(8,128)} %dynamic-slice_bitcast_fusion.1), channel_id=1, source_target_pairs={{0,1},{1,0},{2,3},{3,2},{4,5},{5,4},{6,7},{7,6},{8,9},{9,8},{10,11... | collective-permute-start | bytes 1572872 | tf_op jit(solution)/shard_map/ppermute | solution.py:14
  50.2 5.0 %copy-start.3 = (f32[4,2,64,512]{3,2,1,0:T(8,128)S(1)}, f32[4,2,64,512]{3,2,1,0:T(8,128)}, u32[]{:S(2)}) copy-start(f32[4,2,64,512]{3,2,1,0:T(8,128)} %copy-done.2) | copy-start | bytes 3145732
  55.2 6.7 %copy-start.10 = (s32[16]{0:T(128)S(1)}, s32[16]{0:T(128)}, u32[]{:S(2)}) copy-start(s32[16]{0:T(128)} %param.14) | copy-start | bytes 196
  55.3 25.8 %collective-permute-start.9 = (f32[4,64,512]{2,1,0:T(8,128)}, f32[4,64,512]{2,1,0:T(8,128)}, u32[]{:S(2)}, u32[]{:S(2)}) collective-permute-start(f32[4,64,512]{2,1,0:T(8,128)} %dynamic-slice_bitcast_fusion), channel_id=1, source_target_pairs={{0,1},{1,0},{2,3},{3,2},{4,5},{5,4},{6,7},{7,6},{8,9},{9,8},{10,11... | collective-permute-start | bytes 1572872 | tf_op jit(solution)/shard_map/ppermute | solution.py:14
  57.2 26.0 %all-to-all-start = ((f32[4,64,512]{2,1,0:T(8,128)}), f32[4,64,512]{2,1,0:T(8,128)S(1)}, u32[]{:S(2)}, u32[]{:S(2)}) async-start(f32[4,64,512]{2,1,0:T(8,128)} %bitcast_add_fusion.1), calls=%async_computation | async-start | bytes 1048576 | tf_op jit(solution)/shard_map/all_to_all | solution.py:74
  62.8 13.9 %collective-permute-start.10 = (bf16[16,1024]{1,0:T(8,128)(2,1)S(1)}, bf16[16,1024]{1,0:T(8,128)(2,1)S(1)}, u32[]{:S(2)}, u32[]{:S(2)}) collective-permute-start(bf16[16,1024]{1,0:T(8,128)(2,1)S(1)} %multiply_convert_fusion.2), channel_id=1, source_target_pairs={{0,4},{4,8},{8,12},{12,0},{1,5},{5,9},{9,13},{13,1},{2,6},{6,10},{... | collective-permute-start | bytes 98312 | tf_op jit(solution)/shard_map/ppermute | solution.py:10
  64.9 14.6 %collective-permute-start.11 = (bf16[16,1024]{1,0:T(8,128)(2,1)S(1)}, bf16[16,1024]{1,0:T(8,128)(2,1)S(1)}, u32[]{:S(2)}, u32[]{:S(2)}) collective-permute-start(bf16[16,1024]{1,0:T(8,128)(2,1)S(1)} %multiply_convert_fusion.2), channel_id=1, source_target_pairs={{0,8},{4,12},{8,0},{12,4},{1,9},{5,13},{9,1},{13,5},{2,10},{6,14},... | collective-permute-start | bytes 98312 | tf_op jit(solution)/shard_map/ppermute | solution.py:10
  67.1 12.4 %collective-permute-start.12 = (bf16[16,1024]{1,0:T(8,128)(2,1)S(1)}, bf16[16,1024]{1,0:T(8,128)(2,1)S(1)}, u32[]{:S(2)}, u32[]{:S(2)}) collective-permute-start(bf16[16,1024]{1,0:T(8,128)(2,1)S(1)} %multiply_convert_fusion.2), channel_id=1, source_target_pairs={{0,12},{4,0},{8,4},{12,8},{1,13},{5,1},{9,5},{13,9},{2,14},{6,2},{... | collective-permute-start | bytes 98312 | tf_op jit(solution)/shard_map/ppermute | solution.py:10
  79.5 7.8 %collective-permute-start.13 = (bf16[4,16,1024]{2,1,0:T(8,128)(2,1)S(1)}, bf16[4,16,1024]{2,1,0:T(8,128)(2,1)S(1)}, u32[]{:S(2)}, u32[]{:S(2)}) collective-permute-start(bf16[4,16,1024]{2,1,0:T(8,128)(2,1)S(1)} %get-tuple-element.27), channel_id=1, source_target_pairs={{0,2},{1,3},{2,0},{3,1},{4,6},{5,7},{6,4},{7,5},{8,10},{9,11},{10,... | collective-permute-start | bytes 393224 | tf_op jit(solution)/shard_map/ppermute | solution.py:14
  83.2 18.2 %all-to-all-start.1 = ((f32[4,64,512]{2,1,0:T(8,128)}), f32[4,64,512]{2,1,0:T(8,128)}, u32[]{:S(2)}, u32[]{:S(2)}) async-start(f32[4,64,512]{2,1,0:T(8,128)} %bitcast_add_fusion), calls=%async_computation.1 | async-start | bytes 1048576 | tf_op jit(solution)/shard_map/all_to_all | solution.py:74
  87.4 1.6 %collective-permute-start.14 = (bf16[2,4,16,1024]{3,2,1,0:T(8,128)(2,1)S(1)}, bf16[2,4,16,1024]{3,2,1,0:T(8,128)(2,1)S(1)}, u32[]{:S(2)}, u32[]{:S(2)}) collective-permute-start(bf16[2,4,16,1024]{3,2,1,0:T(8,128)(2,1)S(1)} %get-tuple-element.25), channel_id=1, source_target_pairs={{0,1},{1,0},{2,3},{3,2},{4,5},{5,4},{6,7},{7,6},{8,9},{9,8},{10,11... | collective-permute-start | bytes 786440 | tf_op jit(solution)/shard_map/ppermute | solution.py:14
  (4 other events, 11.0 us)

commit v12 on v7

--- a/solution.py
+++ b/solution.py
@@ -56,7 +56,7 @@
     got_x = swap(other, "dp", n_dp, hb)
     xs = jnp.concatenate([mine, got_x], axis=0).reshape(2 * q_dev, n_q * hb * share)
     rest = bits[1:]
-    halves = 2
+    halves = 4
     cols = width // halves
     out = []
     for h in range(halves):

time: 86.4 us -> 90.1 us (1.043)
  starting transfers between devices: 24.1 us -> 32.4 us
  waiting for transfers between devices: 33.7 us -> 28.9 us
    ppermute x12 -> x18, waiting for transfers between devices: 17.5 us -> 9.7 us  [shift(): return lax.ppermute(x, axis, [(i, (i + step) % n) for i in range(n)])]
    ppermute x12 -> x18, starting transfers between devices: 17.7 us -> 25.2 us  [shift(): return lax.ppermute(x, axis, [(i, (i + step) % n) for i in range(n)])]
    ppermute x9 -> x13, waiting for transfers between devices: 16.2 us -> 19.2 us  [swap(): return lax.ppermute(x, axis, [(i, i ^ bit) for i in range(n)])]
    another operation x3, other arithmetic: 1.28 us -> 3.56 us  [gather_queue(): payload = jnp.stack([payload, swap(payload, 'dp', n_dp, bit)], axis=t)]
    another operation x3, other arithmetic: 1.67 us -> 0.11 us  [gather_blocks(): got = jnp.stack([got, swap(got, 'dp', n_dp, bit)], axis=t)]
    dot_general x1, matrix products: 0.35 us -> 1.32 us  [body(): jnp.dot(pick_near, queue_keys, preferred_element_type=jnp.float32)]
    ppermute x9 -> x13, starting transfers between devices: 6.44 us -> 7.23 us  [swap(): return lax.ppermute(x, axis, [(i, i ^ bit) for i in range(n)])]
    dot_general x2 -> x4, matrix products: 1.9 us -> 1.17 us  [reduce_scatter_grad(): lax.dot_general(xs, gs, (((0,), (0,)), ((), ())), preferred_element_type=...]
  transfers between devices with their start and end apart: 21 -> 31, of which waited for: 8 -> 11; matrix products, arithmetic and copies ran while one was open for 27% -> 20% of each run, Pallas kernels for 0% -> 0%
where the time goes in v12:
time: 90.1 us; the launch traced here: 89.7 us
  starting transfers between devices  32.4 us (36%)
  waiting for transfers between devices  28.9 us (32%)
  matrix products  10.5 us (12%)
  other arithmetic  8.52 us (9%)
  local copies, waits for them, and re-layouts  7.61 us (8%)
  between operations  1.75 us (2%)
    ppermute x18, starting transfers between devices, shift(): return lax.ppermute(x, axis, [(i, (i + step) % n) for i in range(n)])  25.2 us
    ppermute x13, waiting for transfers between devices, swap(): return lax.ppermute(x, axis, [(i, i ^ bit) for i in range(n)])  19.2 us
    ppermute x18, waiting for transfers between devices, shift(): return lax.ppermute(x, axis, [(i, (i + step) % n) for i in range(n)])  9.7 us
    ppermute x13, starting transfers between devices, swap(): return lax.ppermute(x, axis, [(i, i ^ bit) for i in range(n)])  7.23 us
    another operation x3, other arithmetic, gather_queue(): payload = jnp.stack([payload, swap(payload, 'dp', n_dp, bit)], axis=t)  3.56 us
    gather x1, other arithmetic, body(): b = jnp.take(owner_block, sub_block)  2.37 us
    dot_general x1, matrix products, body(): fresh = jnp.dot(key_inputs, key_weight, preferred_element_type=jnp.float32)  2.09 us
  transfers between devices with their start and end apart: 31, of which 11 were waited for; matrix products, arithmetic and copies ran while one was open for 20% of the time, Pallas kernels for 0%

profile of v12, /device:TPU:0, one launch (start us, length us, event | category | flops | bytes accessed | tf_op | source)
XLA Modules:
  0.0 89.7 jit_solution(15959257012734770245)
XLA Ops:
  0.7 1.7 %constant_dynamic-slice_fusion.2 = bf16[64,1024]{1,0:T(8,128)(2,1)} fusion(bf16[256,1024]{1,0:T(8,128)(2,1)} %param.12, s32[]{:T(128)S(6)} %select_n.225), kind=kLoop, calls=%fused_computation.94 | loop fusion | bytes 262148 | tf_op jit(solution)/shard_map/dynamic_slice | solution.py:30
  2.4 3.1 %collective-permute-start = (bf16[64,1024]{1,0:T(8,128)(2,1)}, bf16[64,1024]{1,0:T(8,128)(2,1)}, u32[]{:S(2)}, u32[]{:S(2)}) collective-permute-start(bf16[64,1024]{1,0:T(8,128)(2,1)} %constant_dynamic-slice_fusion.2), channel_id=1, source_target_pairs={{0,4},{4,8},{8,12},{12,0},{1,5},{5,9},{9,13},{13,1},{2,6},{6,10},{... | collective-permute-start | bytes 393224 | tf_op jit(solution)/shard_map/ppermute | solution.py:10
  5.4 2.6 %collective-permute-start.1 = (bf16[64,1024]{1,0:T(8,128)(2,1)}, bf16[64,1024]{1,0:T(8,128)(2,1)}, u32[]{:S(2)}, u32[]{:S(2)}) collective-permute-start(bf16[64,1024]{1,0:T(8,128)(2,1)} %constant_dynamic-slice_fusion.2), channel_id=1, source_target_pairs={{0,8},{4,12},{8,0},{12,4},{1,9},{5,13},{9,1},{13,5},{2,10},{6,14},... | collective-permute-start | bytes 393224 | tf_op jit(solution)/shard_map/ppermute | solution.py:10
  12.2 1.5 %collective-permute-start.5 = (bf16[256,4,128]{2,0,1:T(8,128)(2,1)}, bf16[256,4,128]{2,0,1:T(8,128)(2,1)}, u32[]{:S(2)}, u32[]{:S(2)}) collective-permute-start(bf16[256,4,128]{2,0,1:T(8,128)(2,1)} %bitcast.11), channel_id=1, source_target_pairs={{0,2},{1,3},{2,0},{3,1},{4,6},{5,7},{6,4},{7,5},{8,10},{9,11},{10,... | collective-permute-start | bytes 786440 | tf_op jit(solution)/shard_map/ppermute | solution.py:14
  13.7 1.7 %multiply_reduce_fusion.2 = (f32[256]{0:T(256)S(1)}, f32[256,1024]{1,0:T(8,128)}) fusion(bf16[256,1024]{1,0:T(8,128)(2,1)S(1)} %copy-done.4, bf16[1024,1024]{1,0:T(8,128)(2,1)S(1)} %copy-done), kind=kOutput, calls=%fused_computation.13 | convolution fusion | flops 537394944 | bytes 3671040 | tf_op jit(solution)/shard_map/dot_general | solution.py:109
  16.9 2.1 %multiply_reduce_fusion.3 = (f32[16]{0:T(128)S(1)}, f32[16,1024]{1,0:T(8,128)S(1)}) fusion(bf16[16,1024]{1,0:T(8,128)(2,1)S(1)} %copy-done.7, bf16[1024,1024]{1,0:T(8,128)(2,1)} %param.11), kind=kOutput, calls=%fused_computation.91 | convolution fusion | flops 33587184 | bytes 2195520 | tf_op jit(solution)/shard_map/dot_general | solution.py:102
  19.0 2.4 %compare_select_fusion.3 = s32[256,1]{0,1:T(1,128)S(1)} fusion(s32[]{:T(128)} %bitcast.49, s32[]{:T(128)} %bitcast.50, s32[]{:T(128)} %bitcast.52, s32[]{:T(128)} %bitcast.51, s32[]{:T(128)} %bitcast.138), kind=kLoop, calls=%fused_computation.98 | loop fusion | flops 9472 | bytes 1044 | tf_op jit(solution)/shard_map/jit(_take)/gather | solution.py:160
  23.3 9.2 %collective-permute-done.3 = bf16[3,64,1024]{2,1,0:T(8,128)(2,1)S(1)} collective-permute-done((bf16[3,64,1024]{2,1,0:T(8,128)(2,1)S(1)}, bf16[3,64,1024]{2,1,0:T(8,128)(2,1)S(1)}, u32[]{:S(2)}, u32[]{:S(2)}) %collective-permute-start.3) | collective-permute-done | bytes 393248 | tf_op jit(solution)/shard_map/ppermute | solution.py:14
  34.9 1.8 %copy.22 = bf16[256,4,128]{0,2,1:T(8,128)(2,1)} copy(bf16[256,4,128]{2,0,1:T(8,128)(2,1)} %collective-permute-done.5) | data formatting | bytes 524288 | tf_op jit(solution)/shard_map/ppermute | solution.py:14
  43.8 2.8 %collective-permute-start.28 = (bf16[16,1024]{1,0:T(8,128)(2,1)S(1)}, bf16[16,1024]{1,0:T(8,128)(2,1)S(1)}, u32[]{:S(2)}, u32[]{:S(2)}) collective-permute-start(bf16[16,1024]{1,0:T(8,128)(2,1)S(1)} %multiply_convert_fusion.2), channel_id=1, source_target_pairs={{0,12},{4,0},{8,4},{12,8},{1,13},{5,1},{9,5},{13,9},{2,14},{6,2},{... | collective-permute-start | bytes 98312 | tf_op jit(solution)/shard_map/ppermute | solution.py:10
  47.3 1.6 %collective-permute-start.11 = (bf16[256,256]{1,0:T(8,128)(2,1)S(1)}, bf16[256,256]{1,0:T(8,128)(2,1)S(1)}, u32[]{:S(2)}, u32[]{:S(2)}) collective-permute-start(bf16[256,256]{1,0:T(8,128)(2,1)S(1)} %get-tuple-element.21), channel_id=1, source_target_pairs={{0,2},{1,3},{2,0},{3,1},{4,6},{5,7},{6,4},{7,5},{8,10},{9,11},{10,... | collective-permute-start | bytes 393224 | tf_op jit(solution)/shard_map/ppermute | solution.py:14
  51.6 1.5 %collective-permute-done.6 = bf16[256,256]{1,0:T(8,128)(2,1)S(1)} collective-permute-done((bf16[256,256]{1,0:T(8,128)(2,1)S(1)}, bf16[256,256]{1,0:T(8,128)(2,1)S(1)}, u32[]{:S(2)}, u32[]{:S(2)}) %collective-permute-start.6) | collective-permute-done | bytes 131104 | tf_op jit(solution)/shard_map/ppermute | solution.py:14
  53.5 2.4 %collective-permute-done.11 = bf16[256,256]{1,0:T(8,128)(2,1)S(1)} collective-permute-done((bf16[256,256]{1,0:T(8,128)(2,1)S(1)}, bf16[256,256]{1,0:T(8,128)(2,1)S(1)}, u32[]{:S(2)}, u32[]{:S(2)}) %collective-permute-start.11) | collective-permute-done | bytes 131104 | tf_op jit(solution)/shard_map/ppermute | solution.py:14
  56.3 2.4 %collective-permute-done.16 = bf16[256,256]{1,0:T(8,128)(2,1)S(1)} collective-permute-done((bf16[256,256]{1,0:T(8,128)(2,1)S(1)}, bf16[256,256]{1,0:T(8,128)(2,1)S(1)}, u32[]{:S(2)}, u32[]{:S(2)}) %collective-permute-start.16) | collective-permute-done | bytes 131104 | tf_op jit(solution)/shard_map/ppermute | solution.py:14
  59.1 2.4 %collective-permute-done.21 = bf16[256,256]{1,0:T(8,128)(2,1)S(1)} collective-permute-done((bf16[256,256]{1,0:T(8,128)(2,1)S(1)}, bf16[256,256]{1,0:T(8,128)(2,1)S(1)}, u32[]{:S(2)}, u32[]{:S(2)}) %collective-permute-start.21) | collective-permute-done | bytes 131104 | tf_op jit(solution)/shard_map/ppermute | solution.py:14
  65.7 1.8 %collective-permute-start.9 = (f32[64,256]{1,0:T(8,128)S(1)}, f32[64,256]{1,0:T(8,128)S(1)}, u32[]{:S(2)}, u32[]{:S(2)}) collective-permute-start(f32[64,256]{1,0:T(8,128)S(1)} %get-tuple-element.30), channel_id=1, source_target_pairs={{0,8},{4,12},{8,0},{12,4},{1,9},{5,13},{9,1},{13,5},{2,10},{6,14},... | collective-permute-start | bytes 196616 | tf_op jit(solution)/shard_map/ppermute | solution.py:10
  67.5 1.6 %collective-permute-start.13 = (f32[64,256]{1,0:T(8,128)S(1)}, f32[64,256]{1,0:T(8,128)S(1)}, u32[]{:S(2)}, u32[]{:S(2)}) collective-permute-start(f32[64,256]{1,0:T(8,128)S(1)} %get-tuple-element.31), channel_id=1, source_target_pairs={{0,4},{4,8},{8,12},{12,0},{1,5},{5,9},{9,13},{13,1},{2,6},{6,10},{... | collective-permute-start | bytes 196616 | tf_op jit(solution)/shard_map/ppermute | solution.py:10
  70.7 2.4 %collective-permute-start.15 = (f32[64,256]{1,0:T(8,128)S(1)}, f32[64,256]{1,0:T(8,128)S(1)}, u32[]{:S(2)}, u32[]{:S(2)}) collective-permute-start(f32[64,256]{1,0:T(8,128)S(1)} %get-tuple-element.32), channel_id=1, source_target_pairs={{0,12},{4,0},{8,4},{12,8},{1,13},{5,1},{9,5},{13,9},{2,14},{6,2},{... | collective-permute-start | bytes 196616 | tf_op jit(solution)/shard_map/ppermute | solution.py:10
  73.4 2.9 %collective-permute-done.9 = f32[64,256]{1,0:T(8,128)S(1)} collective-permute-done((f32[64,256]{1,0:T(8,128)S(1)}, f32[64,256]{1,0:T(8,128)S(1)}, u32[]{:S(2)}, u32[]{:S(2)}) %collective-permute-start.9) | collective-permute-done | bytes 65568 | tf_op jit(solution)/shard_map/ppermute | solution.py:10
  76.3 1.5 %collective-permute-start.20 = (f32[64,256]{1,0:T(8,128)S(1)}, f32[64,256]{1,0:T(8,128)S(1)}, u32[]{:S(2)}, u32[]{:S(2)}) collective-permute-start(f32[64,256]{1,0:T(8,128)S(1)} %get-tuple-element.35), channel_id=1, source_target_pairs={{0,12},{4,0},{8,4},{12,8},{1,13},{5,1},{9,5},{13,9},{2,14},{6,2},{... | collective-permute-start | bytes 196616 | tf_op jit(solution)/shard_map/ppermute | solution.py:10
  77.9 2.7 %collective-permute-done.14 = f32[64,256]{1,0:T(8,128)S(1)} collective-permute-done((f32[64,256]{1,0:T(8,128)S(1)}, f32[64,256]{1,0:T(8,128)S(1)}, u32[]{:S(2)}, u32[]{:S(2)}) %collective-permute-start.14) | collective-permute-done | bytes 65568 | tf_op jit(solution)/shard_map/ppermute | solution.py:10
  81.5 3.4 %collective-permute-start.25 = (f32[64,256]{1,0:T(8,128)S(1)}, f32[64,256]{1,0:T(8,128)S(1)}, u32[]{:S(2)}, u32[]{:S(2)}) collective-permute-start(f32[64,256]{1,0:T(8,128)S(1)} %get-tuple-element.38), channel_id=1, source_target_pairs={{0,12},{4,0},{8,4},{12,8},{1,13},{5,1},{9,5},{13,9},{2,14},{6,2},{... | collective-permute-start | bytes 196616 | tf_op jit(solution)/shard_map/ppermute | solution.py:10
  85.0 2.3 %collective-permute-done.23 = f32[64,256]{1,0:T(8,128)S(1)} collective-permute-done((f32[64,256]{1,0:T(8,128)S(1)}, f32[64,256]{1,0:T(8,128)S(1)}, u32[]{:S(2)}, u32[]{:S(2)}) %collective-permute-start.23) | collective-permute-done | bytes 65568 | tf_op jit(solution)/shard_map/ppermute | solution.py:10
  87.3 1.7 %collective-permute-done.24 = f32[64,256]{1,0:T(8,128)S(1)} collective-permute-done((f32[64,256]{1,0:T(8,128)S(1)}, f32[64,256]{1,0:T(8,128)S(1)}, u32[]{:S(2)}, u32[]{:S(2)}) %collective-permute-start.24) | collective-permute-done | bytes 65568 | tf_op jit(solution)/shard_map/ppermute | solution.py:10
  (118 shorter events, 28.7 us)
Async XLA Ops:
  2.4 19.1 %collective-permute-start = (bf16[64,1024]{1,0:T(8,128)(2,1)}, bf16[64,1024]{1,0:T(8,128)(2,1)}, u32[]{:S(2)}, u32[]{:S(2)}) collective-permute-start(bf16[64,1024]{1,0:T(8,128)(2,1)} %constant_dynamic-slice_fusion.2), channel_id=1, source_target_pairs={{0,4},{4,8},{8,12},{12,0},{1,5},{5,9},{9,13},{13,1},{2,6},{6,10},{... | collective-permute-start | bytes 393224 | tf_op jit(solution)/shard_map/ppermute | solution.py:10
  5.4 16.0 %collective-permute-start.1 = (bf16[64,1024]{1,0:T(8,128)(2,1)}, bf16[64,1024]{1,0:T(8,128)(2,1)}, u32[]{:S(2)}, u32[]{:S(2)}) collective-permute-start(bf16[64,1024]{1,0:T(8,128)(2,1)} %constant_dynamic-slice_fusion.2), channel_id=1, source_target_pairs={{0,8},{4,12},{8,0},{12,4},{1,9},{5,13},{9,1},{13,5},{2,10},{6,14},... | collective-permute-start | bytes 393224 | tf_op jit(solution)/shard_map/ppermute | solution.py:10
  8.0 13.5 %collective-permute-start.2 = (bf16[64,1024]{1,0:T(8,128)(2,1)}, bf16[64,1024]{1,0:T(8,128)(2,1)}, u32[]{:S(2)}, u32[]{:S(2)}) collective-permute-start(bf16[64,1024]{1,0:T(8,128)(2,1)} %constant_dynamic-slice_fusion.2), channel_id=1, source_target_pairs={{0,12},{4,0},{8,4},{12,8},{1,13},{5,1},{9,5},{13,9},{2,14},{6,2},{... | collective-permute-start | bytes 393224 | tf_op jit(solution)/shard_map/ppermute | solution.py:10
  12.2 22.7 %collective-permute-start.5 = (bf16[256,4,128]{2,0,1:T(8,128)(2,1)}, bf16[256,4,128]{2,0,1:T(8,128)(2,1)}, u32[]{:S(2)}, u32[]{:S(2)}) collective-permute-start(bf16[256,4,128]{2,0,1:T(8,128)(2,1)} %bitcast.11), channel_id=1, source_target_pairs={{0,2},{1,3},{2,0},{3,1},{4,6},{5,7},{6,4},{7,5},{8,10},{9,11},{10,... | collective-permute-start | bytes 786440 | tf_op jit(solution)/shard_map/ppermute | solution.py:14
  22.6 9.8 %collective-permute-start.3 = (bf16[3,64,1024]{2,1,0:T(8,128)(2,1)S(1)}, bf16[3,64,1024]{2,1,0:T(8,128)(2,1)S(1)}, u32[]{:S(2)}, u32[]{:S(2)}) collective-permute-start(bf16[3,64,1024]{2,1,0:T(8,128)(2,1)S(1)} %get-tuple-element.25), channel_id=1, source_target_pairs={{0,2},{1,3},{2,0},{3,1},{4,6},{5,7},{6,4},{7,5},{8,10},{9,11},{10,... | collective-permute-start | bytes 1179656 | tf_op jit(solution)/shard_map/ppermute | solution.py:14
  43.8 7.1 %collective-permute-start.28 = (bf16[16,1024]{1,0:T(8,128)(2,1)S(1)}, bf16[16,1024]{1,0:T(8,128)(2,1)S(1)}, u32[]{:S(2)}, u32[]{:S(2)}) collective-permute-start(bf16[16,1024]{1,0:T(8,128)(2,1)S(1)} %multiply_convert_fusion.2), channel_id=1, source_target_pairs={{0,12},{4,0},{8,4},{12,8},{1,13},{5,1},{9,5},{13,9},{2,14},{6,2},{... | collective-permute-start | bytes 98312 | tf_op jit(solution)/shard_map/ppermute | solution.py:10
  47.3 8.6 %collective-permute-start.11 = (bf16[256,256]{1,0:T(8,128)(2,1)S(1)}, bf16[256,256]{1,0:T(8,128)(2,1)S(1)}, u32[]{:S(2)}, u32[]{:S(2)}) collective-permute-start(bf16[256,256]{1,0:T(8,128)(2,1)S(1)} %get-tuple-element.21), channel_id=1, source_target_pairs={{0,2},{1,3},{2,0},{3,1},{4,6},{5,7},{6,4},{7,5},{8,10},{9,11},{10,... | collective-permute-start | bytes 393224 | tf_op jit(solution)/shard_map/ppermute | solution.py:14
  48.8 9.8 %collective-permute-start.16 = (bf16[256,256]{1,0:T(8,128)(2,1)S(1)}, bf16[256,256]{1,0:T(8,128)(2,1)S(1)}, u32[]{:S(2)}, u32[]{:S(2)}) collective-permute-start(bf16[256,256]{1,0:T(8,128)(2,1)S(1)} %get-tuple-element.20), channel_id=1, source_target_pairs={{0,2},{1,3},{2,0},{3,1},{4,6},{5,7},{6,4},{7,5},{8,10},{9,11},{10,... | collective-permute-start | bytes 393224 | tf_op jit(solution)/shard_map/ppermute | solution.py:14
  49.5 12.0 %collective-permute-start.21 = (bf16[256,256]{1,0:T(8,128)(2,1)S(1)}, bf16[256,256]{1,0:T(8,128)(2,1)S(1)}, u32[]{:S(2)}, u32[]{:S(2)}) collective-permute-start(bf16[256,256]{1,0:T(8,128)(2,1)S(1)} %get-tuple-element.19), channel_id=1, source_target_pairs={{0,2},{1,3},{2,0},{3,1},{4,6},{5,7},{6,4},{7,5},{8,10},{9,11},{10,... | collective-permute-start | bytes 393224 | tf_op jit(solution)/shard_map/ppermute | solution.py:14
  50.9 12.4 %collective-permute-start.29 = (bf16[4,16,1024]{2,1,0:T(8,128)(2,1)S(1)}, bf16[4,16,1024]{2,1,0:T(8,128)(2,1)S(1)}, u32[]{:S(2)}, u32[]{:S(2)}) collective-permute-start(bf16[4,16,1024]{2,1,0:T(8,128)(2,1)S(1)} %get-tuple-element.41), channel_id=1, source_target_pairs={{0,2},{1,3},{2,0},{3,1},{4,6},{5,7},{6,4},{7,5},{8,10},{9,11},{10,... | collective-permute-start | bytes 393224 | tf_op jit(solution)/shard_map/ppermute | solution.py:14
  53.4 10.0 %collective-permute-start.7 = (f32[4,64,256]{2,1,0:T(8,128)S(1)}, f32[4,64,256]{2,1,0:T(8,128)S(1)}, u32[]{:S(2)}, u32[]{:S(2)}) collective-permute-start(f32[4,64,256]{2,1,0:T(8,128)S(1)} %dynamic-slice_bitcast_fusion.3), channel_id=1, source_target_pairs={{0,1},{1,0},{2,3},{3,2},{4,5},{5,4},{6,7},{7,6},{8,9},{9,8},{10,11... | collective-permute-start | bytes 786440 | tf_op jit(solution)/shard_map/ppermute | solution.py:14
  56.2 8.3 %collective-permute-start.12 = (f32[4,64,256]{2,1,0:T(8,128)S(1)}, f32[4,64,256]{2,1,0:T(8,128)S(1)}, u32[]{:S(2)}, u32[]{:S(2)}) collective-permute-start(f32[4,64,256]{2,1,0:T(8,128)S(1)} %dynamic-slice_bitcast_fusion.2), channel_id=1, source_target_pairs={{0,1},{1,0},{2,3},{3,2},{4,5},{5,4},{6,7},{7,6},{8,9},{9,8},{10,11... | collective-permute-start | bytes 786440 | tf_op jit(solution)/shard_map/ppermute | solution.py:14
  63.5 7.2 %collective-permute-start.10 = (f32[64,256]{1,0:T(8,128)S(1)}, f32[64,256]{1,0:T(8,128)S(1)}, u32[]{:S(2)}, u32[]{:S(2)}) collective-permute-start(f32[64,256]{1,0:T(8,128)S(1)} %get-tuple-element.29), channel_id=1, source_target_pairs={{0,12},{4,0},{8,4},{12,8},{1,13},{5,1},{9,5},{13,9},{2,14},{6,2},{... | collective-permute-start | bytes 196616 | tf_op jit(solution)/shard_map/ppermute | solution.py:10
  64.5 8.6 %collective-permute-start.8 = (f32[64,256]{1,0:T(8,128)S(1)}, f32[64,256]{1,0:T(8,128)S(1)}, u32[]{:S(2)}, u32[]{:S(2)}) collective-permute-start(f32[64,256]{1,0:T(8,128)S(1)} %get-tuple-element.28), channel_id=1, source_target_pairs={{0,4},{4,8},{8,12},{12,0},{1,5},{5,9},{9,13},{13,1},{2,6},{6,10},{... | collective-permute-start | bytes 196616 | tf_op jit(solution)/shard_map/ppermute | solution.py:10
  65.7 10.7 %collective-permute-start.9 = (f32[64,256]{1,0:T(8,128)S(1)}, f32[64,256]{1,0:T(8,128)S(1)}, u32[]{:S(2)}, u32[]{:S(2)}) collective-permute-start(f32[64,256]{1,0:T(8,128)S(1)} %get-tuple-element.30), channel_id=1, source_target_pairs={{0,8},{4,12},{8,0},{12,4},{1,9},{5,13},{9,1},{13,5},{2,10},{6,14},... | collective-permute-start | bytes 196616 | tf_op jit(solution)/shard_map/ppermute | solution.py:10
  67.5 8.8 %collective-permute-start.13 = (f32[64,256]{1,0:T(8,128)S(1)}, f32[64,256]{1,0:T(8,128)S(1)}, u32[]{:S(2)}, u32[]{:S(2)}) collective-permute-start(f32[64,256]{1,0:T(8,128)S(1)} %get-tuple-element.31), channel_id=1, source_target_pairs={{0,4},{4,8},{8,12},{12,0},{1,5},{5,9},{9,13},{13,1},{2,6},{6,10},{... | collective-permute-start | bytes 196616 | tf_op jit(solution)/shard_map/ppermute | solution.py:10
  69.3 11.3 %collective-permute-start.14 = (f32[64,256]{1,0:T(8,128)S(1)}, f32[64,256]{1,0:T(8,128)S(1)}, u32[]{:S(2)}, u32[]{:S(2)}) collective-permute-start(f32[64,256]{1,0:T(8,128)S(1)} %get-tuple-element.33), channel_id=1, source_target_pairs={{0,8},{4,12},{8,0},{12,4},{1,9},{5,13},{9,1},{13,5},{2,10},{6,14},... | collective-permute-start | bytes 196616 | tf_op jit(solution)/shard_map/ppermute | solution.py:10
  70.7 9.8 %collective-permute-start.15 = (f32[64,256]{1,0:T(8,128)S(1)}, f32[64,256]{1,0:T(8,128)S(1)}, u32[]{:S(2)}, u32[]{:S(2)}) collective-permute-start(f32[64,256]{1,0:T(8,128)S(1)} %get-tuple-element.32), channel_id=1, source_target_pairs={{0,12},{4,0},{8,4},{12,8},{1,13},{5,1},{9,5},{13,9},{2,14},{6,2},{... | collective-permute-start | bytes 196616 | tf_op jit(solution)/shard_map/ppermute | solution.py:10
  73.1 8.4 %collective-permute-start.18 = (f32[64,256]{1,0:T(8,128)S(1)}, f32[64,256]{1,0:T(8,128)S(1)}, u32[]{:S(2)}, u32[]{:S(2)}) collective-permute-start(f32[64,256]{1,0:T(8,128)S(1)} %get-tuple-element.34), channel_id=1, source_target_pairs={{0,4},{4,8},{8,12},{12,0},{1,5},{5,9},{9,13},{13,1},{2,6},{6,10},{... | collective-permute-start | bytes 196616 | tf_op jit(solution)/shard_map/ppermute | solution.py:10
  76.3 8.6 %collective-permute-start.19 = (f32[64,256]{1,0:T(8,128)S(1)}, f32[64,256]{1,0:T(8,128)S(1)}, u32[]{:S(2)}, u32[]{:S(2)}) collective-permute-start(f32[64,256]{1,0:T(8,128)S(1)} %get-tuple-element.36), channel_id=1, source_target_pairs={{0,8},{4,12},{8,0},{12,4},{1,9},{5,13},{9,1},{13,5},{2,10},{6,14},... | collective-permute-start | bytes 196616 | tf_op jit(solution)/shard_map/ppermute | solution.py:10
  76.3 8.6 %collective-permute-start.20 = (f32[64,256]{1,0:T(8,128)S(1)}, f32[64,256]{1,0:T(8,128)S(1)}, u32[]{:S(2)}, u32[]{:S(2)}) collective-permute-start(f32[64,256]{1,0:T(8,128)S(1)} %get-tuple-element.35), channel_id=1, source_target_pairs={{0,12},{4,0},{8,4},{12,8},{1,13},{5,1},{9,5},{13,9},{2,14},{6,2},{... | collective-permute-start | bytes 196616 | tf_op jit(solution)/shard_map/ppermute | solution.py:10
  80.5 6.8 %collective-permute-start.23 = (f32[64,256]{1,0:T(8,128)S(1)}, f32[64,256]{1,0:T(8,128)S(1)}, u32[]{:S(2)}, u32[]{:S(2)}) collective-permute-start(f32[64,256]{1,0:T(8,128)S(1)} %get-tuple-element.37), channel_id=1, source_target_pairs={{0,4},{4,8},{8,12},{12,0},{1,5},{5,9},{9,13},{13,1},{2,6},{6,10},{... | collective-permute-start | bytes 196616 | tf_op jit(solution)/shard_map/ppermute | solution.py:10
  80.5 8.4 %collective-permute-start.24 = (f32[64,256]{1,0:T(8,128)S(1)}, f32[64,256]{1,0:T(8,128)S(1)}, u32[]{:S(2)}, u32[]{:S(2)}) collective-permute-start(f32[64,256]{1,0:T(8,128)S(1)} %get-tuple-element.39), channel_id=1, source_target_pairs={{0,8},{4,12},{8,0},{12,4},{1,9},{5,13},{9,1},{13,5},{2,10},{6,14},... | collective-permute-start | bytes 196616 | tf_op jit(solution)/shard_map/ppermute | solution.py:10
  81.5 7.5 %collective-permute-start.25 = (f32[64,256]{1,0:T(8,128)S(1)}, f32[64,256]{1,0:T(8,128)S(1)}, u32[]{:S(2)}, u32[]{:S(2)}) collective-permute-start(f32[64,256]{1,0:T(8,128)S(1)} %get-tuple-element.38), channel_id=1, source_target_pairs={{0,12},{4,0},{8,4},{12,8},{1,13},{5,1},{9,5},{13,9},{2,14},{6,2},{... | collective-permute-start | bytes 196616 | tf_op jit(solution)/shard_map/ppermute | solution.py:10
  (17 other events, 102.3 us)

commit v13 on v8

--- a/solution.py
+++ b/solution.py
@@ -34,8 +34,12 @@
     return payload.reshape(-1, width)
 
 
-def gather_blocks(block, n_q, n_dp):
-    got = jnp.stack([block] + [shift(block, "queue", n_q, s) for s in range(1, n_q)])
+def blocks_over_queue(block, n_q):
+    return jnp.stack([block] + [shift(block, "queue", n_q, s) for s in range(1, n_q)])
+
+
+def gather_blocks(got, n_q, n_dp):
+    block = got[0]
     for t, bit in enumerate(dp_bits(n_dp)):
         got = jnp.stack([got, swap(got, "dp", n_dp, bit)], axis=t)
     return got.reshape(n_dp * n_q * block.shape[0], block.shape[1])
@@ -61,7 +65,10 @@
     out = []
     for h in range(halves):
         g_h = grad_query[:, h * cols:(h + 1) * cols]
-        gs = jnp.concatenate([g_h, swap(g_h, "dp", n_dp, hb)], axis=0)
+        got_g = swap(g_h, "dp", n_dp, hb)
+        if h == halves - 1:
+            held, got_g = lax.optimization_barrier((held, got_g))
+        gs = jnp.concatenate([g_h, got_g], axis=0)
         term = lax.dot_general(xs, gs, (((0,), (0,)), ((), ())), preferred_element_type=jnp.float32)
         t = term.reshape((n_q,) + (2,) * len(rest) + (share, cols))
         for axis in reversed(range(len(rest))):
@@ -71,8 +78,6 @@
             send = lax.dynamic_index_in_dim(t, 1 - me, 1 + axis, keepdims=False)
             t = keep + swap(send, "dp", n_dp, bit)
         t = t.reshape(n_q, share, cols)
-        if h == halves - 1:
-            held, t = lax.optimization_barrier((held, t))
         acc = lax.dynamic_index_in_dim(t, q, 0, keepdims=False)
         for s in range(1, n_q):
             part = lax.dynamic_index_in_dim(t, (q + s) % n_q, 0, keepdims=False)
@@ -148,8 +153,10 @@
     grad_query = (
         (grad_unit - unit_f * jnp.sum(unit_f * grad_unit, -1, keepdims=True)) * inv_len
     ).astype(jnp.bfloat16)
-    grad_rows, fresh = reduce_scatter_grad(query_inputs, grad_query, n_q, n_dp, fresh)
-    blocks = gather_blocks(fresh, n_q, n_dp)
+    fresh, grad_query = lax.optimization_barrier((fresh, grad_query))
+    along = blocks_over_queue(fresh, n_q)
+    grad_rows, along = reduce_scatter_grad(query_inputs, grad_query, n_q, n_dp, along)
+    blocks = gather_blocks(along, n_q, n_dp)
 
     n_blocks = slot_owner.shape[0]
     slots_here = q * n_dp + jnp.arange(n_dp, dtype=jnp.int32)

time: 88.9 us -> 85.9 us (0.966)
  other arithmetic: 9.86 us -> 6.36 us
  local copies, waits for them, and re-layouts: 10.2 us -> 8.34 us
  matrix products: 10.3 us -> 11.2 us
    ppermute x12, waiting for transfers between devices: 11.2 us -> 17.5 us  [shift(): return lax.ppermute(x, axis, [(i, (i + step) % n) for i in range(n)])]
    ppermute x9, waiting for transfers between devices: 17.9 us -> 12.2 us  [swap(): return lax.ppermute(x, axis, [(i, i ^ bit) for i in range(n)])]
    another operation x3, other arithmetic: 3.47 us -> 1.28 us  [gather_queue(): payload = jnp.stack([payload, swap(payload, 'dp', n_dp, bit)], axis=t)]
    squeeze x2, local copies, waits for them, and re-layouts: 1.7 us -> 0.09 us  [reduce_scatter_grad(): send = lax.dynamic_index_in_dim(t, 1 - me, 1 + axis, keepdims=False)]
    add x2, other arithmetic: 1.45 us -> 0.17 us  [reduce_scatter_grad(): t = keep + swap(send, 'dp', n_dp, bit)]
    dot_general x2, matrix products: 1.9 us -> 2.84 us  [reduce_scatter_grad(): lax.dot_general(xs, gs, (((0,), (0,)), ((), ())), preferred_element_type=...]
    unnamed x23 -> x17, local copies, waits for them, and re-layouts: 2.63 us -> 2.36 us
  transfers between devices with their start and end apart: 21 -> 21, of which waited for: 7 -> 9; matrix products, arithmetic and copies ran while one was open for 29% -> 26% of each run, Pallas kernels for 0% -> 0%
where the time goes in v13:
time: 85.9 us; the launch traced here: 85.5 us
  waiting for transfers between devices  29.7 us (35%)
  starting transfers between devices  28.2 us (33%)
  matrix products  11.2 us (13%)
  local copies, waits for them, and re-layouts  8.34 us (10%)
  other arithmetic  6.36 us (7%)
  between operations  1.68 us (2%)
    ppermute x12, starting transfers between devices, shift(): return lax.ppermute(x, axis, [(i, (i + step) % n) for i in range(n)])  21.8 us
    ppermute x12, waiting for transfers between devices, shift(): return lax.ppermute(x, axis, [(i, (i + step) % n) for i in range(n)])  17.5 us
    ppermute x9, waiting for transfers between devices, swap(): return lax.ppermute(x, axis, [(i, i ^ bit) for i in range(n)])  12.2 us
    ppermute x9, starting transfers between devices, swap(): return lax.ppermute(x, axis, [(i, i ^ bit) for i in range(n)])  6.44 us
    dot_general x2, matrix products, reduce_scatter_grad(): lax.dot_general(xs, gs, (((0,), (0,)), ((), ())), preferred_element_type=...  2.84 us
    gather x1, other arithmetic, body(): b = jnp.take(owner_block, sub_block)  2.46 us
    unnamed x17, local copies, waits for them, and re-layouts  2.36 us
    dot_general x1, matrix products, body(): fresh = jnp.dot(key_inputs, key_weight, preferred_element_type=jnp.float32)  2.09 us
  transfers between devices with their start and end apart: 21, of which 9 were waited for; matrix products, arithmetic and copies ran while one was open for 26% of the time, Pallas kernels for 0%

profile of v13, /device:TPU:0, one launch (start us, length us, event | category | flops | bytes accessed | tf_op | source)
XLA Modules:
  0.0 85.5 jit_solution(3576360233651532659)
XLA Ops:
  0.7 1.7 %constant_dynamic-slice_fusion.2 = bf16[64,1024]{1,0:T(8,128)(2,1)} fusion(bf16[256,1024]{1,0:T(8,128)(2,1)} %param.12, s32[]{:T(128)S(6)} %select_n.195), kind=kLoop, calls=%fused_computation.79 | loop fusion | bytes 262148 | tf_op jit(solution)/shard_map/dynamic_slice | solution.py:30
  2.4 3.1 %collective-permute-start = (bf16[64,1024]{1,0:T(8,128)(2,1)}, bf16[64,1024]{1,0:T(8,128)(2,1)S(1)}, u32[]{:S(2)}, u32[]{:S(2)}) collective-permute-start(bf16[64,1024]{1,0:T(8,128)(2,1)} %constant_dynamic-slice_fusion.2), channel_id=1, source_target_pairs={{0,4},{4,8},{8,12},{12,0},{1,5},{5,9},{9,13},{13,1},{2,6},{6,10},{... | collective-permute-start | bytes 393224 | tf_op jit(solution)/shard_map/ppermute | solution.py:10
  5.4 2.6 %collective-permute-start.1 = (bf16[64,1024]{1,0:T(8,128)(2,1)}, bf16[64,1024]{1,0:T(8,128)(2,1)}, u32[]{:S(2)}, u32[]{:S(2)}) collective-permute-start(bf16[64,1024]{1,0:T(8,128)(2,1)} %constant_dynamic-slice_fusion.2), channel_id=1, source_target_pairs={{0,8},{4,12},{8,0},{12,4},{1,9},{5,13},{9,1},{13,5},{2,10},{6,14},... | collective-permute-start | bytes 393224 | tf_op jit(solution)/shard_map/ppermute | solution.py:10
  8.0 1.3 %collective-permute-start.2 = (bf16[64,1024]{1,0:T(8,128)(2,1)}, bf16[64,1024]{1,0:T(8,128)(2,1)}, u32[]{:S(2)}, u32[]{:S(2)}) collective-permute-start(bf16[64,1024]{1,0:T(8,128)(2,1)} %constant_dynamic-slice_fusion.2), channel_id=1, source_target_pairs={{0,12},{4,0},{8,4},{12,8},{1,13},{5,1},{9,5},{13,9},{2,14},{6,2},{... | collective-permute-start | bytes 393224 | tf_op jit(solution)/shard_map/ppermute | solution.py:10
  12.2 1.5 %collective-permute-start.5 = (bf16[256,4,128]{2,0,1:T(8,128)(2,1)}, bf16[256,4,128]{2,0,1:T(8,128)(2,1)}, u32[]{:S(2)}, u32[]{:S(2)}) collective-permute-start(bf16[256,4,128]{2,0,1:T(8,128)(2,1)} %bitcast.11), channel_id=1, source_target_pairs={{0,2},{1,3},{2,0},{3,1},{4,6},{5,7},{6,4},{7,5},{8,10},{9,11},{10,... | collective-permute-start | bytes 786440 | tf_op jit(solution)/shard_map/ppermute | solution.py:14
  13.7 1.7 %multiply_reduce_fusion.2 = (f32[256]{0:T(256)S(1)}, f32[256,1024]{1,0:T(8,128)}) fusion(bf16[256,1024]{1,0:T(8,128)(2,1)S(1)} %copy-done.3, bf16[1024,1024]{1,0:T(8,128)(2,1)S(1)} %copy-done), kind=kOutput, calls=%fused_computation.13 | convolution fusion | flops 537394944 | bytes 3671040 | tf_op jit(solution)/shard_map/dot_general | solution.py:116
  17.0 2.5 %compare_select_fusion.3 = s32[256,1]{0,1:T(1,128)S(1)} fusion(s32[]{:T(128)} %bitcast.37, s32[]{:T(128)} %bitcast.38, s32[]{:T(128)} %bitcast.40, s32[]{:T(128)} %bitcast.39, s32[]{:T(128)} %bitcast.93), kind=kLoop, calls=%fused_computation.71 | loop fusion | flops 9472 | bytes 1044 | tf_op jit(solution)/shard_map/jit(_take)/gather | solution.py:168
  21.2 2.1 %multiply_reduce_fusion.3 = (f32[16]{0:T(128)S(1)}, f32[16,1024]{1,0:T(8,128)S(1)}) fusion(bf16[16,1024]{1,0:T(8,128)(2,1)S(1)} %copy-done.5, bf16[1024,1024]{1,0:T(8,128)(2,1)} %param.11), kind=kOutput, calls=%fused_computation.67 | convolution fusion | flops 33587184 | bytes 2195520 | tf_op jit(solution)/shard_map/dot_general | solution.py:109
  23.3 7.0 %collective-permute-done.3 = bf16[3,64,1024]{2,1,0:T(8,128)(2,1)S(1)} collective-permute-done((bf16[3,64,1024]{2,1,0:T(8,128)(2,1)S(1)}, bf16[3,64,1024]{2,1,0:T(8,128)(2,1)S(1)}, u32[]{:S(2)}, u32[]{:S(2)}) %collective-permute-start.3) | collective-permute-done | bytes 393248 | tf_op jit(solution)/shard_map/ppermute | solution.py:14
  31.0 1.8 %collective-permute-done.4 = bf16[2,3,64,1024]{3,2,1,0:T(8,128)(2,1)S(1)} collective-permute-done((bf16[2,3,64,1024]{3,2,1,0:T(8,128)(2,1)S(1)}, bf16[2,3,64,1024]{3,2,1,0:T(8,128)(2,1)S(1)}, u32[]{:S(2)}, u32[]{:S(2)}) %collective-permute-start.4) | collective-permute-done | bytes 786464 | tf_op jit(solution)/shard_map/ppermute | solution.py:14
  39.5 1.5 %collective-permute-start.6 = (bf16[256,512]{1,0:T(8,128)(2,1)}, bf16[256,512]{1,0:T(8,128)(2,1)}, u32[]{:S(2)}, u32[]{:S(2)}) collective-permute-start(bf16[256,512]{1,0:T(8,128)(2,1)} %get-tuple-element.25), channel_id=1, source_target_pairs={{0,2},{1,3},{2,0},{3,1},{4,6},{5,7},{6,4},{7,5},{8,10},{9,11},{10,... | collective-permute-start | bytes 786440 | tf_op jit(solution)/shard_map/ppermute | solution.py:14
  42.2 2.1 %collective-permute-start.11 = (bf16[16,1024]{1,0:T(8,128)(2,1)S(1)}, bf16[16,1024]{1,0:T(8,128)(2,1)S(1)}, u32[]{:S(2)}, u32[]{:S(2)}) collective-permute-start(bf16[16,1024]{1,0:T(8,128)(2,1)S(1)} %multiply_convert_fusion.2), channel_id=1, source_target_pairs={{0,4},{4,8},{8,12},{12,0},{1,5},{5,9},{9,13},{13,1},{2,6},{6,10},{... | collective-permute-start | bytes 98312 | tf_op jit(solution)/shard_map/ppermute | solution.py:10
  44.9 1.9 %collective-permute-start.13 = (bf16[16,1024]{1,0:T(8,128)(2,1)S(1)}, bf16[16,1024]{1,0:T(8,128)(2,1)S(1)}, u32[]{:S(2)}, u32[]{:S(2)}) collective-permute-start(bf16[16,1024]{1,0:T(8,128)(2,1)S(1)} %multiply_convert_fusion.2), channel_id=1, source_target_pairs={{0,12},{4,0},{8,4},{12,8},{1,13},{5,1},{9,5},{13,9},{2,14},{6,2},{... | collective-permute-start | bytes 98312 | tf_op jit(solution)/shard_map/ppermute | solution.py:10
  48.0 1.3 %collective-permute-done.12 = bf16[16,1024]{1,0:T(8,128)(2,1)S(1)} collective-permute-done((bf16[16,1024]{1,0:T(8,128)(2,1)S(1)}, bf16[16,1024]{1,0:T(8,128)(2,1)S(1)}, u32[]{:S(2)}, u32[]{:S(2)}) %collective-permute-start.12) | collective-permute-done | bytes 32800 | tf_op jit(solution)/shard_map/ppermute | solution.py:10
  49.3 1.5 %collective-permute-start.19 = (bf16[4,16,1024]{2,1,0:T(8,128)(2,1)S(1)}, bf16[4,16,1024]{2,1,0:T(8,128)(2,1)S(1)}, u32[]{:S(2)}, u32[]{:S(2)}) collective-permute-start(bf16[4,16,1024]{2,1,0:T(8,128)(2,1)S(1)} %pad_maximum_fusion.7), channel_id=1, source_target_pairs={{0,2},{1,3},{2,0},{3,1},{4,6},{5,7},{6,4},{7,5},{8,10},{9,11},{10,... | collective-permute-start | bytes 393224 | tf_op jit(solution)/shard_map/ppermute | solution.py:14
  50.8 3.1 %collective-permute-done.6 = bf16[256,512]{1,0:T(8,128)(2,1)} collective-permute-done((bf16[256,512]{1,0:T(8,128)(2,1)}, bf16[256,512]{1,0:T(8,128)(2,1)}, u32[]{:S(2)}, u32[]{:S(2)}) %collective-permute-start.6) | collective-permute-done | bytes 262176 | tf_op jit(solution)/shard_map/ppermute | solution.py:14
  53.9 1.5 %fusion.8 = f32[4,2,64,512]{3,2,1,0:T(8,128)S(1)} fusion(bf16[4,2,64,512]{3,2,1,0:T(8,128)(2,1)S(1)} %bitcast.98, bf16[256,512]{1,0:T(8,128)(2,1)} %collective-permute-done.6, bf16[256,512]{1,0:T(8,128)(2,1)} %get-tuple-element.25), kind=kOutput, calls=%fused_computation.23 | convolution fusion | flops 269484032 | bytes 2097152 | tf_op jit(solution)/shard_map/dot_general | solution.py:72
  56.1 1.4 %fusion.11 = f32[4,2,64,512]{3,2,1,0:T(8,128)S(1)} fusion(bf16[4,2,64,512]{3,2,1,0:T(8,128)(2,1)S(1)} %bitcast.99, bf16[256,512]{1,0:T(8,128)(2,1)} %collective-permute-done.14, bf16[256,512]{1,0:T(8,128)(2,1)S(1)} %get-tuple-element.26), kind=kOutput, calls=%fused_computation.27 | convolution fusion | flops 269484032 | bytes 2097152 | tf_op jit(solution)/shard_map/dot_general | solution.py:72
  59.3 2.2 %collective-permute-start.10 = (f32[64,512]{1,0:T(8,128)S(1)}, f32[64,512]{1,0:T(8,128)S(1)}, u32[]{:S(2)}, u32[]{:S(2)}) collective-permute-start(f32[64,512]{1,0:T(8,128)S(1)} %get-tuple-element.23), channel_id=1, source_target_pairs={{0,12},{4,0},{8,4},{12,8},{1,13},{5,1},{9,5},{13,9},{2,14},{6,2},{... | collective-permute-start | bytes 393224 | tf_op jit(solution)/shard_map/ppermute | solution.py:10
  61.5 1.4 %collective-permute-start.9 = (f32[64,512]{1,0:T(8,128)S(1)}, f32[64,512]{1,0:T(8,128)S(1)}, u32[]{:S(2)}, u32[]{:S(2)}) collective-permute-start(f32[64,512]{1,0:T(8,128)S(1)} %get-tuple-element.24), channel_id=1, source_target_pairs={{0,8},{4,12},{8,0},{12,4},{1,9},{5,13},{9,1},{13,5},{2,10},{6,14},... | collective-permute-start | bytes 393224 | tf_op jit(solution)/shard_map/ppermute | solution.py:10
  63.0 3.0 %collective-permute-start.16 = (f32[64,512]{1,0:T(8,128)S(1)}, f32[64,512]{1,0:T(8,128)S(1)}, u32[]{:S(2)}, u32[]{:S(2)}) collective-permute-start(f32[64,512]{1,0:T(8,128)S(1)} %get-tuple-element.27), channel_id=1, source_target_pairs={{0,4},{4,8},{8,12},{12,0},{1,5},{5,9},{9,13},{13,1},{2,6},{6,10},{... | collective-permute-start | bytes 393224 | tf_op jit(solution)/shard_map/ppermute | solution.py:10
  66.5 3.1 %collective-permute-start.18 = (f32[64,512]{1,0:T(8,128)S(1)}, f32[64,512]{1,0:T(8,128)S(1)}, u32[]{:S(2)}, u32[]{:S(2)}) collective-permute-start(f32[64,512]{1,0:T(8,128)S(1)} %get-tuple-element.28), channel_id=1, source_target_pairs={{0,12},{4,0},{8,4},{12,8},{1,13},{5,1},{9,5},{13,9},{2,14},{6,2},{... | collective-permute-start | bytes 393224 | tf_op jit(solution)/shard_map/ppermute | solution.py:10
  69.6 11.7 %collective-permute-done.9 = f32[64,512]{1,0:T(8,128)S(1)} collective-permute-done((f32[64,512]{1,0:T(8,128)S(1)}, f32[64,512]{1,0:T(8,128)S(1)}, u32[]{:S(2)}, u32[]{:S(2)}) %collective-permute-start.9) | collective-permute-done | bytes 131104 | tf_op jit(solution)/shard_map/ppermute | solution.py:10
  81.4 2.7 %collective-permute-done.17 = f32[64,512]{1,0:T(8,128)S(1)} collective-permute-done((f32[64,512]{1,0:T(8,128)S(1)}, f32[64,512]{1,0:T(8,128)S(1)}, u32[]{:S(2)}, u32[]{:S(2)}) %collective-permute-start.17) | collective-permute-done | bytes 131104 | tf_op jit(solution)/shard_map/ppermute | solution.py:10
  (84 shorter events, 20.2 us)
Async XLA Ops:
  0.6 13.1 %copy-start = (bf16[1024,1024]{1,0:T(8,128)(2,1)S(1)}, bf16[1024,1024]{1,0:T(8,128)(2,1)}, u32[]{:S(2)}) copy-start(bf16[1024,1024]{1,0:T(8,128)(2,1)} %param.10) | copy-start | bytes 6291460
  0.6 13.1 %copy-start.3 = (bf16[256,1024]{1,0:T(8,128)(2,1)S(1)}, bf16[256,1024]{1,0:T(8,128)(2,1)}, u32[]{:S(2)}) copy-start(bf16[256,1024]{1,0:T(8,128)(2,1)} %param.8) | copy-start | bytes 1572868
  2.4 17.1 %collective-permute-start = (bf16[64,1024]{1,0:T(8,128)(2,1)}, bf16[64,1024]{1,0:T(8,128)(2,1)S(1)}, u32[]{:S(2)}, u32[]{:S(2)}) collective-permute-start(bf16[64,1024]{1,0:T(8,128)(2,1)} %constant_dynamic-slice_fusion.2), channel_id=1, source_target_pairs={{0,4},{4,8},{8,12},{12,0},{1,5},{5,9},{9,13},{13,1},{2,6},{6,10},{... | collective-permute-start | bytes 393224 | tf_op jit(solution)/shard_map/ppermute | solution.py:10
  5.4 14.0 %collective-permute-start.1 = (bf16[64,1024]{1,0:T(8,128)(2,1)}, bf16[64,1024]{1,0:T(8,128)(2,1)}, u32[]{:S(2)}, u32[]{:S(2)}) collective-permute-start(bf16[64,1024]{1,0:T(8,128)(2,1)} %constant_dynamic-slice_fusion.2), channel_id=1, source_target_pairs={{0,8},{4,12},{8,0},{12,4},{1,9},{5,13},{9,1},{13,5},{2,10},{6,14},... | collective-permute-start | bytes 393224 | tf_op jit(solution)/shard_map/ppermute | solution.py:10
  8.0 11.5 %collective-permute-start.2 = (bf16[64,1024]{1,0:T(8,128)(2,1)}, bf16[64,1024]{1,0:T(8,128)(2,1)}, u32[]{:S(2)}, u32[]{:S(2)}) collective-permute-start(bf16[64,1024]{1,0:T(8,128)(2,1)} %constant_dynamic-slice_fusion.2), channel_id=1, source_target_pairs={{0,12},{4,0},{8,4},{12,8},{1,13},{5,1},{9,5},{13,9},{2,14},{6,2},{... | collective-permute-start | bytes 393224 | tf_op jit(solution)/shard_map/ppermute | solution.py:10
  12.2 28.9 %collective-permute-start.5 = (bf16[256,4,128]{2,0,1:T(8,128)(2,1)}, bf16[256,4,128]{2,0,1:T(8,128)(2,1)}, u32[]{:S(2)}, u32[]{:S(2)}) collective-permute-start(bf16[256,4,128]{2,0,1:T(8,128)(2,1)} %bitcast.11), channel_id=1, source_target_pairs={{0,2},{1,3},{2,0},{3,1},{4,6},{5,7},{6,4},{7,5},{8,10},{9,11},{10,... | collective-permute-start | bytes 786440 | tf_op jit(solution)/shard_map/ppermute | solution.py:14
  20.5 9.8 %collective-permute-start.3 = (bf16[3,64,1024]{2,1,0:T(8,128)(2,1)S(1)}, bf16[3,64,1024]{2,1,0:T(8,128)(2,1)S(1)}, u32[]{:S(2)}, u32[]{:S(2)}) collective-permute-start(bf16[3,64,1024]{2,1,0:T(8,128)(2,1)S(1)} %get-tuple-element.33), channel_id=1, source_target_pairs={{0,2},{1,3},{2,0},{3,1},{4,6},{5,7},{6,4},{7,5},{8,10},{9,11},{10,... | collective-permute-start | bytes 1179656 | tf_op jit(solution)/shard_map/ppermute | solution.py:14
  30.4 2.4 %collective-permute-start.4 = (bf16[2,3,64,1024]{3,2,1,0:T(8,128)(2,1)S(1)}, bf16[2,3,64,1024]{3,2,1,0:T(8,128)(2,1)S(1)}, u32[]{:S(2)}, u32[]{:S(2)}) collective-permute-start(bf16[2,3,64,1024]{3,2,1,0:T(8,128)(2,1)S(1)} %get-tuple-element.21), channel_id=1, source_target_pairs={{0,1},{1,0},{2,3},{3,2},{4,5},{5,4},{6,7},{7,6},{8,9},{9,8},{10,11... | collective-permute-start | bytes 2359304 | tf_op jit(solution)/shard_map/ppermute | solution.py:14
  38.0 8.7 %copy-start.4 = (bf16[256,4,1,128]{0,3,2,1:T(8,128)(2,1)S(1)}, bf16[256,4,1,128]{0,3,2,1:T(8,128)(2,1)}, u32[]{:S(2)}) copy-start(bf16[256,4,1,128]{0,3,2,1:T(8,128)(2,1)} %get-tuple-element.30) | copy-start | bytes 786436
  39.0 10.3 %collective-permute-start.14 = (bf16[256,512]{1,0:T(8,128)(2,1)S(1)}, bf16[256,512]{1,0:T(8,128)(2,1)}, u32[]{:S(2)}, u32[]{:S(2)}) collective-permute-start(bf16[256,512]{1,0:T(8,128)(2,1)S(1)} %get-tuple-element.26), channel_id=1, source_target_pairs={{0,2},{1,3},{2,0},{3,1},{4,6},{5,7},{6,4},{7,5},{8,10},{9,11},{10,... | collective-permute-start | bytes 786440 | tf_op jit(solution)/shard_map/ppermute | solution.py:14
  39.5 14.4 %collective-permute-start.6 = (bf16[256,512]{1,0:T(8,128)(2,1)}, bf16[256,512]{1,0:T(8,128)(2,1)}, u32[]{:S(2)}, u32[]{:S(2)}) collective-permute-start(bf16[256,512]{1,0:T(8,128)(2,1)} %get-tuple-element.25), channel_id=1, source_target_pairs={{0,2},{1,3},{2,0},{3,1},{4,6},{5,7},{6,4},{7,5},{8,10},{9,11},{10,... | collective-permute-start | bytes 786440 | tf_op jit(solution)/shard_map/ppermute | solution.py:14
  42.2 5.8 %collective-permute-start.11 = (bf16[16,1024]{1,0:T(8,128)(2,1)S(1)}, bf16[16,1024]{1,0:T(8,128)(2,1)S(1)}, u32[]{:S(2)}, u32[]{:S(2)}) collective-permute-start(bf16[16,1024]{1,0:T(8,128)(2,1)S(1)} %multiply_convert_fusion.2), channel_id=1, source_target_pairs={{0,4},{4,8},{8,12},{12,0},{1,5},{5,9},{9,13},{13,1},{2,6},{6,10},{... | collective-permute-start | bytes 98312 | tf_op jit(solution)/shard_map/ppermute | solution.py:10
  44.3 4.9 %collective-permute-start.12 = (bf16[16,1024]{1,0:T(8,128)(2,1)S(1)}, bf16[16,1024]{1,0:T(8,128)(2,1)S(1)}, u32[]{:S(2)}, u32[]{:S(2)}) collective-permute-start(bf16[16,1024]{1,0:T(8,128)(2,1)S(1)} %multiply_convert_fusion.2), channel_id=1, source_target_pairs={{0,8},{4,12},{8,0},{12,4},{1,9},{5,13},{9,1},{13,5},{2,10},{6,14},... | collective-permute-start | bytes 98312 | tf_op jit(solution)/shard_map/ppermute | solution.py:10
  44.9 4.3 %collective-permute-start.13 = (bf16[16,1024]{1,0:T(8,128)(2,1)S(1)}, bf16[16,1024]{1,0:T(8,128)(2,1)S(1)}, u32[]{:S(2)}, u32[]{:S(2)}) collective-permute-start(bf16[16,1024]{1,0:T(8,128)(2,1)S(1)} %multiply_convert_fusion.2), channel_id=1, source_target_pairs={{0,12},{4,0},{8,4},{12,8},{1,13},{5,1},{9,5},{13,9},{2,14},{6,2},{... | collective-permute-start | bytes 98312 | tf_op jit(solution)/shard_map/ppermute | solution.py:10
  49.3 6.5 %collective-permute-start.19 = (bf16[4,16,1024]{2,1,0:T(8,128)(2,1)S(1)}, bf16[4,16,1024]{2,1,0:T(8,128)(2,1)S(1)}, u32[]{:S(2)}, u32[]{:S(2)}) collective-permute-start(bf16[4,16,1024]{2,1,0:T(8,128)(2,1)S(1)} %pad_maximum_fusion.7), channel_id=1, source_target_pairs={{0,2},{1,3},{2,0},{3,1},{4,6},{5,7},{6,4},{7,5},{8,10},{9,11},{10,... | collective-permute-start | bytes 393224 | tf_op jit(solution)/shard_map/ppermute | solution.py:14
  55.4 3.7 %collective-permute-start.7 = (f32[4,64,512]{2,1,0:T(8,128)S(1)}, f32[4,64,512]{2,1,0:T(8,128)S(1)}, u32[]{:S(2)}, u32[]{:S(2)}) collective-permute-start(f32[4,64,512]{2,1,0:T(8,128)S(1)} %dynamic-slice_bitcast_fusion.1), channel_id=1, source_target_pairs={{0,1},{1,0},{2,3},{3,2},{4,5},{5,4},{6,7},{7,6},{8,9},{9,8},{10,11... | collective-permute-start | bytes 1572872 | tf_op jit(solution)/shard_map/ppermute | solution.py:14
  55.8 2.1 %collective-permute-start.20 = (bf16[2,4,16,1024]{3,2,1,0:T(8,128)(2,1)S(1)}, bf16[2,4,16,1024]{3,2,1,0:T(8,128)(2,1)S(1)}, u32[]{:S(2)}, u32[]{:S(2)}) collective-permute-start(bf16[2,4,16,1024]{3,2,1,0:T(8,128)(2,1)S(1)} %get-tuple-element.35), channel_id=1, source_target_pairs={{0,1},{1,0},{2,3},{3,2},{4,5},{5,4},{6,7},{7,6},{8,9},{9,8},{10,11... | collective-permute-start | bytes 786440 | tf_op jit(solution)/shard_map/ppermute | solution.py:14
  57.5 5.3 %collective-permute-start.15 = (f32[4,64,512]{2,1,0:T(8,128)S(1)}, f32[4,64,512]{2,1,0:T(8,128)S(1)}, u32[]{:S(2)}, u32[]{:S(2)}) collective-permute-start(f32[4,64,512]{2,1,0:T(8,128)S(1)} %dynamic-slice_bitcast_fusion), channel_id=1, source_target_pairs={{0,1},{1,0},{2,3},{3,2},{4,5},{5,4},{6,7},{7,6},{8,9},{9,8},{10,11... | collective-permute-start | bytes 1572872 | tf_op jit(solution)/shard_map/ppermute | solution.py:14
  59.3 7.3 %collective-permute-start.10 = (f32[64,512]{1,0:T(8,128)S(1)}, f32[64,512]{1,0:T(8,128)S(1)}, u32[]{:S(2)}, u32[]{:S(2)}) collective-permute-start(f32[64,512]{1,0:T(8,128)S(1)} %get-tuple-element.23), channel_id=1, source_target_pairs={{0,12},{4,0},{8,4},{12,8},{1,13},{5,1},{9,5},{13,9},{2,14},{6,2},{... | collective-permute-start | bytes 393224 | tf_op jit(solution)/shard_map/ppermute | solution.py:10
  61.4 8.2 %collective-permute-start.8 = (f32[64,512]{1,0:T(8,128)S(1)}, f32[64,512]{1,0:T(8,128)S(1)}, u32[]{:S(2)}, u32[]{:S(2)}) collective-permute-start(f32[64,512]{1,0:T(8,128)S(1)} %get-tuple-element.22), channel_id=1, source_target_pairs={{0,4},{4,8},{8,12},{12,0},{1,5},{5,9},{9,13},{13,1},{2,6},{6,10},{... | collective-permute-start | bytes 393224 | tf_op jit(solution)/shard_map/ppermute | solution.py:10
  61.5 19.9 %collective-permute-start.9 = (f32[64,512]{1,0:T(8,128)S(1)}, f32[64,512]{1,0:T(8,128)S(1)}, u32[]{:S(2)}, u32[]{:S(2)}) collective-permute-start(f32[64,512]{1,0:T(8,128)S(1)} %get-tuple-element.24), channel_id=1, source_target_pairs={{0,8},{4,12},{8,0},{12,4},{1,9},{5,13},{9,1},{13,5},{2,10},{6,14},... | collective-permute-start | bytes 393224 | tf_op jit(solution)/shard_map/ppermute | solution.py:10
  63.0 18.4 %collective-permute-start.16 = (f32[64,512]{1,0:T(8,128)S(1)}, f32[64,512]{1,0:T(8,128)S(1)}, u32[]{:S(2)}, u32[]{:S(2)}) collective-permute-start(f32[64,512]{1,0:T(8,128)S(1)} %get-tuple-element.27), channel_id=1, source_target_pairs={{0,4},{4,8},{8,12},{12,0},{1,5},{5,9},{9,13},{13,1},{2,6},{6,10},{... | collective-permute-start | bytes 393224 | tf_op jit(solution)/shard_map/ppermute | solution.py:10
  66.0 18.1 %collective-permute-start.17 = (f32[64,512]{1,0:T(8,128)S(1)}, f32[64,512]{1,0:T(8,128)S(1)}, u32[]{:S(2)}, u32[]{:S(2)}) collective-permute-start(f32[64,512]{1,0:T(8,128)S(1)} %get-tuple-element.29), channel_id=1, source_target_pairs={{0,8},{4,12},{8,0},{12,4},{1,9},{5,13},{9,1},{13,5},{2,10},{6,14},... | collective-permute-start | bytes 393224 | tf_op jit(solution)/shard_map/ppermute | solution.py:10
  66.5 18.2 %collective-permute-start.18 = (f32[64,512]{1,0:T(8,128)S(1)}, f32[64,512]{1,0:T(8,128)S(1)}, u32[]{:S(2)}, u32[]{:S(2)}) collective-permute-start(f32[64,512]{1,0:T(8,128)S(1)} %get-tuple-element.28), channel_id=1, source_target_pairs={{0,12},{4,0},{8,4},{12,8},{1,13},{5,1},{9,5},{13,9},{2,14},{6,2},{... | collective-permute-start | bytes 393224 | tf_op jit(solution)/shard_map/ppermute | solution.py:10
  (5 other events, 19.5 us)

commit v14 on v13

--- a/solution.py
+++ b/solution.py
@@ -29,9 +29,17 @@
     piece_rows = k_dev // n_dp
     piece = lax.dynamic_slice_in_dim(queue_keys, dp * piece_rows, piece_rows, 0)
     payload = jnp.stack([shift(piece, "queue", n_q, s) for s in range(1, n_q)])
-    for t, bit in enumerate(dp_bits(n_dp)):
-        payload = jnp.stack([payload, swap(payload, "dp", n_dp, bit)], axis=t)
+    for bit in dp_bits(n_dp):
+        payload = jnp.stack([payload, swap(payload, "dp", n_dp, bit)], axis=0)
     return payload.reshape(-1, width)
+
+
+def reversed_bits(m, n_dp):
+    bits = dp_bits(n_dp)
+    r = jnp.zeros_like(m)
+    for t, bit in enumerate(bits):
+        r = r + ((m // bit) % 2) * (1 << t)
+    return r
 
 
 def blocks_over_queue(block, n_q):
@@ -133,7 +141,7 @@
     q_src = j // k_dev
     within = j % k_dev
     local = q_src == q
-    e = dp ^ (within // piece_rows)
+    e = reversed_bits(dp ^ (within // piece_rows), n_dp)
     s = (q - q_src) % n_q
     far_at = e * rows0 + (s - 1) * piece_rows + within % piece_rows
     pick_near = (local[:, None] & (within[:, None] == jnp.arange(k_dev)[None, :])).astype(

time: 85.9 us -> 85.9 us (level)
  no operation moved by 1% of the time
where the time goes in v14:
time: 85.9 us; the launch traced here: 85.5 us
  waiting for transfers between devices  29.7 us (35%)
  starting transfers between devices  28.2 us (33%)
  matrix products  11.2 us (13%)
  local copies, waits for them, and re-layouts  8.34 us (10%)
  other arithmetic  6.37 us (7%)
  between operations  1.67 us (2%)
    ppermute x12, starting transfers between devices, shift(): return lax.ppermute(x, axis, [(i, (i + step) % n) for i in range(n)])  21.8 us
    ppermute x12, waiting for transfers between devices, shift(): return lax.ppermute(x, axis, [(i, (i + step) % n) for i in range(n)])  17.5 us
    ppermute x9, waiting for transfers between devices, swap(): return lax.ppermute(x, axis, [(i, i ^ bit) for i in range(n)])  12.2 us
    ppermute x9, starting transfers between devices, swap(): return lax.ppermute(x, axis, [(i, i ^ bit) for i in range(n)])  6.44 us
    dot_general x2, matrix products, reduce_scatter_grad(): lax.dot_general(xs, gs, (((0,), (0,)), ((), ())), preferred_element_type=...  2.84 us
    gather x1, other arithmetic, body(): b = jnp.take(owner_block, sub_block)  2.46 us
    unnamed x17, local copies, waits for them, and re-layouts  2.36 us
    dot_general x1, matrix products, body(): fresh = jnp.dot(key_inputs, key_weight, preferred_element_type=jnp.float32)  2.09 us
  transfers between devices with their start and end apart: 21, of which 9 were waited for; matrix products, arithmetic and copies ran while one was open for 26% of the time, Pallas kernels for 0%

profile of v14, /device:TPU:0, one launch (start us, length us, event | category | flops | bytes accessed | tf_op | source)
XLA Modules:
  0.0 85.5 jit_solution(5267455985407752461)
XLA Ops:
  0.7 1.7 %constant_dynamic-slice_fusion.2 = bf16[64,1024]{1,0:T(8,128)(2,1)} fusion(bf16[256,1024]{1,0:T(8,128)(2,1)} %param.12, s32[]{:T(128)S(6)} %select_n.207), kind=kLoop, calls=%fused_computation.79 | loop fusion | bytes 262148 | tf_op jit(solution)/shard_map/dynamic_slice | solution.py:30
  2.4 3.1 %collective-permute-start = (bf16[64,1024]{1,0:T(8,128)(2,1)}, bf16[64,1024]{1,0:T(8,128)(2,1)S(1)}, u32[]{:S(2)}, u32[]{:S(2)}) collective-permute-start(bf16[64,1024]{1,0:T(8,128)(2,1)} %constant_dynamic-slice_fusion.2), channel_id=1, source_target_pairs={{0,4},{4,8},{8,12},{12,0},{1,5},{5,9},{9,13},{13,1},{2,6},{6,10},{... | collective-permute-start | bytes 393224 | tf_op jit(solution)/shard_map/ppermute | solution.py:10
  5.4 2.6 %collective-permute-start.1 = (bf16[64,1024]{1,0:T(8,128)(2,1)}, bf16[64,1024]{1,0:T(8,128)(2,1)}, u32[]{:S(2)}, u32[]{:S(2)}) collective-permute-start(bf16[64,1024]{1,0:T(8,128)(2,1)} %constant_dynamic-slice_fusion.2), channel_id=1, source_target_pairs={{0,8},{4,12},{8,0},{12,4},{1,9},{5,13},{9,1},{13,5},{2,10},{6,14},... | collective-permute-start | bytes 393224 | tf_op jit(solution)/shard_map/ppermute | solution.py:10
  8.0 1.3 %collective-permute-start.2 = (bf16[64,1024]{1,0:T(8,128)(2,1)}, bf16[64,1024]{1,0:T(8,128)(2,1)}, u32[]{:S(2)}, u32[]{:S(2)}) collective-permute-start(bf16[64,1024]{1,0:T(8,128)(2,1)} %constant_dynamic-slice_fusion.2), channel_id=1, source_target_pairs={{0,12},{4,0},{8,4},{12,8},{1,13},{5,1},{9,5},{13,9},{2,14},{6,2},{... | collective-permute-start | bytes 393224 | tf_op jit(solution)/shard_map/ppermute | solution.py:10
  12.2 1.5 %collective-permute-start.5 = (bf16[256,4,128]{2,0,1:T(8,128)(2,1)}, bf16[256,4,128]{2,0,1:T(8,128)(2,1)}, u32[]{:S(2)}, u32[]{:S(2)}) collective-permute-start(bf16[256,4,128]{2,0,1:T(8,128)(2,1)} %bitcast.10), channel_id=1, source_target_pairs={{0,2},{1,3},{2,0},{3,1},{4,6},{5,7},{6,4},{7,5},{8,10},{9,11},{10,... | collective-permute-start | bytes 786440 | tf_op jit(solution)/shard_map/ppermute | solution.py:14
  13.7 1.7 %multiply_reduce_fusion.2 = (f32[256]{0:T(256)S(1)}, f32[256,1024]{1,0:T(8,128)}) fusion(bf16[256,1024]{1,0:T(8,128)(2,1)S(1)} %copy-done.3, bf16[1024,1024]{1,0:T(8,128)(2,1)S(1)} %copy-done), kind=kOutput, calls=%fused_computation.13 | convolution fusion | flops 537394944 | bytes 3671040 | tf_op jit(solution)/shard_map/dot_general | solution.py:124
  17.0 2.5 %compare_select_fusion.3 = s32[256,1]{0,1:T(1,128)S(1)} fusion(s32[]{:T(128)} %bitcast.36, s32[]{:T(128)} %bitcast.37, s32[]{:T(128)} %bitcast.39, s32[]{:T(128)} %bitcast.38, s32[]{:T(128)} %bitcast.91), kind=kLoop, calls=%fused_computation.71 | loop fusion | flops 9472 | bytes 1044 | tf_op jit(solution)/shard_map/jit(_take)/gather | solution.py:176
  21.2 2.1 %multiply_reduce_fusion.3 = (f32[16]{0:T(128)S(1)}, f32[16,1024]{1,0:T(8,128)S(1)}) fusion(bf16[16,1024]{1,0:T(8,128)(2,1)S(1)} %copy-done.5, bf16[1024,1024]{1,0:T(8,128)(2,1)} %param.11), kind=kOutput, calls=%fused_computation.67 | convolution fusion | flops 33587184 | bytes 2195520 | tf_op jit(solution)/shard_map/dot_general | solution.py:117
  23.3 7.0 %collective-permute-done.3 = bf16[3,64,1024]{2,1,0:T(8,128)(2,1)S(1)} collective-permute-done((bf16[3,64,1024]{2,1,0:T(8,128)(2,1)S(1)}, bf16[3,64,1024]{2,1,0:T(8,128)(2,1)S(1)}, u32[]{:S(2)}, u32[]{:S(2)}) %collective-permute-start.3) | collective-permute-done | bytes 393248 | tf_op jit(solution)/shard_map/ppermute | solution.py:14
  31.0 1.8 %collective-permute-done.4 = bf16[2,3,64,1024]{3,2,1,0:T(8,128)(2,1)S(1)} collective-permute-done((bf16[2,3,64,1024]{3,2,1,0:T(8,128)(2,1)S(1)}, bf16[2,3,64,1024]{3,2,1,0:T(8,128)(2,1)S(1)}, u32[]{:S(2)}, u32[]{:S(2)}) %collective-permute-start.4) | collective-permute-done | bytes 786464 | tf_op jit(solution)/shard_map/ppermute | solution.py:14
  39.5 1.5 %collective-permute-start.6 = (bf16[256,512]{1,0:T(8,128)(2,1)}, bf16[256,512]{1,0:T(8,128)(2,1)}, u32[]{:S(2)}, u32[]{:S(2)}) collective-permute-start(bf16[256,512]{1,0:T(8,128)(2,1)} %get-tuple-element.25), channel_id=1, source_target_pairs={{0,2},{1,3},{2,0},{3,1},{4,6},{5,7},{6,4},{7,5},{8,10},{9,11},{10,... | collective-permute-start | bytes 786440 | tf_op jit(solution)/shard_map/ppermute | solution.py:14
  42.2 2.1 %collective-permute-start.11 = (bf16[16,1024]{1,0:T(8,128)(2,1)S(1)}, bf16[16,1024]{1,0:T(8,128)(2,1)S(1)}, u32[]{:S(2)}, u32[]{:S(2)}) collective-permute-start(bf16[16,1024]{1,0:T(8,128)(2,1)S(1)} %multiply_convert_fusion.2), channel_id=1, source_target_pairs={{0,4},{4,8},{8,12},{12,0},{1,5},{5,9},{9,13},{13,1},{2,6},{6,10},{... | collective-permute-start | bytes 98312 | tf_op jit(solution)/shard_map/ppermute | solution.py:10
  44.9 1.9 %collective-permute-start.13 = (bf16[16,1024]{1,0:T(8,128)(2,1)S(1)}, bf16[16,1024]{1,0:T(8,128)(2,1)S(1)}, u32[]{:S(2)}, u32[]{:S(2)}) collective-permute-start(bf16[16,1024]{1,0:T(8,128)(2,1)S(1)} %multiply_convert_fusion.2), channel_id=1, source_target_pairs={{0,12},{4,0},{8,4},{12,8},{1,13},{5,1},{9,5},{13,9},{2,14},{6,2},{... | collective-permute-start | bytes 98312 | tf_op jit(solution)/shard_map/ppermute | solution.py:10
  48.0 1.3 %collective-permute-done.12 = bf16[16,1024]{1,0:T(8,128)(2,1)S(1)} collective-permute-done((bf16[16,1024]{1,0:T(8,128)(2,1)S(1)}, bf16[16,1024]{1,0:T(8,128)(2,1)S(1)}, u32[]{:S(2)}, u32[]{:S(2)}) %collective-permute-start.12) | collective-permute-done | bytes 32800 | tf_op jit(solution)/shard_map/ppermute | solution.py:10
  49.3 1.5 %collective-permute-start.19 = (bf16[4,16,1024]{2,1,0:T(8,128)(2,1)S(1)}, bf16[4,16,1024]{2,1,0:T(8,128)(2,1)S(1)}, u32[]{:S(2)}, u32[]{:S(2)}) collective-permute-start(bf16[4,16,1024]{2,1,0:T(8,128)(2,1)S(1)} %pad_maximum_fusion.7), channel_id=1, source_target_pairs={{0,2},{1,3},{2,0},{3,1},{4,6},{5,7},{6,4},{7,5},{8,10},{9,11},{10,... | collective-permute-start | bytes 393224 | tf_op jit(solution)/shard_map/ppermute | solution.py:14
  50.8 3.1 %collective-permute-done.6 = bf16[256,512]{1,0:T(8,128)(2,1)} collective-permute-done((bf16[256,512]{1,0:T(8,128)(2,1)}, bf16[256,512]{1,0:T(8,128)(2,1)}, u32[]{:S(2)}, u32[]{:S(2)}) %collective-permute-start.6) | collective-permute-done | bytes 262176 | tf_op jit(solution)/shard_map/ppermute | solution.py:14
  53.9 1.5 %fusion.8 = f32[4,2,64,512]{3,2,1,0:T(8,128)S(1)} fusion(bf16[4,2,64,512]{3,2,1,0:T(8,128)(2,1)S(1)} %bitcast.96, bf16[256,512]{1,0:T(8,128)(2,1)} %collective-permute-done.6, bf16[256,512]{1,0:T(8,128)(2,1)} %get-tuple-element.25), kind=kOutput, calls=%fused_computation.23 | convolution fusion | flops 269484032 | bytes 2097152 | tf_op jit(solution)/shard_map/dot_general | solution.py:80
  56.1 1.4 %fusion.11 = f32[4,2,64,512]{3,2,1,0:T(8,128)S(1)} fusion(bf16[4,2,64,512]{3,2,1,0:T(8,128)(2,1)S(1)} %bitcast.97, bf16[256,512]{1,0:T(8,128)(2,1)} %collective-permute-done.14, bf16[256,512]{1,0:T(8,128)(2,1)S(1)} %get-tuple-element.26), kind=kOutput, calls=%fused_computation.27 | convolution fusion | flops 269484032 | bytes 2097152 | tf_op jit(solution)/shard_map/dot_general | solution.py:80
  59.3 2.2 %collective-permute-start.10 = (f32[64,512]{1,0:T(8,128)S(1)}, f32[64,512]{1,0:T(8,128)S(1)}, u32[]{:S(2)}, u32[]{:S(2)}) collective-permute-start(f32[64,512]{1,0:T(8,128)S(1)} %get-tuple-element.23), channel_id=1, source_target_pairs={{0,12},{4,0},{8,4},{12,8},{1,13},{5,1},{9,5},{13,9},{2,14},{6,2},{... | collective-permute-start | bytes 393224 | tf_op jit(solution)/shard_map/ppermute | solution.py:10
  61.5 1.4 %collective-permute-start.9 = (f32[64,512]{1,0:T(8,128)S(1)}, f32[64,512]{1,0:T(8,128)S(1)}, u32[]{:S(2)}, u32[]{:S(2)}) collective-permute-start(f32[64,512]{1,0:T(8,128)S(1)} %get-tuple-element.24), channel_id=1, source_target_pairs={{0,8},{4,12},{8,0},{12,4},{1,9},{5,13},{9,1},{13,5},{2,10},{6,14},... | collective-permute-start | bytes 393224 | tf_op jit(solution)/shard_map/ppermute | solution.py:10
  63.0 3.0 %collective-permute-start.16 = (f32[64,512]{1,0:T(8,128)S(1)}, f32[64,512]{1,0:T(8,128)S(1)}, u32[]{:S(2)}, u32[]{:S(2)}) collective-permute-start(f32[64,512]{1,0:T(8,128)S(1)} %get-tuple-element.27), channel_id=1, source_target_pairs={{0,4},{4,8},{8,12},{12,0},{1,5},{5,9},{9,13},{13,1},{2,6},{6,10},{... | collective-permute-start | bytes 393224 | tf_op jit(solution)/shard_map/ppermute | solution.py:10
  66.5 3.1 %collective-permute-start.18 = (f32[64,512]{1,0:T(8,128)S(1)}, f32[64,512]{1,0:T(8,128)S(1)}, u32[]{:S(2)}, u32[]{:S(2)}) collective-permute-start(f32[64,512]{1,0:T(8,128)S(1)} %get-tuple-element.28), channel_id=1, source_target_pairs={{0,12},{4,0},{8,4},{12,8},{1,13},{5,1},{9,5},{13,9},{2,14},{6,2},{... | collective-permute-start | bytes 393224 | tf_op jit(solution)/shard_map/ppermute | solution.py:10
  69.6 11.7 %collective-permute-done.9 = f32[64,512]{1,0:T(8,128)S(1)} collective-permute-done((f32[64,512]{1,0:T(8,128)S(1)}, f32[64,512]{1,0:T(8,128)S(1)}, u32[]{:S(2)}, u32[]{:S(2)}) %collective-permute-start.9) | collective-permute-done | bytes 131104 | tf_op jit(solution)/shard_map/ppermute | solution.py:10
  81.4 2.7 %collective-permute-done.17 = f32[64,512]{1,0:T(8,128)S(1)} collective-permute-done((f32[64,512]{1,0:T(8,128)S(1)}, f32[64,512]{1,0:T(8,128)S(1)}, u32[]{:S(2)}, u32[]{:S(2)}) %collective-permute-start.17) | collective-permute-done | bytes 131104 | tf_op jit(solution)/shard_map/ppermute | solution.py:10
  (84 shorter events, 20.3 us)
Async XLA Ops:
  0.6 13.1 %copy-start = (bf16[1024,1024]{1,0:T(8,128)(2,1)S(1)}, bf16[1024,1024]{1,0:T(8,128)(2,1)}, u32[]{:S(2)}) copy-start(bf16[1024,1024]{1,0:T(8,128)(2,1)} %param.10) | copy-start | bytes 6291460
  0.6 13.1 %copy-start.3 = (bf16[256,1024]{1,0:T(8,128)(2,1)S(1)}, bf16[256,1024]{1,0:T(8,128)(2,1)}, u32[]{:S(2)}) copy-start(bf16[256,1024]{1,0:T(8,128)(2,1)} %param.8) | copy-start | bytes 1572868
  2.4 17.1 %collective-permute-start = (bf16[64,1024]{1,0:T(8,128)(2,1)}, bf16[64,1024]{1,0:T(8,128)(2,1)S(1)}, u32[]{:S(2)}, u32[]{:S(2)}) collective-permute-start(bf16[64,1024]{1,0:T(8,128)(2,1)} %constant_dynamic-slice_fusion.2), channel_id=1, source_target_pairs={{0,4},{4,8},{8,12},{12,0},{1,5},{5,9},{9,13},{13,1},{2,6},{6,10},{... | collective-permute-start | bytes 393224 | tf_op jit(solution)/shard_map/ppermute | solution.py:10
  5.4 14.0 %collective-permute-start.1 = (bf16[64,1024]{1,0:T(8,128)(2,1)}, bf16[64,1024]{1,0:T(8,128)(2,1)}, u32[]{:S(2)}, u32[]{:S(2)}) collective-permute-start(bf16[64,1024]{1,0:T(8,128)(2,1)} %constant_dynamic-slice_fusion.2), channel_id=1, source_target_pairs={{0,8},{4,12},{8,0},{12,4},{1,9},{5,13},{9,1},{13,5},{2,10},{6,14},... | collective-permute-start | bytes 393224 | tf_op jit(solution)/shard_map/ppermute | solution.py:10
  8.0 11.5 %collective-permute-start.2 = (bf16[64,1024]{1,0:T(8,128)(2,1)}, bf16[64,1024]{1,0:T(8,128)(2,1)}, u32[]{:S(2)}, u32[]{:S(2)}) collective-permute-start(bf16[64,1024]{1,0:T(8,128)(2,1)} %constant_dynamic-slice_fusion.2), channel_id=1, source_target_pairs={{0,12},{4,0},{8,4},{12,8},{1,13},{5,1},{9,5},{13,9},{2,14},{6,2},{... | collective-permute-start | bytes 393224 | tf_op jit(solution)/shard_map/ppermute | solution.py:10
  12.2 28.9 %collective-permute-start.5 = (bf16[256,4,128]{2,0,1:T(8,128)(2,1)}, bf16[256,4,128]{2,0,1:T(8,128)(2,1)}, u32[]{:S(2)}, u32[]{:S(2)}) collective-permute-start(bf16[256,4,128]{2,0,1:T(8,128)(2,1)} %bitcast.10), channel_id=1, source_target_pairs={{0,2},{1,3},{2,0},{3,1},{4,6},{5,7},{6,4},{7,5},{8,10},{9,11},{10,... | collective-permute-start | bytes 786440 | tf_op jit(solution)/shard_map/ppermute | solution.py:14
  20.5 9.8 %collective-permute-start.3 = (bf16[3,64,1024]{2,1,0:T(8,128)(2,1)S(1)}, bf16[3,64,1024]{2,1,0:T(8,128)(2,1)S(1)}, u32[]{:S(2)}, u32[]{:S(2)}) collective-permute-start(bf16[3,64,1024]{2,1,0:T(8,128)(2,1)S(1)} %get-tuple-element.33), channel_id=1, source_target_pairs={{0,2},{1,3},{2,0},{3,1},{4,6},{5,7},{6,4},{7,5},{8,10},{9,11},{10,... | collective-permute-start | bytes 1179656 | tf_op jit(solution)/shard_map/ppermute | solution.py:14
  30.4 2.4 %collective-permute-start.4 = (bf16[2,3,64,1024]{3,2,1,0:T(8,128)(2,1)S(1)}, bf16[2,3,64,1024]{3,2,1,0:T(8,128)(2,1)S(1)}, u32[]{:S(2)}, u32[]{:S(2)}) collective-permute-start(bf16[2,3,64,1024]{3,2,1,0:T(8,128)(2,1)S(1)} %get-tuple-element.21), channel_id=1, source_target_pairs={{0,1},{1,0},{2,3},{3,2},{4,5},{5,4},{6,7},{7,6},{8,9},{9,8},{10,11... | collective-permute-start | bytes 2359304 | tf_op jit(solution)/shard_map/ppermute | solution.py:14
  38.0 8.7 %copy-start.4 = (bf16[256,4,1,128]{0,3,2,1:T(8,128)(2,1)S(1)}, bf16[256,4,1,128]{0,3,2,1:T(8,128)(2,1)}, u32[]{:S(2)}) copy-start(bf16[256,4,1,128]{0,3,2,1:T(8,128)(2,1)} %get-tuple-element.30) | copy-start | bytes 786436
  39.0 10.3 %collective-permute-start.14 = (bf16[256,512]{1,0:T(8,128)(2,1)S(1)}, bf16[256,512]{1,0:T(8,128)(2,1)}, u32[]{:S(2)}, u32[]{:S(2)}) collective-permute-start(bf16[256,512]{1,0:T(8,128)(2,1)S(1)} %get-tuple-element.26), channel_id=1, source_target_pairs={{0,2},{1,3},{2,0},{3,1},{4,6},{5,7},{6,4},{7,5},{8,10},{9,11},{10,... | collective-permute-start | bytes 786440 | tf_op jit(solution)/shard_map/ppermute | solution.py:14
  39.5 14.4 %collective-permute-start.6 = (bf16[256,512]{1,0:T(8,128)(2,1)}, bf16[256,512]{1,0:T(8,128)(2,1)}, u32[]{:S(2)}, u32[]{:S(2)}) collective-permute-start(bf16[256,512]{1,0:T(8,128)(2,1)} %get-tuple-element.25), channel_id=1, source_target_pairs={{0,2},{1,3},{2,0},{3,1},{4,6},{5,7},{6,4},{7,5},{8,10},{9,11},{10,... | collective-permute-start | bytes 786440 | tf_op jit(solution)/shard_map/ppermute | solution.py:14
  42.2 5.8 %collective-permute-start.11 = (bf16[16,1024]{1,0:T(8,128)(2,1)S(1)}, bf16[16,1024]{1,0:T(8,128)(2,1)S(1)}, u32[]{:S(2)}, u32[]{:S(2)}) collective-permute-start(bf16[16,1024]{1,0:T(8,128)(2,1)S(1)} %multiply_convert_fusion.2), channel_id=1, source_target_pairs={{0,4},{4,8},{8,12},{12,0},{1,5},{5,9},{9,13},{13,1},{2,6},{6,10},{... | collective-permute-start | bytes 98312 | tf_op jit(solution)/shard_map/ppermute | solution.py:10
  44.3 4.9 %collective-permute-start.12 = (bf16[16,1024]{1,0:T(8,128)(2,1)S(1)}, bf16[16,1024]{1,0:T(8,128)(2,1)S(1)}, u32[]{:S(2)}, u32[]{:S(2)}) collective-permute-start(bf16[16,1024]{1,0:T(8,128)(2,1)S(1)} %multiply_convert_fusion.2), channel_id=1, source_target_pairs={{0,8},{4,12},{8,0},{12,4},{1,9},{5,13},{9,1},{13,5},{2,10},{6,14},... | collective-permute-start | bytes 98312 | tf_op jit(solution)/shard_map/ppermute | solution.py:10
  44.9 4.3 %collective-permute-start.13 = (bf16[16,1024]{1,0:T(8,128)(2,1)S(1)}, bf16[16,1024]{1,0:T(8,128)(2,1)S(1)}, u32[]{:S(2)}, u32[]{:S(2)}) collective-permute-start(bf16[16,1024]{1,0:T(8,128)(2,1)S(1)} %multiply_convert_fusion.2), channel_id=1, source_target_pairs={{0,12},{4,0},{8,4},{12,8},{1,13},{5,1},{9,5},{13,9},{2,14},{6,2},{... | collective-permute-start | bytes 98312 | tf_op jit(solution)/shard_map/ppermute | solution.py:10
  49.3 6.5 %collective-permute-start.19 = (bf16[4,16,1024]{2,1,0:T(8,128)(2,1)S(1)}, bf16[4,16,1024]{2,1,0:T(8,128)(2,1)S(1)}, u32[]{:S(2)}, u32[]{:S(2)}) collective-permute-start(bf16[4,16,1024]{2,1,0:T(8,128)(2,1)S(1)} %pad_maximum_fusion.7), channel_id=1, source_target_pairs={{0,2},{1,3},{2,0},{3,1},{4,6},{5,7},{6,4},{7,5},{8,10},{9,11},{10,... | collective-permute-start | bytes 393224 | tf_op jit(solution)/shard_map/ppermute | solution.py:14
  55.4 3.7 %collective-permute-start.7 = (f32[4,64,512]{2,1,0:T(8,128)S(1)}, f32[4,64,512]{2,1,0:T(8,128)S(1)}, u32[]{:S(2)}, u32[]{:S(2)}) collective-permute-start(f32[4,64,512]{2,1,0:T(8,128)S(1)} %dynamic-slice_bitcast_fusion.1), channel_id=1, source_target_pairs={{0,1},{1,0},{2,3},{3,2},{4,5},{5,4},{6,7},{7,6},{8,9},{9,8},{10,11... | collective-permute-start | bytes 1572872 | tf_op jit(solution)/shard_map/ppermute | solution.py:14
  55.8 2.1 %collective-permute-start.20 = (bf16[2,4,16,1024]{3,2,1,0:T(8,128)(2,1)S(1)}, bf16[2,4,16,1024]{3,2,1,0:T(8,128)(2,1)S(1)}, u32[]{:S(2)}, u32[]{:S(2)}) collective-permute-start(bf16[2,4,16,1024]{3,2,1,0:T(8,128)(2,1)S(1)} %get-tuple-element.35), channel_id=1, source_target_pairs={{0,1},{1,0},{2,3},{3,2},{4,5},{5,4},{6,7},{7,6},{8,9},{9,8},{10,11... | collective-permute-start | bytes 786440 | tf_op jit(solution)/shard_map/ppermute | solution.py:14
  57.5 5.3 %collective-permute-start.15 = (f32[4,64,512]{2,1,0:T(8,128)S(1)}, f32[4,64,512]{2,1,0:T(8,128)S(1)}, u32[]{:S(2)}, u32[]{:S(2)}) collective-permute-start(f32[4,64,512]{2,1,0:T(8,128)S(1)} %dynamic-slice_bitcast_fusion), channel_id=1, source_target_pairs={{0,1},{1,0},{2,3},{3,2},{4,5},{5,4},{6,7},{7,6},{8,9},{9,8},{10,11... | collective-permute-start | bytes 1572872 | tf_op jit(solution)/shard_map/ppermute | solution.py:14
  59.3 7.3 %collective-permute-start.10 = (f32[64,512]{1,0:T(8,128)S(1)}, f32[64,512]{1,0:T(8,128)S(1)}, u32[]{:S(2)}, u32[]{:S(2)}) collective-permute-start(f32[64,512]{1,0:T(8,128)S(1)} %get-tuple-element.23), channel_id=1, source_target_pairs={{0,12},{4,0},{8,4},{12,8},{1,13},{5,1},{9,5},{13,9},{2,14},{6,2},{... | collective-permute-start | bytes 393224 | tf_op jit(solution)/shard_map/ppermute | solution.py:10
  61.4 8.2 %collective-permute-start.8 = (f32[64,512]{1,0:T(8,128)S(1)}, f32[64,512]{1,0:T(8,128)S(1)}, u32[]{:S(2)}, u32[]{:S(2)}) collective-permute-start(f32[64,512]{1,0:T(8,128)S(1)} %get-tuple-element.22), channel_id=1, source_target_pairs={{0,4},{4,8},{8,12},{12,0},{1,5},{5,9},{9,13},{13,1},{2,6},{6,10},{... | collective-permute-start | bytes 393224 | tf_op jit(solution)/shard_map/ppermute | solution.py:10
  61.5 19.9 %collective-permute-start.9 = (f32[64,512]{1,0:T(8,128)S(1)}, f32[64,512]{1,0:T(8,128)S(1)}, u32[]{:S(2)}, u32[]{:S(2)}) collective-permute-start(f32[64,512]{1,0:T(8,128)S(1)} %get-tuple-element.24), channel_id=1, source_target_pairs={{0,8},{4,12},{8,0},{12,4},{1,9},{5,13},{9,1},{13,5},{2,10},{6,14},... | collective-permute-start | bytes 393224 | tf_op jit(solution)/shard_map/ppermute | solution.py:10
  63.0 18.4 %collective-permute-start.16 = (f32[64,512]{1,0:T(8,128)S(1)}, f32[64,512]{1,0:T(8,128)S(1)}, u32[]{:S(2)}, u32[]{:S(2)}) collective-permute-start(f32[64,512]{1,0:T(8,128)S(1)} %get-tuple-element.27), channel_id=1, source_target_pairs={{0,4},{4,8},{8,12},{12,0},{1,5},{5,9},{9,13},{13,1},{2,6},{6,10},{... | collective-permute-start | bytes 393224 | tf_op jit(solution)/shard_map/ppermute | solution.py:10
  66.0 18.1 %collective-permute-start.17 = (f32[64,512]{1,0:T(8,128)S(1)}, f32[64,512]{1,0:T(8,128)S(1)}, u32[]{:S(2)}, u32[]{:S(2)}) collective-permute-start(f32[64,512]{1,0:T(8,128)S(1)} %get-tuple-element.29), channel_id=1, source_target_pairs={{0,8},{4,12},{8,0},{12,4},{1,9},{5,13},{9,1},{13,5},{2,10},{6,14},... | collective-permute-start | bytes 393224 | tf_op jit(solution)/shard_map/ppermute | solution.py:10
  66.5 18.2 %collective-permute-start.18 = (f32[64,512]{1,0:T(8,128)S(1)}, f32[64,512]{1,0:T(8,128)S(1)}, u32[]{:S(2)}, u32[]{:S(2)}) collective-permute-start(f32[64,512]{1,0:T(8,128)S(1)} %get-tuple-element.28), channel_id=1, source_target_pairs={{0,12},{4,0},{8,4},{12,8},{1,13},{5,1},{9,5},{13,9},{2,14},{6,2},{... | collective-permute-start | bytes 393224 | tf_op jit(solution)/shard_map/ppermute | solution.py:10
  (5 other events, 19.5 us)

commit v15 on v13

--- a/solution.py
+++ b/solution.py
@@ -58,7 +58,9 @@
     mine = lax.dynamic_index_in_dim(x4, side, 2, keepdims=False)
     other = lax.dynamic_index_in_dim(x4, 1 - side, 2, keepdims=False)
     got_x = swap(other, "dp", n_dp, hb)
-    xs = jnp.concatenate([mine, got_x], axis=0).reshape(2 * q_dev, n_q * hb * share)
+    x_mine = mine.reshape(q_dev, n_q * hb * share)
+    x_got = got_x.reshape(q_dev, n_q * hb * share)
+    tdims = (((0,), (0,)), ((), ()))
     rest = bits[1:]
     halves = 2
     cols = width // halves
@@ -68,8 +70,9 @@
         got_g = swap(g_h, "dp", n_dp, hb)
         if h == halves - 1:
             held, got_g = lax.optimization_barrier((held, got_g))
-        gs = jnp.concatenate([g_h, got_g], axis=0)
-        term = lax.dot_general(xs, gs, (((0,), (0,)), ((), ())), preferred_element_type=jnp.float32)
+        term = lax.dot_general(
+            x_mine, g_h, tdims, preferred_element_type=jnp.float32
+        ) + lax.dot_general(x_got, got_g, tdims, preferred_element_type=jnp.float32)
         t = term.reshape((n_q,) + (2,) * len(rest) + (share, cols))
         for axis in reversed(range(len(rest))):
             bit = rest[axis]

time: 85.9 us -> 90.7 us (1.056)
  waiting for transfers between devices: 29.7 us -> 36.7 us
  starting transfers between devices: 28.2 us -> 25.2 us
  other arithmetic: 6.36 us -> 8.68 us
    ppermute x9, waiting for transfers between devices: 12.2 us -> 22.6 us  [swap(): return lax.ppermute(x, axis, [(i, i ^ bit) for i in range(n)])]
    ppermute x12, waiting for transfers between devices: 17.5 us -> 14.2 us  [shift(): return lax.ppermute(x, axis, [(i, (i + step) % n) for i in range(n)])]
    another operation x3, other arithmetic: 1.28 us -> 3.56 us  [gather_queue(): payload = jnp.stack([payload, swap(payload, 'dp', n_dp, bit)], axis=t)]
    ppermute x12, starting transfers between devices: 21.8 us -> 19.7 us  [shift(): return lax.ppermute(x, axis, [(i, (i + step) % n) for i in range(n)])]
    dot_general x2 -> x4, matrix products: 2.84 us -> 1.18 us  [the longest x2 0.6 us: reduce_scatter_grad(): lax.dot_general(x_got, got_g, tdims, preferred_element_type=jnp.float32)]
    dot_general x1, matrix products: 0.35 us -> 1.33 us  [body(): jnp.dot(pick_near, queue_keys, preferred_element_type=jnp.float32)]
    ppermute x9, starting transfers between devices: 6.44 us -> 5.48 us  [swap(): return lax.ppermute(x, axis, [(i, i ^ bit) for i in range(n)])]
    unnamed x17 -> x21, local copies, waits for them, and re-layouts: 2.36 us -> 1.63 us
  transfers between devices with their start and end apart: 21 -> 21, of which waited for: 9 -> 10; matrix products, arithmetic and copies ran while one was open for 26% -> 20% of each run, Pallas kernels for 0% -> 0%
where the time goes in v15:
time: 90.7 us; the launch traced here: 90.4 us
  waiting for transfers between devices  36.7 us (40%)
  starting transfers between devices  25.2 us (28%)
  matrix products  10.5 us (12%)
  other arithmetic  8.68 us (10%)
  local copies, waits for them, and re-layouts  7.62 us (8%)
  between operations  1.62 us (2%)
    ppermute x9, waiting for transfers between devices, swap(): return lax.ppermute(x, axis, [(i, i ^ bit) for i in range(n)])  22.6 us
    ppermute x12, starting transfers between devices, shift(): return lax.ppermute(x, axis, [(i, (i + step) % n) for i in range(n)])  19.7 us
    ppermute x12, waiting for transfers between devices, shift(): return lax.ppermute(x, axis, [(i, (i + step) % n) for i in range(n)])  14.2 us
    ppermute x9, starting transfers between devices, swap(): return lax.ppermute(x, axis, [(i, i ^ bit) for i in range(n)])  5.48 us
    another operation x3, other arithmetic, gather_queue(): payload = jnp.stack([payload, swap(payload, 'dp', n_dp, bit)], axis=t)  3.56 us
    gather x1, other arithmetic, body(): b = jnp.take(owner_block, sub_block)  2.53 us
    dot_general x1, matrix products, body(): fresh = jnp.dot(key_inputs, key_weight, preferred_element_type=jnp.float32)  2.09 us
  transfers between devices with their start and end apart: 21, of which 10 were waited for; matrix products, arithmetic and copies ran while one was open for 20% of the time, Pallas kernels for 0%

profile of v15, /device:TPU:0, one launch (start us, length us, event | category | flops | bytes accessed | tf_op | source)
XLA Modules:
  0.0 90.4 jit_solution(6799050391617555583)
XLA Ops:
  0.7 1.7 %constant_dynamic-slice_fusion.2 = bf16[64,1024]{1,0:T(8,128)(2,1)} fusion(bf16[256,1024]{1,0:T(8,128)(2,1)} %param.12, s32[]{:T(128)S(6)} %select_n.195), kind=kLoop, calls=%fused_computation.72 | loop fusion | bytes 262148 | tf_op jit(solution)/shard_map/dynamic_slice | solution.py:30
  2.4 3.1 %collective-permute-start = (bf16[64,1024]{1,0:T(8,128)(2,1)}, bf16[64,1024]{1,0:T(8,128)(2,1)}, u32[]{:S(2)}, u32[]{:S(2)}) collective-permute-start(bf16[64,1024]{1,0:T(8,128)(2,1)} %constant_dynamic-slice_fusion.2), channel_id=1, source_target_pairs={{0,4},{4,8},{8,12},{12,0},{1,5},{5,9},{9,13},{13,1},{2,6},{6,10},{... | collective-permute-start | bytes 393224 | tf_op jit(solution)/shard_map/ppermute | solution.py:10
  5.4 2.6 %collective-permute-start.1 = (bf16[64,1024]{1,0:T(8,128)(2,1)}, bf16[64,1024]{1,0:T(8,128)(2,1)}, u32[]{:S(2)}, u32[]{:S(2)}) collective-permute-start(bf16[64,1024]{1,0:T(8,128)(2,1)} %constant_dynamic-slice_fusion.2), channel_id=1, source_target_pairs={{0,8},{4,12},{8,0},{12,4},{1,9},{5,13},{9,1},{13,5},{2,10},{6,14},... | collective-permute-start | bytes 393224 | tf_op jit(solution)/shard_map/ppermute | solution.py:10
  8.0 1.3 %collective-permute-start.2 = (bf16[64,1024]{1,0:T(8,128)(2,1)}, bf16[64,1024]{1,0:T(8,128)(2,1)}, u32[]{:S(2)}, u32[]{:S(2)}) collective-permute-start(bf16[64,1024]{1,0:T(8,128)(2,1)} %constant_dynamic-slice_fusion.2), channel_id=1, source_target_pairs={{0,12},{4,0},{8,4},{12,8},{1,13},{5,1},{9,5},{13,9},{2,14},{6,2},{... | collective-permute-start | bytes 393224 | tf_op jit(solution)/shard_map/ppermute | solution.py:10
  9.4 1.2 %copy.20 = bf16[256,1024]{0,1:T(8,128)(2,1)S(1)} copy(bf16[256,1024]{1,0:T(8,128)(2,1)} %param.8) | data formatting | bytes 1048576 | tf_op args[0]
  12.2 1.5 %collective-permute-start.5 = (bf16[256,4,128]{2,0,1:T(8,128)(2,1)}, bf16[256,4,128]{2,0,1:T(8,128)(2,1)}, u32[]{:S(2)}, u32[]{:S(2)}) collective-permute-start(bf16[256,4,128]{2,0,1:T(8,128)(2,1)} %bitcast.11), channel_id=1, source_target_pairs={{0,2},{1,3},{2,0},{3,1},{4,6},{5,7},{6,4},{7,5},{8,10},{9,11},{10,... | collective-permute-start | bytes 786440 | tf_op jit(solution)/shard_map/ppermute | solution.py:14
  13.7 1.7 %multiply_reduce_fusion.2 = (f32[256]{0:T(256)S(1)}, f32[256,1024]{1,0:T(8,128)}) fusion(bf16[256,1024]{1,0:T(8,128)(2,1)S(1)} %copy-done.6, bf16[1024,1024]{1,0:T(8,128)(2,1)S(1)} %copy-done), kind=kOutput, calls=%fused_computation.15 | convolution fusion | flops 537394944 | bytes 3671040 | tf_op jit(solution)/shard_map/dot_general | solution.py:119
  17.0 2.1 %multiply_reduce_fusion.3 = (f32[16]{0:T(128)S(1)}, f32[16,1024]{1,0:T(8,128)S(1)}) fusion(bf16[16,1024]{1,0:T(8,128)(2,1)S(1)} %copy-done.7, bf16[1024,1024]{1,0:T(8,128)(2,1)} %param.11), kind=kOutput, calls=%fused_computation.60 | convolution fusion | flops 33587184 | bytes 2195520 | tf_op jit(solution)/shard_map/dot_general | solution.py:112
  19.1 2.5 %compare_select_fusion.3 = s32[256,1]{0,1:T(1,128)S(1)} fusion(s32[]{:T(128)} %bitcast.32, s32[]{:T(128)} %bitcast.33, s32[]{:T(128)} %bitcast.35, s32[]{:T(128)} %bitcast.34, s32[]{:T(128)} %bitcast.86), kind=kLoop, calls=%fused_computation.64 | loop fusion | flops 9472 | bytes 1044 | tf_op jit(solution)/shard_map/jit(_take)/gather | solution.py:171
  23.5 9.2 %collective-permute-done.3 = bf16[3,64,1024]{2,1,0:T(8,128)(2,1)S(1)} collective-permute-done((bf16[3,64,1024]{2,1,0:T(8,128)(2,1)S(1)}, bf16[3,64,1024]{2,1,0:T(8,128)(2,1)S(1)}, u32[]{:S(2)}, u32[]{:S(2)}) %collective-permute-start.3) | collective-permute-done | bytes 393248 | tf_op jit(solution)/shard_map/ppermute | solution.py:14
  33.8 1.3 %fusion.13 = f32[256,1024]{1,0:T(8,128)} fusion(bf16[256,1024]{1,0:T(8,128)(2,1)S(1)} %copy-done.1, s32[256]{0:T(256)S(1)} %get-tuple-element.19, pred[256]{0:T(512)(128)(4,1)S(1)} %get-tuple-element.16), kind=kOutput, calls=%fused_computation.38 | convolution fusion | flops 134348800 | bytes 1574144 | tf_op jit(solution)/shard_map/dot_general | solution.py:148
  35.1 1.8 %copy.22 = bf16[256,4,128]{0,2,1:T(8,128)(2,1)} copy(bf16[256,4,128]{2,0,1:T(8,128)(2,1)} %collective-permute-done.5) | data formatting | bytes 524288 | tf_op jit(solution)/shard_map/ppermute | solution.py:14
  36.9 1.4 %pad_maximum_fusion = bf16[2,2,3,64,1024]{4,3,2,1,0:T(8,128)(2,1)S(1)} fusion(bf16[2,1,3,64,1024]{4,3,2,1,0:T(8,128)(2,1)} %bitcast.7, bf16[2,1,3,64,1024]{4,3,2,1,0:T(8,128)(2,1)S(1)} %get-tuple-element.20), kind=kLoop, calls=%fused_computation | loop fusion | flops 786432 | bytes 3145728 | tf_op jit(solution)/shard_map/stack | solution.py:33
  44.0 2.8 %collective-permute-start.13 = (bf16[16,1024]{1,0:T(8,128)(2,1)S(1)}, bf16[16,1024]{1,0:T(8,128)(2,1)S(1)}, u32[]{:S(2)}, u32[]{:S(2)}) collective-permute-start(bf16[16,1024]{1,0:T(8,128)(2,1)S(1)} %multiply_convert_fusion.2), channel_id=1, source_target_pairs={{0,12},{4,0},{8,4},{12,8},{1,13},{5,1},{9,5},{13,9},{2,14},{6,2},{... | collective-permute-start | bytes 98312 | tf_op jit(solution)/shard_map/ppermute | solution.py:10
  47.7 1.6 %collective-permute-start.6 = (bf16[256,512]{1,0:T(8,128)(2,1)S(1)}, bf16[256,512]{1,0:T(8,128)(2,1)S(1)}, u32[]{:S(2)}, u32[]{:S(2)}) collective-permute-start(bf16[256,512]{1,0:T(8,128)(2,1)S(1)} %get-tuple-element.25), channel_id=1, source_target_pairs={{0,2},{1,3},{2,0},{3,1},{4,6},{5,7},{6,4},{7,5},{8,10},{9,11},{10,... | collective-permute-start | bytes 786440 | tf_op jit(solution)/shard_map/ppermute | solution.py:14
  49.7 6.3 %collective-permute-done.14 = bf16[256,512]{1,0:T(8,128)(2,1)S(1)} collective-permute-done((bf16[256,512]{1,0:T(8,128)(2,1)S(1)}, bf16[256,512]{1,0:T(8,128)(2,1)S(1)}, u32[]{:S(2)}, u32[]{:S(2)}) %collective-permute-start.14) | collective-permute-done | bytes 262176 | tf_op jit(solution)/shard_map/ppermute | solution.py:14
  56.6 5.1 %collective-permute-done.6 = bf16[256,512]{1,0:T(8,128)(2,1)S(1)} collective-permute-done((bf16[256,512]{1,0:T(8,128)(2,1)S(1)}, bf16[256,512]{1,0:T(8,128)(2,1)S(1)}, u32[]{:S(2)}, u32[]{:S(2)}) %collective-permute-start.6) | collective-permute-done | bytes 262176 | tf_op jit(solution)/shard_map/ppermute | solution.py:14
  62.1 1.4 %collective-permute-done.19 = bf16[4,16,1024]{2,1,0:T(8,128)(2,1)S(1)} collective-permute-done((bf16[4,16,1024]{2,1,0:T(8,128)(2,1)S(1)}, bf16[4,16,1024]{2,1,0:T(8,128)(2,1)S(1)}, u32[]{:S(2)}, u32[]{:S(2)}) %collective-permute-start.19) | collective-permute-done | bytes 131104 | tf_op jit(solution)/shard_map/ppermute | solution.py:14
  68.6 1.7 %collective-permute-start.9 = (f32[64,512]{1,0:T(8,128)S(1)}, f32[64,512]{1,0:T(8,128)S(1)}, u32[]{:S(2)}, u32[]{:S(2)}) collective-permute-start(f32[64,512]{1,0:T(8,128)S(1)} %get-tuple-element.24), channel_id=1, source_target_pairs={{0,8},{4,12},{8,0},{12,4},{1,9},{5,13},{9,1},{13,5},{2,10},{6,14},... | collective-permute-start | bytes 393224 | tf_op jit(solution)/shard_map/ppermute | solution.py:10
  70.5 1.6 %collective-permute-start.16 = (f32[64,512]{1,0:T(8,128)S(1)}, f32[64,512]{1,0:T(8,128)S(1)}, u32[]{:S(2)}, u32[]{:S(2)}) collective-permute-start(f32[64,512]{1,0:T(8,128)S(1)} %get-tuple-element.27), channel_id=1, source_target_pairs={{0,4},{4,8},{8,12},{12,0},{1,5},{5,9},{9,13},{13,1},{2,6},{6,10},{... | collective-permute-start | bytes 393224 | tf_op jit(solution)/shard_map/ppermute | solution.py:10
  72.5 3.2 %collective-permute-start.18 = (f32[64,512]{1,0:T(8,128)S(1)}, f32[64,512]{1,0:T(8,128)S(1)}, u32[]{:S(2)}, u32[]{:S(2)}) collective-permute-start(f32[64,512]{1,0:T(8,128)S(1)} %get-tuple-element.28), channel_id=1, source_target_pairs={{0,12},{4,0},{8,4},{12,8},{1,13},{5,1},{9,5},{13,9},{2,14},{6,2},{... | collective-permute-start | bytes 393224 | tf_op jit(solution)/shard_map/ppermute | solution.py:10
  75.7 1.3 %collective-permute-done.8 = f32[64,512]{1,0:T(8,128)S(1)} collective-permute-done((f32[64,512]{1,0:T(8,128)S(1)}, f32[64,512]{1,0:T(8,128)S(1)}, u32[]{:S(2)}, u32[]{:S(2)}) %collective-permute-start.8) | collective-permute-done | bytes 131104 | tf_op jit(solution)/shard_map/ppermute | solution.py:10
  77.0 9.8 %collective-permute-done.9 = f32[64,512]{1,0:T(8,128)S(1)} collective-permute-done((f32[64,512]{1,0:T(8,128)S(1)}, f32[64,512]{1,0:T(8,128)S(1)}, u32[]{:S(2)}, u32[]{:S(2)}) %collective-permute-start.9) | collective-permute-done | bytes 131104 | tf_op jit(solution)/shard_map/ppermute | solution.py:10
  86.9 2.8 %collective-permute-done.17 = f32[64,512]{1,0:T(8,128)S(1)} collective-permute-done((f32[64,512]{1,0:T(8,128)S(1)}, f32[64,512]{1,0:T(8,128)S(1)}, u32[]{:S(2)}, u32[]{:S(2)}) %collective-permute-start.17) | collective-permute-done | bytes 131104 | tf_op jit(solution)/shard_map/ppermute | solution.py:10
  (89 shorter events, 19.7 us)
Async XLA Ops:
  0.6 13.1 %copy-start = (bf16[1024,1024]{1,0:T(8,128)(2,1)S(1)}, bf16[1024,1024]{1,0:T(8,128)(2,1)}, u32[]{:S(2)}) copy-start(bf16[1024,1024]{1,0:T(8,128)(2,1)} %param.10) | copy-start | bytes 6291460
  0.6 13.1 %copy-start.6 = (bf16[256,1024]{1,0:T(8,128)(2,1)S(1)}, bf16[256,1024]{1,0:T(8,128)(2,1)}, u32[]{:S(2)}) copy-start(bf16[256,1024]{1,0:T(8,128)(2,1)} %param.8) | copy-start | bytes 1572868
  2.4 19.3 %collective-permute-start = (bf16[64,1024]{1,0:T(8,128)(2,1)}, bf16[64,1024]{1,0:T(8,128)(2,1)}, u32[]{:S(2)}, u32[]{:S(2)}) collective-permute-start(bf16[64,1024]{1,0:T(8,128)(2,1)} %constant_dynamic-slice_fusion.2), channel_id=1, source_target_pairs={{0,4},{4,8},{8,12},{12,0},{1,5},{5,9},{9,13},{13,1},{2,6},{6,10},{... | collective-permute-start | bytes 393224 | tf_op jit(solution)/shard_map/ppermute | solution.py:10
  5.4 16.2 %collective-permute-start.1 = (bf16[64,1024]{1,0:T(8,128)(2,1)}, bf16[64,1024]{1,0:T(8,128)(2,1)}, u32[]{:S(2)}, u32[]{:S(2)}) collective-permute-start(bf16[64,1024]{1,0:T(8,128)(2,1)} %constant_dynamic-slice_fusion.2), channel_id=1, source_target_pairs={{0,8},{4,12},{8,0},{12,4},{1,9},{5,13},{9,1},{13,5},{2,10},{6,14},... | collective-permute-start | bytes 393224 | tf_op jit(solution)/shard_map/ppermute | solution.py:10
  8.0 13.7 %collective-permute-start.2 = (bf16[64,1024]{1,0:T(8,128)(2,1)}, bf16[64,1024]{1,0:T(8,128)(2,1)}, u32[]{:S(2)}, u32[]{:S(2)}) collective-permute-start(bf16[64,1024]{1,0:T(8,128)(2,1)} %constant_dynamic-slice_fusion.2), channel_id=1, source_target_pairs={{0,12},{4,0},{8,4},{12,8},{1,13},{5,1},{9,5},{13,9},{2,14},{6,2},{... | collective-permute-start | bytes 393224 | tf_op jit(solution)/shard_map/ppermute | solution.py:10
  12.2 22.9 %collective-permute-start.5 = (bf16[256,4,128]{2,0,1:T(8,128)(2,1)}, bf16[256,4,128]{2,0,1:T(8,128)(2,1)}, u32[]{:S(2)}, u32[]{:S(2)}) collective-permute-start(bf16[256,4,128]{2,0,1:T(8,128)(2,1)} %bitcast.11), channel_id=1, source_target_pairs={{0,2},{1,3},{2,0},{3,1},{4,6},{5,7},{6,4},{7,5},{8,10},{9,11},{10,... | collective-permute-start | bytes 786440 | tf_op jit(solution)/shard_map/ppermute | solution.py:14
  22.9 9.8 %collective-permute-start.3 = (bf16[3,64,1024]{2,1,0:T(8,128)(2,1)S(1)}, bf16[3,64,1024]{2,1,0:T(8,128)(2,1)S(1)}, u32[]{:S(2)}, u32[]{:S(2)}) collective-permute-start(bf16[3,64,1024]{2,1,0:T(8,128)(2,1)S(1)} %get-tuple-element.33), channel_id=1, source_target_pairs={{0,2},{1,3},{2,0},{3,1},{4,6},{5,7},{6,4},{7,5},{8,10},{9,11},{10,... | collective-permute-start | bytes 1179656 | tf_op jit(solution)/shard_map/ppermute | solution.py:14
  33.6 3.2 %collective-permute-start.4 = (bf16[2,3,64,1024]{3,2,1,0:T(8,128)(2,1)}, bf16[2,3,64,1024]{3,2,1,0:T(8,128)(2,1)}, u32[]{:S(2)}, u32[]{:S(2)}) collective-permute-start(bf16[2,3,64,1024]{3,2,1,0:T(8,128)(2,1)} %get-tuple-element.21), channel_id=1, source_target_pairs={{0,1},{1,0},{2,3},{3,2},{4,5},{5,4},{6,7},{7,6},{8,9},{9,8},{10,11... | collective-permute-start | bytes 2359304 | tf_op jit(solution)/shard_map/ppermute | solution.py:14
  42.9 6.7 %collective-permute-start.11 = (bf16[16,1024]{1,0:T(8,128)(2,1)S(1)}, bf16[16,1024]{1,0:T(8,128)(2,1)S(1)}, u32[]{:S(2)}, u32[]{:S(2)}) collective-permute-start(bf16[16,1024]{1,0:T(8,128)(2,1)S(1)} %multiply_convert_fusion.2), channel_id=1, source_target_pairs={{0,4},{4,8},{8,12},{12,0},{1,5},{5,9},{9,13},{13,1},{2,6},{6,10},{... | collective-permute-start | bytes 98312 | tf_op jit(solution)/shard_map/ppermute | solution.py:10
  43.7 6.1 %collective-permute-start.12 = (bf16[16,1024]{1,0:T(8,128)(2,1)S(1)}, bf16[16,1024]{1,0:T(8,128)(2,1)S(1)}, u32[]{:S(2)}, u32[]{:S(2)}) collective-permute-start(bf16[16,1024]{1,0:T(8,128)(2,1)S(1)} %multiply_convert_fusion.2), channel_id=1, source_target_pairs={{0,8},{4,12},{8,0},{12,4},{1,9},{5,13},{9,1},{13,5},{2,10},{6,14},... | collective-permute-start | bytes 98312 | tf_op jit(solution)/shard_map/ppermute | solution.py:10
  44.0 5.7 %collective-permute-start.13 = (bf16[16,1024]{1,0:T(8,128)(2,1)S(1)}, bf16[16,1024]{1,0:T(8,128)(2,1)S(1)}, u32[]{:S(2)}, u32[]{:S(2)}) collective-permute-start(bf16[16,1024]{1,0:T(8,128)(2,1)S(1)} %multiply_convert_fusion.2), channel_id=1, source_target_pairs={{0,12},{4,0},{8,4},{12,8},{1,13},{5,1},{9,5},{13,9},{2,14},{6,2},{... | collective-permute-start | bytes 98312 | tf_op jit(solution)/shard_map/ppermute | solution.py:10
  46.8 9.2 %collective-permute-start.14 = (bf16[256,512]{1,0:T(8,128)(2,1)S(1)}, bf16[256,512]{1,0:T(8,128)(2,1)S(1)}, u32[]{:S(2)}, u32[]{:S(2)}) collective-permute-start(bf16[256,512]{1,0:T(8,128)(2,1)S(1)} %get-tuple-element.26), channel_id=1, source_target_pairs={{0,2},{1,3},{2,0},{3,1},{4,6},{5,7},{6,4},{7,5},{8,10},{9,11},{10,... | collective-permute-start | bytes 786440 | tf_op jit(solution)/shard_map/ppermute | solution.py:14
  47.4 14.3 %copy-start.4 = (bf16[256,4,128]{0,2,1:T(8,128)(2,1)S(1)}, bf16[256,4,128]{0,2,1:T(8,128)(2,1)}, u32[]{:S(2)}) copy-start(bf16[256,4,128]{0,2,1:T(8,128)(2,1)} %copy.22) | copy-start | bytes 786436
  47.7 14.0 %collective-permute-start.6 = (bf16[256,512]{1,0:T(8,128)(2,1)S(1)}, bf16[256,512]{1,0:T(8,128)(2,1)S(1)}, u32[]{:S(2)}, u32[]{:S(2)}) collective-permute-start(bf16[256,512]{1,0:T(8,128)(2,1)S(1)} %get-tuple-element.25), channel_id=1, source_target_pairs={{0,2},{1,3},{2,0},{3,1},{4,6},{5,7},{6,4},{7,5},{8,10},{9,11},{10,... | collective-permute-start | bytes 786440 | tf_op jit(solution)/shard_map/ppermute | solution.py:14
  56.1 7.4 %collective-permute-start.19 = (bf16[4,16,1024]{2,1,0:T(8,128)(2,1)S(1)}, bf16[4,16,1024]{2,1,0:T(8,128)(2,1)S(1)}, u32[]{:S(2)}, u32[]{:S(2)}) collective-permute-start(bf16[4,16,1024]{2,1,0:T(8,128)(2,1)S(1)} %pad_maximum_fusion.6), channel_id=1, source_target_pairs={{0,2},{1,3},{2,0},{3,1},{4,6},{5,7},{6,4},{7,5},{8,10},{9,11},{10,... | collective-permute-start | bytes 393224 | tf_op jit(solution)/shard_map/ppermute | solution.py:14
  62.1 4.3 %collective-permute-start.7 = (f32[4,64,512]{2,1,0:T(8,128)S(1)}, f32[4,64,512]{2,1,0:T(8,128)S(1)}, u32[]{:S(2)}, u32[]{:S(2)}) collective-permute-start(f32[4,64,512]{2,1,0:T(8,128)S(1)} %dynamic-slice_bitcast_fusion.1), channel_id=1, source_target_pairs={{0,1},{1,0},{2,3},{3,2},{4,5},{5,4},{6,7},{7,6},{8,9},{9,8},{10,11... | collective-permute-start | bytes 1572872 | tf_op jit(solution)/shard_map/ppermute | solution.py:14
  63.5 1.6 %collective-permute-start.20 = (bf16[2,4,16,1024]{3,2,1,0:T(8,128)(2,1)S(1)}, bf16[2,4,16,1024]{3,2,1,0:T(8,128)(2,1)S(1)}, u32[]{:S(2)}, u32[]{:S(2)}) collective-permute-start(bf16[2,4,16,1024]{3,2,1,0:T(8,128)(2,1)S(1)} %get-tuple-element.35), channel_id=1, source_target_pairs={{0,1},{1,0},{2,3},{3,2},{4,5},{5,4},{6,7},{7,6},{8,9},{9,8},{10,11... | collective-permute-start | bytes 786440 | tf_op jit(solution)/shard_map/ppermute | solution.py:14
  64.0 6.4 %collective-permute-start.15 = (f32[4,64,512]{2,1,0:T(8,128)S(1)}, f32[4,64,512]{2,1,0:T(8,128)S(1)}, u32[]{:S(2)}, u32[]{:S(2)}) collective-permute-start(f32[4,64,512]{2,1,0:T(8,128)S(1)} %dynamic-slice_bitcast_fusion), channel_id=1, source_target_pairs={{0,1},{1,0},{2,3},{3,2},{4,5},{5,4},{6,7},{7,6},{8,9},{9,8},{10,11... | collective-permute-start | bytes 1572872 | tf_op jit(solution)/shard_map/ppermute | solution.py:14
  66.5 6.0 %collective-permute-start.10 = (f32[64,512]{1,0:T(8,128)S(1)}, f32[64,512]{1,0:T(8,128)S(1)}, u32[]{:S(2)}, u32[]{:S(2)}) collective-permute-start(f32[64,512]{1,0:T(8,128)S(1)} %get-tuple-element.23), channel_id=1, source_target_pairs={{0,12},{4,0},{8,4},{12,8},{1,13},{5,1},{9,5},{13,9},{2,14},{6,2},{... | collective-permute-start | bytes 393224 | tf_op jit(solution)/shard_map/ppermute | solution.py:10
  67.5 9.5 %collective-permute-start.8 = (f32[64,512]{1,0:T(8,128)S(1)}, f32[64,512]{1,0:T(8,128)S(1)}, u32[]{:S(2)}, u32[]{:S(2)}) collective-permute-start(f32[64,512]{1,0:T(8,128)S(1)} %get-tuple-element.22), channel_id=1, source_target_pairs={{0,4},{4,8},{8,12},{12,0},{1,5},{5,9},{9,13},{13,1},{2,6},{6,10},{... | collective-permute-start | bytes 393224 | tf_op jit(solution)/shard_map/ppermute | solution.py:10
  68.6 18.2 %collective-permute-start.9 = (f32[64,512]{1,0:T(8,128)S(1)}, f32[64,512]{1,0:T(8,128)S(1)}, u32[]{:S(2)}, u32[]{:S(2)}) collective-permute-start(f32[64,512]{1,0:T(8,128)S(1)} %get-tuple-element.24), channel_id=1, source_target_pairs={{0,8},{4,12},{8,0},{12,4},{1,9},{5,13},{9,1},{13,5},{2,10},{6,14},... | collective-permute-start | bytes 393224 | tf_op jit(solution)/shard_map/ppermute | solution.py:10
  70.5 16.4 %collective-permute-start.16 = (f32[64,512]{1,0:T(8,128)S(1)}, f32[64,512]{1,0:T(8,128)S(1)}, u32[]{:S(2)}, u32[]{:S(2)}) collective-permute-start(f32[64,512]{1,0:T(8,128)S(1)} %get-tuple-element.27), channel_id=1, source_target_pairs={{0,4},{4,8},{8,12},{12,0},{1,5},{5,9},{9,13},{13,1},{2,6},{6,10},{... | collective-permute-start | bytes 393224 | tf_op jit(solution)/shard_map/ppermute | solution.py:10
  72.1 17.5 %collective-permute-start.17 = (f32[64,512]{1,0:T(8,128)S(1)}, f32[64,512]{1,0:T(8,128)S(1)}, u32[]{:S(2)}, u32[]{:S(2)}) collective-permute-start(f32[64,512]{1,0:T(8,128)S(1)} %get-tuple-element.29), channel_id=1, source_target_pairs={{0,8},{4,12},{8,0},{12,4},{1,9},{5,13},{9,1},{13,5},{2,10},{6,14},... | collective-permute-start | bytes 393224 | tf_op jit(solution)/shard_map/ppermute | solution.py:10
  72.5 17.1 %collective-permute-start.18 = (f32[64,512]{1,0:T(8,128)S(1)}, f32[64,512]{1,0:T(8,128)S(1)}, u32[]{:S(2)}, u32[]{:S(2)}) collective-permute-start(f32[64,512]{1,0:T(8,128)S(1)} %get-tuple-element.28), channel_id=1, source_target_pairs={{0,12},{4,0},{8,4},{12,8},{1,13},{5,1},{9,5},{13,9},{2,14},{6,2},{... | collective-permute-start | bytes 393224 | tf_op jit(solution)/shard_map/ppermute | solution.py:10
  (7 other events, 31.5 us)
